TPU v7x, 512 devices: a whole 4x4x16 slice. The times are simulated.
512 devices in a mesh: ctx: 128 (over y, z, core), head: 4 (over x).
Axes of the slice: x: 4, y: 4, z: 16, core: 2. Of those that a mesh axis runs over, the one named last changes fastest.
Arguments:
- lin_query: bfloat16 [16384, 2048], P('ctx', 'head'), may hold values from -6 to 6
- lin_key: bfloat16 [16384, 2048], P('ctx', 'head'), may hold values from -6 to 6
- lin_value: bfloat16 [16384, 2048], P('ctx', 'head'), may hold values from -64 to 64
- norm_gain: float32 [2048], P('head'), may hold values from 0.1 to 1.9
- lin_grad: bfloat16 [16384, 2048], P('ctx', 'head'), may hold values from -6 to 6
- sm_query: bfloat16 [16384, 2048], P('ctx', 'head'), may hold values from -5 to 5
- sm_key: bfloat16 [16384, 2048], P('ctx', 'head'), may hold values from -5 to 5
- sm_value: bfloat16 [16384, 2048], P('ctx', 'head'), may hold values from -6 to 6
- sm_grad: bfloat16 [16384, 2048], P('ctx', 'head'), may hold values from -6 to 6
- tile_lists: int32 [128, 3], P('ctx'), may hold values from -1 to 126, as said below
Outputs:
- lin_dq: bfloat16 [16384, 2048], P('ctx', 'head')
- lin_dk: bfloat16 [16384, 2048], P('ctx', 'head')
- lin_dv: bfloat16 [16384, 2048], P('ctx', 'head')
- sm_dq: bfloat16 [16384, 2048], P('ctx', 'head')
- sm_dk: bfloat16 [16384, 2048], P('ctx', 'head')
- sm_dv: bfloat16 [16384, 2048], P('ctx', 'head')
Inputs may be any that keep to these rules, and one draw needn't show every extreme that they name: `tile_lists`: entry 0 of row i is i - 1 (-1 for i = 0). The other entries of row i are -1 or distinct tiles j with j < i - 1 and j >= i - 4.
All inputs are finite; a program needn't handle non-finite values.
Results may differ from a plain program's by a relative error of at most 0.012.
Values may be sent and summed in bfloat16 or wider, within the bound.
No kernel may reach another device: no remote copies, remote signals or barrier semaphores. Data moves between devices by JAX's collectives and lax.ppermute only.
A program may use at most 128 MiB of HBM per device.

v0:
```python
import jax
import jax.numpy as jnp
from jax import lax
from jax.sharding import PartitionSpec as P

HEAD = 128
LIN_HEADS = 16
TILE = 128
LIST = 3
SPAN = 4


def carried_in(shard, axis, join, neutral, backward):
    count = lax.axis_size(axis)
    place = lax.axis_index(axis)
    ahead = count - 1 - place if backward else place
    gathered = lax.all_gather(shard.astype(jnp.bfloat16), axis)
    state = jnp.zeros_like(shard) + jnp.asarray(neutral, shard.dtype)

    def one(turn, state):
        source = count - 1 - turn if backward else turn
        return join(state, lax.dynamic_index_in_dim(gathered, source, 0, False).astype(shard.dtype))

    return lax.fori_loop(0, ahead, one, state)


def from_behind(shard, axis, by):
    length = lax.axis_size(axis)
    pairs = [(i, i + by) for i in range(length) if 0 <= i + by < length]
    return lax.ppermute(shard, axis, pairs)


def add_states(earlier, later):
    return earlier + later


def tile_attention(query, grad, key_window, value_window, lists, shard):
    token_count, width = query.shape
    heads = width // HEAD
    tiles_dev = token_count // TILE
    window_tiles = key_window.shape[0] // TILE
    valid = lists >= 0
    local_index = jnp.where(valid, lists - (shard - SPAN) * tiles_dev, 0)
    own_index = (SPAN * tiles_dev + jnp.arange(tiles_dev, dtype=jnp.int32))[:, None]
    picked = jnp.concatenate([own_index, local_index], axis=1)
    keep = jnp.concatenate([jnp.ones((tiles_dev, 1), jnp.bool_), valid], axis=1)
    key_set = key_window.reshape(window_tiles, TILE, heads, HEAD)[picked].reshape(
        tiles_dev, (LIST + 1) * TILE, heads, HEAD
    )
    value_set = value_window.reshape(window_tiles, TILE, heads, HEAD)[picked].reshape(
        tiles_dev, (LIST + 1) * TILE, heads, HEAD
    )
    query_tiles = query.reshape(tiles_dev, TILE, heads, HEAD)
    grad_tiles = grad.reshape(tiles_dev, TILE, heads, HEAD)
    scale = HEAD ** (-0.5)
    scores = (
        jnp.einsum("athd,ashd->ahts", query_tiles, key_set, preferred_element_type=jnp.float32)
        * scale
    )
    rows_idx = jnp.arange(TILE)[:, None]
    cols_idx = jnp.arange((LIST + 1) * TILE)[None, :]
    allowed = jnp.where(cols_idx // TILE == 0, cols_idx % TILE <= rows_idx, True)
    live = jnp.repeat(keep, TILE, axis=1)
    allowed_all = allowed[None, None, :, :] & live[:, None, None, :]
    scores = jnp.where(allowed_all, scores, -jnp.inf)
    top_score = jnp.max(scores, axis=-1, keepdims=True)
    expo = jnp.exp(scores - top_score)
    probs = expo / jnp.sum(expo, axis=-1, keepdims=True)
    probs_half = probs.astype(jnp.bfloat16)
    attended = jnp.einsum(
        "ahts,ashd->athd", probs_half, value_set, preferred_element_type=jnp.float32
    )
    delta = jnp.transpose(jnp.sum(grad_tiles.astype(jnp.float32) * attended, axis=-1), (0, 2, 1))[
        ..., None
    ]
    grad_probs = jnp.einsum(
        "athd,ashd->ahts", grad_tiles, value_set, preferred_element_type=jnp.float32
    )
    grad_logits = (probs * (grad_probs - delta) * scale).astype(jnp.bfloat16)
    query_grad = (
        jnp.einsum("ahts,ashd->athd", grad_logits, key_set, preferred_element_type=jnp.float32)
        .reshape(token_count, width)
        .astype(jnp.bfloat16)
    )
    key_part = jnp.einsum(
        "ahts,athd->ashd", grad_logits, query_tiles, preferred_element_type=jnp.float32
    ).reshape(tiles_dev * (LIST + 1), TILE, width)
    value_part = jnp.einsum(
        "ahts,athd->ashd", probs_half, grad_tiles, preferred_element_type=jnp.float32
    ).reshape(tiles_dev * (LIST + 1), TILE, width)
    flat_index = picked.reshape(-1)
    key_acc = jnp.zeros((window_tiles, TILE, width), jnp.float32).at[flat_index].add(key_part)
    value_acc = jnp.zeros((window_tiles, TILE, width), jnp.float32).at[flat_index].add(value_part)
    return (query_grad, key_acc, value_acc)


def per_device(
    lin_query,
    lin_key,
    lin_value,
    norm_gain,
    lin_grad,
    sm_query,
    sm_key,
    sm_value,
    sm_grad,
    tile_lists,
):
    token_count = lin_query.shape[0]
    lin_width = lin_query.shape[1]
    heads_lin = lin_width // HEAD
    query_lin = lin_query.reshape(token_count, heads_lin, HEAD)
    key_lin = lin_key.reshape(token_count, heads_lin, HEAD)
    value_lin = lin_value.reshape(token_count, heads_lin, HEAD)
    key_value = jnp.einsum("thi,thj->hij", key_lin, value_lin, preferred_element_type=jnp.float32)
    state_low = carried_in(key_value, "ctx", add_states, jnp.zeros_like(key_value), False)
    state_half = state_low.astype(jnp.bfloat16)
    causal = jnp.tril(jnp.ones((token_count, token_count), jnp.bool_))
    attn_lin = jnp.where(
        causal[None],
        jnp.einsum("thd,shd->hts", query_lin, key_lin, preferred_element_type=jnp.float32),
        0.0,
    ).astype(jnp.bfloat16)
    output_lin = jnp.einsum(
        "hts,shd->thd", attn_lin, value_lin, preferred_element_type=jnp.float32
    ) + jnp.einsum("thi,hij->thj", query_lin, state_half, preferred_element_type=jnp.float32)
    gain_grad = norm_gain.reshape(1, heads_lin, HEAD) * lin_grad.reshape(
        token_count, heads_lin, HEAD
    ).astype(jnp.float32)
    square_sum = jnp.sum(output_lin * output_lin, axis=(1, 2))
    cross_sum = jnp.sum(gain_grad * output_lin, axis=(1, 2))
    square_sum, cross_sum = lax.psum((square_sum, cross_sum), "head")
    full_width = LIN_HEADS * HEAD
    inv_rms = lax.rsqrt(square_sum / full_width + 1e-06)[:, None, None]
    grad_out = (
        gain_grad * inv_rms - output_lin * inv_rms**3 * (cross_sum / full_width)[:, None, None]
    ).astype(jnp.bfloat16)
    adjoint_local = jnp.einsum(
        "thi,thj->hij", query_lin, grad_out, preferred_element_type=jnp.float32
    )
    adjoint_high = carried_in(adjoint_local, "ctx", add_states, jnp.zeros_like(adjoint_local), True)
    adjoint_half = adjoint_high.astype(jnp.bfloat16)
    grad_scores = jnp.where(
        causal[None],
        jnp.einsum("thd,shd->hts", grad_out, value_lin, preferred_element_type=jnp.float32),
        0.0,
    ).astype(jnp.bfloat16)
    lin_dq = jnp.einsum(
        "hts,shd->thd", grad_scores, key_lin, preferred_element_type=jnp.float32
    ) + jnp.einsum("thj,hij->thi", grad_out, state_half, preferred_element_type=jnp.float32)
    lin_dk = jnp.einsum(
        "hts,thd->shd", grad_scores, query_lin, preferred_element_type=jnp.float32
    ) + jnp.einsum("shj,hij->shi", value_lin, adjoint_half, preferred_element_type=jnp.float32)
    lin_dv = jnp.einsum(
        "hts,thd->shd", attn_lin, grad_out, preferred_element_type=jnp.float32
    ) + jnp.einsum("shi,hij->shj", key_lin, adjoint_half, preferred_element_type=jnp.float32)
    lin_dq = lin_dq.reshape(token_count, lin_width).astype(jnp.bfloat16)
    lin_dk = lin_dk.reshape(token_count, lin_width).astype(jnp.bfloat16)
    lin_dv = lin_dv.reshape(token_count, lin_width).astype(jnp.bfloat16)
    arrived = []
    for distance in range(1, SPAN + 1):
        arrived.append(from_behind((sm_key, sm_value), "ctx", distance))
    key_window = jnp.concatenate(
        [arrived[SPAN - 1 - place][0] for place in range(SPAN)] + [sm_key], axis=0
    )
    value_window = jnp.concatenate(
        [arrived[SPAN - 1 - place][1] for place in range(SPAN)] + [sm_value], axis=0
    )
    shard = lax.axis_index("ctx")
    sm_dq, key_acc, value_acc = tile_attention(
        sm_query, sm_grad, key_window, value_window, tile_lists, shard
    )
    key_total = key_acc[SPAN]
    value_total = value_acc[SPAN]
    for distance in range(1, SPAN + 1):
        back_key, back_value = from_behind(
            (
                key_acc[SPAN - distance].astype(jnp.bfloat16),
                value_acc[SPAN - distance].astype(jnp.bfloat16),
            ),
            "ctx",
            -distance,
        )
        key_total = key_total + back_key.astype(jnp.float32)
        value_total = value_total + back_value.astype(jnp.float32)
    return (
        lin_dq,
        lin_dk,
        lin_dv,
        sm_dq,
        key_total.astype(jnp.bfloat16),
        value_total.astype(jnp.bfloat16),
    )


def solution(mesh):
    placed = (
        P("ctx", "head"),
        P("ctx", "head"),
        P("ctx", "head"),
        P("head"),
        P("ctx", "head"),
        P("ctx", "head"),
        P("ctx", "head"),
        P("ctx", "head"),
        P("ctx", "head"),
        P("ctx", None),
    )
    return jax.shard_map(
        per_device,
        mesh=mesh,
        in_specs=placed,
        out_specs=(
            P("ctx", "head"),
            P("ctx", "head"),
            P("ctx", "head"),
            P("ctx", "head"),
            P("ctx", "head"),
            P("ctx", "head"),
        ),
        check_vma=False,
    )
```

profile of v0, /device:TPU:1, one launch (start us, length us, event | category | flops | bytes accessed | tf_op | source)
XLA Modules:
  0.0 595.3 jit_solution(12426632785418705177)
XLA Ops:
  7.2 1.1 copy.198
  8.3 1.7 convolution_convert_fusion.2
  10.1 1.0 copy.84
  11.2 1.2 fusion.15
  12.6 163.4 %all-gather.5.cloned.1.call-done = bf16[512,128,128]{2,1,0:T(8,128)(2,1)} async-done(((bf16[4,128,128]{2,1,0:T(8,128)(2,1)}), bf16[512,128,128]{2,1,0:T(8,128)(2,1)}) %all-gather.5.cloned.1.call-update) | async-done | bytes 16777232 | tf_op jit(solution)/shard_map/all_gather | solution.py:17
  176.1 1.0 while.22
  176.1 1.0 convert_add_fusion.4
  177.4 8.5 %all-reduce = (f32[128]{0:T(128)S(1)}, f32[128]{0:T(128)S(1)}) all-reduce(f32[128]{0:T(128)S(1)} %get-tuple-element.114, f32[128]{0:T(128)S(1)} %get-tuple-element.113), channel_id=1, replica_groups=mesh['ctx'=128,'head'=4] {'head'}, use_global_device_ids=true, to_apply=%region_5.6 | all-reduce | flops 256 | bytes 2048 | tf_op jit(solution)/shard_map/psum | solution.py:132
  187.1 7.0 %collective-permute-start = (bf16[128,512]{1,0:T(8,128)(2,1)S(1)}, bf16[128,512]{1,0:T(8,128)(2,1)S(1)}, u32[]{:S(2)}, u32[]{:S(2)}) collective-permute-start(bf16[128,512]{1,0:T(8,128)(2,1)S(1)} %copy-done.9), channel_id=1, source_target_pairs={{0,16},{4,20},{8,24},{12,28},{16,32},{20,36},{24,40},{28,44},{32,4... | collective-permute-start | bytes 393224 | tf_op jit(solution)/shard_map/ppermute | solution.py:30
  194.2 9.2 %collective-permute-start.1 = (bf16[128,512]{1,0:T(8,128)(2,1)S(1)}, bf16[128,512]{1,0:T(8,128)(2,1)S(1)}, u32[]{:S(2)}, u32[]{:S(2)}) collective-permute-start(bf16[128,512]{1,0:T(8,128)(2,1)S(1)} %copy-done.9), channel_id=1, source_target_pairs={{0,12},{4,16},{8,20},{12,24},{16,28},{20,32},{24,36},{28,40},{32,4... | collective-permute-start | bytes 393224 | tf_op jit(solution)/shard_map/ppermute | solution.py:30
  203.4 4.6 collective-permute-start.2
  208.0 1.9 collective-permute-start.3
  209.9 7.6 %collective-permute-start.4 = (bf16[128,512]{1,0:T(8,128)(2,1)}, bf16[128,512]{1,0:T(8,128)(2,1)S(1)}, u32[]{:S(2)}, u32[]{:S(2)}) collective-permute-start(bf16[128,512]{1,0:T(8,128)(2,1)} %param.21), channel_id=1, source_target_pairs={{0,16},{4,20},{8,24},{12,28},{16,32},{20,36},{24,40},{28,44},{32,4... | collective-permute-start | bytes 393224 | tf_op jit(solution)/shard_map/ppermute | solution.py:30
  220.0 8.3 %collective-permute-start.5 = (bf16[128,512]{1,0:T(8,128)(2,1)}, bf16[128,512]{1,0:T(8,128)(2,1)S(1)}, u32[]{:S(2)}, u32[]{:S(2)}) collective-permute-start(bf16[128,512]{1,0:T(8,128)(2,1)} %param.21), channel_id=1, source_target_pairs={{0,12},{4,16},{8,20},{12,24},{16,28},{20,32},{24,36},{28,40},{32,4... | collective-permute-start | bytes 393224 | tf_op jit(solution)/shard_map/ppermute | solution.py:30
  228.4 4.7 collective-permute-start.6
  233.1 1.9 collective-permute-start.7
  235.3 1.1 gather_fusion
  240.1 1.2 gather_fusion.1
  241.7 1.5 fusion.84
  243.2 1.6 fusion.18
  247.9 1.1 scatter_fusion
  250.0 1.3 collective-permute-start.11
  251.3 1.3 collective-permute-start.10
  252.6 1.3 collective-permute-start.9
  253.9 2.7 collective-permute-start.8
  257.5 1.4 reshape.447
  259.1 2.4 scatter_fusion.1
  261.7 1.3 collective-permute-start.15
  263.6 1.3 collective-permute-start.14
  264.9 3.2 collective-permute-done.10
  268.1 1.3 collective-permute-start.13
  269.4 1.9 collective-permute-start.12
  271.4 1.8 fusion.30
  273.2 1.8 collective-permute-done.15
  275.0 7.5 %collective-permute-done.14 = bf16[128,512]{1,0:T(8,128)(2,1)S(1)} collective-permute-done((bf16[128,512]{1,0:T(8,128)(2,1)S(1)}, bf16[128,512]{1,0:T(8,128)(2,1)S(1)}, u32[]{:S(2)}, u32[]{:S(2)}) %collective-permute-start.14) | collective-permute-done | bytes 131104 | tf_op jit(solution)/shard_map/ppermute | solution.py:30
  284.9 177.0 %all-gather.7.cloned.1.call-done = bf16[512,128,128]{2,1,0:T(8,128)(2,1)} async-done(((bf16[4,128,128]{2,1,0:T(8,128)(2,1)}), bf16[512,128,128]{2,1,0:T(8,128)(2,1)}) %all-gather.7.cloned.1.call-update) | async-done | bytes 16777232 | tf_op jit(solution)/shard_map/all_gather | solution.py:17
  461.9 124.3 %while.23 = (s32[]{:T(128)}, f32[4,128,128]{2,1,0:T(8,128)S(1)}, s32[]{:T(128)}, bf16[128,4,128,128]{3,2,1,0:T(8,128)(2,1)}, s32[]{:T(128)}, /*index=5*/s32[]{:T(128)}, s32[]{:T(128)}, s32[]{:T(128)}) while((s32[]{:T(128)}, f32[4,128,128]{2,1,0:T(8,128)S(1)}, s32[]{:T(128)}, bf16[128,4,128,128]{3,2,1,0:T(8,128)(2,1)}, s32[]{:T(128)}, ...), condition=%wide.region_7.8_spmd, body=%wide.region_6.7_spmd.sunk | while | flops 131078 | bytes 655503 | solution.py:24
  461.9 1.0 convert_add_fusion.5
  466.8 1.0 convert_add_fusion.5
  470.8 1.0 convert_add_fusion.5
  475.7 1.0 convert_add_fusion.5
  480.6 1.0 convert_add_fusion.5
  485.6 1.0 convert_add_fusion.5
  489.5 1.0 convert_add_fusion.5
  494.5 1.0 convert_add_fusion.5
  499.4 1.0 convert_add_fusion.5
  504.3 1.0 convert_add_fusion.5
  508.3 1.0 convert_add_fusion.5
  (228 shorter events, 129.6 us)
Async XLA Ops:
  7.2 234.5 %copy-start = (bf16[128,512]{1,0:T(8,128)(2,1)S(1)}, bf16[128,512]{1,0:T(8,128)(2,1)}, u32[]{:S(2)}) copy-start(bf16[128,512]{1,0:T(8,128)(2,1)} %param.19) | copy-start | bytes 393220
  7.2 5.2 copy-start.1
  7.2 168.8 %all-gather.5.cloned.1.call-start = ((), (), s32[]{:S(2)}) async-start(), calls=%async_computation | async-start | bytes 16908288 | tf_op jit(solution)/shard_map/all_gather | solution.py:17
  10.1 451.8 %all-gather.7.cloned.1.call-start = ((), (), s32[]{:S(2)}) async-start(), calls=%async_computation.1 | async-start | bytes 16908288 | tf_op jit(solution)/shard_map/all_gather | solution.py:17
  12.4 163.7 %copy-start.4 = (bf16[4,128,128]{2,1,0:T(8,128)(2,1)}, bf16[4,128,128]{2,1,0:T(8,128)(2,1)S(1)}, u32[]{:S(2)}) copy-start(bf16[4,128,128]{2,1,0:T(8,128)(2,1)S(1)} %fusion.15) | copy-start | bytes 393220
  176.0 1.1 copy-start.2
  176.0 1.1 copy-start.11
  177.1 10.0 %copy-start.9 = (bf16[128,512]{1,0:T(8,128)(2,1)S(1)}, bf16[128,512]{1,0:T(8,128)(2,1)}, u32[]{:S(2)}) copy-start(bf16[128,512]{1,0:T(8,128)(2,1)} %param.20) | copy-start | bytes 393220
  177.1 40.4 %copy-start.13 = (s32[1,3]{1,0:T(1,128)S(1)}, s32[1,3]{1,0:T(1,128)}, u32[]{:S(2)}) copy-start(s32[1,3]{1,0:T(1,128)} %param.23) | copy-start | bytes 40
  177.1 42.8 %copy-start.6 = (bf16[128,512]{1,0:T(8,128)(2,1)S(1)}, bf16[128,512]{1,0:T(8,128)(2,1)}, u32[]{:S(2)}) copy-start(bf16[128,512]{1,0:T(8,128)(2,1)} %param.22) | copy-start | bytes 393220
  187.1 32.9 %collective-permute-start = (bf16[128,512]{1,0:T(8,128)(2,1)S(1)}, bf16[128,512]{1,0:T(8,128)(2,1)S(1)}, u32[]{:S(2)}, u32[]{:S(2)}) collective-permute-start(bf16[128,512]{1,0:T(8,128)(2,1)S(1)} %copy-done.9), channel_id=1, source_target_pairs={{0,16},{4,20},{8,24},{12,28},{16,32},{20,36},{24,40},{28,44},{32,4... | collective-permute-start | bytes 393224 | tf_op jit(solution)/shard_map/ppermute | solution.py:30
  194.2 34.2 %collective-permute-start.1 = (bf16[128,512]{1,0:T(8,128)(2,1)S(1)}, bf16[128,512]{1,0:T(8,128)(2,1)S(1)}, u32[]{:S(2)}, u32[]{:S(2)}) collective-permute-start(bf16[128,512]{1,0:T(8,128)(2,1)S(1)} %copy-done.9), channel_id=1, source_target_pairs={{0,12},{4,16},{8,20},{12,24},{16,28},{20,32},{24,36},{28,40},{32,4... | collective-permute-start | bytes 393224 | tf_op jit(solution)/shard_map/ppermute | solution.py:30
  203.4 29.7 %collective-permute-start.2 = (bf16[128,512]{1,0:T(8,128)(2,1)S(1)}, bf16[128,512]{1,0:T(8,128)(2,1)S(1)}, u32[]{:S(2)}, u32[]{:S(2)}) collective-permute-start(bf16[128,512]{1,0:T(8,128)(2,1)S(1)} %copy-done.9), channel_id=1, source_target_pairs={{0,8},{4,12},{8,16},{12,20},{16,24},{20,28},{24,32},{28,36},{32,40... | collective-permute-start | bytes 393224 | tf_op jit(solution)/shard_map/ppermute | solution.py:30
  208.0 27.0 %collective-permute-start.3 = (bf16[128,512]{1,0:T(8,128)(2,1)S(1)}, bf16[128,512]{1,0:T(8,128)(2,1)S(1)}, u32[]{:S(2)}, u32[]{:S(2)}) collective-permute-start(bf16[128,512]{1,0:T(8,128)(2,1)S(1)} %copy-done.9), channel_id=1, source_target_pairs={{0,4},{4,8},{8,12},{12,16},{16,20},{20,24},{24,28},{28,32},{32,36}... | collective-permute-start | bytes 393224 | tf_op jit(solution)/shard_map/ppermute | solution.py:30
  209.9 25.2 %collective-permute-start.4 = (bf16[128,512]{1,0:T(8,128)(2,1)}, bf16[128,512]{1,0:T(8,128)(2,1)S(1)}, u32[]{:S(2)}, u32[]{:S(2)}) collective-permute-start(bf16[128,512]{1,0:T(8,128)(2,1)} %param.21), channel_id=1, source_target_pairs={{0,16},{4,20},{8,24},{12,28},{16,32},{20,36},{24,40},{28,44},{32,4... | collective-permute-start | bytes 393224 | tf_op jit(solution)/shard_map/ppermute | solution.py:30
  220.0 15.1 %collective-permute-start.5 = (bf16[128,512]{1,0:T(8,128)(2,1)}, bf16[128,512]{1,0:T(8,128)(2,1)S(1)}, u32[]{:S(2)}, u32[]{:S(2)}) collective-permute-start(bf16[128,512]{1,0:T(8,128)(2,1)} %param.21), channel_id=1, source_target_pairs={{0,12},{4,16},{8,20},{12,24},{16,28},{20,32},{24,36},{28,40},{32,4... | collective-permute-start | bytes 393224 | tf_op jit(solution)/shard_map/ppermute | solution.py:30
  228.4 8.4 %collective-permute-start.6 = (bf16[128,512]{1,0:T(8,128)(2,1)}, bf16[128,512]{1,0:T(8,128)(2,1)}, u32[]{:S(2)}, u32[]{:S(2)}) collective-permute-start(bf16[128,512]{1,0:T(8,128)(2,1)} %param.21), channel_id=1, source_target_pairs={{0,8},{4,12},{8,16},{12,20},{16,24},{20,28},{24,32},{28,36},{32,40... | collective-permute-start | bytes 393224 | tf_op jit(solution)/shard_map/ppermute | solution.py:30
  233.1 5.0 collective-permute-start.7
  240.1 1.6 copy-start.10
  243.2 1.6 copy-start.16
  243.2 1.6 copy-start.7
  243.2 1.6 copy-start.14
  247.3 0.6 copy-start.12
  249.0 7.5 %copy-start.8 = (bf16[128,512]{1,0:T(8,128)(2,1)S(1)}, bf16[128,512]{1,0:T(8,128)(2,1)}, u32[]{:S(2)}) copy-start(bf16[128,512]{1,0:T(8,128)(2,1)} %param.22) | copy-start | bytes 393220
  249.1 7.5 %copy-start.15 = (f32[4,128,512]{1,2,0:T(8,128)S(1)}, f32[4,128,512]{1,2,0:T(8,128)}, u32[]{:S(2)}) copy-start(f32[4,128,512]{1,2,0:T(8,128)} %get-tuple-element.145) | copy-start | bytes 3145732
  249.1 7.5 %copy-start.17 = (f32[4,128]{1,0:T(4,128)S(1)}, f32[4,128]{1,0:T(4,128)}, u32[]{:S(2)}) copy-start(f32[4,128]{1,0:T(4,128)} %copy-done.16) | copy-start | bytes 6148
  250.0 13.6 %collective-permute-start.11 = (bf16[128,512]{1,0:T(8,128)(2,1)}, bf16[128,512]{1,0:T(8,128)(2,1)}, u32[]{:S(2)}, u32[]{:S(2)}) collective-permute-start(bf16[128,512]{1,0:T(8,128)(2,1)} %get-tuple-element.138), channel_id=1, source_target_pairs={{16,0},{20,4},{24,8},{28,12},{32,16},{36,20},{40,24},{44,28},{48,3... | collective-permute-start | bytes 393224 | tf_op jit(solution)/shard_map/ppermute | solution.py:30
  251.3 16.9 %collective-permute-start.10 = (bf16[128,512]{1,0:T(8,128)(2,1)}, bf16[128,512]{1,0:T(8,128)(2,1)}, u32[]{:S(2)}, u32[]{:S(2)}) collective-permute-start(bf16[128,512]{1,0:T(8,128)(2,1)} %get-tuple-element.139), channel_id=1, source_target_pairs={{12,0},{16,4},{20,8},{24,12},{28,16},{32,20},{36,24},{40,28},{44,3... | collective-permute-start | bytes 393224 | tf_op jit(solution)/shard_map/ppermute | solution.py:30
  252.6 16.9 %collective-permute-start.9 = (bf16[128,512]{1,0:T(8,128)(2,1)}, bf16[128,512]{1,0:T(8,128)(2,1)}, u32[]{:S(2)}, u32[]{:S(2)}) collective-permute-start(bf16[128,512]{1,0:T(8,128)(2,1)} %get-tuple-element.140), channel_id=1, source_target_pairs={{8,0},{12,4},{16,8},{20,12},{24,16},{28,20},{32,24},{36,28},{40,32... | collective-permute-start | bytes 393224 | tf_op jit(solution)/shard_map/ppermute | solution.py:30
  253.9 17.5 %collective-permute-start.8 = (bf16[128,512]{1,0:T(8,128)(2,1)}, bf16[128,512]{1,0:T(8,128)(2,1)}, u32[]{:S(2)}, u32[]{:S(2)}) collective-permute-start(bf16[128,512]{1,0:T(8,128)(2,1)} %get-tuple-element.137), channel_id=1, source_target_pairs={{4,0},{8,4},{12,8},{16,12},{20,16},{24,20},{28,24},{32,28},{36,32}... | collective-permute-start | bytes 393224 | tf_op jit(solution)/shard_map/ppermute | solution.py:30
  261.7 13.4 %collective-permute-start.15 = (bf16[128,512]{1,0:T(8,128)(2,1)S(1)}, bf16[128,512]{1,0:T(8,128)(2,1)S(1)}, u32[]{:S(2)}, u32[]{:S(2)}) collective-permute-start(bf16[128,512]{1,0:T(8,128)(2,1)S(1)} %get-tuple-element.134), channel_id=1, source_target_pairs={{16,0},{20,4},{24,8},{28,12},{32,16},{36,20},{40,24},{44,28},{48,3... | collective-permute-start | bytes 393224 | tf_op jit(solution)/shard_map/ppermute | solution.py:30
  263.6 19.0 %collective-permute-start.14 = (bf16[128,512]{1,0:T(8,128)(2,1)S(1)}, bf16[128,512]{1,0:T(8,128)(2,1)S(1)}, u32[]{:S(2)}, u32[]{:S(2)}) collective-permute-start(bf16[128,512]{1,0:T(8,128)(2,1)S(1)} %get-tuple-element.135), channel_id=1, source_target_pairs={{12,0},{16,4},{20,8},{24,12},{28,16},{32,20},{36,24},{40,28},{44,3... | collective-permute-start | bytes 393224 | tf_op jit(solution)/shard_map/ppermute | solution.py:30
  268.1 14.4 %collective-permute-start.13 = (bf16[128,512]{1,0:T(8,128)(2,1)S(1)}, bf16[128,512]{1,0:T(8,128)(2,1)S(1)}, u32[]{:S(2)}, u32[]{:S(2)}) collective-permute-start(bf16[128,512]{1,0:T(8,128)(2,1)S(1)} %get-tuple-element.136), channel_id=1, source_target_pairs={{8,0},{12,4},{16,8},{20,12},{24,16},{28,20},{32,24},{36,28},{40,32... | collective-permute-start | bytes 393224 | tf_op jit(solution)/shard_map/ppermute | solution.py:30
  269.4 13.1 %collective-permute-start.12 = (bf16[128,512]{1,0:T(8,128)(2,1)S(1)}, bf16[128,512]{1,0:T(8,128)(2,1)S(1)}, u32[]{:S(2)}, u32[]{:S(2)}) collective-permute-start(bf16[128,512]{1,0:T(8,128)(2,1)S(1)} %get-tuple-element.133), channel_id=1, source_target_pairs={{4,0},{8,4},{12,8},{16,12},{20,16},{24,20},{28,24},{32,28},{36,32}... | collective-permute-start | bytes 393224 | tf_op jit(solution)/shard_map/ppermute | solution.py:30
  273.2 11.5 %copy-start.5 = (bf16[4,128,128]{2,1,0:T(8,128)(2,1)S(1)}, bf16[4,128,128]{2,1,0:T(8,128)(2,1)}, u32[]{:S(2)}) copy-start(bf16[4,128,128]{2,1,0:T(8,128)(2,1)} %copy-done.4) | copy-start | bytes 393220
  586.2 1.2 copy-start.3
Sparse Core Ops, SparseCore 0:
  11.7 164.2 all-gather.4
  187.2 274.6 all-gather.6
where the time goes:
time: 598 us; the launch traced here: 595 us
  waiting for transfers between devices  354 us (59%)
  other arithmetic  131 us (22%)
  starting transfers between devices  57.7 us (10%)
  local copies, waits for them, and re-layouts  16.7 us (3%)
  between operations  14.8 us (2%)
  matrix products  9.43 us (2%)
  blocking collectives  8.53 us (1%)
    all_gather x2, waiting for transfers between devices, carried_in(): gathered = lax.all_gather(shard.astype(jnp.bfloat16), axis)  340 us
    add x127, other arithmetic, add_states(): return earlier + later  122 us
    ppermute x16, starting transfers between devices, from_behind(): return lax.ppermute(shard, axis, pairs)  57.6 us
    ppermute x16, waiting for transfers between devices, from_behind(): return lax.ppermute(shard, axis, pairs)  13.6 us
  transfers between devices with their start and end apart: 18, of which 7 were waited for; matrix products, arithmetic and copies ran while one was open for 5% of the time, Pallas kernels for 0%

commit v1 on v0

--- a/solution.py
+++ b/solution.py
@@ -12,16 +12,16 @@
 
 def carried_in(shard, axis, join, neutral, backward):
     count = lax.axis_size(axis)
-    place = lax.axis_index(axis)
-    ahead = count - 1 - place if backward else place
-    gathered = lax.all_gather(shard.astype(jnp.bfloat16), axis)
-    state = jnp.zeros_like(shard) + jnp.asarray(neutral, shard.dtype)
-
-    def one(turn, state):
-        source = count - 1 - turn if backward else turn
-        return join(state, lax.dynamic_index_in_dim(gathered, source, 0, False).astype(shard.dtype))
-
-    return lax.fori_loop(0, ahead, one, state)
+    total = shard.astype(jnp.float32)
+    distance = 1
+    while distance < count:
+        if backward:
+            pairs = [(i, i - distance) for i in range(distance, count)]
+        else:
+            pairs = [(i, i + distance) for i in range(count - distance)]
+        total = join(total, lax.ppermute(total, axis, pairs))
+        distance *= 2
+    return (total - shard.astype(jnp.float32)).astype(shard.dtype)
 
 
 def from_behind(shard, axis, by):
@@ -157,14 +157,14 @@
     lin_dq = lin_dq.reshape(token_count, lin_width).astype(jnp.bfloat16)
     lin_dk = lin_dk.reshape(token_count, lin_width).astype(jnp.bfloat16)
     lin_dv = lin_dv.reshape(token_count, lin_width).astype(jnp.bfloat16)
-    arrived = []
-    for distance in range(1, SPAN + 1):
-        arrived.append(from_behind((sm_key, sm_value), "ctx", distance))
+    width = sm_key.shape[1]
+    pair = jnp.concatenate([sm_key, sm_value], axis=1)
+    arrived = [from_behind(pair, "ctx", distance) for distance in range(1, SPAN + 1)]
     key_window = jnp.concatenate(
-        [arrived[SPAN - 1 - place][0] for place in range(SPAN)] + [sm_key], axis=0
+        [arrived[SPAN - 1 - place][:, :width] for place in range(SPAN)] + [sm_key], axis=0
     )
     value_window = jnp.concatenate(
-        [arrived[SPAN - 1 - place][1] for place in range(SPAN)] + [sm_value], axis=0
+        [arrived[SPAN - 1 - place][:, width:] for place in range(SPAN)] + [sm_value], axis=0
     )
     shard = lax.axis_index("ctx")
     sm_dq, key_acc, value_acc = tile_attention(
@@ -173,16 +173,15 @@
     key_total = key_acc[SPAN]
     value_total = value_acc[SPAN]
     for distance in range(1, SPAN + 1):
-        back_key, back_value = from_behind(
-            (
-                key_acc[SPAN - distance].astype(jnp.bfloat16),
-                value_acc[SPAN - distance].astype(jnp.bfloat16),
-            ),
+        back = from_behind(
+            jnp.concatenate(
+                [key_acc[SPAN - distance], value_acc[SPAN - distance]], axis=1
+            ).astype(jnp.bfloat16),
             "ctx",
             -distance,
-        )
-        key_total = key_total + back_key.astype(jnp.float32)
-        value_total = value_total + back_value.astype(jnp.float32)
+        ).astype(jnp.float32)
+        key_total = key_total + back[:, :width]
+        value_total = value_total + back[:, width:]
     return (
         lin_dq,
         lin_dk,

time: 598 us -> 308 us (0.52)
  waiting for transfers between devices: 354 us -> 148 us
  other arithmetic: 131 us -> 18.2 us
  starting transfers between devices: 57.7 us -> 99.6 us
  between operations: 14.8 us -> 1.55 us
  local copies, waits for them, and re-layouts: 16.7 us -> 22.7 us
    all_gather x2 -> x0, waiting for transfers between devices: 340 us -> none  [carried_in(): gathered = lax.all_gather(shard.astype(jnp.bfloat16), axis)]
    ppermute x0 -> x14, waiting for transfers between devices: none -> 132 us  [carried_in(): total = join(total, lax.ppermute(total, axis, pairs))]
    add x127 -> x12, other arithmetic: 122 us -> 4.24 us  [add_states(): return earlier + later]
    ppermute x0 -> x14, starting transfers between devices: none -> 74.9 us  [carried_in(): total = join(total, lax.ppermute(total, axis, pairs))]
    ppermute x16 -> x8, starting transfers between devices: 57.6 us -> 24.7 us  [from_behind(): return lax.ppermute(shard, axis, pairs)]
    ppermute x16 -> x8, waiting for transfers between devices: 13.6 us -> 16.6 us  [from_behind(): return lax.ppermute(shard, axis, pairs)]
  transfers between devices with their start and end apart: 18 -> 22, of which waited for: 7 -> 15; matrix products, arithmetic and copies ran while one was open for 5% -> 13% of each run, Pallas kernels for 0% -> 0%
where the time goes in v1:
time: 308 us; the launch traced here: 307 us
  waiting for transfers between devices  148 us (48%)
  starting transfers between devices  99.6 us (32%)
  local copies, waits for them, and re-layouts  22.7 us (7%)
  other arithmetic  18.2 us (6%)
  matrix products  10.3 us (3%)
  blocking collectives  6 us (2%)
    ppermute x14, waiting for transfers between devices, carried_in(): total = join(total, lax.ppermute(total, axis, pairs))  132 us
    ppermute x14, starting transfers between devices, carried_in(): total = join(total, lax.ppermute(total, axis, pairs))  74.9 us
    ppermute x8, starting transfers between devices, from_behind(): return lax.ppermute(shard, axis, pairs)  24.7 us
    ppermute x8, waiting for transfers between devices, from_behind(): return lax.ppermute(shard, axis, pairs)  16.6 us
    unnamed x73, local copies, waits for them, and re-layouts  10.2 us
  transfers between devices with their start and end apart: 22, of which 15 were waited for; matrix products, arithmetic and copies ran while one was open for 13% of the time, Pallas kernels for 0%

profile of v1, /device:TPU:1, one launch (start us, length us, event | category | flops | bytes accessed | tf_op | source)
XLA Modules:
  0.0 306.5 jit_solution(3186351686052688645)
XLA Ops:
  0.7 1.7 constant_dynamic-update-slice_fusion.1
  2.4 1.6 constant_dynamic-update-slice_fusion
  3.9 5.1 %collective-permute-start.17 = (bf16[128,1024]{1,0:T(8,128)(2,1)}, bf16[128,1024]{1,0:T(8,128)(2,1)S(1)}, u32[]{:S(2)}, u32[]{:S(2)}) collective-permute-start(bf16[128,1024]{1,0:T(8,128)(2,1)} %constant_dynamic-update-slice_fusion), channel_id=1, source_target_pairs={{0,4},{4,8},{8,12},{12,16},{16,20},{20,24},{24,28},{28,32},{32,36}... | collective-permute-start | bytes 786440 | tf_op jit(solution)/shard_map/ppermute | solution.py:30
  9.0 3.6 %collective-permute-start.16 = (bf16[128,1024]{1,0:T(8,128)(2,1)}, bf16[128,1024]{1,0:T(8,128)(2,1)S(1)}, u32[]{:S(2)}, u32[]{:S(2)}) collective-permute-start(bf16[128,1024]{1,0:T(8,128)(2,1)} %constant_dynamic-update-slice_fusion), channel_id=1, source_target_pairs={{0,8},{4,12},{8,16},{12,20},{16,24},{20,28},{24,32},{28,36},{32,40... | collective-permute-start | bytes 786440 | tf_op jit(solution)/shard_map/ppermute | solution.py:30
  12.6 4.3 %collective-permute-start.15 = (bf16[128,1024]{1,0:T(8,128)(2,1)}, bf16[128,1024]{1,0:T(8,128)(2,1)}, u32[]{:S(2)}, u32[]{:S(2)}) collective-permute-start(bf16[128,1024]{1,0:T(8,128)(2,1)} %constant_dynamic-update-slice_fusion), channel_id=1, source_target_pairs={{0,12},{4,16},{8,20},{12,24},{16,28},{20,32},{24,36},{28,40},{32,4... | collective-permute-start | bytes 786440 | tf_op jit(solution)/shard_map/ppermute | solution.py:30
  16.8 6.1 %collective-permute-start.14 = (bf16[128,1024]{1,0:T(8,128)(2,1)}, bf16[128,1024]{1,0:T(8,128)(2,1)}, u32[]{:S(2)}, u32[]{:S(2)}) collective-permute-start(bf16[128,1024]{1,0:T(8,128)(2,1)} %constant_dynamic-update-slice_fusion), channel_id=1, source_target_pairs={{0,16},{4,20},{8,24},{12,28},{16,32},{20,36},{24,40},{28,44},{32,4... | collective-permute-start | bytes 786440 | tf_op jit(solution)/shard_map/ppermute | solution.py:30
  25.1 4.1 %collective-permute-start = (f32[4,128,128]{2,1,0:T(8,128)S(1)}, f32[4,128,128]{2,1,0:T(8,128)S(1)}, u32[]{:S(2)}, u32[]{:S(2)}) collective-permute-start(f32[4,128,128]{2,1,0:T(8,128)S(1)} %fusion.31), channel_id=1, source_target_pairs={{0,4},{4,8},{8,12},{12,16},{16,20},{20,24},{24,28},{28,32},{32,36}... | collective-permute-start | bytes 786440 | tf_op jit(solution)/shard_map/ppermute | solution.py:22
  31.5 6.2 %collective-permute-done = f32[4,128,128]{2,1,0:T(8,128)S(1)} collective-permute-done((f32[4,128,128]{2,1,0:T(8,128)S(1)}, f32[4,128,128]{2,1,0:T(8,128)S(1)}, u32[]{:S(2)}, u32[]{:S(2)}) %collective-permute-start) | collective-permute-done | bytes 262176 | tf_op jit(solution)/shard_map/ppermute | solution.py:22
  37.8 6.4 %collective-permute-start.1 = (f32[4,128,128]{2,1,0:T(8,128)S(1)}, f32[4,128,128]{2,1,0:T(8,128)S(1)}, u32[]{:S(2)}, u32[]{:S(2)}) collective-permute-start(f32[4,128,128]{2,1,0:T(8,128)S(1)} %add.135), channel_id=1, source_target_pairs={{0,8},{4,12},{8,16},{12,20},{16,24},{20,28},{24,32},{28,36},{32,40... | collective-permute-start | bytes 786440 | tf_op jit(solution)/shard_map/ppermute | solution.py:22
  45.7 1.6 slice_dynamic-update-slice_fusion.3
  47.4 2.9 collective-permute-done.1
  50.3 6.1 %collective-permute-start.2 = (f32[4,128,128]{2,1,0:T(8,128)S(1)}, f32[4,128,128]{2,1,0:T(8,128)S(1)}, u32[]{:S(2)}, u32[]{:S(2)}) collective-permute-start(f32[4,128,128]{2,1,0:T(8,128)S(1)} %add.136), channel_id=1, source_target_pairs={{0,16},{4,20},{8,24},{12,28},{16,32},{20,36},{24,40},{28,44},{32,4... | collective-permute-start | bytes 786440 | tf_op jit(solution)/shard_map/ppermute | solution.py:22
  56.4 1.6 slice_dynamic-update-slice_fusion.2
  58.7 7.1 %collective-permute-done.2 = f32[4,128,128]{2,1,0:T(8,128)S(1)} collective-permute-done((f32[4,128,128]{2,1,0:T(8,128)S(1)}, f32[4,128,128]{2,1,0:T(8,128)S(1)}, u32[]{:S(2)}, u32[]{:S(2)}) %collective-permute-start.2) | collective-permute-done | bytes 262176 | tf_op jit(solution)/shard_map/ppermute | solution.py:22
  65.9 11.0 %collective-permute-start.3 = (f32[4,128,128]{2,1,0:T(8,128)S(1)}, f32[4,128,128]{2,1,0:T(8,128)}, u32[]{:S(2)}, u32[]{:S(2)}) collective-permute-start(f32[4,128,128]{2,1,0:T(8,128)S(1)} %add.137), channel_id=1, source_target_pairs={{0,32},{4,36},{8,40},{12,44},{16,48},{20,52},{24,56},{28,60},{32,6... | collective-permute-start | bytes 786440 | tf_op jit(solution)/shard_map/ppermute | solution.py:22
  78.3 1.6 reshape.394
  81.4 16.6 %collective-permute-done.3 = f32[4,128,128]{2,1,0:T(8,128)} collective-permute-done((f32[4,128,128]{2,1,0:T(8,128)S(1)}, f32[4,128,128]{2,1,0:T(8,128)}, u32[]{:S(2)}, u32[]{:S(2)}) %collective-permute-start.3) | collective-permute-done | bytes 262176 | tf_op jit(solution)/shard_map/ppermute | solution.py:22
  99.0 2.0 collective-permute-start.4
  101.0 1.5 fusion.72
  104.2 2.6 convolution_bitcast_fusion
  106.8 4.6 %collective-permute-done.4 = f32[4,128,128]{2,1,0:T(8,128)} collective-permute-done((f32[4,128,128]{2,1,0:T(8,128)S(1)}, f32[4,128,128]{2,1,0:T(8,128)}, u32[]{:S(2)}, u32[]{:S(2)}) %collective-permute-start.4) | collective-permute-done | bytes 262176 | tf_op jit(solution)/shard_map/ppermute | solution.py:22
  112.4 25.7 %collective-permute-start.5 = (f32[4,128,128]{2,1,0:T(8,128)S(1)}, f32[4,128,128]{2,1,0:T(8,128)S(1)}, u32[]{:S(2)}, u32[]{:S(2)}) collective-permute-start(f32[4,128,128]{2,1,0:T(8,128)S(1)} %add.139), channel_id=1, source_target_pairs={{0,128},{4,132},{8,136},{12,140},{16,144},{20,148},{24,152},{28,15... | collective-permute-start | bytes 786440 | tf_op jit(solution)/shard_map/ppermute | solution.py:22
  139.2 3.2 %collective-permute-done.5 = f32[4,128,128]{2,1,0:T(8,128)S(1)} collective-permute-done((f32[4,128,128]{2,1,0:T(8,128)S(1)}, f32[4,128,128]{2,1,0:T(8,128)S(1)}, u32[]{:S(2)}, u32[]{:S(2)}) %collective-permute-start.5) | collective-permute-done | bytes 262176 | tf_op jit(solution)/shard_map/ppermute | solution.py:22
  142.4 4.7 %collective-permute-start.6 = (f32[4,128,128]{2,1,0:T(8,128)S(1)}, f32[4,128,128]{2,1,0:T(8,128)S(1)}, u32[]{:S(2)}, u32[]{:S(2)}) collective-permute-start(f32[4,128,128]{2,1,0:T(8,128)S(1)} %add.140), channel_id=1, source_target_pairs={{0,256},{4,260},{8,264},{12,268},{16,272},{20,276},{24,280},{28,28... | collective-permute-start | bytes 786440 | tf_op jit(solution)/shard_map/ppermute | solution.py:22
  147.6 3.2 %collective-permute-done.6 = f32[4,128,128]{2,1,0:T(8,128)S(1)} collective-permute-done((f32[4,128,128]{2,1,0:T(8,128)S(1)}, f32[4,128,128]{2,1,0:T(8,128)S(1)}, u32[]{:S(2)}, u32[]{:S(2)}) %collective-permute-start.6) | collective-permute-done | bytes 262176 | tf_op jit(solution)/shard_map/ppermute | solution.py:22
  151.8 6.0 %all-reduce = (f32[128]{0:T(128)S(1)}, f32[128]{0:T(128)S(1)}) all-reduce(f32[128]{0:T(128)S(1)} %get-tuple-element.19, f32[128]{0:T(128)S(1)} %get-tuple-element.18), channel_id=1, replica_groups=mesh['ctx'=128,'head'=4] {'head'}, use_global_device_ids=true, to_apply=%region_3.4 | all-reduce | flops 256 | bytes 2048 | tf_op jit(solution)/shard_map/psum | solution.py:132
  158.8 6.5 %collective-permute-start.7 = (f32[4,128,128]{1,2,0:T(8,128)}, f32[4,128,128]{1,2,0:T(8,128)}, u32[]{:S(2)}, u32[]{:S(2)}) collective-permute-start(f32[4,128,128]{1,2,0:T(8,128)} %convolution_bitcast_fusion.5), channel_id=1, source_target_pairs={{4,0},{8,4},{12,8},{16,12},{20,16},{24,20},{28,24},{32,28},{36,32}... | collective-permute-start | bytes 786440 | tf_op jit(solution)/shard_map/ppermute | solution.py:22
  167.5 1.4 reshape.425
  169.1 1.2 scatter_fusion.1
  170.5 2.3 scatter_fusion
  174.0 1.3 collective-permute-start.8
  176.1 1.3 collective-permute-start.19
  177.3 9.3 %collective-permute-done.8 = f32[4,128,128]{1,2,0:T(8,128)S(1)} collective-permute-done((f32[4,128,128]{1,2,0:T(8,128)S(1)}, f32[4,128,128]{1,2,0:T(8,128)S(1)}, u32[]{:S(2)}, u32[]{:S(2)}) %collective-permute-start.8) | collective-permute-done | bytes 262176 | tf_op jit(solution)/shard_map/ppermute | solution.py:22
  186.7 1.4 collective-permute-start.9
  188.8 1.3 collective-permute-start.20
  190.9 1.3 collective-permute-start.21
  192.9 1.9 collective-permute-start.18
  194.8 13.2 %collective-permute-done.9 = f32[4,128,128]{1,2,0:T(8,128)S(1)} collective-permute-done((f32[4,128,128]{1,2,0:T(8,128)S(1)}, f32[4,128,128]{1,2,0:T(8,128)S(1)}, u32[]{:S(2)}, u32[]{:S(2)}) %collective-permute-start.9) | collective-permute-done | bytes 262176 | tf_op jit(solution)/shard_map/ppermute | solution.py:22
  208.1 1.3 collective-permute-start.10
  210.5 6.0 %collective-permute-done.20 = bf16[128,1024]{1,0:T(8,128)(2,1)} collective-permute-done((bf16[128,1024]{1,0:T(8,128)(2,1)}, bf16[128,1024]{1,0:T(8,128)(2,1)}, u32[]{:S(2)}, u32[]{:S(2)}) %collective-permute-start.20) | collective-permute-done | bytes 262176 | tf_op jit(solution)/shard_map/ppermute | solution.py:30
  217.5 10.5 %collective-permute-done.21 = bf16[128,1024]{1,0:T(8,128)(2,1)} collective-permute-done((bf16[128,1024]{1,0:T(8,128)(2,1)}, bf16[128,1024]{1,0:T(8,128)(2,1)}, u32[]{:S(2)}, u32[]{:S(2)}) %collective-permute-start.21) | collective-permute-done | bytes 262176 | tf_op jit(solution)/shard_map/ppermute | solution.py:30
  230.1 20.0 %collective-permute-done.10 = f32[4,128,128]{1,2,0:T(8,128)} collective-permute-done((f32[4,128,128]{1,2,0:T(8,128)S(1)}, f32[4,128,128]{1,2,0:T(8,128)}, u32[]{:S(2)}, u32[]{:S(2)}) %collective-permute-start.10) | collective-permute-done | bytes 262176 | tf_op jit(solution)/shard_map/ppermute | solution.py:22
  251.2 1.4 collective-permute-start.11
  253.8 13.4 %collective-permute-done.11 = f32[4,128,128]{1,2,0:T(8,128)S(1)} collective-permute-done((f32[4,128,128]{1,2,0:T(8,128)S(1)}, f32[4,128,128]{1,2,0:T(8,128)S(1)}, u32[]{:S(2)}, u32[]{:S(2)}) %collective-permute-start.11) | collective-permute-done | bytes 262176 | tf_op jit(solution)/shard_map/ppermute | solution.py:22
  267.3 1.4 collective-permute-start.12
  269.1 17.4 %collective-permute-done.12 = f32[4,128,128]{1,2,0:T(8,128)S(1)} collective-permute-done((f32[4,128,128]{1,2,0:T(8,128)S(1)}, f32[4,128,128]{1,2,0:T(8,128)S(1)}, u32[]{:S(2)}, u32[]{:S(2)}) %collective-permute-start.12) | collective-permute-done | bytes 262176 | tf_op jit(solution)/shard_map/ppermute | solution.py:22
  286.6 1.4 collective-permute-start.13
  289.2 14.3 %collective-permute-done.13 = f32[4,128,128]{1,2,0:T(8,128)S(1)} collective-permute-done((f32[4,128,128]{1,2,0:T(8,128)S(1)}, f32[4,128,128]{1,2,0:T(8,128)S(1)}, u32[]{:S(2)}, u32[]{:S(2)}) %collective-permute-start.13) | collective-permute-done | bytes 262176 | tf_op jit(solution)/shard_map/ppermute | solution.py:22
  (148 shorter events, 34.0 us)
Async XLA Ops:
  0.6 100.4 %copy-start = (bf16[128,512]{1,0:T(8,128)(2,1)S(1)}, bf16[128,512]{1,0:T(8,128)(2,1)}, u32[]{:S(2)}) copy-start(bf16[128,512]{1,0:T(8,128)(2,1)} %param.15) | copy-start | bytes 393220
  0.6 28.8 %copy-start.16 = (bf16[128,512]{1,0:T(8,128)(2,1)S(1)}, bf16[128,512]{1,0:T(8,128)(2,1)}, u32[]{:S(2)}) copy-start(bf16[128,512]{1,0:T(8,128)(2,1)} %param.11) | copy-start | bytes 393220
  0.7 29.0 %copy-start.11 = (bf16[128,512]{1,0:T(8,128)(2,1)S(1)}, bf16[128,512]{1,0:T(8,128)(2,1)}, u32[]{:S(2)}) copy-start(bf16[128,512]{1,0:T(8,128)(2,1)} %param.12) | copy-start | bytes 393220
  0.7 28.6 %copy-start.28 = (s32[1,3]{1,0:T(1,128)S(1)}, s32[1,3]{1,0:T(1,128)}, u32[]{:S(2)}) copy-start(s32[1,3]{1,0:T(1,128)} %param.19) | copy-start | bytes 40
  0.7 28.8 %copy-start.9 = (bf16[128,512]{1,0:T(8,128)(2,1)S(1)}, bf16[128,512]{1,0:T(8,128)(2,1)}, u32[]{:S(2)}) copy-start(bf16[128,512]{1,0:T(8,128)(2,1)} %param.10) | copy-start | bytes 393220
  3.9 40.9 %copy-start.23 = (bf16[128,512]{1,0:T(8,128)(2,1)S(1)}, bf16[128,512]{1,0:T(8,128)(2,1)}, u32[]{:S(2)}) copy-start(bf16[128,512]{1,0:T(8,128)(2,1)} %param.14) | copy-start | bytes 393220
  3.9 73.0 %collective-permute-start.17 = (bf16[128,1024]{1,0:T(8,128)(2,1)}, bf16[128,1024]{1,0:T(8,128)(2,1)S(1)}, u32[]{:S(2)}, u32[]{:S(2)}) collective-permute-start(bf16[128,1024]{1,0:T(8,128)(2,1)} %constant_dynamic-update-slice_fusion), channel_id=1, source_target_pairs={{0,4},{4,8},{8,12},{12,16},{16,20},{20,24},{24,28},{28,32},{32,36}... | collective-permute-start | bytes 786440 | tf_op jit(solution)/shard_map/ppermute | solution.py:30
  9.0 49.0 %collective-permute-start.16 = (bf16[128,1024]{1,0:T(8,128)(2,1)}, bf16[128,1024]{1,0:T(8,128)(2,1)S(1)}, u32[]{:S(2)}, u32[]{:S(2)}) collective-permute-start(bf16[128,1024]{1,0:T(8,128)(2,1)} %constant_dynamic-update-slice_fusion), channel_id=1, source_target_pairs={{0,8},{4,12},{8,16},{12,20},{16,24},{20,28},{24,32},{28,36},{32,40... | collective-permute-start | bytes 786440 | tf_op jit(solution)/shard_map/ppermute | solution.py:30
  12.6 43.8 %collective-permute-start.15 = (bf16[128,1024]{1,0:T(8,128)(2,1)}, bf16[128,1024]{1,0:T(8,128)(2,1)}, u32[]{:S(2)}, u32[]{:S(2)}) collective-permute-start(bf16[128,1024]{1,0:T(8,128)(2,1)} %constant_dynamic-update-slice_fusion), channel_id=1, source_target_pairs={{0,12},{4,16},{8,20},{12,24},{16,28},{20,32},{24,36},{28,40},{32,4... | collective-permute-start | bytes 786440 | tf_op jit(solution)/shard_map/ppermute | solution.py:30
  16.8 28.9 %collective-permute-start.14 = (bf16[128,1024]{1,0:T(8,128)(2,1)}, bf16[128,1024]{1,0:T(8,128)(2,1)}, u32[]{:S(2)}, u32[]{:S(2)}) collective-permute-start(bf16[128,1024]{1,0:T(8,128)(2,1)} %constant_dynamic-update-slice_fusion), channel_id=1, source_target_pairs={{0,16},{4,20},{8,24},{12,28},{16,32},{20,36},{24,40},{28,44},{32,4... | collective-permute-start | bytes 786440 | tf_op jit(solution)/shard_map/ppermute | solution.py:30
  24.0 20.2 %copy-start.13 = (bf16[128,512]{0,1:T(8,128)(2,1)}, bf16[128,512]{0,1:T(8,128)(2,1)S(1)}, u32[]{:S(2)}) copy-start(bf16[128,512]{0,1:T(8,128)(2,1)S(1)} %copy.161) | copy-start | bytes 393220
  24.0 20.9 %copy-start.24 = (bf16[128,512]{1,0:T(8,128)(2,1)S(1)}, bf16[128,512]{1,0:T(8,128)(2,1)}, u32[]{:S(2)}) copy-start(bf16[128,512]{1,0:T(8,128)(2,1)} %param.18) | copy-start | bytes 393220
  25.1 12.7 %collective-permute-start = (f32[4,128,128]{2,1,0:T(8,128)S(1)}, f32[4,128,128]{2,1,0:T(8,128)S(1)}, u32[]{:S(2)}, u32[]{:S(2)}) collective-permute-start(f32[4,128,128]{2,1,0:T(8,128)S(1)} %fusion.31), channel_id=1, source_target_pairs={{0,4},{4,8},{8,12},{12,16},{16,20},{20,24},{24,28},{28,32},{32,36}... | collective-permute-start | bytes 786440 | tf_op jit(solution)/shard_map/ppermute | solution.py:22
  29.7 17.6 %copy-start.20 = (bf16[4,128,128]{2,1,0:T(8,128)(2,1)}, bf16[4,128,128]{2,1,0:T(8,128)(2,1)S(1)}, u32[]{:S(2)}) copy-start(bf16[4,128,128]{2,1,0:T(8,128)(2,1)S(1)} %fusion.15) | copy-start | bytes 393220
  37.8 12.4 %collective-permute-start.1 = (f32[4,128,128]{2,1,0:T(8,128)S(1)}, f32[4,128,128]{2,1,0:T(8,128)S(1)}, u32[]{:S(2)}, u32[]{:S(2)}) collective-permute-start(f32[4,128,128]{2,1,0:T(8,128)S(1)} %add.135), channel_id=1, source_target_pairs={{0,8},{4,12},{8,16},{12,20},{16,24},{20,28},{24,32},{28,36},{32,40... | collective-permute-start | bytes 786440 | tf_op jit(solution)/shard_map/ppermute | solution.py:22
  50.2 27.4 %copy-start.18 = (bf16[128,512]{1,0:T(8,128)(2,1)S(1)}, bf16[128,512]{1,0:T(8,128)(2,1)}, u32[]{:S(2)}) copy-start(bf16[128,512]{1,0:T(8,128)(2,1)} %param.16) | copy-start | bytes 393220
  50.3 27.4 %copy-start.19 = (bf16[128,512]{1,0:T(8,128)(2,1)S(1)}, bf16[128,512]{1,0:T(8,128)(2,1)}, u32[]{:S(2)}) copy-start(bf16[128,512]{1,0:T(8,128)(2,1)} %param.17) | copy-start | bytes 393220
  50.3 15.6 %collective-permute-start.2 = (f32[4,128,128]{2,1,0:T(8,128)S(1)}, f32[4,128,128]{2,1,0:T(8,128)S(1)}, u32[]{:S(2)}, u32[]{:S(2)}) collective-permute-start(f32[4,128,128]{2,1,0:T(8,128)S(1)} %add.136), channel_id=1, source_target_pairs={{0,16},{4,20},{8,24},{12,28},{16,32},{20,36},{24,40},{28,44},{32,4... | collective-permute-start | bytes 786440 | tf_op jit(solution)/shard_map/ppermute | solution.py:22
  65.9 32.1 %collective-permute-start.3 = (f32[4,128,128]{2,1,0:T(8,128)S(1)}, f32[4,128,128]{2,1,0:T(8,128)}, u32[]{:S(2)}, u32[]{:S(2)}) collective-permute-start(f32[4,128,128]{2,1,0:T(8,128)S(1)} %add.137), channel_id=1, source_target_pairs={{0,32},{4,36},{8,40},{12,44},{16,48},{20,52},{24,56},{28,60},{32,6... | collective-permute-start | bytes 786440 | tf_op jit(solution)/shard_map/ppermute | solution.py:22
  81.1 19.9 %copy-start.25 = (pred[128,512]{0,1:T(8,128)(4,1)S(1)}, pred[128,512]{0,1:T(8,128)(4,1)}, u32[]{:S(2)}) copy-start(pred[128,512]{0,1:T(8,128)(4,1)} %fusion.23) | copy-start | bytes 196612
  81.4 21.1 %copy-start.1 = (bf16[512,4,128]{0,2,1:T(8,128)(2,1)}, bf16[512,4,128]{0,2,1:T(8,128)(2,1)S(1)}, u32[]{:S(2)}) copy-start(bf16[512,4,128]{0,2,1:T(8,128)(2,1)S(1)} %copy.90) | copy-start | bytes 1572868
  99.0 12.4 %collective-permute-start.4 = (f32[4,128,128]{2,1,0:T(8,128)S(1)}, f32[4,128,128]{2,1,0:T(8,128)}, u32[]{:S(2)}, u32[]{:S(2)}) collective-permute-start(f32[4,128,128]{2,1,0:T(8,128)S(1)} %add.138), channel_id=1, source_target_pairs={{0,64},{4,68},{8,72},{12,76},{16,80},{20,84},{24,88},{28,92},{32,9... | collective-permute-start | bytes 786440 | tf_op jit(solution)/shard_map/ppermute | solution.py:22
  104.2 34.0 %copy-start.22 = (f32[128,512]{0,1:T(8,128)S(1)}, f32[128,512]{0,1:T(8,128)}, u32[]{:S(2)}) copy-start(f32[128,512]{0,1:T(8,128)} %copy.71) | copy-start | bytes 786436
  104.2 34.0 %copy-start.29 = (f32[4,128,512]{1,2,0:T(8,128)S(1)}, f32[4,128,512]{1,2,0:T(8,128)}, u32[]{:S(2)}) copy-start(f32[4,128,512]{1,2,0:T(8,128)} %get-tuple-element.44) | copy-start | bytes 3145732
  112.4 30.0 %collective-permute-start.5 = (f32[4,128,128]{2,1,0:T(8,128)S(1)}, f32[4,128,128]{2,1,0:T(8,128)S(1)}, u32[]{:S(2)}, u32[]{:S(2)}) collective-permute-start(f32[4,128,128]{2,1,0:T(8,128)S(1)} %add.139), channel_id=1, source_target_pairs={{0,128},{4,132},{8,136},{12,140},{16,144},{20,148},{24,152},{28,15... | collective-permute-start | bytes 786440 | tf_op jit(solution)/shard_map/ppermute | solution.py:22
  138.2 9.0 %copy-start.31 = (f32[4,128]{1,0:T(4,128)S(1)}, f32[4,128]{1,0:T(4,128)}, u32[]{:S(2)}) copy-start(f32[4,128]{1,0:T(4,128)} %copy-done.30) | copy-start | bytes 6148
  142.4 8.3 %collective-permute-start.6 = (f32[4,128,128]{2,1,0:T(8,128)S(1)}, f32[4,128,128]{2,1,0:T(8,128)S(1)}, u32[]{:S(2)}, u32[]{:S(2)}) collective-permute-start(f32[4,128,128]{2,1,0:T(8,128)S(1)} %add.140), channel_id=1, source_target_pairs={{0,256},{4,260},{8,264},{12,268},{16,272},{20,276},{24,280},{28,28... | collective-permute-start | bytes 786440 | tf_op jit(solution)/shard_map/ppermute | solution.py:22
  147.6 17.8 %copy-start.3 = (bf16[4,128,512]{1,2,0:T(8,128)(2,1)}, bf16[4,128,512]{1,2,0:T(8,128)(2,1)S(1)}, u32[]{:S(2)}) copy-start(bf16[4,128,512]{1,2,0:T(8,128)(2,1)S(1)} %fusion.8) | copy-start | bytes 1572868
  157.8 7.9 %copy-start.15 = (f32[1,512,4,128]{3,1,2,0:T(8,128)S(1)}, f32[1,512,4,128]{3,1,2,0:T(8,128)}, u32[]{:S(2)}) copy-start(f32[1,512,4,128]{3,1,2,0:T(8,128)} %convolution_bitcast_fusion) | copy-start | bytes 3145732
  157.9 7.4 %copy-start.5 = (bf16[128,4,128]{0,2,1:T(8,128)(2,1)}, bf16[128,4,128]{0,2,1:T(8,128)(2,1)S(1)}, u32[]{:S(2)}) copy-start(bf16[128,4,128]{0,2,1:T(8,128)(2,1)S(1)} %subtract_convert_fusion.1) | copy-start | bytes 393220
  158.8 14.1 %collective-permute-start.7 = (f32[4,128,128]{1,2,0:T(8,128)}, f32[4,128,128]{1,2,0:T(8,128)}, u32[]{:S(2)}, u32[]{:S(2)}) collective-permute-start(f32[4,128,128]{1,2,0:T(8,128)} %convolution_bitcast_fusion.5), channel_id=1, source_target_pairs={{4,0},{8,4},{12,8},{16,12},{20,16},{24,20},{28,24},{32,28},{36,32}... | collective-permute-start | bytes 786440 | tf_op jit(solution)/shard_map/ppermute | solution.py:22
  174.0 12.6 %collective-permute-start.8 = (f32[4,128,128]{1,2,0:T(8,128)S(1)}, f32[4,128,128]{1,2,0:T(8,128)S(1)}, u32[]{:S(2)}, u32[]{:S(2)}) collective-permute-start(f32[4,128,128]{1,2,0:T(8,128)S(1)} %add.146), channel_id=1, source_target_pairs={{8,0},{12,4},{16,8},{20,12},{24,16},{28,20},{32,24},{36,28},{40,32... | collective-permute-start | bytes 786440 | tf_op jit(solution)/shard_map/ppermute | solution.py:22
  176.1 34.4 %collective-permute-start.19 = (bf16[128,1024]{1,0:T(8,128)(2,1)}, bf16[128,1024]{1,0:T(8,128)(2,1)S(1)}, u32[]{:S(2)}, u32[]{:S(2)}) collective-permute-start(bf16[128,1024]{1,0:T(8,128)(2,1)} %pad_maximum_fusion.1), channel_id=1, source_target_pairs={{8,0},{12,4},{16,8},{20,12},{24,16},{28,20},{32,24},{36,28},{40,32... | collective-permute-start | bytes 786440 | tf_op jit(solution)/shard_map/ppermute | solution.py:30
  186.7 22.7 %copy-start.2 = (bf16[512,4,128]{0,2,1:T(8,128)(2,1)S(1)}, bf16[512,4,128]{0,2,1:T(8,128)(2,1)}, u32[]{:S(2)}) copy-start(bf16[512,4,128]{0,2,1:T(8,128)(2,1)} %copy-done.1) | copy-start | bytes 1572868
  186.7 22.7 %copy-start.4 = (bf16[4,128,512]{1,2,0:T(8,128)(2,1)S(1)}, bf16[4,128,512]{1,2,0:T(8,128)(2,1)}, u32[]{:S(2)}) copy-start(bf16[4,128,512]{1,2,0:T(8,128)(2,1)} %copy-done.3) | copy-start | bytes 1572868
  186.7 21.4 %collective-permute-start.9 = (f32[4,128,128]{1,2,0:T(8,128)S(1)}, f32[4,128,128]{1,2,0:T(8,128)S(1)}, u32[]{:S(2)}, u32[]{:S(2)}) collective-permute-start(f32[4,128,128]{1,2,0:T(8,128)S(1)} %add.147), channel_id=1, source_target_pairs={{16,0},{20,4},{24,8},{28,12},{32,16},{36,20},{40,24},{44,28},{48,3... | collective-permute-start | bytes 786440 | tf_op jit(solution)/shard_map/ppermute | solution.py:22
  188.8 27.7 %collective-permute-start.20 = (bf16[128,1024]{1,0:T(8,128)(2,1)}, bf16[128,1024]{1,0:T(8,128)(2,1)}, u32[]{:S(2)}, u32[]{:S(2)}) collective-permute-start(bf16[128,1024]{1,0:T(8,128)(2,1)} %pad_maximum_fusion.2), channel_id=1, source_target_pairs={{12,0},{16,4},{20,8},{24,12},{28,16},{32,20},{36,24},{40,28},{44,3... | collective-permute-start | bytes 786440 | tf_op jit(solution)/shard_map/ppermute | solution.py:30
  190.9 37.2 %collective-permute-start.21 = (bf16[128,1024]{1,0:T(8,128)(2,1)}, bf16[128,1024]{1,0:T(8,128)(2,1)}, u32[]{:S(2)}, u32[]{:S(2)}) collective-permute-start(bf16[128,1024]{1,0:T(8,128)(2,1)} %pad_maximum_fusion.3), channel_id=1, source_target_pairs={{16,0},{20,4},{24,8},{28,12},{32,16},{36,20},{40,24},{44,28},{48,3... | collective-permute-start | bytes 786440 | tf_op jit(solution)/shard_map/ppermute | solution.py:30
  192.9 36.2 %collective-permute-start.18 = (bf16[128,1024]{1,0:T(8,128)(2,1)}, bf16[128,1024]{1,0:T(8,128)(2,1)}, u32[]{:S(2)}, u32[]{:S(2)}) collective-permute-start(bf16[128,1024]{1,0:T(8,128)(2,1)} %pad_maximum_fusion), channel_id=1, source_target_pairs={{4,0},{8,4},{12,8},{16,12},{20,16},{24,20},{28,24},{32,28},{36,32}... | collective-permute-start | bytes 786440 | tf_op jit(solution)/shard_map/ppermute | solution.py:30
  208.1 42.1 %collective-permute-start.10 = (f32[4,128,128]{1,2,0:T(8,128)S(1)}, f32[4,128,128]{1,2,0:T(8,128)}, u32[]{:S(2)}, u32[]{:S(2)}) collective-permute-start(f32[4,128,128]{1,2,0:T(8,128)S(1)} %add.148), channel_id=1, source_target_pairs={{32,0},{36,4},{40,8},{44,12},{48,16},{52,20},{56,24},{60,28},{64,3... | collective-permute-start | bytes 786440 | tf_op jit(solution)/shard_map/ppermute | solution.py:22
  251.1 17.5 %copy-start.14 = (bf16[128,512]{0,1:T(8,128)(2,1)S(1)}, bf16[128,512]{0,1:T(8,128)(2,1)}, u32[]{:S(2)}) copy-start(bf16[128,512]{0,1:T(8,128)(2,1)} %copy-done.13) | copy-start | bytes 393220
  251.2 16.1 %collective-permute-start.11 = (f32[4,128,128]{1,2,0:T(8,128)S(1)}, f32[4,128,128]{1,2,0:T(8,128)S(1)}, u32[]{:S(2)}, u32[]{:S(2)}) collective-permute-start(f32[4,128,128]{1,2,0:T(8,128)S(1)} %add.149), channel_id=1, source_target_pairs={{64,0},{68,4},{72,8},{76,12},{80,16},{84,20},{88,24},{92,28},{96,3... | collective-permute-start | bytes 786440 | tf_op jit(solution)/shard_map/ppermute | solution.py:22
  253.5 15.4 %copy-start.8 = (bf16[4,128,128]{2,1,0:T(8,128)(2,1)S(1)}, bf16[4,128,128]{2,1,0:T(8,128)(2,1)}, u32[]{:S(2)}) copy-start(bf16[4,128,128]{2,1,0:T(8,128)(2,1)} %copy-done.7) | copy-start | bytes 393220
  253.8 34.2 %copy-start.10 = (bf16[128,512]{1,0:T(8,128)(2,1)S(1)}, bf16[128,512]{1,0:T(8,128)(2,1)}, u32[]{:S(2)}) copy-start(bf16[128,512]{1,0:T(8,128)(2,1)} %param.10) | copy-start | bytes 393220
  267.2 21.8 %copy-start.21 = (bf16[4,128,128]{2,1,0:T(8,128)(2,1)S(1)}, bf16[4,128,128]{2,1,0:T(8,128)(2,1)}, u32[]{:S(2)}) copy-start(bf16[4,128,128]{2,1,0:T(8,128)(2,1)} %copy-done.20) | copy-start | bytes 393220
  267.3 19.3 %collective-permute-start.12 = (f32[4,128,128]{1,2,0:T(8,128)S(1)}, f32[4,128,128]{1,2,0:T(8,128)S(1)}, u32[]{:S(2)}, u32[]{:S(2)}) collective-permute-start(f32[4,128,128]{1,2,0:T(8,128)S(1)} %add.150), channel_id=1, source_target_pairs={{128,0},{132,4},{136,8},{140,12},{144,16},{148,20},{152,24},{156,2... | collective-permute-start | bytes 786440 | tf_op jit(solution)/shard_map/ppermute | solution.py:22
  286.5 17.9 %copy-start.17 = (bf16[128,512]{1,0:T(8,128)(2,1)S(1)}, bf16[128,512]{1,0:T(8,128)(2,1)}, u32[]{:S(2)}) copy-start(bf16[128,512]{1,0:T(8,128)(2,1)} %param.11) | copy-start | bytes 393220
  286.6 16.9 %collective-permute-start.13 = (f32[4,128,128]{1,2,0:T(8,128)S(1)}, f32[4,128,128]{1,2,0:T(8,128)S(1)}, u32[]{:S(2)}, u32[]{:S(2)}) collective-permute-start(f32[4,128,128]{1,2,0:T(8,128)S(1)} %add.151), channel_id=1, source_target_pairs={{256,0},{260,4},{264,8},{268,12},{272,16},{276,20},{280,24},{284,2... | collective-permute-start | bytes 786440 | tf_op jit(solution)/shard_map/ppermute | solution.py:22
  (6 other events, 13.0 us)

commit v2 on v1

--- a/solution.py
+++ b/solution.py
@@ -10,18 +10,24 @@
 SPAN = 4
 
 
-def carried_in(shard, axis, join, neutral, backward):
-    count = lax.axis_size(axis)
-    total = shard.astype(jnp.float32)
-    distance = 1
-    while distance < count:
-        if backward:
-            pairs = [(i, i - distance) for i in range(distance, count)]
-        else:
-            pairs = [(i, i + distance) for i in range(count - distance)]
-        total = join(total, lax.ppermute(total, axis, pairs))
-        distance *= 2
-    return (total - shard.astype(jnp.float32)).astype(shard.dtype)
+CTX = ("outer", "inner")
+INNER = 8
+
+
+def carried_in(shard, backward):
+    wide = shard.astype(jnp.float32)
+
+    def before(axis, full):
+        place = lax.axis_index(axis)
+        index = jnp.arange(lax.axis_size(axis))
+        mask = index > place if backward else index < place
+        gathered = lax.all_gather(full.astype(jnp.bfloat16), axis).astype(jnp.float32)
+        picked = jnp.where(mask.reshape((-1,) + (1,) * full.ndim), gathered, 0.0)
+        return jnp.sum(picked, axis=0), jnp.sum(gathered, axis=0)
+
+    near, group = before("inner", wide)
+    far, _ = before("outer", group)
+    return near + far
 
 
 def from_behind(shard, axis, by):
@@ -113,7 +119,7 @@
     key_lin = lin_key.reshape(token_count, heads_lin, HEAD)
     value_lin = lin_value.reshape(token_count, heads_lin, HEAD)
     key_value = jnp.einsum("thi,thj->hij", key_lin, value_lin, preferred_element_type=jnp.float32)
-    state_low = carried_in(key_value, "ctx", add_states, jnp.zeros_like(key_value), False)
+    state_low = carried_in(key_value, False)
     state_half = state_low.astype(jnp.bfloat16)
     causal = jnp.tril(jnp.ones((token_count, token_count), jnp.bool_))
     attn_lin = jnp.where(
@@ -138,7 +144,7 @@
     adjoint_local = jnp.einsum(
         "thi,thj->hij", query_lin, grad_out, preferred_element_type=jnp.float32
     )
-    adjoint_high = carried_in(adjoint_local, "ctx", add_states, jnp.zeros_like(adjoint_local), True)
+    adjoint_high = carried_in(adjoint_local, True)
     adjoint_half = adjoint_high.astype(jnp.bfloat16)
     grad_scores = jnp.where(
         causal[None],
@@ -159,14 +165,14 @@
     lin_dv = lin_dv.reshape(token_count, lin_width).astype(jnp.bfloat16)
     width = sm_key.shape[1]
     pair = jnp.concatenate([sm_key, sm_value], axis=1)
-    arrived = [from_behind(pair, "ctx", distance) for distance in range(1, SPAN + 1)]
+    arrived = [from_behind(pair, CTX, distance) for distance in range(1, SPAN + 1)]
     key_window = jnp.concatenate(
         [arrived[SPAN - 1 - place][:, :width] for place in range(SPAN)] + [sm_key], axis=0
     )
     value_window = jnp.concatenate(
         [arrived[SPAN - 1 - place][:, width:] for place in range(SPAN)] + [sm_value], axis=0
     )
-    shard = lax.axis_index("ctx")
+    shard = lax.axis_index(CTX)
     sm_dq, key_acc, value_acc = tile_attention(
         sm_query, sm_grad, key_window, value_window, tile_lists, shard
     )
@@ -177,7 +183,7 @@
             jnp.concatenate(
                 [key_acc[SPAN - distance], value_acc[SPAN - distance]], axis=1
             ).astype(jnp.bfloat16),
-            "ctx",
+            CTX,
             -distance,
         ).astype(jnp.float32)
         key_total = key_total + back[:, :width]
@@ -194,28 +200,33 @@
 
 def solution(mesh):
     placed = (
-        P("ctx", "head"),
-        P("ctx", "head"),
-        P("ctx", "head"),
+        P(CTX, "head"),
+        P(CTX, "head"),
+        P(CTX, "head"),
         P("head"),
-        P("ctx", "head"),
-        P("ctx", "head"),
-        P("ctx", "head"),
-        P("ctx", "head"),
-        P("ctx", "head"),
-        P("ctx", None),
+        P(CTX, "head"),
+        P(CTX, "head"),
+        P(CTX, "head"),
+        P(CTX, "head"),
+        P(CTX, "head"),
+        P(CTX, None),
+    )
+    count = mesh.shape["ctx"]
+    inner = INNER if count % INNER == 0 else 1
+    split = jax.sharding.Mesh(
+        mesh.devices.reshape(count // inner, inner, mesh.shape["head"]), CTX + ("head",)
     )
     return jax.shard_map(
         per_device,
-        mesh=mesh,
+        mesh=split,
         in_specs=placed,
         out_specs=(
-            P("ctx", "head"),
-            P("ctx", "head"),
-            P("ctx", "head"),
-            P("ctx", "head"),
-            P("ctx", "head"),
-            P("ctx", "head"),
+            P(CTX, "head"),
+            P(CTX, "head"),
+            P(CTX, "head"),
+            P(CTX, "head"),
+            P(CTX, "head"),
+            P(CTX, "head"),
         ),
         check_vma=False,
     )

time: 308 us -> 322 us (1.045)
  the two profiles are of different devices: /device:TPU:1 before, /device:TPU:24 now
where the time goes in v2:
time: 322 us; the launch traced here: 320 us
  waiting for transfers between devices  207 us (64%)
  starting transfers between devices  31.1 us (10%)
  other arithmetic  23.6 us (7%)
  local copies, waits for them, and re-layouts  20.4 us (6%)
  between operations  14.6 us (5%)
  matrix products  12.2 us (4%)
  blocking collectives  10.4 us (3%)
    all_gather x4, waiting for transfers between devices, before(): lax.all_gather(full.astype(jnp.bfloat16), axis).astype(jnp.float32)  191 us
    ppermute x8, starting transfers between devices, from_behind(): return lax.ppermute(shard, axis, pairs)  30.9 us
    ppermute x8, waiting for transfers between devices, from_behind(): return lax.ppermute(shard, axis, pairs)  16.1 us
    psum x1, blocking collectives, per_device(): square_sum, cross_sum = lax.psum((square_sum, cross_sum), 'head')  10.4 us
    unnamed x77, local copies, waits for them, and re-layouts  10.2 us
    reduce_sum x6, other arithmetic, before(): return (jnp.sum(picked, axis=0), jnp.sum(gathered, axis=0))  8.98 us
  transfers between devices with their start and end apart: 12, of which 7 were waited for; matrix products, arithmetic and copies ran while one was open for 13% of the time, Pallas kernels for 0%

profile of v2, /device:TPU:24, one launch (start us, length us, event | category | flops | bytes accessed | tf_op | source)
XLA Modules:
  0.0 319.7 jit_solution(6362415980906119720)
XLA Ops:
  7.3 1.2 copy.201
  8.5 1.8 convolution_convert_fusion.2
  10.4 47.0 %all-gather.9.cloned.1.call-done = bf16[32,128,128]{2,1,0:T(8,128)(2,1)} async-done(((bf16[4,128,128]{2,1,0:T(8,128)(2,1)}), bf16[32,128,128]{2,1,0:T(8,128)(2,1)}) %all-gather.9.cloned.1.call-update) | async-done | bytes 1048592 | tf_op jit(solution)/shard_map/all_gather | solution.py:24
  57.5 2.1 reduce_sum.99
  61.1 1.9 collective-permute-start.3
  63.0 1.9 collective-permute-start.2
  64.9 2.2 collective-permute-start.1
  67.1 8.2 %collective-permute-start = (bf16[128,1024]{1,0:T(8,128)(2,1)}, bf16[128,1024]{1,0:T(8,128)(2,1)}, u32[]{:S(2)}, u32[]{:S(2)}) collective-permute-start(bf16[128,1024]{1,0:T(8,128)(2,1)} %constant_dynamic-update-slice_fusion), channel_id=1, source_target_pairs={{0,16},{4,20},{8,24},{12,28},{16,32},{20,36},{24,40},{28,44},{32,4... | collective-permute-start | bytes 786440 | tf_op jit(solution)/shard_map/ppermute | solution.py:36
  76.2 0.9 fusion.17
  77.0 1.1 convolution_bitcast_fusion.8
  78.5 80.2 %all-gather.11.cloned.1.call-done = bf16[64,128,128]{2,1,0:T(8,128)(2,1)} async-done(((bf16[4,128,128]{2,1,0:T(8,128)(2,1)}), bf16[64,128,128]{2,1,0:T(8,128)(2,1)}) %all-gather.11.cloned.1.call-update) | async-done | bytes 2097168 | tf_op jit(solution)/shard_map/all_gather | solution.py:24
  158.7 2.1 fusion.2
  161.8 10.4 %all-reduce = (f32[128]{0:T(128)S(1)}, f32[128]{0:T(128)S(1)}) all-reduce(f32[128]{0:T(128)S(1)} %get-tuple-element.25, f32[128]{0:T(128)S(1)} %get-tuple-element.24), channel_id=1, replica_groups=mesh['outer'=16,'inner'=8,'head'=4] {'head'}, use_global_device_ids=true, to_apply=%region_6.7 | all-reduce | flops 256 | bytes 2048 | tf_op jit(solution)/shard_map/psum | solution.py:138
  172.5 0.8 copy.98
  173.4 0.9 fusion.26
  175.0 0.8 copy.110
  175.8 1.0 slice_dynamic-update-slice_fusion.3
  176.8 1.0 slice_dynamic-update-slice_fusion.2
  177.8 1.0 slice_dynamic-update-slice_fusion.1
  178.8 1.0 slice_dynamic-update-slice_fusion
  180.0 1.0 gather_fusion
  181.5 1.1 gather_fusion.1
  183.0 26.1 %all-gather.13.cloned.1.call-done = bf16[32,128,128]{2,1,0:T(8,128)(2,1)} async-done(((bf16[4,128,128]{2,1,0:T(8,128)(2,1)}), bf16[32,128,128]{2,1,0:T(8,128)(2,1)}) %all-gather.13.cloned.1.call-update) | async-done | bytes 1048592 | tf_op jit(solution)/shard_map/all_gather | solution.py:24
  209.0 2.1 reduce_sum.104
  211.2 1.5 fusion.74
  213.2 1.5 convolution_bitcast_fusion
  216.1 1.6 fusion.20
  218.2 0.8 copy-done.5
  219.9 1.4 reshape.445
  221.5 1.2 scatter_fusion.1
  222.9 2.4 scatter_fusion
  226.3 2.5 collective-permute-start.5
  229.5 2.2 collective-permute-start.6
  232.5 9.9 %collective-permute-start.7 = (bf16[128,1024]{1,0:T(8,128)(2,1)}, bf16[128,1024]{1,0:T(8,128)(2,1)}, u32[]{:S(2)}, u32[]{:S(2)}) collective-permute-start(bf16[128,1024]{1,0:T(8,128)(2,1)} %pad_maximum_fusion.3), channel_id=1, source_target_pairs={{16,0},{20,4},{24,8},{28,12},{32,16},{36,20},{40,24},{44,28},{48,3... | collective-permute-start | bytes 786440 | tf_op jit(solution)/shard_map/ppermute | solution.py:36
  243.1 2.1 collective-permute-start.4
  246.9 1.0 convert_element_type.151
  247.9 2.3 collective-permute-done.6
  250.2 1.0 convert_element_type.152
  251.2 10.8 %collective-permute-done.7 = bf16[128,1024]{1,0:T(8,128)(2,1)} collective-permute-done((bf16[128,1024]{1,0:T(8,128)(2,1)}, bf16[128,1024]{1,0:T(8,128)(2,1)}, u32[]{:S(2)}, u32[]{:S(2)}) %collective-permute-start.7) | collective-permute-done | bytes 262176 | tf_op jit(solution)/shard_map/ppermute | solution.py:36
  262.0 1.0 convert_element_type.153
  263.0 2.9 collective-permute-done.4
  266.0 1.0 convert_element_type.150
  267.0 0.9 fusion.23
  268.6 0.8 copy.117
  269.3 1.1 fusion.77
  270.7 38.0 %all-gather.15.cloned.1.call-done = bf16[64,128,128]{2,1,0:T(8,128)(2,1)} async-done(((bf16[4,128,128]{2,1,0:T(8,128)(2,1)}), bf16[64,128,128]{2,1,0:T(8,128)(2,1)}) %all-gather.15.cloned.1.call-update) | async-done | bytes 2097168 | tf_op jit(solution)/shard_map/all_gather | solution.py:24
  308.7 2.1 fusion.1
  311.4 0.8 copy.119
  (135 shorter events, 16.5 us)
Async XLA Ops:
  7.2 204.0 %copy-start = (bf16[128,512]{1,0:T(8,128)(2,1)S(1)}, bf16[128,512]{1,0:T(8,128)(2,1)}, u32[]{:S(2)}) copy-start(bf16[128,512]{1,0:T(8,128)(2,1)} %param.15) | copy-start | bytes 393220
  7.2 69.0 %copy-start.16 = (bf16[128,512]{1,0:T(8,128)(2,1)S(1)}, bf16[128,512]{1,0:T(8,128)(2,1)}, u32[]{:S(2)}) copy-start(bf16[128,512]{1,0:T(8,128)(2,1)} %param.11) | copy-start | bytes 393220
  7.2 69.8 %copy-start.13 = (bf16[128,512]{1,0:T(8,128)(2,1)S(1)}, bf16[128,512]{1,0:T(8,128)(2,1)}, u32[]{:S(2)}) copy-start(bf16[128,512]{1,0:T(8,128)(2,1)} %param.12) | copy-start | bytes 393220
  7.2 52.5 %copy-start.18 = (bf16[128,512]{1,0:T(8,128)(2,1)S(1)}, bf16[128,512]{1,0:T(8,128)(2,1)}, u32[]{:S(2)}) copy-start(bf16[128,512]{1,0:T(8,128)(2,1)} %param.16) | copy-start | bytes 393220
  7.2 53.2 %copy-start.19 = (bf16[128,512]{1,0:T(8,128)(2,1)S(1)}, bf16[128,512]{1,0:T(8,128)(2,1)}, u32[]{:S(2)}) copy-start(bf16[128,512]{1,0:T(8,128)(2,1)} %param.17) | copy-start | bytes 393220
  7.2 68.1 %copy-start.21 = (bf16[128,512]{1,0:T(8,128)(2,1)S(1)}, bf16[128,512]{1,0:T(8,128)(2,1)}, u32[]{:S(2)}) copy-start(bf16[128,512]{1,0:T(8,128)(2,1)} %param.14) | copy-start | bytes 393220
  7.2 68.7 %copy-start.30 = (s32[1,3]{1,0:T(1,128)S(1)}, s32[1,3]{1,0:T(1,128)}, u32[]{:S(2)}) copy-start(s32[1,3]{1,0:T(1,128)} %param.19) | copy-start | bytes 40
  7.2 68.9 %copy-start.7 = (bf16[128,512]{1,0:T(8,128)(2,1)S(1)}, bf16[128,512]{1,0:T(8,128)(2,1)}, u32[]{:S(2)}) copy-start(bf16[128,512]{1,0:T(8,128)(2,1)} %param.10) | copy-start | bytes 393220
  7.3 50.2 %all-gather.9.cloned.1.call-start = ((), (), s32[]{:S(2)}) async-start(), calls=%async_computation | async-start | bytes 1179648 | tf_op jit(solution)/shard_map/all_gather | solution.py:24
  8.5 1.9 copy-start.11
  10.4 148.3 %all-gather.11.cloned.1.call-start = ((), (), s32[]{:S(2)}) async-start(), calls=%async_computation.1 | async-start | bytes 2228224 | tf_op jit(solution)/shard_map/all_gather | solution.py:24
  57.4 20.7 %copy-start.2 = (bf16[32,128,128]{2,1,0:T(8,128)(2,1)S(1)}, bf16[32,128,128]{2,1,0:T(8,128)(2,1)}, u32[]{:S(2)}) copy-start(bf16[32,128,128]{2,1,0:T(8,128)(2,1)} %all-gather.9.cloned.1.call-done) | copy-start | bytes 3145732
  59.6 149.4 %all-gather.13.cloned.1.call-start = ((), (), s32[]{:S(2)}) async-start(), calls=%async_computation.2 | async-start | bytes 1179648 | tf_op jit(solution)/shard_map/all_gather | solution.py:24
  61.1 117.8 %collective-permute-start.3 = (bf16[128,1024]{1,0:T(8,128)(2,1)}, bf16[128,1024]{1,0:T(8,128)(2,1)}, u32[]{:S(2)}, u32[]{:S(2)}) collective-permute-start(bf16[128,1024]{1,0:T(8,128)(2,1)} %constant_dynamic-update-slice_fusion), channel_id=1, source_target_pairs={{0,4},{4,8},{8,12},{12,16},{16,20},{20,24},{24,28},{28,32},{32,36}... | collective-permute-start | bytes 786440 | tf_op jit(solution)/shard_map/ppermute | solution.py:36
  63.0 114.8 %collective-permute-start.2 = (bf16[128,1024]{1,0:T(8,128)(2,1)}, bf16[128,1024]{1,0:T(8,128)(2,1)}, u32[]{:S(2)}, u32[]{:S(2)}) collective-permute-start(bf16[128,1024]{1,0:T(8,128)(2,1)} %constant_dynamic-update-slice_fusion), channel_id=1, source_target_pairs={{0,8},{4,12},{8,16},{12,20},{16,24},{20,28},{24,32},{28,36},{32,40... | collective-permute-start | bytes 786440 | tf_op jit(solution)/shard_map/ppermute | solution.py:36
  64.9 111.9 %collective-permute-start.1 = (bf16[128,1024]{1,0:T(8,128)(2,1)}, bf16[128,1024]{1,0:T(8,128)(2,1)}, u32[]{:S(2)}, u32[]{:S(2)}) collective-permute-start(bf16[128,1024]{1,0:T(8,128)(2,1)} %constant_dynamic-update-slice_fusion), channel_id=1, source_target_pairs={{0,12},{4,16},{8,20},{12,24},{16,28},{20,32},{24,36},{28,40},{32,4... | collective-permute-start | bytes 786440 | tf_op jit(solution)/shard_map/ppermute | solution.py:36
  67.1 108.7 %collective-permute-start = (bf16[128,1024]{1,0:T(8,128)(2,1)}, bf16[128,1024]{1,0:T(8,128)(2,1)}, u32[]{:S(2)}, u32[]{:S(2)}) collective-permute-start(bf16[128,1024]{1,0:T(8,128)(2,1)} %constant_dynamic-update-slice_fusion), channel_id=1, source_target_pairs={{0,16},{4,20},{8,24},{12,28},{16,32},{20,36},{24,40},{28,44},{32,4... | collective-permute-start | bytes 786440 | tf_op jit(solution)/shard_map/ppermute | solution.py:36
  78.2 83.3 %copy-start.25 = (f32[512]{0:T(512)S(1)}, f32[512]{0:T(512)}, u32[]{:S(2)}) copy-start(f32[512]{0:T(512)} %param.13) | copy-start | bytes 6148
  160.8 14.2 %copy-start.22 = (bf16[128,512]{1,0:T(8,128)(2,1)S(1)}, bf16[128,512]{1,0:T(8,128)(2,1)}, u32[]{:S(2)}) copy-start(bf16[128,512]{1,0:T(8,128)(2,1)} %param.18) | copy-start | bytes 393220
  160.8 0.7 copy-start.9
  173.3 135.4 %all-gather.15.cloned.1.call-start = ((), (), s32[]{:S(2)}) async-start(), calls=%async_computation.3 | async-start | bytes 2228224 | tf_op jit(solution)/shard_map/all_gather | solution.py:24
  174.4 5.6 %copy-start.26 = (s32[1024]{0:T(1024)}, s32[1024]{0:T(1024)S(1)}, u32[]{:S(2)}) copy-start(s32[1024]{0:T(1024)S(1)} %pad_clamp_fusion) | copy-start | bytes 12292
  181.3 29.8 %copy-start.3 = (bf16[512,4,128]{0,2,1:T(8,128)(2,1)}, bf16[512,4,128]{0,2,1:T(8,128)(2,1)S(1)}, u32[]{:S(2)}) copy-start(bf16[512,4,128]{0,2,1:T(8,128)(2,1)S(1)} %copy.129) | copy-start | bytes 1572868
  181.4 29.8 %copy-start.24 = (pred[128,512]{0,1:T(8,128)(4,1)S(1)}, pred[128,512]{0,1:T(8,128)(4,1)}, u32[]{:S(2)}) copy-start(pred[128,512]{0,1:T(8,128)(4,1)} %fusion.26) | copy-start | bytes 196612
  183.0 30.3 %copy-start.23 = (bf16[128,512]{1,0:T(8,128)(2,1)S(1)}, bf16[128,512]{1,0:T(8,128)(2,1)}, u32[]{:S(2)}) copy-start(bf16[128,512]{1,0:T(8,128)(2,1)} %param.18) | copy-start | bytes 393220
  212.7 0.6 copy-start.32
  214.7 1.1 copy-start.20
  215.4 0.7 copy-start.33
  216.1 1.6 copy-start.31
  218.2 0.8 copy-start.5
  219.9 1.6 copy-start.27
  225.5 20.4 %copy-start.4 = (bf16[512,4,128]{0,2,1:T(8,128)(2,1)S(1)}, bf16[512,4,128]{0,2,1:T(8,128)(2,1)}, u32[]{:S(2)}) copy-start(bf16[512,4,128]{0,2,1:T(8,128)(2,1)} %copy-done.3) | copy-start | bytes 1572868
  225.5 20.3 %copy-start.6 = (bf16[4,128,512]{1,2,0:T(8,128)(2,1)S(1)}, bf16[4,128,512]{1,2,0:T(8,128)(2,1)}, u32[]{:S(2)}) copy-start(bf16[4,128,512]{1,2,0:T(8,128)(2,1)} %copy-done.5) | copy-start | bytes 1572868
  226.3 20.6 %collective-permute-start.5 = (bf16[128,1024]{1,0:T(8,128)(2,1)}, bf16[128,1024]{1,0:T(8,128)(2,1)}, u32[]{:S(2)}, u32[]{:S(2)}) collective-permute-start(bf16[128,1024]{1,0:T(8,128)(2,1)} %pad_maximum_fusion.1), channel_id=1, source_target_pairs={{8,0},{12,4},{16,8},{20,12},{24,16},{28,20},{32,24},{36,28},{40,32... | collective-permute-start | bytes 786440 | tf_op jit(solution)/shard_map/ppermute | solution.py:36
  229.5 20.7 %collective-permute-start.6 = (bf16[128,1024]{1,0:T(8,128)(2,1)}, bf16[128,1024]{1,0:T(8,128)(2,1)}, u32[]{:S(2)}, u32[]{:S(2)}) collective-permute-start(bf16[128,1024]{1,0:T(8,128)(2,1)} %pad_maximum_fusion.2), channel_id=1, source_target_pairs={{12,0},{16,4},{20,8},{24,12},{28,16},{32,20},{36,24},{40,28},{44,3... | collective-permute-start | bytes 786440 | tf_op jit(solution)/shard_map/ppermute | solution.py:36
  232.5 29.5 %collective-permute-start.7 = (bf16[128,1024]{1,0:T(8,128)(2,1)}, bf16[128,1024]{1,0:T(8,128)(2,1)}, u32[]{:S(2)}, u32[]{:S(2)}) collective-permute-start(bf16[128,1024]{1,0:T(8,128)(2,1)} %pad_maximum_fusion.3), channel_id=1, source_target_pairs={{16,0},{20,4},{24,8},{28,12},{32,16},{36,20},{40,24},{44,28},{48,3... | collective-permute-start | bytes 786440 | tf_op jit(solution)/shard_map/ppermute | solution.py:36
  243.1 22.8 %collective-permute-start.4 = (bf16[128,1024]{1,0:T(8,128)(2,1)}, bf16[128,1024]{1,0:T(8,128)(2,1)}, u32[]{:S(2)}, u32[]{:S(2)}) collective-permute-start(bf16[128,1024]{1,0:T(8,128)(2,1)} %pad_maximum_fusion), channel_id=1, source_target_pairs={{4,0},{8,4},{12,8},{16,12},{20,16},{24,20},{28,24},{32,28},{36,32}... | collective-permute-start | bytes 786440 | tf_op jit(solution)/shard_map/ppermute | solution.py:36
  251.2 16.7 %copy-start.14 = (bf16[128,512]{1,0:T(8,128)(2,1)S(1)}, bf16[128,512]{1,0:T(8,128)(2,1)}, u32[]{:S(2)}) copy-start(bf16[128,512]{1,0:T(8,128)(2,1)} %param.12) | copy-start | bytes 393220
  263.0 5.1 %copy-start.12 = (bf16[128,512]{0,1:T(8,128)(2,1)S(1)}, bf16[128,512]{0,1:T(8,128)(2,1)}, u32[]{:S(2)}) copy-start(bf16[128,512]{0,1:T(8,128)(2,1)} %copy-done.11) | copy-start | bytes 393220
  267.0 1.4 copy-start.10
  267.9 2.5 copy-start.1
  267.9 2.5 copy-start.28
  267.9 40.8 %copy-start.29 = (pred[16]{0:T(512)(128)(4,1)S(1)}, pred[16]{0:T(512)(128)(4,1)}, u32[]{:S(2)}) copy-start(pred[16]{0:T(512)(128)(4,1)} %iota_compare_fusion.2) | copy-start | bytes 52
  270.4 40.5 %copy-start.15 = (bf16[128,512]{1,0:T(8,128)(2,1)S(1)}, bf16[128,512]{1,0:T(8,128)(2,1)}, u32[]{:S(2)}) copy-start(bf16[128,512]{1,0:T(8,128)(2,1)} %param.12) | copy-start | bytes 393220
  270.7 40.4 %copy-start.17 = (bf16[128,512]{1,0:T(8,128)(2,1)S(1)}, bf16[128,512]{1,0:T(8,128)(2,1)}, u32[]{:S(2)}) copy-start(bf16[128,512]{1,0:T(8,128)(2,1)} %param.11) | copy-start | bytes 393220
  308.7 3.4 %copy-start.8 = (bf16[128,512]{1,0:T(8,128)(2,1)S(1)}, bf16[128,512]{1,0:T(8,128)(2,1)}, u32[]{:S(2)}) copy-start(bf16[128,512]{1,0:T(8,128)(2,1)} %param.10) | copy-start | bytes 393220
Sparse Core Ops, SparseCore 0:
  10.7 46.6 all-gather.8
  61.0 97.5 all-gather.10
  173.4 35.5 all-gather.12
  211.9 96.7 all-gather.14

commit v3 on v1

--- a/solution.py
+++ b/solution.py
@@ -10,17 +10,27 @@
 SPAN = 4
 
 
+RADIX = 4
+
+
 def carried_in(shard, axis, join, neutral, backward):
     count = lax.axis_size(axis)
     total = shard.astype(jnp.float32)
-    distance = 1
-    while distance < count:
-        if backward:
-            pairs = [(i, i - distance) for i in range(distance, count)]
-        else:
-            pairs = [(i, i + distance) for i in range(count - distance)]
-        total = join(total, lax.ppermute(total, axis, pairs))
-        distance *= 2
+    stride = 1
+    while stride < count:
+        arrived = []
+        for step in range(1, RADIX):
+            distance = step * stride
+            if distance >= count:
+                break
+            if backward:
+                pairs = [(i, i - distance) for i in range(distance, count)]
+            else:
+                pairs = [(i, i + distance) for i in range(count - distance)]
+            arrived.append(lax.ppermute(total, axis, pairs))
+        for part in arrived:
+            total = join(total, part)
+        stride *= RADIX
     return (total - shard.astype(jnp.float32)).astype(shard.dtype)
 
 

time: 308 us -> 387 us (1.26)
  waiting for transfers between devices: 148 us -> 212 us
  starting transfers between devices: 99.6 us -> 117 us
  local copies, waits for them, and re-layouts: 22.7 us -> 16.4 us
    ppermute x14 -> x20, waiting for transfers between devices: 132 us -> 212 us  [carried_in(): arrived.append(lax.ppermute(total, axis, pairs))]
    ppermute x14 -> x20, starting transfers between devices: 74.9 us -> 91.9 us  [carried_in(): arrived.append(lax.ppermute(total, axis, pairs))]
    ppermute x8, waiting for transfers between devices: 16.6 us -> 0.02 us  [from_behind(): return lax.ppermute(shard, axis, pairs)]
  transfers between devices with their start and end apart: 22 -> 28, of which waited for: 15 -> 14; matrix products, arithmetic and copies ran while one was open for 13% -> 10% of each run, Pallas kernels for 0% -> 0%
where the time goes in v3:
time: 387 us; the launch traced here: 385 us
  waiting for transfers between devices  212 us (55%)
  starting transfers between devices  117 us (30%)
  other arithmetic  17.7 us (5%)
  local copies, waits for them, and re-layouts  16.4 us (4%)
  matrix products  11.4 us (3%)
  blocking collectives  9.57 us (2%)
    ppermute x20, waiting for transfers between devices, carried_in(): arrived.append(lax.ppermute(total, axis, pairs))  212 us
    ppermute x20, starting transfers between devices, carried_in(): arrived.append(lax.ppermute(total, axis, pairs))  91.9 us
    ppermute x8, starting transfers between devices, from_behind(): return lax.ppermute(shard, axis, pairs)  25.2 us
    psum x1, blocking collectives, per_device(): square_sum, cross_sum = lax.psum((square_sum, cross_sum), 'head')  9.57 us
  transfers between devices with their start and end apart: 28, of which 14 were waited for; matrix products, arithmetic and copies ran while one was open for 10% of the time, Pallas kernels for 0%

profile of v3, /device:TPU:1, one launch (start us, length us, event | category | flops | bytes accessed | tf_op | source)
XLA Modules:
  0.0 385.3 jit_solution(12385042598503995477)
XLA Ops:
  2.7 4.9 %collective-permute-start.23 = (bf16[128,1024]{1,0:T(8,128)(2,1)S(1)}, bf16[128,1024]{1,0:T(8,128)(2,1)S(1)}, u32[]{:S(2)}, u32[]{:S(2)}) collective-permute-start(bf16[128,1024]{1,0:T(8,128)(2,1)S(1)} %constant_dynamic-update-slice_fusion), channel_id=1, source_target_pairs={{0,4},{4,8},{8,12},{12,16},{16,20},{20,24},{24,28},{28,32},{32,36}... | collective-permute-start | bytes 786440 | tf_op jit(solution)/shard_map/ppermute | solution.py:40
  7.6 4.9 %collective-permute-start.20 = (bf16[128,1024]{1,0:T(8,128)(2,1)S(1)}, bf16[128,1024]{1,0:T(8,128)(2,1)S(1)}, u32[]{:S(2)}, u32[]{:S(2)}) collective-permute-start(bf16[128,1024]{1,0:T(8,128)(2,1)S(1)} %constant_dynamic-update-slice_fusion), channel_id=1, source_target_pairs={{0,16},{4,20},{8,24},{12,28},{16,32},{20,36},{24,40},{28,44},{32,4... | collective-permute-start | bytes 786440 | tf_op jit(solution)/shard_map/ppermute | solution.py:40
  14.7 4.8 %collective-permute-start.2 = (f32[4,128,128]{2,1,0:T(8,128)S(1)}, f32[4,128,128]{2,1,0:T(8,128)S(1)}, u32[]{:S(2)}, u32[]{:S(2)}) collective-permute-start(f32[4,128,128]{2,1,0:T(8,128)S(1)} %fusion.31), channel_id=1, source_target_pairs={{0,12},{4,16},{8,20},{12,24},{16,28},{20,32},{24,36},{28,40},{32,4... | collective-permute-start | bytes 786440 | tf_op jit(solution)/shard_map/ppermute | solution.py:30
  19.5 3.5 collective-permute-start.1
  23.1 4.1 %collective-permute-start = (f32[4,128,128]{2,1,0:T(8,128)S(1)}, f32[4,128,128]{2,1,0:T(8,128)S(1)}, u32[]{:S(2)}, u32[]{:S(2)}) collective-permute-start(f32[4,128,128]{2,1,0:T(8,128)S(1)} %fusion.31), channel_id=1, source_target_pairs={{0,4},{4,8},{8,12},{12,16},{16,20},{20,24},{24,28},{28,32},{32,36}... | collective-permute-start | bytes 786440 | tf_op jit(solution)/shard_map/ppermute | solution.py:30
  30.5 5.2 %collective-permute-start.22 = (bf16[128,1024]{1,0:T(8,128)(2,1)S(1)}, bf16[128,1024]{1,0:T(8,128)(2,1)S(1)}, u32[]{:S(2)}, u32[]{:S(2)}) collective-permute-start(bf16[128,1024]{1,0:T(8,128)(2,1)S(1)} %constant_dynamic-update-slice_fusion), channel_id=1, source_target_pairs={{0,8},{4,12},{8,16},{12,20},{16,24},{20,28},{24,32},{28,36},{32,40... | collective-permute-start | bytes 786440 | tf_op jit(solution)/shard_map/ppermute | solution.py:40
  35.8 2.5 collective-permute-done.1
  38.2 4.2 %collective-permute-start.21 = (bf16[128,1024]{1,0:T(8,128)(2,1)S(1)}, bf16[128,1024]{1,0:T(8,128)(2,1)S(1)}, u32[]{:S(2)}, u32[]{:S(2)}) collective-permute-start(bf16[128,1024]{1,0:T(8,128)(2,1)S(1)} %constant_dynamic-update-slice_fusion), channel_id=1, source_target_pairs={{0,12},{4,16},{8,20},{12,24},{16,28},{20,32},{24,36},{28,40},{32,4... | collective-permute-start | bytes 786440 | tf_op jit(solution)/shard_map/ppermute | solution.py:40
  42.4 1.4 collective-permute-done
  44.6 12.9 %collective-permute-start.5 = (f32[4,128,128]{2,1,0:T(8,128)}, f32[4,128,128]{2,1,0:T(8,128)}, u32[]{:S(2)}, u32[]{:S(2)}) collective-permute-start(f32[4,128,128]{2,1,0:T(8,128)} %add_add_fusion.5), channel_id=1, source_target_pairs={{0,48},{4,52},{8,56},{12,60},{16,64},{20,68},{24,72},{28,76},{32,8... | collective-permute-start | bytes 786440 | tf_op jit(solution)/shard_map/ppermute | solution.py:30
  57.5 4.7 %collective-permute-start.4 = (f32[4,128,128]{2,1,0:T(8,128)}, f32[4,128,128]{2,1,0:T(8,128)}, u32[]{:S(2)}, u32[]{:S(2)}) collective-permute-start(f32[4,128,128]{2,1,0:T(8,128)} %add_add_fusion.5), channel_id=1, source_target_pairs={{0,32},{4,36},{8,40},{12,44},{16,48},{20,52},{24,56},{28,60},{32,6... | collective-permute-start | bytes 786440 | tf_op jit(solution)/shard_map/ppermute | solution.py:30
  62.2 2.1 collective-permute-start.3
  67.5 1.5 fusion.72
  69.0 1.6 convolution_bitcast_fusion
  74.0 1.4 reshape.425
  77.4 2.3 scatter_fusion
  79.9 2.8 collective-permute-done.5
  82.7 16.3 %collective-permute-done.4 = f32[4,128,128]{2,1,0:T(8,128)} collective-permute-done((f32[4,128,128]{2,1,0:T(8,128)}, f32[4,128,128]{2,1,0:T(8,128)}, u32[]{:S(2)}, u32[]{:S(2)}) %collective-permute-start.4) | collective-permute-done | bytes 262176 | tf_op jit(solution)/shard_map/ppermute | solution.py:30
  99.0 15.7 %collective-permute-done.3 = f32[4,128,128]{2,1,0:T(8,128)} collective-permute-done((f32[4,128,128]{2,1,0:T(8,128)}, f32[4,128,128]{2,1,0:T(8,128)}, u32[]{:S(2)}, u32[]{:S(2)}) %collective-permute-start.3) | collective-permute-done | bytes 262176 | tf_op jit(solution)/shard_map/ppermute | solution.py:30
  115.9 24.4 %collective-permute-start.8 = (f32[4,128,128]{2,1,0:T(8,128)S(1)}, f32[4,128,128]{2,1,0:T(8,128)S(1)}, u32[]{:S(2)}, u32[]{:S(2)}) collective-permute-start(f32[4,128,128]{2,1,0:T(8,128)S(1)} %add_add_fusion.4), channel_id=1, source_target_pairs={{0,192},{4,196},{8,200},{12,204},{16,208},{20,212},{24,216},{28,22... | collective-permute-start | bytes 786440 | tf_op jit(solution)/shard_map/ppermute | solution.py:30
  140.3 5.2 %collective-permute-start.7 = (f32[4,128,128]{2,1,0:T(8,128)S(1)}, f32[4,128,128]{2,1,0:T(8,128)S(1)}, u32[]{:S(2)}, u32[]{:S(2)}) collective-permute-start(f32[4,128,128]{2,1,0:T(8,128)S(1)} %add_add_fusion.4), channel_id=1, source_target_pairs={{0,128},{4,132},{8,136},{12,140},{16,144},{20,148},{24,152},{28,15... | collective-permute-start | bytes 786440 | tf_op jit(solution)/shard_map/ppermute | solution.py:30
  145.5 1.3 collective-permute-start.6
  147.6 1.4 collective-permute-start.25
  149.0 11.4 %collective-permute-done.8 = f32[4,128,128]{2,1,0:T(8,128)S(1)} collective-permute-done((f32[4,128,128]{2,1,0:T(8,128)S(1)}, f32[4,128,128]{2,1,0:T(8,128)S(1)}, u32[]{:S(2)}, u32[]{:S(2)}) %collective-permute-start.8) | collective-permute-done | bytes 262176 | tf_op jit(solution)/shard_map/ppermute | solution.py:30
  160.5 10.9 %collective-permute-done.6 = f32[4,128,128]{2,1,0:T(8,128)S(1)} collective-permute-done((f32[4,128,128]{2,1,0:T(8,128)S(1)}, f32[4,128,128]{2,1,0:T(8,128)S(1)}, u32[]{:S(2)}, u32[]{:S(2)}) %collective-permute-start.6) | collective-permute-done | bytes 262176 | tf_op jit(solution)/shard_map/ppermute | solution.py:30
  171.5 14.9 %collective-permute-start.9 = (f32[4,128,128]{2,1,0:T(8,128)S(1)}, f32[4,128,128]{2,1,0:T(8,128)S(1)}, u32[]{:S(2)}, u32[]{:S(2)}) collective-permute-start(f32[4,128,128]{2,1,0:T(8,128)S(1)} %add_add_fusion.3), channel_id=1, source_target_pairs={{0,256},{4,260},{8,264},{12,268},{16,272},{20,276},{24,280},{28,28... | collective-permute-start | bytes 786440 | tf_op jit(solution)/shard_map/ppermute | solution.py:30
  187.1 1.3 collective-permute-start.26
  191.1 1.9 collective-permute-start.24
  193.8 1.5 multiply_reduce_fusion.1
  195.3 9.6 %all-reduce = (f32[128]{0:T(128)}, f32[128]{0:T(128)}) all-reduce(f32[128]{0:T(128)} %get-tuple-element.19, f32[128]{0:T(128)} %get-tuple-element.18), channel_id=1, replica_groups=mesh['ctx'=128,'head'=4] {'head'}, use_global_device_ids=true, to_apply=%region_3.4 | all-reduce | flops 256 | bytes 2048 | tf_op jit(solution)/shard_map/psum | solution.py:142
  207.8 1.3 collective-permute-start.12
  209.1 1.3 collective-permute-start.11
  210.4 1.9 collective-permute-start.10
  213.3 1.7 copy.81
  219.0 3.8 collective-permute-done.12
  222.8 1.9 collective-permute-done.10
  225.9 1.4 collective-permute-start.15
  227.4 1.3 collective-permute-start.14
  228.7 1.3 collective-permute-start.13
  231.2 56.9 %collective-permute-done.15 = f32[4,128,128]{1,2,0:T(8,128)S(1)} collective-permute-done((f32[4,128,128]{1,2,0:T(8,128)S(1)}, f32[4,128,128]{1,2,0:T(8,128)S(1)}, u32[]{:S(2)}, u32[]{:S(2)}) %collective-permute-start.15) | collective-permute-done | bytes 262176 | tf_op jit(solution)/shard_map/ppermute | solution.py:30
  288.1 1.4 collective-permute-start.18
  289.6 1.3 collective-permute-start.17
  290.9 1.3 collective-permute-start.16
  292.6 34.7 %collective-permute-done.18 = f32[4,128,128]{1,2,0:T(8,128)S(1)} collective-permute-done((f32[4,128,128]{1,2,0:T(8,128)S(1)}, f32[4,128,128]{1,2,0:T(8,128)S(1)}, u32[]{:S(2)}, u32[]{:S(2)}) %collective-permute-start.18) | collective-permute-done | bytes 262176 | tf_op jit(solution)/shard_map/ppermute | solution.py:30
  327.3 3.4 collective-permute-done.17
  330.7 3.1 collective-permute-done.16
  333.8 1.4 collective-permute-start.19
  336.4 46.8 %collective-permute-done.19 = f32[4,128,128]{1,2,0:T(8,128)S(1)} collective-permute-done((f32[4,128,128]{1,2,0:T(8,128)S(1)}, f32[4,128,128]{1,2,0:T(8,128)S(1)}, u32[]{:S(2)}, u32[]{:S(2)}) %collective-permute-start.19) | collective-permute-done | bytes 262176 | tf_op jit(solution)/shard_map/ppermute | solution.py:30
  (154 shorter events, 36.8 us)
Async XLA Ops:
  0.6 66.9 %copy-start = (bf16[128,512]{1,0:T(8,128)(2,1)S(1)}, bf16[128,512]{1,0:T(8,128)(2,1)}, u32[]{:S(2)}) copy-start(bf16[128,512]{1,0:T(8,128)(2,1)} %param.15) | copy-start | bytes 393220
  0.6 26.8 %copy-start.20 = (bf16[128,512]{1,0:T(8,128)(2,1)S(1)}, bf16[128,512]{1,0:T(8,128)(2,1)}, u32[]{:S(2)}) copy-start(bf16[128,512]{1,0:T(8,128)(2,1)} %param.11) | copy-start | bytes 393220
  0.7 27.0 %copy-start.15 = (bf16[128,512]{1,0:T(8,128)(2,1)S(1)}, bf16[128,512]{1,0:T(8,128)(2,1)}, u32[]{:S(2)}) copy-start(bf16[128,512]{1,0:T(8,128)(2,1)} %param.12) | copy-start | bytes 393220
  0.7 26.5 %copy-start.30 = (s32[1,3]{1,0:T(1,128)S(1)}, s32[1,3]{1,0:T(1,128)}, u32[]{:S(2)}) copy-start(s32[1,3]{1,0:T(1,128)} %param.19) | copy-start | bytes 40
  0.7 26.7 %copy-start.12 = (bf16[128,512]{1,0:T(8,128)(2,1)S(1)}, bf16[128,512]{1,0:T(8,128)(2,1)}, u32[]{:S(2)}) copy-start(bf16[128,512]{1,0:T(8,128)(2,1)} %param.10) | copy-start | bytes 393220
  0.7 28.9 %copy-start.26 = (bf16[128,512]{1,0:T(8,128)(2,1)S(1)}, bf16[128,512]{1,0:T(8,128)(2,1)}, u32[]{:S(2)}) copy-start(bf16[128,512]{1,0:T(8,128)(2,1)} %param.14) | copy-start | bytes 393220
  1.7 28.7 %copy-start.27 = (bf16[128,512]{1,0:T(8,128)(2,1)S(1)}, bf16[128,512]{1,0:T(8,128)(2,1)}, u32[]{:S(2)}) copy-start(bf16[128,512]{1,0:T(8,128)(2,1)} %param.18) | copy-start | bytes 393220
  2.7 61.7 %collective-permute-start.23 = (bf16[128,1024]{1,0:T(8,128)(2,1)S(1)}, bf16[128,1024]{1,0:T(8,128)(2,1)S(1)}, u32[]{:S(2)}, u32[]{:S(2)}) collective-permute-start(bf16[128,1024]{1,0:T(8,128)(2,1)S(1)} %constant_dynamic-update-slice_fusion), channel_id=1, source_target_pairs={{0,4},{4,8},{8,12},{12,16},{16,20},{20,24},{24,28},{28,32},{32,36}... | collective-permute-start | bytes 786440 | tf_op jit(solution)/shard_map/ppermute | solution.py:40
  7.6 49.9 %collective-permute-start.20 = (bf16[128,1024]{1,0:T(8,128)(2,1)S(1)}, bf16[128,1024]{1,0:T(8,128)(2,1)S(1)}, u32[]{:S(2)}, u32[]{:S(2)}) collective-permute-start(bf16[128,1024]{1,0:T(8,128)(2,1)S(1)} %constant_dynamic-update-slice_fusion), channel_id=1, source_target_pairs={{0,16},{4,20},{8,24},{12,28},{16,32},{20,36},{24,40},{28,44},{32,4... | collective-permute-start | bytes 786440 | tf_op jit(solution)/shard_map/ppermute | solution.py:40
  13.6 31.0 %copy-start.17 = (bf16[128,512]{0,1:T(8,128)(2,1)}, bf16[128,512]{0,1:T(8,128)(2,1)S(1)}, u32[]{:S(2)}) copy-start(bf16[128,512]{0,1:T(8,128)(2,1)S(1)} %copy.161) | copy-start | bytes 393220
  14.7 29.9 %copy-start.1 = (f32[4,128,128]{2,1,0:T(8,128)}, f32[4,128,128]{2,1,0:T(8,128)S(1)}, u32[]{:S(2)}) copy-start(f32[4,128,128]{2,1,0:T(8,128)S(1)} %fusion.31) | copy-start | bytes 786436
  14.7 15.8 %collective-permute-start.2 = (f32[4,128,128]{2,1,0:T(8,128)S(1)}, f32[4,128,128]{2,1,0:T(8,128)S(1)}, u32[]{:S(2)}, u32[]{:S(2)}) collective-permute-start(f32[4,128,128]{2,1,0:T(8,128)S(1)} %fusion.31), channel_id=1, source_target_pairs={{0,12},{4,16},{8,20},{12,24},{16,28},{20,32},{24,36},{28,40},{32,4... | collective-permute-start | bytes 786440 | tf_op jit(solution)/shard_map/ppermute | solution.py:30
  19.5 18.7 %collective-permute-start.1 = (f32[4,128,128]{2,1,0:T(8,128)S(1)}, f32[4,128,128]{2,1,0:T(8,128)S(1)}, u32[]{:S(2)}, u32[]{:S(2)}) collective-permute-start(f32[4,128,128]{2,1,0:T(8,128)S(1)} %fusion.31), channel_id=1, source_target_pairs={{0,8},{4,12},{8,16},{12,20},{16,24},{20,28},{24,32},{28,36},{32,40... | collective-permute-start | bytes 786440 | tf_op jit(solution)/shard_map/ppermute | solution.py:30
  23.1 20.8 %collective-permute-start = (f32[4,128,128]{2,1,0:T(8,128)S(1)}, f32[4,128,128]{2,1,0:T(8,128)S(1)}, u32[]{:S(2)}, u32[]{:S(2)}) collective-permute-start(f32[4,128,128]{2,1,0:T(8,128)S(1)} %fusion.31), channel_id=1, source_target_pairs={{0,4},{4,8},{8,12},{12,16},{16,20},{20,24},{24,28},{28,32},{32,36}... | collective-permute-start | bytes 786440 | tf_op jit(solution)/shard_map/ppermute | solution.py:30
  30.5 33.9 %collective-permute-start.22 = (bf16[128,1024]{1,0:T(8,128)(2,1)S(1)}, bf16[128,1024]{1,0:T(8,128)(2,1)S(1)}, u32[]{:S(2)}, u32[]{:S(2)}) collective-permute-start(bf16[128,1024]{1,0:T(8,128)(2,1)S(1)} %constant_dynamic-update-slice_fusion), channel_id=1, source_target_pairs={{0,8},{4,12},{8,16},{12,20},{16,24},{20,28},{24,32},{28,36},{32,40... | collective-permute-start | bytes 786440 | tf_op jit(solution)/shard_map/ppermute | solution.py:40
  38.2 24.0 %collective-permute-start.21 = (bf16[128,1024]{1,0:T(8,128)(2,1)S(1)}, bf16[128,1024]{1,0:T(8,128)(2,1)S(1)}, u32[]{:S(2)}, u32[]{:S(2)}) collective-permute-start(bf16[128,1024]{1,0:T(8,128)(2,1)S(1)} %constant_dynamic-update-slice_fusion), channel_id=1, source_target_pairs={{0,12},{4,16},{8,20},{12,24},{16,28},{20,32},{24,36},{28,40},{32,4... | collective-permute-start | bytes 786440 | tf_op jit(solution)/shard_map/ppermute | solution.py:40
  44.6 19.9 %copy-start.23 = (bf16[128,512]{1,0:T(8,128)(2,1)S(1)}, bf16[128,512]{1,0:T(8,128)(2,1)}, u32[]{:S(2)}) copy-start(bf16[128,512]{1,0:T(8,128)(2,1)} %param.17) | copy-start | bytes 393220
  44.6 38.1 %collective-permute-start.5 = (f32[4,128,128]{2,1,0:T(8,128)}, f32[4,128,128]{2,1,0:T(8,128)}, u32[]{:S(2)}, u32[]{:S(2)}) collective-permute-start(f32[4,128,128]{2,1,0:T(8,128)} %add_add_fusion.5), channel_id=1, source_target_pairs={{0,48},{4,52},{8,56},{12,60},{16,64},{20,68},{24,72},{28,76},{32,8... | collective-permute-start | bytes 786440 | tf_op jit(solution)/shard_map/ppermute | solution.py:30
  57.5 41.5 %collective-permute-start.4 = (f32[4,128,128]{2,1,0:T(8,128)}, f32[4,128,128]{2,1,0:T(8,128)}, u32[]{:S(2)}, u32[]{:S(2)}) collective-permute-start(f32[4,128,128]{2,1,0:T(8,128)} %add_add_fusion.5), channel_id=1, source_target_pairs={{0,32},{4,36},{8,40},{12,44},{16,48},{20,52},{24,56},{28,60},{32,6... | collective-permute-start | bytes 786440 | tf_op jit(solution)/shard_map/ppermute | solution.py:30
  62.2 52.4 %collective-permute-start.3 = (f32[4,128,128]{2,1,0:T(8,128)}, f32[4,128,128]{2,1,0:T(8,128)}, u32[]{:S(2)}, u32[]{:S(2)}) collective-permute-start(f32[4,128,128]{2,1,0:T(8,128)} %add_add_fusion.5), channel_id=1, source_target_pairs={{0,16},{4,20},{8,24},{12,28},{16,32},{20,36},{24,40},{28,44},{32,4... | collective-permute-start | bytes 786440 | tf_op jit(solution)/shard_map/ppermute | solution.py:30
  115.9 44.6 %collective-permute-start.8 = (f32[4,128,128]{2,1,0:T(8,128)S(1)}, f32[4,128,128]{2,1,0:T(8,128)S(1)}, u32[]{:S(2)}, u32[]{:S(2)}) collective-permute-start(f32[4,128,128]{2,1,0:T(8,128)S(1)} %add_add_fusion.4), channel_id=1, source_target_pairs={{0,192},{4,196},{8,200},{12,204},{16,208},{20,212},{24,216},{28,22... | collective-permute-start | bytes 786440 | tf_op jit(solution)/shard_map/ppermute | solution.py:30
  140.3 20.2 %collective-permute-start.7 = (f32[4,128,128]{2,1,0:T(8,128)S(1)}, f32[4,128,128]{2,1,0:T(8,128)S(1)}, u32[]{:S(2)}, u32[]{:S(2)}) collective-permute-start(f32[4,128,128]{2,1,0:T(8,128)S(1)} %add_add_fusion.4), channel_id=1, source_target_pairs={{0,128},{4,132},{8,136},{12,140},{16,144},{20,148},{24,152},{28,15... | collective-permute-start | bytes 786440 | tf_op jit(solution)/shard_map/ppermute | solution.py:30
  145.5 25.8 %collective-permute-start.6 = (f32[4,128,128]{2,1,0:T(8,128)S(1)}, f32[4,128,128]{2,1,0:T(8,128)S(1)}, u32[]{:S(2)}, u32[]{:S(2)}) collective-permute-start(f32[4,128,128]{2,1,0:T(8,128)S(1)} %add_add_fusion.4), channel_id=1, source_target_pairs={{0,64},{4,68},{8,72},{12,76},{16,80},{20,84},{24,88},{28,92},{32,9... | collective-permute-start | bytes 786440 | tf_op jit(solution)/shard_map/ppermute | solution.py:30
  147.6 45.4 %copy-start.2 = (f32[4,128,128]{2,1,0:T(8,128)S(1)}, f32[4,128,128]{2,1,0:T(8,128)}, u32[]{:S(2)}) copy-start(f32[4,128,128]{2,1,0:T(8,128)} %copy-done.1) | copy-start | bytes 786436
  147.6 61.5 %collective-permute-start.25 = (bf16[128,1024]{1,0:T(8,128)(2,1)}, bf16[128,1024]{1,0:T(8,128)(2,1)}, u32[]{:S(2)}, u32[]{:S(2)}) collective-permute-start(bf16[128,1024]{1,0:T(8,128)(2,1)} %pad_maximum_fusion.1), channel_id=1, source_target_pairs={{8,0},{12,4},{16,8},{20,12},{24,16},{28,20},{32,24},{36,28},{40,32... | collective-permute-start | bytes 786440 | tf_op jit(solution)/shard_map/ppermute | solution.py:40
  171.4 22.3 %copy-start.3 = (f32[128,512]{0,1:T(8,128)S(1)}, f32[128,512]{0,1:T(8,128)}, u32[]{:S(2)}) copy-start(f32[128,512]{0,1:T(8,128)} %copy.48) | copy-start | bytes 786436
  171.4 22.3 %copy-start.13 = (bf16[128,512]{1,0:T(8,128)(2,1)S(1)}, bf16[128,512]{1,0:T(8,128)(2,1)}, u32[]{:S(2)}) copy-start(bf16[128,512]{1,0:T(8,128)(2,1)} %param.10) | copy-start | bytes 393220
  171.5 22.3 %copy-start.19 = (f32[128,4,128]{0,2,1:T(8,128)S(1)}, f32[128,4,128]{0,2,1:T(8,128)}, u32[]{:S(2)}) copy-start(f32[128,4,128]{0,2,1:T(8,128)} %convolution_bitcast_fusion.9) | copy-start | bytes 786436
  171.5 22.3 %copy-start.28 = (f32[512]{0:T(512)S(1)}, f32[512]{0:T(512)}, u32[]{:S(2)}) copy-start(f32[512]{0:T(512)} %param.13) | copy-start | bytes 6148
  171.5 21.5 %collective-permute-start.9 = (f32[4,128,128]{2,1,0:T(8,128)S(1)}, f32[4,128,128]{2,1,0:T(8,128)S(1)}, u32[]{:S(2)}, u32[]{:S(2)}) collective-permute-start(f32[4,128,128]{2,1,0:T(8,128)S(1)} %add_add_fusion.3), channel_id=1, source_target_pairs={{0,256},{4,260},{8,264},{12,268},{16,272},{20,276},{24,280},{28,28... | collective-permute-start | bytes 786440 | tf_op jit(solution)/shard_map/ppermute | solution.py:30
  187.1 23.3 %collective-permute-start.26 = (bf16[128,1024]{1,0:T(8,128)(2,1)}, bf16[128,1024]{1,0:T(8,128)(2,1)}, u32[]{:S(2)}, u32[]{:S(2)}) collective-permute-start(bf16[128,1024]{1,0:T(8,128)(2,1)} %pad_maximum_fusion.2), channel_id=1, source_target_pairs={{12,0},{16,4},{20,8},{24,12},{28,16},{32,20},{36,24},{40,28},{44,3... | collective-permute-start | bytes 786440 | tf_op jit(solution)/shard_map/ppermute | solution.py:40
  189.1 27.9 %collective-permute-start.27 = (bf16[128,1024]{1,0:T(8,128)(2,1)}, bf16[128,1024]{1,0:T(8,128)(2,1)}, u32[]{:S(2)}, u32[]{:S(2)}) collective-permute-start(bf16[128,1024]{1,0:T(8,128)(2,1)} %pad_maximum_fusion.3), channel_id=1, source_target_pairs={{16,0},{20,4},{24,8},{28,12},{32,16},{36,20},{40,24},{44,28},{48,3... | collective-permute-start | bytes 786440 | tf_op jit(solution)/shard_map/ppermute | solution.py:40
  191.1 26.9 %collective-permute-start.24 = (bf16[128,1024]{1,0:T(8,128)(2,1)}, bf16[128,1024]{1,0:T(8,128)(2,1)}, u32[]{:S(2)}, u32[]{:S(2)}) collective-permute-start(bf16[128,1024]{1,0:T(8,128)(2,1)} %pad_maximum_fusion), channel_id=1, source_target_pairs={{4,0},{8,4},{12,8},{16,12},{20,16},{24,20},{28,24},{32,28},{36,32}... | collective-permute-start | bytes 786440 | tf_op jit(solution)/shard_map/ppermute | solution.py:40
  207.8 15.0 %collective-permute-start.12 = (f32[4,128,128]{1,2,0:T(8,128)S(1)}, f32[4,128,128]{1,2,0:T(8,128)}, u32[]{:S(2)}, u32[]{:S(2)}) collective-permute-start(f32[4,128,128]{1,2,0:T(8,128)S(1)} %convolution_bitcast_fusion.5), channel_id=1, source_target_pairs={{12,0},{16,4},{20,8},{24,12},{28,16},{32,20},{36,24},{40,28},{44,3... | collective-permute-start | bytes 786440 | tf_op jit(solution)/shard_map/ppermute | solution.py:30
  209.1 13.7 %collective-permute-start.11 = (f32[4,128,128]{1,2,0:T(8,128)S(1)}, f32[4,128,128]{1,2,0:T(8,128)}, u32[]{:S(2)}, u32[]{:S(2)}) collective-permute-start(f32[4,128,128]{1,2,0:T(8,128)S(1)} %convolution_bitcast_fusion.5), channel_id=1, source_target_pairs={{8,0},{12,4},{16,8},{20,12},{24,16},{28,20},{32,24},{36,28},{40,32... | collective-permute-start | bytes 786440 | tf_op jit(solution)/shard_map/ppermute | solution.py:30
  210.4 14.3 %collective-permute-start.10 = (f32[4,128,128]{1,2,0:T(8,128)S(1)}, f32[4,128,128]{1,2,0:T(8,128)}, u32[]{:S(2)}, u32[]{:S(2)}) collective-permute-start(f32[4,128,128]{1,2,0:T(8,128)S(1)} %convolution_bitcast_fusion.5), channel_id=1, source_target_pairs={{4,0},{8,4},{12,8},{16,12},{20,16},{24,20},{28,24},{32,28},{36,32}... | collective-permute-start | bytes 786440 | tf_op jit(solution)/shard_map/ppermute | solution.py:30
  225.9 62.1 %collective-permute-start.15 = (f32[4,128,128]{1,2,0:T(8,128)S(1)}, f32[4,128,128]{1,2,0:T(8,128)S(1)}, u32[]{:S(2)}, u32[]{:S(2)}) collective-permute-start(f32[4,128,128]{1,2,0:T(8,128)S(1)} %add_add_fusion.2), channel_id=1, source_target_pairs={{48,0},{52,4},{56,8},{60,12},{64,16},{68,20},{72,24},{76,28},{80,3... | collective-permute-start | bytes 786440 | tf_op jit(solution)/shard_map/ppermute | solution.py:30
  227.4 60.7 %collective-permute-start.14 = (f32[4,128,128]{1,2,0:T(8,128)S(1)}, f32[4,128,128]{1,2,0:T(8,128)S(1)}, u32[]{:S(2)}, u32[]{:S(2)}) collective-permute-start(f32[4,128,128]{1,2,0:T(8,128)S(1)} %add_add_fusion.2), channel_id=1, source_target_pairs={{32,0},{36,4},{40,8},{44,12},{48,16},{52,20},{56,24},{60,28},{64,3... | collective-permute-start | bytes 786440 | tf_op jit(solution)/shard_map/ppermute | solution.py:30
  228.7 59.4 %collective-permute-start.13 = (f32[4,128,128]{1,2,0:T(8,128)S(1)}, f32[4,128,128]{1,2,0:T(8,128)S(1)}, u32[]{:S(2)}, u32[]{:S(2)}) collective-permute-start(f32[4,128,128]{1,2,0:T(8,128)S(1)} %add_add_fusion.2), channel_id=1, source_target_pairs={{16,0},{20,4},{24,8},{28,12},{32,16},{36,20},{40,24},{44,28},{48,3... | collective-permute-start | bytes 786440 | tf_op jit(solution)/shard_map/ppermute | solution.py:30
  230.9 61.3 %copy-start.18 = (bf16[128,512]{0,1:T(8,128)(2,1)S(1)}, bf16[128,512]{0,1:T(8,128)(2,1)}, u32[]{:S(2)}) copy-start(bf16[128,512]{0,1:T(8,128)(2,1)} %copy-done.17) | copy-start | bytes 393220
  230.9 61.5 %copy-start.11 = (bf16[4,128,128]{2,1,0:T(8,128)(2,1)S(1)}, bf16[4,128,128]{2,1,0:T(8,128)(2,1)}, u32[]{:S(2)}) copy-start(bf16[4,128,128]{2,1,0:T(8,128)(2,1)} %copy-done.10) | copy-start | bytes 393220
  288.1 47.1 %copy-start.14 = (bf16[128,512]{1,0:T(8,128)(2,1)S(1)}, bf16[128,512]{1,0:T(8,128)(2,1)}, u32[]{:S(2)}) copy-start(bf16[128,512]{1,0:T(8,128)(2,1)} %param.10) | copy-start | bytes 393220
  288.1 39.2 %collective-permute-start.18 = (f32[4,128,128]{1,2,0:T(8,128)S(1)}, f32[4,128,128]{1,2,0:T(8,128)S(1)}, u32[]{:S(2)}, u32[]{:S(2)}) collective-permute-start(f32[4,128,128]{1,2,0:T(8,128)S(1)} %add_add_fusion.1), channel_id=1, source_target_pairs={{192,0},{196,4},{200,8},{204,12},{208,16},{212,20},{216,24},{220,2... | collective-permute-start | bytes 786440 | tf_op jit(solution)/shard_map/ppermute | solution.py:30
  289.6 41.1 %collective-permute-start.17 = (f32[4,128,128]{1,2,0:T(8,128)S(1)}, f32[4,128,128]{1,2,0:T(8,128)S(1)}, u32[]{:S(2)}, u32[]{:S(2)}) collective-permute-start(f32[4,128,128]{1,2,0:T(8,128)S(1)} %add_add_fusion.1), channel_id=1, source_target_pairs={{128,0},{132,4},{136,8},{140,12},{144,16},{148,20},{152,24},{156,2... | collective-permute-start | bytes 786440 | tf_op jit(solution)/shard_map/ppermute | solution.py:30
  290.9 42.9 %collective-permute-start.16 = (f32[4,128,128]{1,2,0:T(8,128)S(1)}, f32[4,128,128]{1,2,0:T(8,128)S(1)}, u32[]{:S(2)}, u32[]{:S(2)}) collective-permute-start(f32[4,128,128]{1,2,0:T(8,128)S(1)} %add_add_fusion.1), channel_id=1, source_target_pairs={{64,0},{68,4},{72,8},{76,12},{80,16},{84,20},{88,24},{92,28},{96,3... | collective-permute-start | bytes 786440 | tf_op jit(solution)/shard_map/ppermute | solution.py:30
  292.4 43.9 %copy-start.25 = (bf16[4,128,128]{2,1,0:T(8,128)(2,1)S(1)}, bf16[4,128,128]{2,1,0:T(8,128)(2,1)}, u32[]{:S(2)}) copy-start(bf16[4,128,128]{2,1,0:T(8,128)(2,1)} %copy-done.24) | copy-start | bytes 393220
  333.8 49.5 %copy-start.21 = (bf16[128,512]{1,0:T(8,128)(2,1)S(1)}, bf16[128,512]{1,0:T(8,128)(2,1)}, u32[]{:S(2)}) copy-start(bf16[128,512]{1,0:T(8,128)(2,1)} %param.11) | copy-start | bytes 393220
  333.8 49.5 %collective-permute-start.19 = (f32[4,128,128]{1,2,0:T(8,128)S(1)}, f32[4,128,128]{1,2,0:T(8,128)S(1)}, u32[]{:S(2)}, u32[]{:S(2)}) collective-permute-start(f32[4,128,128]{1,2,0:T(8,128)S(1)} %add_add_fusion), channel_id=1, source_target_pairs={{256,0},{260,4},{264,8},{268,12},{272,16},{276,20},{280,24},{284,2... | collective-permute-start | bytes 786440 | tf_op jit(solution)/shard_map/ppermute | solution.py:30
  (12 other events, 69.5 us)

commit v4 on v1

--- a/solution.py
+++ b/solution.py
@@ -19,7 +19,8 @@
             pairs = [(i, i - distance) for i in range(distance, count)]
         else:
             pairs = [(i, i + distance) for i in range(count - distance)]
-        total = join(total, lax.ppermute(total, axis, pairs))
+        sent = lax.ppermute(total.astype(jnp.bfloat16), axis, pairs)
+        total = join(total, sent.astype(jnp.float32))
         distance *= 2
     return (total - shard.astype(jnp.float32)).astype(shard.dtype)
 

time: 308 us -> 233 us (0.76)
  the two profiles are of different devices: /device:TPU:1 before, /device:TPU:72 now
where the time goes in v4:
time: 233 us; the launch traced here: 232 us
  starting transfers between devices  86.3 us (37%)
  waiting for transfers between devices  84 us (36%)
  other arithmetic  20.5 us (9%)
  local copies, waits for them, and re-layouts  19.8 us (8%)
  blocking collectives  11.2 us (5%)
  matrix products  8.33 us (4%)
    ppermute x14, waiting for transfers between devices, carried_in(): sent = lax.ppermute(total.astype(jnp.bfloat16), axis, pairs)  78.2 us
    ppermute x14, starting transfers between devices, carried_in(): sent = lax.ppermute(total.astype(jnp.bfloat16), axis, pairs)  57.9 us
    ppermute x8, starting transfers between devices, from_behind(): return lax.ppermute(shard, axis, pairs)  28.5 us
    psum x1, blocking collectives, per_device(): square_sum, cross_sum = lax.psum((square_sum, cross_sum), 'head')  11.2 us
    unnamed x91, local copies, waits for them, and re-layouts  9 us
    ppermute x8, waiting for transfers between devices, from_behind(): return lax.ppermute(shard, axis, pairs)  5.84 us
    convert_element_type x12, other arithmetic, carried_in(): sent = lax.ppermute(total.astype(jnp.bfloat16), axis, pairs)  5.35 us
  transfers between devices with their start and end apart: 22, of which 12 were waited for; matrix products, arithmetic and copies ran while one was open for 16% of the time, Pallas kernels for 0%

profile of v4, /device:TPU:72, one launch (start us, length us, event | category | flops | bytes accessed | tf_op | source)
XLA Modules:
  0.0 231.8 jit_solution(4610234562117210082)
XLA Ops:
  0.7 1.7 constant_dynamic-update-slice_fusion.1
  2.3 1.6 constant_dynamic-update-slice_fusion
  3.9 2.0 collective-permute-start.17
  6.0 3.8 %collective-permute-start.16 = (bf16[128,1024]{1,0:T(8,128)(2,1)}, bf16[128,1024]{1,0:T(8,128)(2,1)S(1)}, u32[]{:S(2)}, u32[]{:S(2)}) collective-permute-start(bf16[128,1024]{1,0:T(8,128)(2,1)} %constant_dynamic-update-slice_fusion), channel_id=1, source_target_pairs={{0,8},{4,12},{8,16},{12,20},{16,24},{20,28},{24,32},{28,36},{32,40... | collective-permute-start | bytes 786440 | tf_op jit(solution)/shard_map/ppermute | solution.py:31
  9.8 6.4 %collective-permute-start.15 = (bf16[128,1024]{1,0:T(8,128)(2,1)}, bf16[128,1024]{1,0:T(8,128)(2,1)}, u32[]{:S(2)}, u32[]{:S(2)}) collective-permute-start(bf16[128,1024]{1,0:T(8,128)(2,1)} %constant_dynamic-update-slice_fusion), channel_id=1, source_target_pairs={{0,12},{4,16},{8,20},{12,24},{16,28},{20,32},{24,36},{28,40},{32,4... | collective-permute-start | bytes 786440 | tf_op jit(solution)/shard_map/ppermute | solution.py:31
  16.2 5.2 %collective-permute-start.14 = (bf16[128,1024]{1,0:T(8,128)(2,1)}, bf16[128,1024]{1,0:T(8,128)(2,1)}, u32[]{:S(2)}, u32[]{:S(2)}) collective-permute-start(bf16[128,1024]{1,0:T(8,128)(2,1)} %constant_dynamic-update-slice_fusion), channel_id=1, source_target_pairs={{0,16},{4,20},{8,24},{12,28},{16,32},{20,36},{24,40},{28,44},{32,4... | collective-permute-start | bytes 786440 | tf_op jit(solution)/shard_map/ppermute | solution.py:31
  21.4 1.0 copy.161
  22.4 1.1 fusion.84
  23.6 1.9 collective-permute-start
  27.3 11.4 %collective-permute-done = bf16[4,128,128]{2,1,0:T(8,128)(2,1)S(1)} collective-permute-done((bf16[4,128,128]{2,1,0:T(8,128)(2,1)S(1)}, bf16[4,128,128]{2,1,0:T(8,128)(2,1)S(1)}, u32[]{:S(2)}, u32[]{:S(2)}) %collective-permute-start) | collective-permute-done | bytes 131104 | tf_op jit(solution)/shard_map/ppermute | solution.py:22
  38.7 3.8 %collective-permute-start.1 = (bf16[4,128,128]{2,1,0:T(8,128)(2,1)S(1)}, bf16[4,128,128]{2,1,0:T(8,128)(2,1)S(1)}, u32[]{:S(2)}, u32[]{:S(2)}) collective-permute-start(bf16[4,128,128]{2,1,0:T(8,128)(2,1)S(1)} %fusion.24), channel_id=1, source_target_pairs={{0,8},{4,12},{8,16},{12,20},{16,24},{20,28},{24,32},{28,36},{32,40... | collective-permute-start | bytes 393224 | tf_op jit(solution)/shard_map/ppermute | solution.py:22
  43.4 2.8 %collective-permute-done.1 = bf16[4,128,128]{2,1,0:T(8,128)(2,1)S(1)} collective-permute-done((bf16[4,128,128]{2,1,0:T(8,128)(2,1)S(1)}, bf16[4,128,128]{2,1,0:T(8,128)(2,1)S(1)}, u32[]{:S(2)}, u32[]{:S(2)}) %collective-permute-start.1) | collective-permute-done | bytes 131104 | tf_op jit(solution)/shard_map/ppermute | solution.py:22
  46.9 8.2 %collective-permute-start.2 = (bf16[4,128,128]{2,1,0:T(8,128)(2,1)}, bf16[4,128,128]{2,1,0:T(8,128)(2,1)}, u32[]{:S(2)}, u32[]{:S(2)}) collective-permute-start(bf16[4,128,128]{2,1,0:T(8,128)(2,1)} %fusion.78), channel_id=1, source_target_pairs={{0,16},{4,20},{8,24},{12,28},{16,32},{20,36},{24,40},{28,44},{32,4... | collective-permute-start | bytes 393224 | tf_op jit(solution)/shard_map/ppermute | solution.py:22
  57.4 1.0 gather_fusion
  58.9 1.0 gather_fusion.1
  62.2 1.7 convolution_bitcast_fusion
  65.6 1.6 fusion.25
  67.2 9.1 %collective-permute-start.3 = (bf16[4,128,128]{2,1,0:T(8,128)(2,1)}, bf16[4,128,128]{2,1,0:T(8,128)(2,1)}, u32[]{:S(2)}, u32[]{:S(2)}) collective-permute-start(bf16[4,128,128]{2,1,0:T(8,128)(2,1)} %fusion.25), channel_id=1, source_target_pairs={{0,32},{4,36},{8,40},{12,44},{16,48},{20,52},{24,56},{28,60},{32,6... | collective-permute-start | bytes 393224 | tf_op jit(solution)/shard_map/ppermute | solution.py:22
  77.3 1.4 reshape.425
  78.9 1.2 scatter_fusion.1
  81.2 2.3 scatter_fusion
  84.4 1.0 fusion.83
  85.5 7.0 %collective-permute-start.4 = (bf16[4,128,128]{2,1,0:T(8,128)(2,1)S(1)}, bf16[4,128,128]{2,1,0:T(8,128)(2,1)S(1)}, u32[]{:S(2)}, u32[]{:S(2)}) collective-permute-start(bf16[4,128,128]{2,1,0:T(8,128)(2,1)S(1)} %get-tuple-element.24), channel_id=1, source_target_pairs={{0,64},{4,68},{8,72},{12,76},{16,80},{20,84},{24,88},{28,92},{32,9... | collective-permute-start | bytes 393224 | tf_op jit(solution)/shard_map/ppermute | solution.py:22
  93.3 11.4 %collective-permute-done.4 = bf16[4,128,128]{2,1,0:T(8,128)(2,1)S(1)} collective-permute-done((bf16[4,128,128]{2,1,0:T(8,128)(2,1)S(1)}, bf16[4,128,128]{2,1,0:T(8,128)(2,1)S(1)}, u32[]{:S(2)}, u32[]{:S(2)}) %collective-permute-start.4) | collective-permute-done | bytes 131104 | tf_op jit(solution)/shard_map/ppermute | solution.py:22
  104.7 3.3 %collective-permute-start.5 = (bf16[4,128,128]{2,1,0:T(8,128)(2,1)S(1)}, bf16[4,128,128]{2,1,0:T(8,128)(2,1)S(1)}, u32[]{:S(2)}, u32[]{:S(2)}) collective-permute-start(bf16[4,128,128]{2,1,0:T(8,128)(2,1)S(1)} %fusion.26), channel_id=1, source_target_pairs={{0,128},{4,132},{8,136},{12,140},{16,144},{20,148},{24,152},{28,15... | collective-permute-start | bytes 393224 | tf_op jit(solution)/shard_map/ppermute | solution.py:22
  108.8 2.8 %collective-permute-done.5 = bf16[4,128,128]{2,1,0:T(8,128)(2,1)S(1)} collective-permute-done((bf16[4,128,128]{2,1,0:T(8,128)(2,1)S(1)}, bf16[4,128,128]{2,1,0:T(8,128)(2,1)S(1)}, u32[]{:S(2)}, u32[]{:S(2)}) %collective-permute-start.5) | collective-permute-done | bytes 131104 | tf_op jit(solution)/shard_map/ppermute | solution.py:22
  111.7 4.1 %collective-permute-start.6 = (bf16[4,128,128]{2,1,0:T(8,128)(2,1)S(1)}, bf16[4,128,128]{2,1,0:T(8,128)(2,1)S(1)}, u32[]{:S(2)}, u32[]{:S(2)}) collective-permute-start(bf16[4,128,128]{2,1,0:T(8,128)(2,1)S(1)} %fusion.51), channel_id=1, source_target_pairs={{0,256},{4,260},{8,264},{12,268},{16,272},{20,276},{24,280},{28,28... | collective-permute-start | bytes 393224 | tf_op jit(solution)/shard_map/ppermute | solution.py:22
  116.5 3.3 %collective-permute-start.19 = (bf16[128,1024]{1,0:T(8,128)(2,1)}, bf16[128,1024]{1,0:T(8,128)(2,1)}, u32[]{:S(2)}, u32[]{:S(2)}) collective-permute-start(bf16[128,1024]{1,0:T(8,128)(2,1)} %pad_maximum_fusion.1), channel_id=1, source_target_pairs={{8,0},{12,4},{16,8},{20,12},{24,16},{28,20},{32,24},{36,28},{40,32... | collective-permute-start | bytes 786440 | tf_op jit(solution)/shard_map/ppermute | solution.py:31
  120.6 2.1 collective-permute-start.20
  123.8 11.2 %all-reduce = (f32[128]{0:T(128)}, f32[128]{0:T(128)}) all-reduce(f32[128]{0:T(128)} %get-tuple-element.19, f32[128]{0:T(128)} %get-tuple-element.18), channel_id=1, replica_groups=mesh['ctx'=128,'head'=4] {'head'}, use_global_device_ids=true, to_apply=%region_3.4 | all-reduce | flops 256 | bytes 2048 | tf_op jit(solution)/shard_map/psum | solution.py:133
  136.8 5.9 %collective-permute-start.7 = (bf16[4,128,128]{1,2,0:T(8,128)(2,1)S(1)}, bf16[4,128,128]{1,2,0:T(8,128)(2,1)S(1)}, u32[]{:S(2)}, u32[]{:S(2)}) collective-permute-start(bf16[4,128,128]{1,2,0:T(8,128)(2,1)S(1)} %get-tuple-element.49), channel_id=1, source_target_pairs={{4,0},{8,4},{12,8},{16,12},{20,16},{24,20},{28,24},{32,28},{36,32}... | collective-permute-start | bytes 393224 | tf_op jit(solution)/shard_map/ppermute | solution.py:22
  143.4 3.7 %collective-permute-start.21 = (bf16[128,1024]{1,0:T(8,128)(2,1)}, bf16[128,1024]{1,0:T(8,128)(2,1)}, u32[]{:S(2)}, u32[]{:S(2)}) collective-permute-start(bf16[128,1024]{1,0:T(8,128)(2,1)} %pad_maximum_fusion.3), channel_id=1, source_target_pairs={{16,0},{20,4},{24,8},{28,12},{32,16},{36,20},{40,24},{44,28},{48,3... | collective-permute-start | bytes 786440 | tf_op jit(solution)/shard_map/ppermute | solution.py:31
  147.8 1.9 collective-permute-start.18
  150.4 2.6 %collective-permute-start.8 = (bf16[4,128,128]{1,2,0:T(8,128)(2,1)}, bf16[4,128,128]{1,2,0:T(8,128)(2,1)S(1)}, u32[]{:S(2)}, u32[]{:S(2)}) collective-permute-start(bf16[4,128,128]{1,2,0:T(8,128)(2,1)} %fusion.27), channel_id=1, source_target_pairs={{8,0},{12,4},{16,8},{20,12},{24,16},{28,20},{32,24},{36,28},{40,32... | collective-permute-start | bytes 393224 | tf_op jit(solution)/shard_map/ppermute | solution.py:22
  155.1 1.0 convert_element_type.234
  156.1 3.9 %collective-permute-done.21 = bf16[128,1024]{1,0:T(8,128)(2,1)} collective-permute-done((bf16[128,1024]{1,0:T(8,128)(2,1)}, bf16[128,1024]{1,0:T(8,128)(2,1)}, u32[]{:S(2)}, u32[]{:S(2)}) %collective-permute-start.21) | collective-permute-done | bytes 262176 | tf_op jit(solution)/shard_map/ppermute | solution.py:31
  161.0 1.9 collective-permute-done.18
  163.9 1.0 collective-permute-done.8
  165.0 3.8 %collective-permute-start.9 = (bf16[4,128,128]{1,2,0:T(8,128)(2,1)S(1)}, bf16[4,128,128]{1,2,0:T(8,128)(2,1)S(1)}, u32[]{:S(2)}, u32[]{:S(2)}) collective-permute-start(bf16[4,128,128]{1,2,0:T(8,128)(2,1)S(1)} %fusion.79), channel_id=1, source_target_pairs={{16,0},{20,4},{24,8},{28,12},{32,16},{36,20},{40,24},{44,28},{48,3... | collective-permute-start | bytes 393224 | tf_op jit(solution)/shard_map/ppermute | solution.py:22
  169.7 7.2 %collective-permute-done.9 = bf16[4,128,128]{1,2,0:T(8,128)(2,1)S(1)} collective-permute-done((bf16[4,128,128]{1,2,0:T(8,128)(2,1)S(1)}, bf16[4,128,128]{1,2,0:T(8,128)(2,1)S(1)}, u32[]{:S(2)}, u32[]{:S(2)}) %collective-permute-start.9) | collective-permute-done | bytes 131104 | tf_op jit(solution)/shard_map/ppermute | solution.py:22
  177.0 2.1 collective-permute-start.10
  179.3 14.8 %collective-permute-done.10 = bf16[4,128,128]{1,2,0:T(8,128)(2,1)S(1)} collective-permute-done((bf16[4,128,128]{1,2,0:T(8,128)(2,1)S(1)}, bf16[4,128,128]{1,2,0:T(8,128)(2,1)S(1)}, u32[]{:S(2)}, u32[]{:S(2)}) %collective-permute-start.10) | collective-permute-done | bytes 131104 | tf_op jit(solution)/shard_map/ppermute | solution.py:22
  195.2 2.9 %collective-permute-start.11 = (bf16[4,128,128]{1,2,0:T(8,128)(2,1)S(1)}, bf16[4,128,128]{1,2,0:T(8,128)(2,1)S(1)}, u32[]{:S(2)}, u32[]{:S(2)}) collective-permute-start(bf16[4,128,128]{1,2,0:T(8,128)(2,1)S(1)} %get-tuple-element.22), channel_id=1, source_target_pairs={{64,0},{68,4},{72,8},{76,12},{80,16},{84,20},{88,24},{92,28},{96,3... | collective-permute-start | bytes 393224 | tf_op jit(solution)/shard_map/ppermute | solution.py:22
  198.3 15.9 %collective-permute-done.11 = bf16[4,128,128]{1,2,0:T(8,128)(2,1)S(1)} collective-permute-done((bf16[4,128,128]{1,2,0:T(8,128)(2,1)S(1)}, bf16[4,128,128]{1,2,0:T(8,128)(2,1)S(1)}, u32[]{:S(2)}, u32[]{:S(2)}) %collective-permute-start.11) | collective-permute-done | bytes 131104 | tf_op jit(solution)/shard_map/ppermute | solution.py:22
  214.2 1.9 collective-permute-start.12
  217.1 4.0 %collective-permute-done.12 = bf16[4,128,128]{1,2,0:T(8,128)(2,1)S(1)} collective-permute-done((bf16[4,128,128]{1,2,0:T(8,128)(2,1)S(1)}, bf16[4,128,128]{1,2,0:T(8,128)(2,1)S(1)}, u32[]{:S(2)}, u32[]{:S(2)}) %collective-permute-start.12) | collective-permute-done | bytes 131104 | tf_op jit(solution)/shard_map/ppermute | solution.py:22
  221.1 1.3 collective-permute-start.13
  222.6 6.9 %collective-permute-done.13 = bf16[4,128,128]{1,2,0:T(8,128)(2,1)S(1)} collective-permute-done((bf16[4,128,128]{1,2,0:T(8,128)(2,1)S(1)}, bf16[4,128,128]{1,2,0:T(8,128)(2,1)S(1)}, u32[]{:S(2)}, u32[]{:S(2)}) %collective-permute-start.13) | collective-permute-done | bytes 131104 | tf_op jit(solution)/shard_map/ppermute | solution.py:22
  (166 shorter events, 31.0 us)
Async XLA Ops:
  0.6 59.6 %copy-start = (bf16[128,512]{1,0:T(8,128)(2,1)S(1)}, bf16[128,512]{1,0:T(8,128)(2,1)}, u32[]{:S(2)}) copy-start(bf16[128,512]{1,0:T(8,128)(2,1)} %param.15) | copy-start | bytes 393220
  0.6 25.1 %copy-start.24 = (bf16[128,512]{1,0:T(8,128)(2,1)S(1)}, bf16[128,512]{1,0:T(8,128)(2,1)}, u32[]{:S(2)}) copy-start(bf16[128,512]{1,0:T(8,128)(2,1)} %param.11) | copy-start | bytes 393220
  0.7 25.3 %copy-start.18 = (bf16[128,512]{1,0:T(8,128)(2,1)S(1)}, bf16[128,512]{1,0:T(8,128)(2,1)}, u32[]{:S(2)}) copy-start(bf16[128,512]{1,0:T(8,128)(2,1)} %param.12) | copy-start | bytes 393220
  0.7 24.9 %copy-start.39 = (s32[1,3]{1,0:T(1,128)S(1)}, s32[1,3]{1,0:T(1,128)}, u32[]{:S(2)}) copy-start(s32[1,3]{1,0:T(1,128)} %param.19) | copy-start | bytes 40
  0.7 25.1 %copy-start.9 = (bf16[128,512]{1,0:T(8,128)(2,1)S(1)}, bf16[128,512]{1,0:T(8,128)(2,1)}, u32[]{:S(2)}) copy-start(bf16[128,512]{1,0:T(8,128)(2,1)} %param.10) | copy-start | bytes 393220
  3.9 39.2 %copy-start.34 = (bf16[128,512]{1,0:T(8,128)(2,1)S(1)}, bf16[128,512]{1,0:T(8,128)(2,1)}, u32[]{:S(2)}) copy-start(bf16[128,512]{1,0:T(8,128)(2,1)} %param.14) | copy-start | bytes 393220
  3.9 53.2 %collective-permute-start.17 = (bf16[128,1024]{1,0:T(8,128)(2,1)}, bf16[128,1024]{1,0:T(8,128)(2,1)S(1)}, u32[]{:S(2)}, u32[]{:S(2)}) collective-permute-start(bf16[128,1024]{1,0:T(8,128)(2,1)} %constant_dynamic-update-slice_fusion), channel_id=1, source_target_pairs={{0,4},{4,8},{8,12},{12,16},{16,20},{20,24},{24,28},{28,32},{32,36}... | collective-permute-start | bytes 786440 | tf_op jit(solution)/shard_map/ppermute | solution.py:31
  6.0 51.1 %collective-permute-start.16 = (bf16[128,1024]{1,0:T(8,128)(2,1)}, bf16[128,1024]{1,0:T(8,128)(2,1)S(1)}, u32[]{:S(2)}, u32[]{:S(2)}) collective-permute-start(bf16[128,1024]{1,0:T(8,128)(2,1)} %constant_dynamic-update-slice_fusion), channel_id=1, source_target_pairs={{0,8},{4,12},{8,16},{12,20},{16,24},{20,28},{24,32},{28,36},{32,40... | collective-permute-start | bytes 786440 | tf_op jit(solution)/shard_map/ppermute | solution.py:31
  9.8 46.3 %collective-permute-start.15 = (bf16[128,1024]{1,0:T(8,128)(2,1)}, bf16[128,1024]{1,0:T(8,128)(2,1)}, u32[]{:S(2)}, u32[]{:S(2)}) collective-permute-start(bf16[128,1024]{1,0:T(8,128)(2,1)} %constant_dynamic-update-slice_fusion), channel_id=1, source_target_pairs={{0,12},{4,16},{8,20},{12,24},{16,28},{20,32},{24,36},{28,40},{32,4... | collective-permute-start | bytes 786440 | tf_op jit(solution)/shard_map/ppermute | solution.py:31
  16.2 38.9 %collective-permute-start.14 = (bf16[128,1024]{1,0:T(8,128)(2,1)}, bf16[128,1024]{1,0:T(8,128)(2,1)}, u32[]{:S(2)}, u32[]{:S(2)}) collective-permute-start(bf16[128,1024]{1,0:T(8,128)(2,1)} %constant_dynamic-update-slice_fusion), channel_id=1, source_target_pairs={{0,16},{4,20},{8,24},{12,28},{16,32},{20,36},{24,40},{28,44},{32,4... | collective-permute-start | bytes 786440 | tf_op jit(solution)/shard_map/ppermute | solution.py:31
  22.4 20.1 %copy-start.16 = (bf16[128,512]{0,1:T(8,128)(2,1)}, bf16[128,512]{0,1:T(8,128)(2,1)S(1)}, u32[]{:S(2)}) copy-start(bf16[128,512]{0,1:T(8,128)(2,1)S(1)} %copy.161) | copy-start | bytes 393220
  22.4 20.8 %copy-start.35 = (bf16[128,512]{1,0:T(8,128)(2,1)S(1)}, bf16[128,512]{1,0:T(8,128)(2,1)}, u32[]{:S(2)}) copy-start(bf16[128,512]{1,0:T(8,128)(2,1)} %param.18) | copy-start | bytes 393220
  23.6 15.1 %collective-permute-start = (bf16[4,128,128]{2,1,0:T(8,128)(2,1)S(1)}, bf16[4,128,128]{2,1,0:T(8,128)(2,1)S(1)}, u32[]{:S(2)}, u32[]{:S(2)}) collective-permute-start(bf16[4,128,128]{2,1,0:T(8,128)(2,1)S(1)} %get-tuple-element.46), channel_id=1, source_target_pairs={{0,4},{4,8},{8,12},{12,16},{16,20},{20,24},{24,28},{28,32},{32,36}... | collective-permute-start | bytes 393224 | tf_op jit(solution)/shard_map/ppermute | solution.py:22
  26.0 16.5 %copy-start.28 = (bf16[4,128,128]{2,1,0:T(8,128)(2,1)}, bf16[4,128,128]{2,1,0:T(8,128)(2,1)S(1)}, u32[]{:S(2)}) copy-start(bf16[4,128,128]{2,1,0:T(8,128)(2,1)S(1)} %fusion.15) | copy-start | bytes 393220
  38.7 18.4 %copy-start.6 = (bf16[4,128,128]{2,1,0:T(8,128)(2,1)}, bf16[4,128,128]{2,1,0:T(8,128)(2,1)S(1)}, u32[]{:S(2)}) copy-start(bf16[4,128,128]{2,1,0:T(8,128)(2,1)S(1)} %collective-permute-done) | copy-start | bytes 393220
  38.7 7.5 %collective-permute-start.1 = (bf16[4,128,128]{2,1,0:T(8,128)(2,1)S(1)}, bf16[4,128,128]{2,1,0:T(8,128)(2,1)S(1)}, u32[]{:S(2)}, u32[]{:S(2)}) collective-permute-start(bf16[4,128,128]{2,1,0:T(8,128)(2,1)S(1)} %fusion.24), channel_id=1, source_target_pairs={{0,8},{4,12},{8,16},{12,20},{16,24},{20,28},{24,32},{28,36},{32,40... | collective-permute-start | bytes 393224 | tf_op jit(solution)/shard_map/ppermute | solution.py:22
  43.4 13.9 %copy-start.26 = (bf16[128,512]{1,0:T(8,128)(2,1)S(1)}, bf16[128,512]{1,0:T(8,128)(2,1)}, u32[]{:S(2)}) copy-start(bf16[128,512]{1,0:T(8,128)(2,1)} %param.16) | copy-start | bytes 393220
  43.4 13.8 %copy-start.27 = (bf16[128,512]{1,0:T(8,128)(2,1)S(1)}, bf16[128,512]{1,0:T(8,128)(2,1)}, u32[]{:S(2)}) copy-start(bf16[128,512]{1,0:T(8,128)(2,1)} %param.17) | copy-start | bytes 393220
  46.9 18.2 %collective-permute-start.2 = (bf16[4,128,128]{2,1,0:T(8,128)(2,1)}, bf16[4,128,128]{2,1,0:T(8,128)(2,1)}, u32[]{:S(2)}, u32[]{:S(2)}) collective-permute-start(bf16[4,128,128]{2,1,0:T(8,128)(2,1)} %fusion.78), channel_id=1, source_target_pairs={{0,16},{4,20},{8,24},{12,28},{16,32},{20,36},{24,40},{28,44},{32,4... | collective-permute-start | bytes 393224 | tf_op jit(solution)/shard_map/ppermute | solution.py:22
  62.2 14.1 %copy-start.4 = (bf16[4,128,512]{1,2,0:T(8,128)(2,1)}, bf16[4,128,512]{1,2,0:T(8,128)(2,1)S(1)}, u32[]{:S(2)}) copy-start(bf16[4,128,512]{1,2,0:T(8,128)(2,1)S(1)} %fusion.8) | copy-start | bytes 1572868
  67.2 16.4 %collective-permute-start.3 = (bf16[4,128,128]{2,1,0:T(8,128)(2,1)}, bf16[4,128,128]{2,1,0:T(8,128)(2,1)}, u32[]{:S(2)}, u32[]{:S(2)}) collective-permute-start(bf16[4,128,128]{2,1,0:T(8,128)(2,1)} %fusion.25), channel_id=1, source_target_pairs={{0,32},{4,36},{8,40},{12,44},{16,48},{20,52},{24,56},{28,60},{32,6... | collective-permute-start | bytes 393224 | tf_op jit(solution)/shard_map/ppermute | solution.py:22
  85.5 19.2 %collective-permute-start.4 = (bf16[4,128,128]{2,1,0:T(8,128)(2,1)S(1)}, bf16[4,128,128]{2,1,0:T(8,128)(2,1)S(1)}, u32[]{:S(2)}, u32[]{:S(2)}) collective-permute-start(bf16[4,128,128]{2,1,0:T(8,128)(2,1)S(1)} %get-tuple-element.24), channel_id=1, source_target_pairs={{0,64},{4,68},{8,72},{12,76},{16,80},{20,84},{24,88},{28,92},{32,9... | collective-permute-start | bytes 393224 | tf_op jit(solution)/shard_map/ppermute | solution.py:22
  104.7 6.9 %collective-permute-start.5 = (bf16[4,128,128]{2,1,0:T(8,128)(2,1)S(1)}, bf16[4,128,128]{2,1,0:T(8,128)(2,1)S(1)}, u32[]{:S(2)}, u32[]{:S(2)}) collective-permute-start(bf16[4,128,128]{2,1,0:T(8,128)(2,1)S(1)} %fusion.26), channel_id=1, source_target_pairs={{0,128},{4,132},{8,136},{12,140},{16,144},{20,148},{24,152},{28,15... | collective-permute-start | bytes 393224 | tf_op jit(solution)/shard_map/ppermute | solution.py:22
  108.8 14.0 %copy-start.10 = (bf16[128,512]{1,0:T(8,128)(2,1)S(1)}, bf16[128,512]{1,0:T(8,128)(2,1)}, u32[]{:S(2)}) copy-start(bf16[128,512]{1,0:T(8,128)(2,1)} %param.10) | copy-start | bytes 393220
  108.8 14.0 %copy-start.23 = (f32[128,4,128]{0,2,1:T(8,128)S(1)}, f32[128,4,128]{0,2,1:T(8,128)}, u32[]{:S(2)}) copy-start(f32[128,4,128]{0,2,1:T(8,128)} %convolution_bitcast_fusion.9) | copy-start | bytes 786436
  108.8 14.1 %copy-start.37 = (f32[512]{0:T(512)S(1)}, f32[512]{0:T(512)}, u32[]{:S(2)}) copy-start(f32[512]{0:T(512)} %param.13) | copy-start | bytes 6148
  111.7 11.1 %collective-permute-start.6 = (bf16[4,128,128]{2,1,0:T(8,128)(2,1)S(1)}, bf16[4,128,128]{2,1,0:T(8,128)(2,1)S(1)}, u32[]{:S(2)}, u32[]{:S(2)}) collective-permute-start(bf16[4,128,128]{2,1,0:T(8,128)(2,1)S(1)} %fusion.51), channel_id=1, source_target_pairs={{0,256},{4,260},{8,264},{12,268},{16,272},{20,276},{24,280},{28,28... | collective-permute-start | bytes 393224 | tf_op jit(solution)/shard_map/ppermute | solution.py:22
  116.5 37.6 %collective-permute-start.19 = (bf16[128,1024]{1,0:T(8,128)(2,1)}, bf16[128,1024]{1,0:T(8,128)(2,1)}, u32[]{:S(2)}, u32[]{:S(2)}) collective-permute-start(bf16[128,1024]{1,0:T(8,128)(2,1)} %pad_maximum_fusion.1), channel_id=1, source_target_pairs={{8,0},{12,4},{16,8},{20,12},{24,16},{28,20},{32,24},{36,28},{40,32... | collective-permute-start | bytes 786440 | tf_op jit(solution)/shard_map/ppermute | solution.py:31
  120.6 34.5 %collective-permute-start.20 = (bf16[128,1024]{1,0:T(8,128)(2,1)}, bf16[128,1024]{1,0:T(8,128)(2,1)}, u32[]{:S(2)}, u32[]{:S(2)}) collective-permute-start(bf16[128,1024]{1,0:T(8,128)(2,1)} %pad_maximum_fusion.2), channel_id=1, source_target_pairs={{12,0},{16,4},{20,8},{24,12},{28,16},{32,20},{36,24},{40,28},{44,3... | collective-permute-start | bytes 786440 | tf_op jit(solution)/shard_map/ppermute | solution.py:31
  122.8 12.8 %copy-start.21 = (bf16[4,128,128]{2,1,0:T(8,128)(2,1)}, bf16[4,128,128]{2,1,0:T(8,128)(2,1)S(1)}, u32[]{:S(2)}) copy-start(bf16[4,128,128]{2,1,0:T(8,128)(2,1)S(1)} %subtract_convert_fusion.2) | copy-start | bytes 393220
  135.7 17.3 %copy-start.3 = (bf16[512,4,128]{0,2,1:T(8,128)(2,1)S(1)}, bf16[512,4,128]{0,2,1:T(8,128)(2,1)}, u32[]{:S(2)}) copy-start(bf16[512,4,128]{0,2,1:T(8,128)(2,1)} %copy-done.2) | copy-start | bytes 1572868
  135.7 17.3 %copy-start.5 = (bf16[4,128,512]{1,2,0:T(8,128)(2,1)S(1)}, bf16[4,128,512]{1,2,0:T(8,128)(2,1)}, u32[]{:S(2)}) copy-start(bf16[4,128,512]{1,2,0:T(8,128)(2,1)} %copy-done.4) | copy-start | bytes 1572868
  136.8 13.0 %collective-permute-start.7 = (bf16[4,128,128]{1,2,0:T(8,128)(2,1)S(1)}, bf16[4,128,128]{1,2,0:T(8,128)(2,1)S(1)}, u32[]{:S(2)}, u32[]{:S(2)}) collective-permute-start(bf16[4,128,128]{1,2,0:T(8,128)(2,1)S(1)} %get-tuple-element.49), channel_id=1, source_target_pairs={{4,0},{8,4},{12,8},{16,12},{20,16},{24,20},{28,24},{32,28},{36,32}... | collective-permute-start | bytes 393224 | tf_op jit(solution)/shard_map/ppermute | solution.py:22
  143.4 16.6 %collective-permute-start.21 = (bf16[128,1024]{1,0:T(8,128)(2,1)}, bf16[128,1024]{1,0:T(8,128)(2,1)}, u32[]{:S(2)}, u32[]{:S(2)}) collective-permute-start(bf16[128,1024]{1,0:T(8,128)(2,1)} %pad_maximum_fusion.3), channel_id=1, source_target_pairs={{16,0},{20,4},{24,8},{28,12},{32,16},{36,20},{40,24},{44,28},{48,3... | collective-permute-start | bytes 786440 | tf_op jit(solution)/shard_map/ppermute | solution.py:31
  147.8 15.1 %collective-permute-start.18 = (bf16[128,1024]{1,0:T(8,128)(2,1)}, bf16[128,1024]{1,0:T(8,128)(2,1)}, u32[]{:S(2)}, u32[]{:S(2)}) collective-permute-start(bf16[128,1024]{1,0:T(8,128)(2,1)} %pad_maximum_fusion), channel_id=1, source_target_pairs={{4,0},{8,4},{12,8},{16,12},{20,16},{24,20},{28,24},{32,28},{36,32}... | collective-permute-start | bytes 786440 | tf_op jit(solution)/shard_map/ppermute | solution.py:31
  150.4 14.5 %collective-permute-start.8 = (bf16[4,128,128]{1,2,0:T(8,128)(2,1)}, bf16[4,128,128]{1,2,0:T(8,128)(2,1)S(1)}, u32[]{:S(2)}, u32[]{:S(2)}) collective-permute-start(bf16[4,128,128]{1,2,0:T(8,128)(2,1)} %fusion.27), channel_id=1, source_target_pairs={{8,0},{12,4},{16,8},{20,12},{24,16},{28,20},{32,24},{36,28},{40,32... | collective-permute-start | bytes 393224 | tf_op jit(solution)/shard_map/ppermute | solution.py:22
  164.9 14.4 %copy-start.15 = (bf16[4,128,128]{1,2,0:T(8,128)(2,1)}, bf16[4,128,128]{1,2,0:T(8,128)(2,1)S(1)}, u32[]{:S(2)}) copy-start(bf16[4,128,128]{1,2,0:T(8,128)(2,1)S(1)} %collective-permute-done.8) | copy-start | bytes 393220
  165.0 14.0 %copy-start.19 = (bf16[128,512]{1,0:T(8,128)(2,1)S(1)}, bf16[128,512]{1,0:T(8,128)(2,1)}, u32[]{:S(2)}) copy-start(bf16[128,512]{1,0:T(8,128)(2,1)} %param.12) | copy-start | bytes 393220
  165.0 11.9 %collective-permute-start.9 = (bf16[4,128,128]{1,2,0:T(8,128)(2,1)S(1)}, bf16[4,128,128]{1,2,0:T(8,128)(2,1)S(1)}, u32[]{:S(2)}, u32[]{:S(2)}) collective-permute-start(bf16[4,128,128]{1,2,0:T(8,128)(2,1)S(1)} %fusion.79), channel_id=1, source_target_pairs={{16,0},{20,4},{24,8},{28,12},{32,16},{36,20},{40,24},{44,28},{48,3... | collective-permute-start | bytes 393224 | tf_op jit(solution)/shard_map/ppermute | solution.py:22
  169.7 28.3 %copy-start.17 = (bf16[128,512]{0,1:T(8,128)(2,1)S(1)}, bf16[128,512]{0,1:T(8,128)(2,1)}, u32[]{:S(2)}) copy-start(bf16[128,512]{0,1:T(8,128)(2,1)} %copy-done.16) | copy-start | bytes 393220
  177.0 39.2 %copy-start.22 = (bf16[4,128,128]{2,1,0:T(8,128)(2,1)S(1)}, bf16[4,128,128]{2,1,0:T(8,128)(2,1)}, u32[]{:S(2)}) copy-start(bf16[4,128,128]{2,1,0:T(8,128)(2,1)} %copy-done.21) | copy-start | bytes 393220
  177.0 17.2 %collective-permute-start.10 = (bf16[4,128,128]{1,2,0:T(8,128)(2,1)S(1)}, bf16[4,128,128]{1,2,0:T(8,128)(2,1)S(1)}, u32[]{:S(2)}, u32[]{:S(2)}) collective-permute-start(bf16[4,128,128]{1,2,0:T(8,128)(2,1)S(1)} %fusion.28), channel_id=1, source_target_pairs={{32,0},{36,4},{40,8},{44,12},{48,16},{52,20},{56,24},{60,28},{64,3... | collective-permute-start | bytes 393224 | tf_op jit(solution)/shard_map/ppermute | solution.py:22
  195.1 27.3 %copy-start.29 = (bf16[4,128,128]{2,1,0:T(8,128)(2,1)S(1)}, bf16[4,128,128]{2,1,0:T(8,128)(2,1)}, u32[]{:S(2)}) copy-start(bf16[4,128,128]{2,1,0:T(8,128)(2,1)} %copy-done.28) | copy-start | bytes 393220
  195.2 19.0 %collective-permute-start.11 = (bf16[4,128,128]{1,2,0:T(8,128)(2,1)S(1)}, bf16[4,128,128]{1,2,0:T(8,128)(2,1)S(1)}, u32[]{:S(2)}, u32[]{:S(2)}) collective-permute-start(bf16[4,128,128]{1,2,0:T(8,128)(2,1)S(1)} %get-tuple-element.22), channel_id=1, source_target_pairs={{64,0},{68,4},{72,8},{76,12},{80,16},{84,20},{88,24},{92,28},{96,3... | collective-permute-start | bytes 393224 | tf_op jit(solution)/shard_map/ppermute | solution.py:22
  214.2 6.9 %collective-permute-start.12 = (bf16[4,128,128]{1,2,0:T(8,128)(2,1)S(1)}, bf16[4,128,128]{1,2,0:T(8,128)(2,1)S(1)}, u32[]{:S(2)}, u32[]{:S(2)}) collective-permute-start(bf16[4,128,128]{1,2,0:T(8,128)(2,1)S(1)} %fusion.29), channel_id=1, source_target_pairs={{128,0},{132,4},{136,8},{140,12},{144,16},{148,20},{152,24},{156,2... | collective-permute-start | bytes 393224 | tf_op jit(solution)/shard_map/ppermute | solution.py:22
  216.3 13.2 %copy-start.20 = (bf16[128,512]{1,0:T(8,128)(2,1)S(1)}, bf16[128,512]{1,0:T(8,128)(2,1)}, u32[]{:S(2)}) copy-start(bf16[128,512]{1,0:T(8,128)(2,1)} %param.12) | copy-start | bytes 393220
  217.1 12.7 %copy-start.25 = (bf16[128,512]{1,0:T(8,128)(2,1)S(1)}, bf16[128,512]{1,0:T(8,128)(2,1)}, u32[]{:S(2)}) copy-start(bf16[128,512]{1,0:T(8,128)(2,1)} %param.11) | copy-start | bytes 393220
  221.1 8.4 %collective-permute-start.13 = (bf16[4,128,128]{1,2,0:T(8,128)(2,1)S(1)}, bf16[4,128,128]{1,2,0:T(8,128)(2,1)S(1)}, u32[]{:S(2)}, u32[]{:S(2)}) collective-permute-start(bf16[4,128,128]{1,2,0:T(8,128)(2,1)S(1)} %fusion.52), channel_id=1, source_target_pairs={{256,0},{260,4},{264,8},{268,12},{272,16},{276,20},{280,24},{284,2... | collective-permute-start | bytes 393224 | tf_op jit(solution)/shard_map/ppermute | solution.py:22
  (15 other events, 76.9 us)

commit v5 on v4

--- a/solution.py
+++ b/solution.py
@@ -160,7 +160,11 @@
     lin_dv = lin_dv.reshape(token_count, lin_width).astype(jnp.bfloat16)
     width = sm_key.shape[1]
     pair = jnp.concatenate([sm_key, sm_value], axis=1)
-    arrived = [from_behind(pair, "ctx", distance) for distance in range(1, SPAN + 1)]
+    arrived = []
+    moving = pair
+    for distance in range(1, SPAN + 1):
+        moving = from_behind(moving, "ctx", 1)
+        arrived.append(moving)
     key_window = jnp.concatenate(
         [arrived[SPAN - 1 - place][:, :width] for place in range(SPAN)] + [sm_key], axis=0
     )
@@ -173,16 +177,15 @@
     )
     key_total = key_acc[SPAN]
     value_total = value_acc[SPAN]
-    for distance in range(1, SPAN + 1):
-        back = from_behind(
-            jnp.concatenate(
-                [key_acc[SPAN - distance], value_acc[SPAN - distance]], axis=1
-            ).astype(jnp.bfloat16),
-            "ctx",
-            -distance,
-        ).astype(jnp.float32)
-        key_total = key_total + back[:, :width]
-        value_total = value_total + back[:, width:]
+    owed = None
+    for distance in range(SPAN, 0, -1):
+        term = jnp.concatenate(
+            [key_acc[SPAN - distance], value_acc[SPAN - distance]], axis=1
+        ).astype(jnp.bfloat16).astype(jnp.float32)
+        owed = term if owed is None else owed + term
+        owed = from_behind(owed.astype(jnp.bfloat16), "ctx", -1).astype(jnp.float32)
+    key_total = key_total + owed[:, :width]
+    value_total = value_total + owed[:, width:]
     return (
         lin_dq,
         lin_dk,

time: 233 us -> 215 us (0.923)
  the two profiles are of different devices: /device:TPU:72 before, /device:TPU:24 now
where the time goes in v5:
time: 215 us; the launch traced here: 214 us
  starting transfers between devices  81.1 us (38%)
  waiting for transfers between devices  76.7 us (36%)
  other arithmetic  20.4 us (9%)
  local copies, waits for them, and re-layouts  14.8 us (7%)
  blocking collectives  10.5 us (5%)
  matrix products  9.15 us (4%)
    ppermute x14, waiting for transfers between devices, carried_in(): sent = lax.ppermute(total.astype(jnp.bfloat16), axis, pairs)  61.4 us
    ppermute x14, starting transfers between devices, carried_in(): sent = lax.ppermute(total.astype(jnp.bfloat16), axis, pairs)  55.5 us
    ppermute x8, starting transfers between devices, from_behind(): return lax.ppermute(shard, axis, pairs)  25.6 us
    ppermute x8, waiting for transfers between devices, from_behind(): return lax.ppermute(shard, axis, pairs)  15.4 us
    psum x1, blocking collectives, per_device(): square_sum, cross_sum = lax.psum((square_sum, cross_sum), 'head')  10.5 us
    convert_element_type x12, other arithmetic, carried_in(): sent = lax.ppermute(total.astype(jnp.bfloat16), axis, pairs)  6.25 us
    unnamed x82, local copies, waits for them, and re-layouts  5.53 us
    convert_element_type x4, other arithmetic, per_device(): owed = from_behind(owed.astype(jnp.bfloat16), 'ctx', -1).astype(jnp.float32)  4.69 us
  transfers between devices with their start and end apart: 22, of which 15 were waited for; matrix products, arithmetic and copies ran while one was open for 18% of the time, Pallas kernels for 0%

profile of v5, /device:TPU:24, one launch (start us, length us, event | category | flops | bytes accessed | tf_op | source)
XLA Modules:
  0.0 214.2 jit_solution(5472877520338197775)
XLA Ops:
  0.7 1.1 pad_maximum_fusion
  1.8 1.9 collective-permute-start.14
  3.7 1.0 copy.161
  4.7 1.1 fusion.84
  5.8 3.9 %collective-permute-start = (bf16[4,128,128]{2,1,0:T(8,128)(2,1)S(1)}, bf16[4,128,128]{2,1,0:T(8,128)(2,1)S(1)}, u32[]{:S(2)}, u32[]{:S(2)}) collective-permute-start(bf16[4,128,128]{2,1,0:T(8,128)(2,1)S(1)} %get-tuple-element.46), channel_id=1, source_target_pairs={{0,4},{4,8},{8,12},{12,16},{16,20},{20,24},{24,28},{28,32},{32,36}... | collective-permute-start | bytes 393224 | tf_op jit(solution)/shard_map/ppermute | solution.py:22
  10.4 9.1 %collective-permute-done = bf16[4,128,128]{2,1,0:T(8,128)(2,1)S(1)} collective-permute-done((bf16[4,128,128]{2,1,0:T(8,128)(2,1)S(1)}, bf16[4,128,128]{2,1,0:T(8,128)(2,1)S(1)}, u32[]{:S(2)}, u32[]{:S(2)}) %collective-permute-start) | collective-permute-done | bytes 131104 | tf_op jit(solution)/shard_map/ppermute | solution.py:22
  19.5 1.9 collective-permute-start.1
  21.5 7.1 %collective-permute-done.1 = bf16[4,128,128]{2,1,0:T(8,128)(2,1)S(1)} collective-permute-done((bf16[4,128,128]{2,1,0:T(8,128)(2,1)S(1)}, bf16[4,128,128]{2,1,0:T(8,128)(2,1)S(1)}, u32[]{:S(2)}, u32[]{:S(2)}) %collective-permute-start.1) | collective-permute-done | bytes 131104 | tf_op jit(solution)/shard_map/ppermute | solution.py:22
  28.7 1.9 collective-permute-start.2
  30.7 7.9 %collective-permute-done.2 = bf16[4,128,128]{2,1,0:T(8,128)(2,1)S(1)} collective-permute-done((bf16[4,128,128]{2,1,0:T(8,128)(2,1)S(1)}, bf16[4,128,128]{2,1,0:T(8,128)(2,1)S(1)}, u32[]{:S(2)}, u32[]{:S(2)}) %collective-permute-start.2) | collective-permute-done | bytes 131104 | tf_op jit(solution)/shard_map/ppermute | solution.py:22
  38.7 2.1 collective-permute-start.3
  41.6 9.1 %collective-permute-done.3 = bf16[4,128,128]{2,1,0:T(8,128)(2,1)S(1)} collective-permute-done((bf16[4,128,128]{2,1,0:T(8,128)(2,1)S(1)}, bf16[4,128,128]{2,1,0:T(8,128)(2,1)S(1)}, u32[]{:S(2)}, u32[]{:S(2)}) %collective-permute-start.3) | collective-permute-done | bytes 131104 | tf_op jit(solution)/shard_map/ppermute | solution.py:22
  50.8 12.0 %collective-permute-start.4 = (bf16[4,128,128]{2,1,0:T(8,128)(2,1)S(1)}, bf16[4,128,128]{2,1,0:T(8,128)(2,1)S(1)}, u32[]{:S(2)}, u32[]{:S(2)}) collective-permute-start(bf16[4,128,128]{2,1,0:T(8,128)(2,1)S(1)} %get-tuple-element.24), channel_id=1, source_target_pairs={{0,64},{4,68},{8,72},{12,76},{16,80},{20,84},{24,88},{28,92},{32,9... | collective-permute-start | bytes 393224 | tf_op jit(solution)/shard_map/ppermute | solution.py:22
  62.9 1.9 collective-permute-start.15
  64.8 2.8 %collective-permute-done.4 = bf16[4,128,128]{2,1,0:T(8,128)(2,1)S(1)} collective-permute-done((bf16[4,128,128]{2,1,0:T(8,128)(2,1)S(1)}, bf16[4,128,128]{2,1,0:T(8,128)(2,1)S(1)}, u32[]{:S(2)}, u32[]{:S(2)}) %collective-permute-start.4) | collective-permute-done | bytes 131104 | tf_op jit(solution)/shard_map/ppermute | solution.py:22
  67.6 1.3 collective-permute-start.5
  69.0 4.6 %collective-permute-done.15 = bf16[128,1024]{1,0:T(8,128)(2,1)S(1)} collective-permute-done((bf16[128,1024]{1,0:T(8,128)(2,1)S(1)}, bf16[128,1024]{1,0:T(8,128)(2,1)S(1)}, u32[]{:S(2)}, u32[]{:S(2)}) %collective-permute-start.15) | collective-permute-done | bytes 262176 | tf_op jit(solution)/shard_map/ppermute | solution.py:31
  73.6 1.9 collective-permute-start.16
  75.8 1.3 collective-permute-start.6
  77.5 6.0 %collective-permute-done.16 = bf16[128,1024]{1,0:T(8,128)(2,1)S(1)} collective-permute-done((bf16[128,1024]{1,0:T(8,128)(2,1)S(1)}, bf16[128,1024]{1,0:T(8,128)(2,1)S(1)}, u32[]{:S(2)}, u32[]{:S(2)}) %collective-permute-start.16) | collective-permute-done | bytes 262176 | tf_op jit(solution)/shard_map/ppermute | solution.py:31
  83.4 1.9 collective-permute-start.17
  85.7 10.5 %all-reduce = (f32[128]{0:T(128)S(1)}, f32[128]{0:T(128)S(1)}) all-reduce(f32[128]{0:T(128)S(1)} %get-tuple-element.19, f32[128]{0:T(128)S(1)} %get-tuple-element.18), channel_id=1, replica_groups=mesh['ctx'=128,'head'=4] {'head'}, use_global_device_ids=true, to_apply=%region_3.4 | all-reduce | flops 256 | bytes 2048 | tf_op jit(solution)/shard_map/psum | solution.py:133
  97.3 3.7 %collective-permute-start.7 = (bf16[4,128,128]{1,2,0:T(8,128)(2,1)S(1)}, bf16[4,128,128]{1,2,0:T(8,128)(2,1)S(1)}, u32[]{:S(2)}, u32[]{:S(2)}) collective-permute-start(bf16[4,128,128]{1,2,0:T(8,128)(2,1)S(1)} %get-tuple-element.49), channel_id=1, source_target_pairs={{4,0},{8,4},{12,8},{16,12},{20,16},{24,20},{28,24},{32,28},{36,32}... | collective-permute-start | bytes 393224 | tf_op jit(solution)/shard_map/ppermute | solution.py:22
  101.9 1.7 collective-permute-done.7
  104.2 1.9 collective-permute-start.8
  110.3 1.5 fusion.86
  111.9 1.6 convolution_bitcast_fusion
  116.2 1.4 reshape.425
  117.8 1.2 scatter_fusion.1
  120.1 2.3 %scatter_fusion = f32[5,128,512]{2,1,0:T(8,128)S(1)} fusion(f32[5,128,512]{2,1,0:T(8,128)S(1)} %broadcast.196.clone.1, s32[4]{0:T(128)S(1)} %fusion.72, f32[4,128,512]{2,1,0:T(8,128)} %reshape.425), kind=kCustom, calls=%fused_computation.2 | custom fusion | flops 262144 | bytes 3145744 | tf_op jit(solution)/shard_map/scatter-add | solution.py:93
  125.2 7.8 %collective-permute-start.9 = (bf16[4,128,128]{1,2,0:T(8,128)(2,1)S(1)}, bf16[4,128,128]{1,2,0:T(8,128)(2,1)S(1)}, u32[]{:S(2)}, u32[]{:S(2)}) collective-permute-start(bf16[4,128,128]{1,2,0:T(8,128)(2,1)S(1)} %fusion.79), channel_id=1, source_target_pairs={{16,0},{20,4},{24,8},{28,12},{32,16},{36,20},{40,24},{44,28},{48,3... | collective-permute-start | bytes 393224 | tf_op jit(solution)/shard_map/ppermute | solution.py:22
  134.6 3.5 %collective-permute-start.18 = (bf16[128,1024]{1,0:T(8,128)(2,1)}, bf16[128,1024]{1,0:T(8,128)(2,1)}, u32[]{:S(2)}, u32[]{:S(2)}) collective-permute-start(bf16[128,1024]{1,0:T(8,128)(2,1)} %pad_maximum_fusion.1), channel_id=1, source_target_pairs={{4,0},{8,4},{12,8},{16,12},{20,16},{24,20},{28,24},{32,28},{36,32}... | collective-permute-start | bytes 786440 | tf_op jit(solution)/shard_map/ppermute | solution.py:31
  138.7 1.6 fusion.28
  140.3 3.8 %collective-permute-start.10 = (bf16[4,128,128]{1,2,0:T(8,128)(2,1)}, bf16[4,128,128]{1,2,0:T(8,128)(2,1)}, u32[]{:S(2)}, u32[]{:S(2)}) collective-permute-start(bf16[4,128,128]{1,2,0:T(8,128)(2,1)} %fusion.28), channel_id=1, source_target_pairs={{32,0},{36,4},{40,8},{44,12},{48,16},{52,20},{56,24},{60,28},{64,3... | collective-permute-start | bytes 393224 | tf_op jit(solution)/shard_map/ppermute | solution.py:22
  145.8 12.2 %collective-permute-done.10 = bf16[4,128,128]{1,2,0:T(8,128)(2,1)} collective-permute-done((bf16[4,128,128]{1,2,0:T(8,128)(2,1)}, bf16[4,128,128]{1,2,0:T(8,128)(2,1)}, u32[]{:S(2)}, u32[]{:S(2)}) %collective-permute-start.10) | collective-permute-done | bytes 131104 | tf_op jit(solution)/shard_map/ppermute | solution.py:22
  157.9 1.1 fusion.82
  159.0 10.4 %collective-permute-start.11 = (bf16[4,128,128]{1,2,0:T(8,128)(2,1)S(1)}, bf16[4,128,128]{1,2,0:T(8,128)(2,1)S(1)}, u32[]{:S(2)}, u32[]{:S(2)}) collective-permute-start(bf16[4,128,128]{1,2,0:T(8,128)(2,1)S(1)} %get-tuple-element.22), channel_id=1, source_target_pairs={{64,0},{68,4},{72,8},{76,12},{80,16},{84,20},{88,24},{92,28},{96,3... | collective-permute-start | bytes 393224 | tf_op jit(solution)/shard_map/ppermute | solution.py:22
  169.4 1.8 add_convert_fusion.2
  171.3 1.9 collective-permute-start.19
  173.2 9.5 %collective-permute-done.11 = bf16[4,128,128]{1,2,0:T(8,128)(2,1)S(1)} collective-permute-done((bf16[4,128,128]{1,2,0:T(8,128)(2,1)S(1)}, bf16[4,128,128]{1,2,0:T(8,128)(2,1)S(1)}, u32[]{:S(2)}, u32[]{:S(2)}) %collective-permute-start.11) | collective-permute-done | bytes 131104 | tf_op jit(solution)/shard_map/ppermute | solution.py:22
  183.4 1.9 collective-permute-start.12
  186.4 1.1 collective-permute-done.12
  188.5 1.4 collective-permute-start.13
  189.9 1.1 add_convert_fusion.1
  191.1 6.6 %collective-permute-start.20 = (bf16[128,1024]{1,0:T(8,128)(2,1)S(1)}, bf16[128,1024]{1,0:T(8,128)(2,1)S(1)}, u32[]{:S(2)}, u32[]{:S(2)}) collective-permute-start(bf16[128,1024]{1,0:T(8,128)(2,1)S(1)} %add_convert_fusion.1), channel_id=1, source_target_pairs={{4,0},{8,4},{12,8},{16,12},{20,16},{24,20},{28,24},{32,28},{36,32}... | collective-permute-start | bytes 786440 | tf_op jit(solution)/shard_map/ppermute | solution.py:31
  199.0 2.6 %collective-permute-done.20 = bf16[128,1024]{1,0:T(8,128)(2,1)S(1)} collective-permute-done((bf16[128,1024]{1,0:T(8,128)(2,1)S(1)}, bf16[128,1024]{1,0:T(8,128)(2,1)S(1)}, u32[]{:S(2)}, u32[]{:S(2)}) %collective-permute-start.20) | collective-permute-done | bytes 262176 | tf_op jit(solution)/shard_map/ppermute | solution.py:31
  202.3 5.9 %collective-permute-start.21 = (bf16[128,1024]{1,0:T(8,128)(2,1)}, bf16[128,1024]{1,0:T(8,128)(2,1)}, u32[]{:S(2)}, u32[]{:S(2)}) collective-permute-start(bf16[128,1024]{1,0:T(8,128)(2,1)} %add_convert_fusion), channel_id=1, source_target_pairs={{4,0},{8,4},{12,8},{16,12},{20,16},{24,20},{28,24},{32,28},{36,32}... | collective-permute-start | bytes 786440 | tf_op jit(solution)/shard_map/ppermute | solution.py:31
  210.3 2.1 collective-permute-done.21
  (154 shorter events, 28.5 us)
Async XLA Ops:
  0.6 109.7 %copy-start = (bf16[128,512]{1,0:T(8,128)(2,1)S(1)}, bf16[128,512]{1,0:T(8,128)(2,1)}, u32[]{:S(2)}) copy-start(bf16[128,512]{1,0:T(8,128)(2,1)} %param.15) | copy-start | bytes 393220
  0.6 9.1 %copy-start.15 = (bf16[128,512]{1,0:T(8,128)(2,1)S(1)}, bf16[128,512]{1,0:T(8,128)(2,1)}, u32[]{:S(2)}) copy-start(bf16[128,512]{1,0:T(8,128)(2,1)} %param.11) | copy-start | bytes 393220
  0.7 9.4 %copy-start.12 = (bf16[128,512]{1,0:T(8,128)(2,1)S(1)}, bf16[128,512]{1,0:T(8,128)(2,1)}, u32[]{:S(2)}) copy-start(bf16[128,512]{1,0:T(8,128)(2,1)} %param.12) | copy-start | bytes 393220
  0.7 9.1 %copy-start.10 = (bf16[128,512]{1,0:T(8,128)(2,1)S(1)}, bf16[128,512]{1,0:T(8,128)(2,1)}, u32[]{:S(2)}) copy-start(bf16[128,512]{1,0:T(8,128)(2,1)} %param.10) | copy-start | bytes 393220
  0.7 9.6 %copy-start.35 = (s32[1,3]{1,0:T(1,128)S(1)}, s32[1,3]{1,0:T(1,128)}, u32[]{:S(2)}) copy-start(s32[1,3]{1,0:T(1,128)} %param.19) | copy-start | bytes 40
  1.8 61.1 %collective-permute-start.14 = (bf16[128,1024]{1,0:T(8,128)(2,1)S(1)}, bf16[128,1024]{1,0:T(8,128)(2,1)S(1)}, u32[]{:S(2)}, u32[]{:S(2)}) collective-permute-start(bf16[128,1024]{1,0:T(8,128)(2,1)S(1)} %pad_maximum_fusion), channel_id=1, source_target_pairs={{0,4},{4,8},{8,12},{12,16},{16,20},{20,24},{24,28},{28,32},{32,36}... | collective-permute-start | bytes 786440 | tf_op jit(solution)/shard_map/ppermute | solution.py:31
  5.8 13.7 %collective-permute-start = (bf16[4,128,128]{2,1,0:T(8,128)(2,1)S(1)}, bf16[4,128,128]{2,1,0:T(8,128)(2,1)S(1)}, u32[]{:S(2)}, u32[]{:S(2)}) collective-permute-start(bf16[4,128,128]{2,1,0:T(8,128)(2,1)S(1)} %get-tuple-element.46), channel_id=1, source_target_pairs={{0,4},{4,8},{8,12},{12,16},{16,20},{20,24},{24,28},{28,32},{32,36}... | collective-permute-start | bytes 393224 | tf_op jit(solution)/shard_map/ppermute | solution.py:22
  10.0 31.6 %copy-start.22 = (bf16[4,128,128]{2,1,0:T(8,128)(2,1)}, bf16[4,128,128]{2,1,0:T(8,128)(2,1)S(1)}, u32[]{:S(2)}) copy-start(bf16[4,128,128]{2,1,0:T(8,128)(2,1)S(1)} %fusion.15) | copy-start | bytes 393220
  19.5 9.1 %collective-permute-start.1 = (bf16[4,128,128]{2,1,0:T(8,128)(2,1)S(1)}, bf16[4,128,128]{2,1,0:T(8,128)(2,1)S(1)}, u32[]{:S(2)}, u32[]{:S(2)}) collective-permute-start(bf16[4,128,128]{2,1,0:T(8,128)(2,1)S(1)} %fusion.24), channel_id=1, source_target_pairs={{0,8},{4,12},{8,16},{12,20},{16,24},{20,28},{24,32},{28,36},{32,40... | collective-permute-start | bytes 393224 | tf_op jit(solution)/shard_map/ppermute | solution.py:22
  28.7 9.9 %collective-permute-start.2 = (bf16[4,128,128]{2,1,0:T(8,128)(2,1)S(1)}, bf16[4,128,128]{2,1,0:T(8,128)(2,1)S(1)}, u32[]{:S(2)}, u32[]{:S(2)}) collective-permute-start(bf16[4,128,128]{2,1,0:T(8,128)(2,1)S(1)} %fusion.78), channel_id=1, source_target_pairs={{0,16},{4,20},{8,24},{12,28},{16,32},{20,36},{24,40},{28,44},{32,4... | collective-permute-start | bytes 393224 | tf_op jit(solution)/shard_map/ppermute | solution.py:22
  38.6 38.6 %copy-start.30 = (bf16[128,512]{1,0:T(8,128)(2,1)S(1)}, bf16[128,512]{1,0:T(8,128)(2,1)}, u32[]{:S(2)}) copy-start(bf16[128,512]{1,0:T(8,128)(2,1)} %param.14) | copy-start | bytes 393220
  38.7 12.1 %collective-permute-start.3 = (bf16[4,128,128]{2,1,0:T(8,128)(2,1)S(1)}, bf16[4,128,128]{2,1,0:T(8,128)(2,1)S(1)}, u32[]{:S(2)}, u32[]{:S(2)}) collective-permute-start(bf16[4,128,128]{2,1,0:T(8,128)(2,1)S(1)} %fusion.25), channel_id=1, source_target_pairs={{0,32},{4,36},{8,40},{12,44},{16,48},{20,52},{24,56},{28,60},{32,6... | collective-permute-start | bytes 393224 | tf_op jit(solution)/shard_map/ppermute | solution.py:22
  41.6 35.7 %copy-start.31 = (bf16[128,512]{1,0:T(8,128)(2,1)S(1)}, bf16[128,512]{1,0:T(8,128)(2,1)}, u32[]{:S(2)}) copy-start(bf16[128,512]{1,0:T(8,128)(2,1)} %param.18) | copy-start | bytes 393220
  50.8 16.8 %collective-permute-start.4 = (bf16[4,128,128]{2,1,0:T(8,128)(2,1)S(1)}, bf16[4,128,128]{2,1,0:T(8,128)(2,1)S(1)}, u32[]{:S(2)}, u32[]{:S(2)}) collective-permute-start(bf16[4,128,128]{2,1,0:T(8,128)(2,1)S(1)} %get-tuple-element.24), channel_id=1, source_target_pairs={{0,64},{4,68},{8,72},{12,76},{16,80},{20,84},{24,88},{28,92},{32,9... | collective-permute-start | bytes 393224 | tf_op jit(solution)/shard_map/ppermute | solution.py:22
  62.9 10.7 %collective-permute-start.15 = (bf16[128,1024]{1,0:T(8,128)(2,1)S(1)}, bf16[128,1024]{1,0:T(8,128)(2,1)S(1)}, u32[]{:S(2)}, u32[]{:S(2)}) collective-permute-start(bf16[128,1024]{1,0:T(8,128)(2,1)S(1)} %collective-permute-done.14), channel_id=1, source_target_pairs={{0,4},{4,8},{8,12},{12,16},{16,20},{20,24},{24,28},{28,32},{32,36}... | collective-permute-start | bytes 786440 | tf_op jit(solution)/shard_map/ppermute | solution.py:31
  67.6 17.8 %copy-start.34 = (f32[512]{0:T(512)S(1)}, f32[512]{0:T(512)}, u32[]{:S(2)}) copy-start(f32[512]{0:T(512)} %param.13) | copy-start | bytes 6148
  67.6 8.2 %collective-permute-start.5 = (bf16[4,128,128]{2,1,0:T(8,128)(2,1)S(1)}, bf16[4,128,128]{2,1,0:T(8,128)(2,1)S(1)}, u32[]{:S(2)}, u32[]{:S(2)}) collective-permute-start(bf16[4,128,128]{2,1,0:T(8,128)(2,1)S(1)} %fusion.26), channel_id=1, source_target_pairs={{0,128},{4,132},{8,136},{12,140},{16,144},{20,148},{24,152},{28,15... | collective-permute-start | bytes 393224 | tf_op jit(solution)/shard_map/ppermute | solution.py:22
  73.6 12.1 %copy-start.26 = (bf16[128,1024]{1,0:T(8,128)(2,1)}, bf16[128,1024]{1,0:T(8,128)(2,1)S(1)}, u32[]{:S(2)}) copy-start(bf16[128,1024]{1,0:T(8,128)(2,1)S(1)} %collective-permute-done.15) | copy-start | bytes 786436
  73.6 9.8 %collective-permute-start.16 = (bf16[128,1024]{1,0:T(8,128)(2,1)S(1)}, bf16[128,1024]{1,0:T(8,128)(2,1)S(1)}, u32[]{:S(2)}, u32[]{:S(2)}) collective-permute-start(bf16[128,1024]{1,0:T(8,128)(2,1)S(1)} %collective-permute-done.15), channel_id=1, source_target_pairs={{0,4},{4,8},{8,12},{12,16},{16,20},{20,24},{24,28},{28,32},{32,36}... | collective-permute-start | bytes 786440 | tf_op jit(solution)/shard_map/ppermute | solution.py:31
  75.8 9.5 %collective-permute-start.6 = (bf16[4,128,128]{2,1,0:T(8,128)(2,1)S(1)}, bf16[4,128,128]{2,1,0:T(8,128)(2,1)S(1)}, u32[]{:S(2)}, u32[]{:S(2)}) collective-permute-start(bf16[4,128,128]{2,1,0:T(8,128)(2,1)S(1)} %fusion.51), channel_id=1, source_target_pairs={{0,256},{4,260},{8,264},{12,268},{16,272},{20,276},{24,280},{28,28... | collective-permute-start | bytes 393224 | tf_op jit(solution)/shard_map/ppermute | solution.py:22
  83.4 13.0 %copy-start.28 = (bf16[128,1024]{1,0:T(8,128)(2,1)}, bf16[128,1024]{1,0:T(8,128)(2,1)S(1)}, u32[]{:S(2)}) copy-start(bf16[128,1024]{1,0:T(8,128)(2,1)S(1)} %collective-permute-done.16) | copy-start | bytes 786436
  83.4 22.7 %collective-permute-start.17 = (bf16[128,1024]{1,0:T(8,128)(2,1)S(1)}, bf16[128,1024]{1,0:T(8,128)(2,1)}, u32[]{:S(2)}, u32[]{:S(2)}) collective-permute-start(bf16[128,1024]{1,0:T(8,128)(2,1)S(1)} %collective-permute-done.16), channel_id=1, source_target_pairs={{0,4},{4,8},{8,12},{12,16},{16,20},{20,24},{24,28},{28,32},{32,36}... | collective-permute-start | bytes 786440 | tf_op jit(solution)/shard_map/ppermute | solution.py:31
  96.4 7.8 %copy-start.6 = (bf16[128,4,128]{0,2,1:T(8,128)(2,1)}, bf16[128,4,128]{0,2,1:T(8,128)(2,1)S(1)}, u32[]{:S(2)}) copy-start(bf16[128,4,128]{0,2,1:T(8,128)(2,1)S(1)} %subtract_convert_fusion.1) | copy-start | bytes 393220
  96.7 10.5 %copy-start.29 = (bf16[128,1024]{1,0:T(8,128)(2,1)S(1)}, bf16[128,1024]{1,0:T(8,128)(2,1)}, u32[]{:S(2)}) copy-start(bf16[128,1024]{1,0:T(8,128)(2,1)} %copy-done.28) | copy-start | bytes 786436
  96.9 10.3 %copy-start.27 = (bf16[128,1024]{1,0:T(8,128)(2,1)S(1)}, bf16[128,1024]{1,0:T(8,128)(2,1)}, u32[]{:S(2)}) copy-start(bf16[128,1024]{1,0:T(8,128)(2,1)} %copy-done.26) | copy-start | bytes 786436
  97.3 6.2 %collective-permute-start.7 = (bf16[4,128,128]{1,2,0:T(8,128)(2,1)S(1)}, bf16[4,128,128]{1,2,0:T(8,128)(2,1)S(1)}, u32[]{:S(2)}, u32[]{:S(2)}) collective-permute-start(bf16[4,128,128]{1,2,0:T(8,128)(2,1)S(1)} %get-tuple-element.49), channel_id=1, source_target_pairs={{4,0},{8,4},{12,8},{16,12},{20,16},{24,20},{28,24},{32,28},{36,32}... | collective-permute-start | bytes 393224 | tf_op jit(solution)/shard_map/ppermute | solution.py:22
  104.2 20.0 %collective-permute-start.8 = (bf16[4,128,128]{1,2,0:T(8,128)(2,1)}, bf16[4,128,128]{1,2,0:T(8,128)(2,1)}, u32[]{:S(2)}, u32[]{:S(2)}) collective-permute-start(bf16[4,128,128]{1,2,0:T(8,128)(2,1)} %fusion.27), channel_id=1, source_target_pairs={{8,0},{12,4},{16,8},{20,12},{24,16},{28,20},{32,24},{36,28},{40,32... | collective-permute-start | bytes 393224 | tf_op jit(solution)/shard_map/ppermute | solution.py:22
  125.2 18.9 %copy-start.7 = (bf16[128,4,128]{0,2,1:T(8,128)(2,1)S(1)}, bf16[128,4,128]{0,2,1:T(8,128)(2,1)}, u32[]{:S(2)}) copy-start(bf16[128,4,128]{0,2,1:T(8,128)(2,1)} %copy-done.6) | copy-start | bytes 393220
  125.2 18.9 %copy-start.23 = (bf16[4,128,128]{2,1,0:T(8,128)(2,1)S(1)}, bf16[4,128,128]{2,1,0:T(8,128)(2,1)}, u32[]{:S(2)}) copy-start(bf16[4,128,128]{2,1,0:T(8,128)(2,1)} %copy-done.22) | copy-start | bytes 393220
  125.2 19.8 %copy-start.17 = (bf16[128,4,128]{0,2,1:T(8,128)(2,1)S(1)}, bf16[128,4,128]{0,2,1:T(8,128)(2,1)}, u32[]{:S(2)}) copy-start(bf16[128,4,128]{0,2,1:T(8,128)(2,1)} %fusion.13) | copy-start | bytes 393220
  125.2 13.5 %collective-permute-start.9 = (bf16[4,128,128]{1,2,0:T(8,128)(2,1)S(1)}, bf16[4,128,128]{1,2,0:T(8,128)(2,1)S(1)}, u32[]{:S(2)}, u32[]{:S(2)}) collective-permute-start(bf16[4,128,128]{1,2,0:T(8,128)(2,1)S(1)} %fusion.79), channel_id=1, source_target_pairs={{16,0},{20,4},{24,8},{28,12},{32,16},{36,20},{40,24},{44,28},{48,3... | collective-permute-start | bytes 393224 | tf_op jit(solution)/shard_map/ppermute | solution.py:22
  134.6 34.9 %collective-permute-start.18 = (bf16[128,1024]{1,0:T(8,128)(2,1)}, bf16[128,1024]{1,0:T(8,128)(2,1)}, u32[]{:S(2)}, u32[]{:S(2)}) collective-permute-start(bf16[128,1024]{1,0:T(8,128)(2,1)} %pad_maximum_fusion.1), channel_id=1, source_target_pairs={{4,0},{8,4},{12,8},{16,12},{20,16},{24,20},{28,24},{32,28},{36,32}... | collective-permute-start | bytes 786440 | tf_op jit(solution)/shard_map/ppermute | solution.py:31
  140.3 17.6 %collective-permute-start.10 = (bf16[4,128,128]{1,2,0:T(8,128)(2,1)}, bf16[4,128,128]{1,2,0:T(8,128)(2,1)}, u32[]{:S(2)}, u32[]{:S(2)}) collective-permute-start(bf16[4,128,128]{1,2,0:T(8,128)(2,1)} %fusion.28), channel_id=1, source_target_pairs={{32,0},{36,4},{40,8},{44,12},{48,16},{52,20},{56,24},{60,28},{64,3... | collective-permute-start | bytes 393224 | tf_op jit(solution)/shard_map/ppermute | solution.py:22
  145.8 39.6 %copy-start.3 = (bf16[512,4,128]{0,2,1:T(8,128)(2,1)S(1)}, bf16[512,4,128]{0,2,1:T(8,128)(2,1)}, u32[]{:S(2)}) copy-start(bf16[512,4,128]{0,2,1:T(8,128)(2,1)} %copy-done.2) | copy-start | bytes 1572868
  145.8 39.6 %copy-start.5 = (bf16[4,128,512]{1,2,0:T(8,128)(2,1)S(1)}, bf16[4,128,512]{1,2,0:T(8,128)(2,1)}, u32[]{:S(2)}) copy-start(bf16[4,128,512]{1,2,0:T(8,128)(2,1)} %copy-done.4) | copy-start | bytes 1572868
  159.0 23.7 %collective-permute-start.11 = (bf16[4,128,128]{1,2,0:T(8,128)(2,1)S(1)}, bf16[4,128,128]{1,2,0:T(8,128)(2,1)S(1)}, u32[]{:S(2)}, u32[]{:S(2)}) collective-permute-start(bf16[4,128,128]{1,2,0:T(8,128)(2,1)S(1)} %get-tuple-element.22), channel_id=1, source_target_pairs={{64,0},{68,4},{72,8},{76,12},{80,16},{84,20},{88,24},{92,28},{96,3... | collective-permute-start | bytes 393224 | tf_op jit(solution)/shard_map/ppermute | solution.py:22
  171.3 18.7 %collective-permute-start.19 = (bf16[128,1024]{1,0:T(8,128)(2,1)}, bf16[128,1024]{1,0:T(8,128)(2,1)}, u32[]{:S(2)}, u32[]{:S(2)}) collective-permute-start(bf16[128,1024]{1,0:T(8,128)(2,1)} %add_convert_fusion.2), channel_id=1, source_target_pairs={{4,0},{8,4},{12,8},{16,12},{20,16},{24,20},{28,24},{32,28},{36,32}... | collective-permute-start | bytes 786440 | tf_op jit(solution)/shard_map/ppermute | solution.py:31
  183.4 4.1 %collective-permute-start.12 = (bf16[4,128,128]{1,2,0:T(8,128)(2,1)}, bf16[4,128,128]{1,2,0:T(8,128)(2,1)}, u32[]{:S(2)}, u32[]{:S(2)}) collective-permute-start(bf16[4,128,128]{1,2,0:T(8,128)(2,1)} %fusion.29), channel_id=1, source_target_pairs={{128,0},{132,4},{136,8},{140,12},{144,16},{148,20},{152,24},{156,2... | collective-permute-start | bytes 393224 | tf_op jit(solution)/shard_map/ppermute | solution.py:22
  186.4 12.3 %copy-start.14 = (f32[4,128,128]{2,1,0:T(8,128)S(1)}, f32[4,128,128]{2,1,0:T(8,128)}, u32[]{:S(2)}) copy-start(f32[4,128,128]{2,1,0:T(8,128)} %fusion.89) | copy-start | bytes 786436
  186.4 12.3 %copy-start.16 = (bf16[128,512]{1,0:T(8,128)(2,1)S(1)}, bf16[128,512]{1,0:T(8,128)(2,1)}, u32[]{:S(2)}) copy-start(bf16[128,512]{1,0:T(8,128)(2,1)} %param.11) | copy-start | bytes 393220
  188.5 13.1 %copy-start.24 = (bf16[128,512]{1,0:T(8,128)(2,1)S(1)}, bf16[128,512]{1,0:T(8,128)(2,1)}, u32[]{:S(2)}) copy-start(bf16[128,512]{1,0:T(8,128)(2,1)} %get-tuple-element.30) | copy-start | bytes 393220
  188.5 13.1 %copy-start.25 = (bf16[128,512]{1,0:T(8,128)(2,1)S(1)}, bf16[128,512]{1,0:T(8,128)(2,1)}, u32[]{:S(2)}) copy-start(bf16[128,512]{1,0:T(8,128)(2,1)} %get-tuple-element.26) | copy-start | bytes 393220
  188.5 9.2 %collective-permute-start.13 = (bf16[4,128,128]{1,2,0:T(8,128)(2,1)S(1)}, bf16[4,128,128]{1,2,0:T(8,128)(2,1)S(1)}, u32[]{:S(2)}, u32[]{:S(2)}) collective-permute-start(bf16[4,128,128]{1,2,0:T(8,128)(2,1)S(1)} %fusion.52), channel_id=1, source_target_pairs={{256,0},{260,4},{264,8},{268,12},{272,16},{276,20},{280,24},{284,2... | collective-permute-start | bytes 393224 | tf_op jit(solution)/shard_map/ppermute | solution.py:22
  191.1 17.2 %copy-start.13 = (bf16[128,512]{1,0:T(8,128)(2,1)S(1)}, bf16[128,512]{1,0:T(8,128)(2,1)}, u32[]{:S(2)}) copy-start(bf16[128,512]{1,0:T(8,128)(2,1)} %param.12) | copy-start | bytes 393220
  191.1 10.5 %collective-permute-start.20 = (bf16[128,1024]{1,0:T(8,128)(2,1)S(1)}, bf16[128,1024]{1,0:T(8,128)(2,1)S(1)}, u32[]{:S(2)}, u32[]{:S(2)}) collective-permute-start(bf16[128,1024]{1,0:T(8,128)(2,1)S(1)} %add_convert_fusion.1), channel_id=1, source_target_pairs={{4,0},{8,4},{12,8},{16,12},{20,16},{24,20},{28,24},{32,28},{36,32}... | collective-permute-start | bytes 786440 | tf_op jit(solution)/shard_map/ppermute | solution.py:31
  198.7 10.6 %copy-start.11 = (bf16[128,512]{1,0:T(8,128)(2,1)S(1)}, bf16[128,512]{1,0:T(8,128)(2,1)}, u32[]{:S(2)}) copy-start(bf16[128,512]{1,0:T(8,128)(2,1)} %param.10) | copy-start | bytes 393220
  198.7 10.6 %copy-start.19 = (bf16[4,128,128]{2,1,0:T(8,128)(2,1)S(1)}, bf16[4,128,128]{2,1,0:T(8,128)(2,1)}, u32[]{:S(2)}) copy-start(bf16[4,128,128]{2,1,0:T(8,128)(2,1)} %copy-done.18) | copy-start | bytes 393220
  202.3 10.1 %collective-permute-start.21 = (bf16[128,1024]{1,0:T(8,128)(2,1)}, bf16[128,1024]{1,0:T(8,128)(2,1)}, u32[]{:S(2)}, u32[]{:S(2)}) collective-permute-start(bf16[128,1024]{1,0:T(8,128)(2,1)} %add_convert_fusion), channel_id=1, source_target_pairs={{4,0},{8,4},{12,8},{16,12},{20,16},{24,20},{28,24},{32,28},{36,32}... | collective-permute-start | bytes 786440 | tf_op jit(solution)/shard_map/ppermute | solution.py:31
  (11 other events, 21.9 us)

commit v6 on v5

--- a/solution.py
+++ b/solution.py
@@ -130,7 +130,13 @@
     ).astype(jnp.float32)
     square_sum = jnp.sum(output_lin * output_lin, axis=(1, 2))
     cross_sum = jnp.sum(gain_grad * output_lin, axis=(1, 2))
-    square_sum, cross_sum = lax.psum((square_sum, cross_sum), "head")
+    sums = jnp.stack([square_sum, cross_sum])
+    heads_dev = lax.axis_size("head")
+    step = 1
+    while step < heads_dev:
+        sums = sums + lax.ppermute(sums, "head", [(i, i ^ step) for i in range(heads_dev)])
+        step *= 2
+    square_sum, cross_sum = sums[0], sums[1]
     full_width = LIN_HEADS * HEAD
     inv_rms = lax.rsqrt(square_sum / full_width + 1e-06)[:, None, None]
     grad_out = (

time: 215 us -> 214 us (level)
  starting transfers between devices: 81.1 us -> 101 us
  waiting for transfers between devices: 76.7 us -> 66.1 us
  blocking collectives: 10.5 us -> 0 us
  other arithmetic: 20.4 us -> 17.2 us
  matrix products: 9.15 us -> 11.5 us
    ppermute x14, starting transfers between devices: 55.5 us -> 68.3 us  [carried_in(): sent = lax.ppermute(total.astype(jnp.bfloat16), axis, pairs)]
    ppermute x8, waiting for transfers between devices: 15.4 us -> 2.68 us  [from_behind(): return lax.ppermute(shard, axis, pairs)]
    psum x1 -> x0, blocking collectives: 10.5 us -> none  [per_device(): square_sum, cross_sum = lax.psum((square_sum, cross_sum), 'head')]
    ppermute x0 -> x2, starting transfers between devices: none -> 8.34 us  [per_device(): lax.ppermute(sums, 'head', [(i, i ^ step) for i in range(heads_dev)])]
    convert_element_type x12, other arithmetic: 6.25 us -> 3.85 us  [carried_in(): sent = lax.ppermute(total.astype(jnp.bfloat16), axis, pairs)]
    unnamed x82 -> x76, local copies, waits for them, and re-layouts: 5.53 us -> 4.95 us
  transfers between devices with their start and end apart: 22 -> 24, of which waited for: 15 -> 14; matrix products, arithmetic and copies ran while one was open for 18% -> 19% of each run, Pallas kernels for 0% -> 0%
where the time goes in v6:
time: 214 us; the launch traced here: 212 us
  starting transfers between devices  101 us (47%)
  waiting for transfers between devices  66.1 us (31%)
  other arithmetic  17.2 us (8%)
  local copies, waits for them, and re-layouts  14.2 us (7%)
  matrix products  11.5 us (5%)
    ppermute x14, starting transfers between devices, carried_in(): sent = lax.ppermute(total.astype(jnp.bfloat16), axis, pairs)  68.3 us
    ppermute x14, waiting for transfers between devices, carried_in(): sent = lax.ppermute(total.astype(jnp.bfloat16), axis, pairs)  63.4 us
    ppermute x8, starting transfers between devices, from_behind(): return lax.ppermute(shard, axis, pairs)  24.4 us
    ppermute x2, starting transfers between devices, per_device(): lax.ppermute(sums, 'head', [(i, i ^ step) for i in range(heads_dev)])  8.34 us
    convert_element_type x4, other arithmetic, per_device(): owed = from_behind(owed.astype(jnp.bfloat16), 'ctx', -1).astype(jnp.float32)  5.44 us
    unnamed x76, local copies, waits for them, and re-layouts  4.95 us
  transfers between devices with their start and end apart: 24, of which 14 were waited for; matrix products, arithmetic and copies ran while one was open for 19% of the time, Pallas kernels for 0%

profile of v6, /device:TPU:24, one launch (start us, length us, event | category | flops | bytes accessed | tf_op | source)
XLA Modules:
  0.0 211.7 jit_solution(4760984365063886385)
XLA Ops:
  0.7 1.1 pad_maximum_fusion
  1.8 1.9 collective-permute-start.16
  4.7 1.1 fusion.85
  5.8 3.9 %collective-permute-start = (bf16[4,128,128]{2,1,0:T(8,128)(2,1)S(1)}, bf16[4,128,128]{2,1,0:T(8,128)(2,1)S(1)}, u32[]{:S(2)}, u32[]{:S(2)}) collective-permute-start(bf16[4,128,128]{2,1,0:T(8,128)(2,1)S(1)} %get-tuple-element.44), channel_id=1, source_target_pairs={{0,4},{4,8},{8,12},{12,16},{16,20},{20,24},{24,28},{28,32},{32,36}... | collective-permute-start | bytes 393224 | tf_op jit(solution)/shard_map/ppermute | solution.py:22
  10.3 9.2 %collective-permute-done = bf16[4,128,128]{2,1,0:T(8,128)(2,1)S(1)} collective-permute-done((bf16[4,128,128]{2,1,0:T(8,128)(2,1)S(1)}, bf16[4,128,128]{2,1,0:T(8,128)(2,1)S(1)}, u32[]{:S(2)}, u32[]{:S(2)}) %collective-permute-start) | collective-permute-done | bytes 131104 | tf_op jit(solution)/shard_map/ppermute | solution.py:22
  19.5 1.9 collective-permute-start.1
  21.5 7.1 %collective-permute-done.1 = bf16[4,128,128]{2,1,0:T(8,128)(2,1)S(1)} collective-permute-done((bf16[4,128,128]{2,1,0:T(8,128)(2,1)S(1)}, bf16[4,128,128]{2,1,0:T(8,128)(2,1)S(1)}, u32[]{:S(2)}, u32[]{:S(2)}) %collective-permute-start.1) | collective-permute-done | bytes 131104 | tf_op jit(solution)/shard_map/ppermute | solution.py:22
  28.7 1.9 collective-permute-start.2
  30.7 7.9 %collective-permute-done.2 = bf16[4,128,128]{2,1,0:T(8,128)(2,1)S(1)} collective-permute-done((bf16[4,128,128]{2,1,0:T(8,128)(2,1)S(1)}, bf16[4,128,128]{2,1,0:T(8,128)(2,1)S(1)}, u32[]{:S(2)}, u32[]{:S(2)}) %collective-permute-start.2) | collective-permute-done | bytes 131104 | tf_op jit(solution)/shard_map/ppermute | solution.py:22
  38.7 2.1 collective-permute-start.3
  40.7 10.0 %collective-permute-done.3 = bf16[4,128,128]{2,1,0:T(8,128)(2,1)S(1)} collective-permute-done((bf16[4,128,128]{2,1,0:T(8,128)(2,1)S(1)}, bf16[4,128,128]{2,1,0:T(8,128)(2,1)S(1)}, u32[]{:S(2)}, u32[]{:S(2)}) %collective-permute-start.3) | collective-permute-done | bytes 131104 | tf_op jit(solution)/shard_map/ppermute | solution.py:22
  50.8 12.1 %collective-permute-start.4 = (bf16[4,128,128]{2,1,0:T(8,128)(2,1)S(1)}, bf16[4,128,128]{2,1,0:T(8,128)(2,1)S(1)}, u32[]{:S(2)}, u32[]{:S(2)}) collective-permute-start(bf16[4,128,128]{2,1,0:T(8,128)(2,1)S(1)} %get-tuple-element.24), channel_id=1, source_target_pairs={{0,64},{4,68},{8,72},{12,76},{16,80},{20,84},{24,88},{28,92},{32,9... | collective-permute-start | bytes 393224 | tf_op jit(solution)/shard_map/ppermute | solution.py:22
  63.8 3.7 %collective-permute-done.4 = bf16[4,128,128]{2,1,0:T(8,128)(2,1)S(1)} collective-permute-done((bf16[4,128,128]{2,1,0:T(8,128)(2,1)S(1)}, bf16[4,128,128]{2,1,0:T(8,128)(2,1)S(1)}, u32[]{:S(2)}, u32[]{:S(2)}) %collective-permute-start.4) | collective-permute-done | bytes 131104 | tf_op jit(solution)/shard_map/ppermute | solution.py:22
  67.5 1.3 collective-permute-start.5
  68.8 5.5 %collective-permute-done.5 = bf16[4,128,128]{2,1,0:T(8,128)(2,1)S(1)} collective-permute-done((bf16[4,128,128]{2,1,0:T(8,128)(2,1)S(1)}, bf16[4,128,128]{2,1,0:T(8,128)(2,1)S(1)}, u32[]{:S(2)}, u32[]{:S(2)}) %collective-permute-start.5) | collective-permute-done | bytes 131104 | tf_op jit(solution)/shard_map/ppermute | solution.py:22
  74.4 1.4 collective-permute-start.6
  76.0 1.9 collective-permute-start.17
  78.0 4.9 %collective-permute-done.6 = bf16[4,128,128]{2,1,0:T(8,128)(2,1)S(1)} collective-permute-done((bf16[4,128,128]{2,1,0:T(8,128)(2,1)S(1)}, bf16[4,128,128]{2,1,0:T(8,128)(2,1)S(1)}, u32[]{:S(2)}, u32[]{:S(2)}) %collective-permute-start.6) | collective-permute-done | bytes 131104 | tf_op jit(solution)/shard_map/ppermute | solution.py:22
  83.9 3.4 %collective-permute-start.7 = (f32[2,128]{1,0:T(2,128)S(1)}, f32[2,128]{1,0:T(2,128)S(1)}, u32[]{:S(2)}, u32[]{:S(2)}) collective-permute-start(f32[2,128]{1,0:T(2,128)S(1)} %pad_maximum_fusion.2), channel_id=1, source_target_pairs={{0,1},{1,0},{2,3},{3,2},{4,5},{5,4},{6,7},{7,6},{8,9},{9,8},{10,11... | collective-permute-start | bytes 3080 | tf_op jit(solution)/shard_map/ppermute | solution.py:137
  87.4 1.9 collective-permute-start.18
  89.4 4.9 %collective-permute-start.8 = (f32[2,128]{1,0:T(2,128)S(1)}, f32[2,128]{1,0:T(2,128)S(1)}, u32[]{:S(2)}, u32[]{:S(2)}) collective-permute-start(f32[2,128]{1,0:T(2,128)S(1)} %fusion.78), channel_id=1, source_target_pairs={{0,2},{1,3},{2,0},{3,1},{4,6},{5,7},{6,4},{7,5},{8,10},{9,11},{10,... | collective-permute-start | bytes 3080 | tf_op jit(solution)/shard_map/ppermute | solution.py:137
  94.5 2.7 %collective-permute-done.18 = bf16[128,1024]{1,0:T(8,128)(2,1)S(1)} collective-permute-done((bf16[128,1024]{1,0:T(8,128)(2,1)S(1)}, bf16[128,1024]{1,0:T(8,128)(2,1)S(1)}, u32[]{:S(2)}, u32[]{:S(2)}) %collective-permute-start.18) | collective-permute-done | bytes 262176 | tf_op jit(solution)/shard_map/ppermute | solution.py:31
  97.2 2.2 %collective-permute-start.19 = (bf16[128,1024]{1,0:T(8,128)(2,1)S(1)}, bf16[128,1024]{1,0:T(8,128)(2,1)S(1)}, u32[]{:S(2)}, u32[]{:S(2)}) collective-permute-start(bf16[128,1024]{1,0:T(8,128)(2,1)S(1)} %collective-permute-done.18), channel_id=1, source_target_pairs={{0,4},{4,8},{8,12},{12,16},{16,20},{20,24},{24,28},{28,32},{32,36}... | collective-permute-start | bytes 786440 | tf_op jit(solution)/shard_map/ppermute | solution.py:31
  100.7 5.6 %collective-permute-start.9 = (bf16[4,128,128]{1,2,0:T(8,128)(2,1)}, bf16[4,128,128]{1,2,0:T(8,128)(2,1)S(1)}, u32[]{:S(2)}, u32[]{:S(2)}) collective-permute-start(bf16[4,128,128]{1,2,0:T(8,128)(2,1)} %get-tuple-element.47), channel_id=1, source_target_pairs={{4,0},{8,4},{12,8},{16,12},{20,16},{24,20},{28,24},{32,28},{36,32}... | collective-permute-start | bytes 393224 | tf_op jit(solution)/shard_map/ppermute | solution.py:22
  111.4 1.5 fusion.87
  113.0 1.6 convolution_bitcast_fusion
  117.4 1.4 reshape.446
  119.0 1.2 scatter_fusion.1
  121.1 2.3 %scatter_fusion = f32[5,128,512]{2,1,0:T(8,128)S(1)} fusion(f32[5,128,512]{2,1,0:T(8,128)S(1)} %broadcast.216.clone.1, s32[4]{0:T(128)S(1)} %fusion.72, f32[4,128,512]{2,1,0:T(8,128)} %reshape.446), kind=kCustom, calls=%fused_computation.2 | custom fusion | flops 262144 | bytes 3145744 | tf_op jit(solution)/shard_map/scatter-add | solution.py:93
  124.3 2.1 collective-permute-start.20
  126.4 5.3 %collective-permute-start.10 = (bf16[4,128,128]{1,2,0:T(8,128)(2,1)S(1)}, bf16[4,128,128]{1,2,0:T(8,128)(2,1)S(1)}, u32[]{:S(2)}, u32[]{:S(2)}) collective-permute-start(bf16[4,128,128]{1,2,0:T(8,128)(2,1)S(1)} %fusion.27), channel_id=1, source_target_pairs={{8,0},{12,4},{16,8},{20,12},{24,16},{28,20},{32,24},{36,28},{40,32... | collective-permute-start | bytes 393224 | tf_op jit(solution)/shard_map/ppermute | solution.py:22
  132.7 2.7 %collective-permute-done.10 = bf16[4,128,128]{1,2,0:T(8,128)(2,1)S(1)} collective-permute-done((bf16[4,128,128]{1,2,0:T(8,128)(2,1)S(1)}, bf16[4,128,128]{1,2,0:T(8,128)(2,1)S(1)}, u32[]{:S(2)}, u32[]{:S(2)}) %collective-permute-start.10) | collective-permute-done | bytes 131104 | tf_op jit(solution)/shard_map/ppermute | solution.py:22
  135.4 5.3 %collective-permute-start.11 = (bf16[4,128,128]{1,2,0:T(8,128)(2,1)S(1)}, bf16[4,128,128]{1,2,0:T(8,128)(2,1)S(1)}, u32[]{:S(2)}, u32[]{:S(2)}) collective-permute-start(bf16[4,128,128]{1,2,0:T(8,128)(2,1)S(1)} %fusion.80), channel_id=1, source_target_pairs={{16,0},{20,4},{24,8},{28,12},{32,16},{36,20},{40,24},{44,28},{48,3... | collective-permute-start | bytes 393224 | tf_op jit(solution)/shard_map/ppermute | solution.py:22
  141.5 3.3 %collective-permute-start.21 = (bf16[128,1024]{1,0:T(8,128)(2,1)}, bf16[128,1024]{1,0:T(8,128)(2,1)}, u32[]{:S(2)}, u32[]{:S(2)}) collective-permute-start(bf16[128,1024]{1,0:T(8,128)(2,1)} %add_convert_fusion.2), channel_id=1, source_target_pairs={{4,0},{8,4},{12,8},{16,12},{20,16},{24,20},{28,24},{32,28},{36,32}... | collective-permute-start | bytes 786440 | tf_op jit(solution)/shard_map/ppermute | solution.py:31
  144.8 1.8 collective-permute-done.11
  147.3 7.9 %collective-permute-start.12 = (bf16[4,128,128]{1,2,0:T(8,128)(2,1)}, bf16[4,128,128]{1,2,0:T(8,128)(2,1)}, u32[]{:S(2)}, u32[]{:S(2)}) collective-permute-start(bf16[4,128,128]{1,2,0:T(8,128)(2,1)} %fusion.28), channel_id=1, source_target_pairs={{32,0},{36,4},{40,8},{44,12},{48,16},{52,20},{56,24},{60,28},{64,3... | collective-permute-start | bytes 393224 | tf_op jit(solution)/shard_map/ppermute | solution.py:22
  157.0 7.7 %collective-permute-done.12 = bf16[4,128,128]{1,2,0:T(8,128)(2,1)} collective-permute-done((bf16[4,128,128]{1,2,0:T(8,128)(2,1)}, bf16[4,128,128]{1,2,0:T(8,128)(2,1)}, u32[]{:S(2)}, u32[]{:S(2)}) %collective-permute-start.12) | collective-permute-done | bytes 131104 | tf_op jit(solution)/shard_map/ppermute | solution.py:22
  164.6 1.1 fusion.83
  165.8 8.1 %collective-permute-start.13 = (bf16[4,128,128]{1,2,0:T(8,128)(2,1)S(1)}, bf16[4,128,128]{1,2,0:T(8,128)(2,1)S(1)}, u32[]{:S(2)}, u32[]{:S(2)}) collective-permute-start(bf16[4,128,128]{1,2,0:T(8,128)(2,1)S(1)} %get-tuple-element.20), channel_id=1, source_target_pairs={{64,0},{68,4},{72,8},{76,12},{80,16},{84,20},{88,24},{92,28},{96,3... | collective-permute-start | bytes 393224 | tf_op jit(solution)/shard_map/ppermute | solution.py:22
  173.9 1.8 add_convert_fusion.1
  175.7 4.3 %collective-permute-start.22 = (bf16[128,1024]{1,0:T(8,128)(2,1)}, bf16[128,1024]{1,0:T(8,128)(2,1)}, u32[]{:S(2)}, u32[]{:S(2)}) collective-permute-start(bf16[128,1024]{1,0:T(8,128)(2,1)} %add_convert_fusion.1), channel_id=1, source_target_pairs={{4,0},{8,4},{12,8},{16,12},{20,16},{24,20},{28,24},{32,28},{36,32}... | collective-permute-start | bytes 786440 | tf_op jit(solution)/shard_map/ppermute | solution.py:31
  180.0 1.8 collective-permute-done.13
  182.5 1.9 collective-permute-start.14
  185.5 1.1 collective-permute-done.14
  187.6 9.4 %collective-permute-start.15 = (bf16[4,128,128]{1,2,0:T(8,128)(2,1)S(1)}, bf16[4,128,128]{1,2,0:T(8,128)(2,1)S(1)}, u32[]{:S(2)}, u32[]{:S(2)}) collective-permute-start(bf16[4,128,128]{1,2,0:T(8,128)(2,1)S(1)} %fusion.52), channel_id=1, source_target_pairs={{256,0},{260,4},{264,8},{268,12},{272,16},{276,20},{280,24},{284,2... | collective-permute-start | bytes 393224 | tf_op jit(solution)/shard_map/ppermute | solution.py:22
  197.1 1.8 add_convert_fusion
  198.9 6.8 %collective-permute-start.23 = (bf16[128,1024]{1,0:T(8,128)(2,1)}, bf16[128,1024]{1,0:T(8,128)(2,1)}, u32[]{:S(2)}, u32[]{:S(2)}) collective-permute-start(bf16[128,1024]{1,0:T(8,128)(2,1)} %add_convert_fusion), channel_id=1, source_target_pairs={{4,0},{8,4},{12,8},{16,12},{20,16},{24,20},{28,24},{32,28},{36,32}... | collective-permute-start | bytes 786440 | tf_op jit(solution)/shard_map/ppermute | solution.py:31
  208.0 1.1 fusion.14
  (155 shorter events, 26.9 us)
Async XLA Ops:
  0.6 110.8 %copy-start = (bf16[128,512]{1,0:T(8,128)(2,1)S(1)}, bf16[128,512]{1,0:T(8,128)(2,1)}, u32[]{:S(2)}) copy-start(bf16[128,512]{1,0:T(8,128)(2,1)} %param.15) | copy-start | bytes 393220
  0.6 9.1 %copy-start.14 = (bf16[128,512]{1,0:T(8,128)(2,1)S(1)}, bf16[128,512]{1,0:T(8,128)(2,1)}, u32[]{:S(2)}) copy-start(bf16[128,512]{1,0:T(8,128)(2,1)} %param.11) | copy-start | bytes 393220
  0.7 9.3 %copy-start.8 = (bf16[128,512]{1,0:T(8,128)(2,1)S(1)}, bf16[128,512]{1,0:T(8,128)(2,1)}, u32[]{:S(2)}) copy-start(bf16[128,512]{1,0:T(8,128)(2,1)} %param.12) | copy-start | bytes 393220
  0.7 9.1 %copy-start.5 = (bf16[128,512]{1,0:T(8,128)(2,1)S(1)}, bf16[128,512]{1,0:T(8,128)(2,1)}, u32[]{:S(2)}) copy-start(bf16[128,512]{1,0:T(8,128)(2,1)} %param.10) | copy-start | bytes 393220
  1.8 19.7 %copy-start.32 = (s32[1,3]{1,0:T(1,128)S(1)}, s32[1,3]{1,0:T(1,128)}, u32[]{:S(2)}) copy-start(s32[1,3]{1,0:T(1,128)} %param.19) | copy-start | bytes 40
  1.8 74.3 %collective-permute-start.16 = (bf16[128,1024]{1,0:T(8,128)(2,1)S(1)}, bf16[128,1024]{1,0:T(8,128)(2,1)S(1)}, u32[]{:S(2)}, u32[]{:S(2)}) collective-permute-start(bf16[128,1024]{1,0:T(8,128)(2,1)S(1)} %pad_maximum_fusion), channel_id=1, source_target_pairs={{0,4},{4,8},{8,12},{12,16},{16,20},{20,24},{24,28},{28,32},{32,36}... | collective-permute-start | bytes 786440 | tf_op jit(solution)/shard_map/ppermute | solution.py:31
  5.8 13.7 %collective-permute-start = (bf16[4,128,128]{2,1,0:T(8,128)(2,1)S(1)}, bf16[4,128,128]{2,1,0:T(8,128)(2,1)S(1)}, u32[]{:S(2)}, u32[]{:S(2)}) collective-permute-start(bf16[4,128,128]{2,1,0:T(8,128)(2,1)S(1)} %get-tuple-element.44), channel_id=1, source_target_pairs={{0,4},{4,8},{8,12},{12,16},{16,20},{20,24},{24,28},{28,32},{32,36}... | collective-permute-start | bytes 393224 | tf_op jit(solution)/shard_map/ppermute | solution.py:22
  10.0 18.6 %copy-start.21 = (bf16[4,128,128]{2,1,0:T(8,128)(2,1)}, bf16[4,128,128]{2,1,0:T(8,128)(2,1)S(1)}, u32[]{:S(2)}) copy-start(bf16[4,128,128]{2,1,0:T(8,128)(2,1)S(1)} %fusion.15) | copy-start | bytes 393220
  19.5 9.1 %collective-permute-start.1 = (bf16[4,128,128]{2,1,0:T(8,128)(2,1)S(1)}, bf16[4,128,128]{2,1,0:T(8,128)(2,1)S(1)}, u32[]{:S(2)}, u32[]{:S(2)}) collective-permute-start(bf16[4,128,128]{2,1,0:T(8,128)(2,1)S(1)} %fusion.24), channel_id=1, source_target_pairs={{0,8},{4,12},{8,16},{12,20},{16,24},{20,28},{24,32},{28,36},{32,40... | collective-permute-start | bytes 393224 | tf_op jit(solution)/shard_map/ppermute | solution.py:22
  28.7 9.9 %collective-permute-start.2 = (bf16[4,128,128]{2,1,0:T(8,128)(2,1)S(1)}, bf16[4,128,128]{2,1,0:T(8,128)(2,1)S(1)}, u32[]{:S(2)}, u32[]{:S(2)}) collective-permute-start(bf16[4,128,128]{2,1,0:T(8,128)(2,1)S(1)} %fusion.79), channel_id=1, source_target_pairs={{0,16},{4,20},{8,24},{12,28},{16,32},{20,36},{24,40},{28,44},{32,4... | collective-permute-start | bytes 393224 | tf_op jit(solution)/shard_map/ppermute | solution.py:22
  38.6 37.2 %copy-start.27 = (bf16[128,512]{1,0:T(8,128)(2,1)S(1)}, bf16[128,512]{1,0:T(8,128)(2,1)}, u32[]{:S(2)}) copy-start(bf16[128,512]{1,0:T(8,128)(2,1)} %param.14) | copy-start | bytes 393220
  38.7 12.1 %collective-permute-start.3 = (bf16[4,128,128]{2,1,0:T(8,128)(2,1)S(1)}, bf16[4,128,128]{2,1,0:T(8,128)(2,1)S(1)}, u32[]{:S(2)}, u32[]{:S(2)}) collective-permute-start(bf16[4,128,128]{2,1,0:T(8,128)(2,1)S(1)} %fusion.25), channel_id=1, source_target_pairs={{0,32},{4,36},{8,40},{12,44},{16,48},{20,52},{24,56},{28,60},{32,6... | collective-permute-start | bytes 393224 | tf_op jit(solution)/shard_map/ppermute | solution.py:22
  50.8 16.6 %collective-permute-start.4 = (bf16[4,128,128]{2,1,0:T(8,128)(2,1)S(1)}, bf16[4,128,128]{2,1,0:T(8,128)(2,1)S(1)}, u32[]{:S(2)}, u32[]{:S(2)}) collective-permute-start(bf16[4,128,128]{2,1,0:T(8,128)(2,1)S(1)} %get-tuple-element.24), channel_id=1, source_target_pairs={{0,64},{4,68},{8,72},{12,76},{16,80},{20,84},{24,88},{28,92},{32,9... | collective-permute-start | bytes 393224 | tf_op jit(solution)/shard_map/ppermute | solution.py:22
  67.4 16.2 %copy-start.31 = (f32[512]{0:T(512)S(1)}, f32[512]{0:T(512)}, u32[]{:S(2)}) copy-start(f32[512]{0:T(512)} %param.13) | copy-start | bytes 6148
  67.5 6.9 %collective-permute-start.5 = (bf16[4,128,128]{2,1,0:T(8,128)(2,1)S(1)}, bf16[4,128,128]{2,1,0:T(8,128)(2,1)S(1)}, u32[]{:S(2)}, u32[]{:S(2)}) collective-permute-start(bf16[4,128,128]{2,1,0:T(8,128)(2,1)S(1)} %fusion.26), channel_id=1, source_target_pairs={{0,128},{4,132},{8,136},{12,140},{16,144},{20,148},{24,152},{28,15... | collective-permute-start | bytes 393224 | tf_op jit(solution)/shard_map/ppermute | solution.py:22
  74.4 20.0 %copy-start.28 = (bf16[128,512]{1,0:T(8,128)(2,1)S(1)}, bf16[128,512]{1,0:T(8,128)(2,1)}, u32[]{:S(2)}) copy-start(bf16[128,512]{1,0:T(8,128)(2,1)} %param.18) | copy-start | bytes 393220
  74.4 8.5 %collective-permute-start.6 = (bf16[4,128,128]{2,1,0:T(8,128)(2,1)S(1)}, bf16[4,128,128]{2,1,0:T(8,128)(2,1)S(1)}, u32[]{:S(2)}, u32[]{:S(2)}) collective-permute-start(bf16[4,128,128]{2,1,0:T(8,128)(2,1)S(1)} %fusion.51), channel_id=1, source_target_pairs={{0,256},{4,260},{8,264},{12,268},{16,272},{20,276},{24,280},{28,28... | collective-permute-start | bytes 393224 | tf_op jit(solution)/shard_map/ppermute | solution.py:22
  76.0 11.3 %collective-permute-start.17 = (bf16[128,1024]{1,0:T(8,128)(2,1)S(1)}, bf16[128,1024]{1,0:T(8,128)(2,1)S(1)}, u32[]{:S(2)}, u32[]{:S(2)}) collective-permute-start(bf16[128,1024]{1,0:T(8,128)(2,1)S(1)} %collective-permute-done.16), channel_id=1, source_target_pairs={{0,4},{4,8},{8,12},{12,16},{16,20},{20,24},{24,28},{28,32},{32,36}... | collective-permute-start | bytes 786440 | tf_op jit(solution)/shard_map/ppermute | solution.py:31
  83.9 5.5 %collective-permute-start.7 = (f32[2,128]{1,0:T(2,128)S(1)}, f32[2,128]{1,0:T(2,128)S(1)}, u32[]{:S(2)}, u32[]{:S(2)}) collective-permute-start(f32[2,128]{1,0:T(2,128)S(1)} %pad_maximum_fusion.2), channel_id=1, source_target_pairs={{0,1},{1,0},{2,3},{3,2},{4,5},{5,4},{6,7},{7,6},{8,9},{9,8},{10,11... | collective-permute-start | bytes 3080 | tf_op jit(solution)/shard_map/ppermute | solution.py:137
  87.4 13.3 %copy-start.24 = (bf16[128,1024]{1,0:T(8,128)(2,1)}, bf16[128,1024]{1,0:T(8,128)(2,1)S(1)}, u32[]{:S(2)}) copy-start(bf16[128,1024]{1,0:T(8,128)(2,1)S(1)} %collective-permute-done.17) | copy-start | bytes 786436
  87.4 9.8 %collective-permute-start.18 = (bf16[128,1024]{1,0:T(8,128)(2,1)S(1)}, bf16[128,1024]{1,0:T(8,128)(2,1)S(1)}, u32[]{:S(2)}, u32[]{:S(2)}) collective-permute-start(bf16[128,1024]{1,0:T(8,128)(2,1)S(1)} %collective-permute-done.17), channel_id=1, source_target_pairs={{0,4},{4,8},{8,12},{12,16},{16,20},{20,24},{24,28},{28,32},{32,36}... | collective-permute-start | bytes 786440 | tf_op jit(solution)/shard_map/ppermute | solution.py:31
  89.4 10.0 %collective-permute-start.8 = (f32[2,128]{1,0:T(2,128)S(1)}, f32[2,128]{1,0:T(2,128)S(1)}, u32[]{:S(2)}, u32[]{:S(2)}) collective-permute-start(f32[2,128]{1,0:T(2,128)S(1)} %fusion.78), channel_id=1, source_target_pairs={{0,2},{1,3},{2,0},{3,1},{4,6},{5,7},{6,4},{7,5},{8,10},{9,11},{10,... | collective-permute-start | bytes 3080 | tf_op jit(solution)/shard_map/ppermute | solution.py:137
  97.2 10.1 %copy-start.26 = (bf16[128,1024]{1,0:T(8,128)(2,1)}, bf16[128,1024]{1,0:T(8,128)(2,1)S(1)}, u32[]{:S(2)}) copy-start(bf16[128,1024]{1,0:T(8,128)(2,1)S(1)} %collective-permute-done.18) | copy-start | bytes 786436
  97.2 10.1 %collective-permute-start.19 = (bf16[128,1024]{1,0:T(8,128)(2,1)S(1)}, bf16[128,1024]{1,0:T(8,128)(2,1)S(1)}, u32[]{:S(2)}, u32[]{:S(2)}) collective-permute-start(bf16[128,1024]{1,0:T(8,128)(2,1)S(1)} %collective-permute-done.18), channel_id=1, source_target_pairs={{0,4},{4,8},{8,12},{12,16},{16,20},{20,24},{24,28},{28,32},{32,36}... | collective-permute-start | bytes 786440 | tf_op jit(solution)/shard_map/ppermute | solution.py:31
  100.7 25.7 %collective-permute-start.9 = (bf16[4,128,128]{1,2,0:T(8,128)(2,1)}, bf16[4,128,128]{1,2,0:T(8,128)(2,1)S(1)}, u32[]{:S(2)}, u32[]{:S(2)}) collective-permute-start(bf16[4,128,128]{1,2,0:T(8,128)(2,1)} %get-tuple-element.47), channel_id=1, source_target_pairs={{4,0},{8,4},{12,8},{16,12},{20,16},{24,20},{28,24},{32,28},{36,32}... | collective-permute-start | bytes 393224 | tf_op jit(solution)/shard_map/ppermute | solution.py:22
  123.5 8.3 %copy-start.11 = (bf16[4,128,128]{2,1,0:T(8,128)(2,1)S(1)}, bf16[4,128,128]{2,1,0:T(8,128)(2,1)}, u32[]{:S(2)}) copy-start(bf16[4,128,128]{2,1,0:T(8,128)(2,1)} %copy-done.10) | copy-start | bytes 393220
  123.5 8.3 %copy-start.12 = (f32[128,4,128]{0,2,1:T(8,128)S(1)}, f32[128,4,128]{0,2,1:T(8,128)}, u32[]{:S(2)}) copy-start(f32[128,4,128]{0,2,1:T(8,128)} %convolution_bitcast_fusion.7) | copy-start | bytes 786436
  124.3 16.4 %copy-start.23 = (bf16[128,512]{1,0:T(8,128)(2,1)S(1)}, bf16[128,512]{1,0:T(8,128)(2,1)}, u32[]{:S(2)}) copy-start(bf16[128,512]{1,0:T(8,128)(2,1)} %get-tuple-element.32) | copy-start | bytes 393220
  124.3 16.4 %collective-permute-start.20 = (bf16[128,1024]{1,0:T(8,128)(2,1)S(1)}, bf16[128,1024]{1,0:T(8,128)(2,1)S(1)}, u32[]{:S(2)}, u32[]{:S(2)}) collective-permute-start(bf16[128,1024]{1,0:T(8,128)(2,1)S(1)} %pad_maximum_fusion.1), channel_id=1, source_target_pairs={{4,0},{8,4},{12,8},{16,12},{20,16},{24,20},{28,24},{32,28},{36,32}... | collective-permute-start | bytes 786440 | tf_op jit(solution)/shard_map/ppermute | solution.py:31
  126.4 28.8 %copy-start.22 = (bf16[4,128,128]{2,1,0:T(8,128)(2,1)S(1)}, bf16[4,128,128]{2,1,0:T(8,128)(2,1)}, u32[]{:S(2)}) copy-start(bf16[4,128,128]{2,1,0:T(8,128)(2,1)} %copy-done.21) | copy-start | bytes 393220
  126.4 8.9 %collective-permute-start.10 = (bf16[4,128,128]{1,2,0:T(8,128)(2,1)S(1)}, bf16[4,128,128]{1,2,0:T(8,128)(2,1)S(1)}, u32[]{:S(2)}, u32[]{:S(2)}) collective-permute-start(bf16[4,128,128]{1,2,0:T(8,128)(2,1)S(1)} %fusion.27), channel_id=1, source_target_pairs={{8,0},{12,4},{16,8},{20,12},{24,16},{28,20},{32,24},{36,28},{40,32... | collective-permute-start | bytes 393224 | tf_op jit(solution)/shard_map/ppermute | solution.py:22
  132.7 23.5 %copy-start.16 = (bf16[128,4,128]{0,2,1:T(8,128)(2,1)S(1)}, bf16[128,4,128]{0,2,1:T(8,128)(2,1)}, u32[]{:S(2)}) copy-start(bf16[128,4,128]{0,2,1:T(8,128)(2,1)} %fusion.13) | copy-start | bytes 393220
  135.3 21.6 %copy-start.7 = (bf16[4,128,128]{1,2,0:T(8,128)(2,1)}, bf16[4,128,128]{1,2,0:T(8,128)(2,1)S(1)}, u32[]{:S(2)}) copy-start(bf16[4,128,128]{1,2,0:T(8,128)(2,1)S(1)} %collective-permute-done.10) | copy-start | bytes 393220
  135.4 11.2 %collective-permute-start.11 = (bf16[4,128,128]{1,2,0:T(8,128)(2,1)S(1)}, bf16[4,128,128]{1,2,0:T(8,128)(2,1)S(1)}, u32[]{:S(2)}, u32[]{:S(2)}) collective-permute-start(bf16[4,128,128]{1,2,0:T(8,128)(2,1)S(1)} %fusion.80), channel_id=1, source_target_pairs={{16,0},{20,4},{24,8},{28,12},{32,16},{36,20},{40,24},{44,28},{48,3... | collective-permute-start | bytes 393224 | tf_op jit(solution)/shard_map/ppermute | solution.py:22
  141.5 32.3 %collective-permute-start.21 = (bf16[128,1024]{1,0:T(8,128)(2,1)}, bf16[128,1024]{1,0:T(8,128)(2,1)}, u32[]{:S(2)}, u32[]{:S(2)}) collective-permute-start(bf16[128,1024]{1,0:T(8,128)(2,1)} %add_convert_fusion.2), channel_id=1, source_target_pairs={{4,0},{8,4},{12,8},{16,12},{20,16},{24,20},{28,24},{32,28},{36,32}... | collective-permute-start | bytes 786440 | tf_op jit(solution)/shard_map/ppermute | solution.py:31
  146.6 9.6 %copy-start.18 = (bf16[4,128,128]{1,2,0:T(8,128)(2,1)}, bf16[4,128,128]{1,2,0:T(8,128)(2,1)S(1)}, u32[]{:S(2)}) copy-start(bf16[4,128,128]{1,2,0:T(8,128)(2,1)S(1)} %collective-permute-done.11) | copy-start | bytes 393220
  147.3 17.3 %collective-permute-start.12 = (bf16[4,128,128]{1,2,0:T(8,128)(2,1)}, bf16[4,128,128]{1,2,0:T(8,128)(2,1)}, u32[]{:S(2)}, u32[]{:S(2)}) collective-permute-start(bf16[4,128,128]{1,2,0:T(8,128)(2,1)} %fusion.28), channel_id=1, source_target_pairs={{32,0},{36,4},{40,8},{44,12},{48,16},{52,20},{56,24},{60,28},{64,3... | collective-permute-start | bytes 393224 | tf_op jit(solution)/shard_map/ppermute | solution.py:22
  156.9 27.5 %copy-start.2 = (bf16[512,4,128]{0,2,1:T(8,128)(2,1)S(1)}, bf16[512,4,128]{0,2,1:T(8,128)(2,1)}, u32[]{:S(2)}) copy-start(bf16[512,4,128]{0,2,1:T(8,128)(2,1)} %copy-done.1) | copy-start | bytes 1572868
  156.9 27.5 %copy-start.4 = (bf16[4,128,512]{1,2,0:T(8,128)(2,1)S(1)}, bf16[4,128,512]{1,2,0:T(8,128)(2,1)}, u32[]{:S(2)}) copy-start(bf16[4,128,512]{1,2,0:T(8,128)(2,1)} %copy-done.3) | copy-start | bytes 1572868
  165.8 16.1 %collective-permute-start.13 = (bf16[4,128,128]{1,2,0:T(8,128)(2,1)S(1)}, bf16[4,128,128]{1,2,0:T(8,128)(2,1)S(1)}, u32[]{:S(2)}, u32[]{:S(2)}) collective-permute-start(bf16[4,128,128]{1,2,0:T(8,128)(2,1)S(1)} %get-tuple-element.20), channel_id=1, source_target_pairs={{64,0},{68,4},{72,8},{76,12},{80,16},{84,20},{88,24},{92,28},{96,3... | collective-permute-start | bytes 393224 | tf_op jit(solution)/shard_map/ppermute | solution.py:22
  175.7 21.3 %collective-permute-start.22 = (bf16[128,1024]{1,0:T(8,128)(2,1)}, bf16[128,1024]{1,0:T(8,128)(2,1)}, u32[]{:S(2)}, u32[]{:S(2)}) collective-permute-start(bf16[128,1024]{1,0:T(8,128)(2,1)} %add_convert_fusion.1), channel_id=1, source_target_pairs={{4,0},{8,4},{12,8},{16,12},{20,16},{24,20},{28,24},{32,28},{36,32}... | collective-permute-start | bytes 786440 | tf_op jit(solution)/shard_map/ppermute | solution.py:31
  182.5 4.1 %collective-permute-start.14 = (bf16[4,128,128]{1,2,0:T(8,128)(2,1)}, bf16[4,128,128]{1,2,0:T(8,128)(2,1)}, u32[]{:S(2)}, u32[]{:S(2)}) collective-permute-start(bf16[4,128,128]{1,2,0:T(8,128)(2,1)} %fusion.29), channel_id=1, source_target_pairs={{128,0},{132,4},{136,8},{140,12},{144,16},{148,20},{152,24},{156,2... | collective-permute-start | bytes 393224 | tf_op jit(solution)/shard_map/ppermute | solution.py:22
  185.5 21.2 %copy-start.13 = (f32[4,128,128]{2,1,0:T(8,128)S(1)}, f32[4,128,128]{2,1,0:T(8,128)}, u32[]{:S(2)}) copy-start(f32[4,128,128]{2,1,0:T(8,128)} %fusion.90) | copy-start | bytes 786436
  185.5 21.2 %copy-start.15 = (bf16[128,512]{1,0:T(8,128)(2,1)S(1)}, bf16[128,512]{1,0:T(8,128)(2,1)}, u32[]{:S(2)}) copy-start(bf16[128,512]{1,0:T(8,128)(2,1)} %param.11) | copy-start | bytes 393220
  187.6 19.4 %copy-start.9 = (bf16[128,512]{1,0:T(8,128)(2,1)S(1)}, bf16[128,512]{1,0:T(8,128)(2,1)}, u32[]{:S(2)}) copy-start(bf16[128,512]{1,0:T(8,128)(2,1)} %param.12) | copy-start | bytes 393220
  187.6 18.1 %collective-permute-start.15 = (bf16[4,128,128]{1,2,0:T(8,128)(2,1)S(1)}, bf16[4,128,128]{1,2,0:T(8,128)(2,1)S(1)}, u32[]{:S(2)}, u32[]{:S(2)}) collective-permute-start(bf16[4,128,128]{1,2,0:T(8,128)(2,1)S(1)} %fusion.52), channel_id=1, source_target_pairs={{256,0},{260,4},{264,8},{268,12},{272,16},{276,20},{280,24},{284,2... | collective-permute-start | bytes 393224 | tf_op jit(solution)/shard_map/ppermute | solution.py:22
  198.9 9.1 %copy-start.6 = (bf16[128,512]{1,0:T(8,128)(2,1)S(1)}, bf16[128,512]{1,0:T(8,128)(2,1)}, u32[]{:S(2)}) copy-start(bf16[128,512]{1,0:T(8,128)(2,1)} %param.10) | copy-start | bytes 393220
  198.9 11.0 %collective-permute-start.23 = (bf16[128,1024]{1,0:T(8,128)(2,1)}, bf16[128,1024]{1,0:T(8,128)(2,1)}, u32[]{:S(2)}, u32[]{:S(2)}) collective-permute-start(bf16[128,1024]{1,0:T(8,128)(2,1)} %add_convert_fusion), channel_id=1, source_target_pairs={{4,0},{8,4},{12,8},{16,12},{20,16},{24,20},{28,24},{32,28},{36,32}... | collective-permute-start | bytes 786440 | tf_op jit(solution)/shard_map/ppermute | solution.py:31
  (10 other events, 38.4 us)

commit v7 on v6

--- a/solution.py
+++ b/solution.py
@@ -1,3 +1,5 @@
+import math
+
 import jax
 import jax.numpy as jnp
 from jax import lax
@@ -10,18 +12,30 @@
 SPAN = 4
 
 
+PLAN = (4, 2, 2, 2, 4)
+
+
 def carried_in(shard, axis, join, neutral, backward):
     count = lax.axis_size(axis)
+    plan = PLAN
+    if math.prod(plan) != count:
+        plan = (2,) * max(1, (count - 1).bit_length())
     total = shard.astype(jnp.float32)
-    distance = 1
-    while distance < count:
-        if backward:
-            pairs = [(i, i - distance) for i in range(distance, count)]
-        else:
-            pairs = [(i, i + distance) for i in range(count - distance)]
-        sent = lax.ppermute(total.astype(jnp.bfloat16), axis, pairs)
-        total = join(total, sent.astype(jnp.float32))
-        distance *= 2
+    stride = 1
+    for radix in plan:
+        arrived = []
+        for step in range(1, radix):
+            distance = step * stride
+            if distance >= count:
+                break
+            if backward:
+                pairs = [(i, i - distance) for i in range(distance, count)]
+            else:
+                pairs = [(i, i + distance) for i in range(count - distance)]
+            arrived.append(lax.ppermute(total.astype(jnp.bfloat16), axis, pairs))
+        for part in arrived:
+            total = join(total, part.astype(jnp.float32))
+        stride *= radix
     return (total - shard.astype(jnp.float32)).astype(shard.dtype)
 
 

time: 214 us -> 208 us (0.972)
  starting transfers between devices: 101 us -> 96.5 us
  matrix products: 11.5 us -> 9.22 us
    ppermute x14 -> x18, starting transfers between devices: 68.3 us -> 62.9 us  [carried_in(): arrived.append(lax.ppermute(total.astype(jnp.bfloat16), axis, pairs))]
    ppermute x8, waiting for transfers between devices: 2.68 us -> 7.05 us  [from_behind(): return lax.ppermute(shard, axis, pairs)]
    ppermute x14 -> x18, waiting for transfers between devices: 63.4 us -> 59.1 us  [carried_in(): arrived.append(lax.ppermute(total.astype(jnp.bfloat16), axis, pairs))]
    unnamed x76 -> x86, local copies, waits for them, and re-layouts: 4.95 us -> 3.95 us
  transfers between devices with their start and end apart: 24 -> 28, of which waited for: 14 -> 13; matrix products, arithmetic and copies ran while one was open for 19% -> 17% of each run, Pallas kernels for 0% -> 0%
where the time goes in v7:
time: 208 us; the launch traced here: 206 us
  starting transfers between devices  96.5 us (46%)
  waiting for transfers between devices  66.2 us (32%)
  other arithmetic  18.3 us (9%)
  local copies, waits for them, and re-layouts  13.7 us (7%)
  matrix products  9.22 us (4%)
    ppermute x18, starting transfers between devices, carried_in(): arrived.append(lax.ppermute(total.astype(jnp.bfloat16), axis, pairs))  62.9 us
    ppermute x18, waiting for transfers between devices, carried_in(): arrived.append(lax.ppermute(total.astype(jnp.bfloat16), axis, pairs))  59.1 us
    ppermute x8, starting transfers between devices, from_behind(): return lax.ppermute(shard, axis, pairs)  25.5 us
    ppermute x2, starting transfers between devices, per_device(): lax.ppermute(sums, 'head', [(i, i ^ step) for i in range(heads_dev)])  8.04 us
    ppermute x8, waiting for transfers between devices, from_behind(): return lax.ppermute(shard, axis, pairs)  7.05 us
    convert_element_type x4, other arithmetic, per_device(): owed = from_behind(owed.astype(jnp.bfloat16), 'ctx', -1).astype(jnp.float32)  4.73 us
  transfers between devices with their start and end apart: 28, of which 13 were waited for; matrix products, arithmetic and copies ran while one was open for 17% of the time, Pallas kernels for 0%

profile of v7, /device:TPU:24, one launch (start us, length us, event | category | flops | bytes accessed | tf_op | source)
XLA Modules:
  0.0 205.7 jit_solution(14091455119280294869)
XLA Ops:
  2.9 3.3 %collective-permute-start.2 = (bf16[4,128,128]{2,1,0:T(8,128)(2,1)S(1)}, bf16[4,128,128]{2,1,0:T(8,128)(2,1)S(1)}, u32[]{:S(2)}, u32[]{:S(2)}) collective-permute-start(bf16[4,128,128]{2,1,0:T(8,128)(2,1)S(1)} %get-tuple-element.44), channel_id=1, source_target_pairs={{0,12},{4,16},{8,20},{12,24},{16,28},{20,32},{24,36},{28,40},{32,4... | collective-permute-start | bytes 393224 | tf_op jit(solution)/shard_map/ppermute | solution.py:35
  6.2 3.8 %collective-permute-start.1 = (bf16[4,128,128]{2,1,0:T(8,128)(2,1)S(1)}, bf16[4,128,128]{2,1,0:T(8,128)(2,1)S(1)}, u32[]{:S(2)}, u32[]{:S(2)}) collective-permute-start(bf16[4,128,128]{2,1,0:T(8,128)(2,1)S(1)} %get-tuple-element.44), channel_id=1, source_target_pairs={{0,8},{4,12},{8,16},{12,20},{16,24},{20,28},{24,32},{28,36},{32,40... | collective-permute-start | bytes 393224 | tf_op jit(solution)/shard_map/ppermute | solution.py:35
  10.0 3.7 %collective-permute-start = (bf16[4,128,128]{2,1,0:T(8,128)(2,1)S(1)}, bf16[4,128,128]{2,1,0:T(8,128)(2,1)S(1)}, u32[]{:S(2)}, u32[]{:S(2)}) collective-permute-start(bf16[4,128,128]{2,1,0:T(8,128)(2,1)S(1)} %get-tuple-element.44), channel_id=1, source_target_pairs={{0,4},{4,8},{8,12},{12,16},{16,20},{20,24},{24,28},{28,32},{32,36}... | collective-permute-start | bytes 393224 | tf_op jit(solution)/shard_map/ppermute | solution.py:35
  14.7 2.2 %collective-permute-start.20 = (bf16[128,1024]{1,0:T(8,128)(2,1)S(1)}, bf16[128,1024]{1,0:T(8,128)(2,1)S(1)}, u32[]{:S(2)}, u32[]{:S(2)}) collective-permute-start(bf16[128,1024]{1,0:T(8,128)(2,1)S(1)} %pad_maximum_fusion), channel_id=1, source_target_pairs={{0,4},{4,8},{8,12},{12,16},{16,20},{20,24},{24,28},{28,32},{32,36}... | collective-permute-start | bytes 786440 | tf_op jit(solution)/shard_map/ppermute | solution.py:45
  17.6 5.1 %collective-permute-done.1 = bf16[4,128,128]{2,1,0:T(8,128)(2,1)S(1)} collective-permute-done((bf16[4,128,128]{2,1,0:T(8,128)(2,1)S(1)}, bf16[4,128,128]{2,1,0:T(8,128)(2,1)S(1)}, u32[]{:S(2)}, u32[]{:S(2)}) %collective-permute-start.1) | collective-permute-done | bytes 131104 | tf_op jit(solution)/shard_map/ppermute | solution.py:35
  23.7 1.9 collective-permute-start.3
  25.6 8.6 %collective-permute-done.3 = bf16[4,128,128]{2,1,0:T(8,128)(2,1)S(1)} collective-permute-done((bf16[4,128,128]{2,1,0:T(8,128)(2,1)S(1)}, bf16[4,128,128]{2,1,0:T(8,128)(2,1)S(1)}, u32[]{:S(2)}, u32[]{:S(2)}) %collective-permute-start.3) | collective-permute-done | bytes 131104 | tf_op jit(solution)/shard_map/ppermute | solution.py:35
  34.3 4.6 %collective-permute-start.4 = (bf16[4,128,128]{2,1,0:T(8,128)(2,1)S(1)}, bf16[4,128,128]{2,1,0:T(8,128)(2,1)S(1)}, u32[]{:S(2)}, u32[]{:S(2)}) collective-permute-start(bf16[4,128,128]{2,1,0:T(8,128)(2,1)S(1)} %fusion.24), channel_id=1, source_target_pairs={{0,32},{4,36},{8,40},{12,44},{16,48},{20,52},{24,56},{28,60},{32,6... | collective-permute-start | bytes 393224 | tf_op jit(solution)/shard_map/ppermute | solution.py:35
  39.8 11.4 %collective-permute-done.4 = bf16[4,128,128]{2,1,0:T(8,128)(2,1)S(1)} collective-permute-done((bf16[4,128,128]{2,1,0:T(8,128)(2,1)S(1)}, bf16[4,128,128]{2,1,0:T(8,128)(2,1)S(1)}, u32[]{:S(2)}, u32[]{:S(2)}) %collective-permute-start.4) | collective-permute-done | bytes 131104 | tf_op jit(solution)/shard_map/ppermute | solution.py:35
  51.3 4.1 %collective-permute-start.5 = (bf16[4,128,128]{2,1,0:T(8,128)(2,1)S(1)}, bf16[4,128,128]{2,1,0:T(8,128)(2,1)S(1)}, u32[]{:S(2)}, u32[]{:S(2)}) collective-permute-start(bf16[4,128,128]{2,1,0:T(8,128)(2,1)S(1)} %fusion.75), channel_id=1, source_target_pairs={{0,64},{4,68},{8,72},{12,76},{16,80},{20,84},{24,88},{28,92},{32,9... | collective-permute-start | bytes 393224 | tf_op jit(solution)/shard_map/ppermute | solution.py:35
  55.4 15.0 %collective-permute-done.5 = bf16[4,128,128]{2,1,0:T(8,128)(2,1)S(1)} collective-permute-done((bf16[4,128,128]{2,1,0:T(8,128)(2,1)S(1)}, bf16[4,128,128]{2,1,0:T(8,128)(2,1)S(1)}, u32[]{:S(2)}, u32[]{:S(2)}) %collective-permute-start.5) | collective-permute-done | bytes 131104 | tf_op jit(solution)/shard_map/ppermute | solution.py:35
  70.4 1.3 collective-permute-start.8
  71.7 1.3 collective-permute-start.7
  73.0 1.3 collective-permute-start.6
  74.5 6.4 %collective-permute-done.8 = bf16[4,128,128]{2,1,0:T(8,128)(2,1)S(1)} collective-permute-done((bf16[4,128,128]{2,1,0:T(8,128)(2,1)S(1)}, bf16[4,128,128]{2,1,0:T(8,128)(2,1)S(1)}, u32[]{:S(2)}, u32[]{:S(2)}) %collective-permute-start.8) | collective-permute-done | bytes 131104 | tf_op jit(solution)/shard_map/ppermute | solution.py:35
  81.0 1.7 collective-permute-done.6
  83.1 3.4 %collective-permute-start.9 = (f32[2,128]{1,0:T(2,128)S(1)}, f32[2,128]{1,0:T(2,128)S(1)}, u32[]{:S(2)}, u32[]{:S(2)}) collective-permute-start(f32[2,128]{1,0:T(2,128)S(1)} %pad_maximum_fusion.2), channel_id=1, source_target_pairs={{0,1},{1,0},{2,3},{3,2},{4,5},{5,4},{6,7},{7,6},{8,9},{9,8},{10,11... | collective-permute-start | bytes 3080 | tf_op jit(solution)/shard_map/ppermute | solution.py:151
  87.1 1.9 collective-permute-start.21
  89.0 4.6 %collective-permute-start.10 = (f32[2,128]{1,0:T(2,128)S(1)}, f32[2,128]{1,0:T(2,128)S(1)}, u32[]{:S(2)}, u32[]{:S(2)}) collective-permute-start(f32[2,128]{1,0:T(2,128)S(1)} %fusion.74), channel_id=1, source_target_pairs={{0,2},{1,3},{2,0},{3,1},{4,6},{5,7},{6,4},{7,5},{8,10},{9,11},{10,... | collective-permute-start | bytes 3080 | tf_op jit(solution)/shard_map/ppermute | solution.py:151
  94.4 2.4 %collective-permute-done.21 = bf16[128,1024]{1,0:T(8,128)(2,1)S(1)} collective-permute-done((bf16[128,1024]{1,0:T(8,128)(2,1)S(1)}, bf16[128,1024]{1,0:T(8,128)(2,1)S(1)}, u32[]{:S(2)}, u32[]{:S(2)}) %collective-permute-start.21) | collective-permute-done | bytes 262176 | tf_op jit(solution)/shard_map/ppermute | solution.py:45
  96.9 1.9 collective-permute-start.22
  99.4 1.9 collective-permute-start.13
  101.4 3.5 %collective-permute-start.12 = (bf16[4,128,128]{1,2,0:T(8,128)(2,1)S(1)}, bf16[4,128,128]{1,2,0:T(8,128)(2,1)S(1)}, u32[]{:S(2)}, u32[]{:S(2)}) collective-permute-start(bf16[4,128,128]{1,2,0:T(8,128)(2,1)S(1)} %get-tuple-element.47), channel_id=1, source_target_pairs={{8,0},{12,4},{16,8},{20,12},{24,16},{28,20},{32,24},{36,28},{40,32... | collective-permute-start | bytes 393224 | tf_op jit(solution)/shard_map/ppermute | solution.py:35
  104.8 4.2 %collective-permute-start.11 = (bf16[4,128,128]{1,2,0:T(8,128)(2,1)S(1)}, bf16[4,128,128]{1,2,0:T(8,128)(2,1)S(1)}, u32[]{:S(2)}, u32[]{:S(2)}) collective-permute-start(bf16[4,128,128]{1,2,0:T(8,128)(2,1)S(1)} %get-tuple-element.47), channel_id=1, source_target_pairs={{4,0},{8,4},{12,8},{16,12},{20,16},{24,20},{28,24},{32,28},{36,32}... | collective-permute-start | bytes 393224 | tf_op jit(solution)/shard_map/ppermute | solution.py:35
  109.3 2.0 collective-permute-start.23
  111.8 3.7 %collective-permute-start.14 = (bf16[4,128,128]{1,2,0:T(8,128)(2,1)S(1)}, bf16[4,128,128]{1,2,0:T(8,128)(2,1)S(1)}, u32[]{:S(2)}, u32[]{:S(2)}) collective-permute-start(bf16[4,128,128]{1,2,0:T(8,128)(2,1)S(1)} %get-tuple-element.20), channel_id=1, source_target_pairs={{16,0},{20,4},{24,8},{28,12},{32,16},{36,20},{40,24},{44,28},{48,3... | collective-permute-start | bytes 393224 | tf_op jit(solution)/shard_map/ppermute | solution.py:35
  116.4 6.3 %collective-permute-done.14 = bf16[4,128,128]{1,2,0:T(8,128)(2,1)S(1)} collective-permute-done((bf16[4,128,128]{1,2,0:T(8,128)(2,1)S(1)}, bf16[4,128,128]{1,2,0:T(8,128)(2,1)S(1)}, u32[]{:S(2)}, u32[]{:S(2)}) %collective-permute-start.14) | collective-permute-done | bytes 131104 | tf_op jit(solution)/shard_map/ppermute | solution.py:35
  123.5 6.4 %collective-permute-start.15 = (bf16[4,128,128]{1,2,0:T(8,128)(2,1)}, bf16[4,128,128]{1,2,0:T(8,128)(2,1)}, u32[]{:S(2)}, u32[]{:S(2)}) collective-permute-start(bf16[4,128,128]{1,2,0:T(8,128)(2,1)} %fusion.26), channel_id=1, source_target_pairs={{32,0},{36,4},{40,8},{44,12},{48,16},{52,20},{56,24},{60,28},{64,3... | collective-permute-start | bytes 393224 | tf_op jit(solution)/shard_map/ppermute | solution.py:35
  131.8 1.2 gather_fusion.1
  133.4 1.5 fusion.83
  135.0 1.6 convolution_bitcast_fusion
  140.0 1.4 reshape.446
  141.6 1.2 scatter_fusion.1
  143.8 2.3 %scatter_fusion = f32[5,128,512]{2,1,0:T(8,128)S(1)} fusion(f32[5,128,512]{2,1,0:T(8,128)S(1)} %broadcast.216.clone.1, s32[4]{0:T(128)S(1)} %copy-done.36, f32[4,128,512]{2,1,0:T(8,128)} %reshape.446), kind=kCustom, calls=%fused_computation.2 | custom fusion | flops 262144 | bytes 3145744 | tf_op jit(solution)/shard_map/scatter-add | solution.py:107
  147.8 4.5 %collective-permute-start.24 = (bf16[128,1024]{1,0:T(8,128)(2,1)}, bf16[128,1024]{1,0:T(8,128)(2,1)}, u32[]{:S(2)}, u32[]{:S(2)}) collective-permute-start(bf16[128,1024]{1,0:T(8,128)(2,1)} %pad_maximum_fusion.1), channel_id=1, source_target_pairs={{4,0},{8,4},{12,8},{16,12},{20,16},{24,20},{28,24},{32,28},{36,32}... | collective-permute-start | bytes 786440 | tf_op jit(solution)/shard_map/ppermute | solution.py:45
  153.9 1.7 fusion.76
  155.6 12.0 %collective-permute-start.16 = (bf16[4,128,128]{1,2,0:T(8,128)(2,1)}, bf16[4,128,128]{1,2,0:T(8,128)(2,1)}, u32[]{:S(2)}, u32[]{:S(2)}) collective-permute-start(bf16[4,128,128]{1,2,0:T(8,128)(2,1)} %fusion.76), channel_id=1, source_target_pairs={{64,0},{68,4},{72,8},{76,12},{80,16},{84,20},{88,24},{92,28},{96,3... | collective-permute-start | bytes 393224 | tf_op jit(solution)/shard_map/ppermute | solution.py:35
  167.6 1.8 add_convert_fusion.2
  169.4 2.3 %collective-permute-start.25 = (bf16[128,1024]{1,0:T(8,128)(2,1)}, bf16[128,1024]{1,0:T(8,128)(2,1)}, u32[]{:S(2)}, u32[]{:S(2)}) collective-permute-start(bf16[128,1024]{1,0:T(8,128)(2,1)} %add_convert_fusion.2), channel_id=1, source_target_pairs={{4,0},{8,4},{12,8},{16,12},{20,16},{24,20},{28,24},{32,28},{36,32}... | collective-permute-start | bytes 786440 | tf_op jit(solution)/shard_map/ppermute | solution.py:45
  172.8 3.2 %collective-permute-done.16 = bf16[4,128,128]{1,2,0:T(8,128)(2,1)} collective-permute-done((bf16[4,128,128]{1,2,0:T(8,128)(2,1)}, bf16[4,128,128]{1,2,0:T(8,128)(2,1)}, u32[]{:S(2)}, u32[]{:S(2)}) %collective-permute-start.16) | collective-permute-done | bytes 131104 | tf_op jit(solution)/shard_map/ppermute | solution.py:35
  177.1 1.4 collective-permute-start.19
  178.6 3.3 %collective-permute-start.18 = (bf16[4,128,128]{1,2,0:T(8,128)(2,1)S(1)}, bf16[4,128,128]{1,2,0:T(8,128)(2,1)S(1)}, u32[]{:S(2)}, u32[]{:S(2)}) collective-permute-start(bf16[4,128,128]{1,2,0:T(8,128)(2,1)S(1)} %fusion.27), channel_id=1, source_target_pairs={{256,0},{260,4},{264,8},{268,12},{272,16},{276,20},{280,24},{284,2... | collective-permute-start | bytes 393224 | tf_op jit(solution)/shard_map/ppermute | solution.py:35
  181.9 1.3 collective-permute-start.17
  183.2 1.2 add_convert_fusion.1
  184.4 4.8 %collective-permute-start.26 = (bf16[128,1024]{1,0:T(8,128)(2,1)S(1)}, bf16[128,1024]{1,0:T(8,128)(2,1)S(1)}, u32[]{:S(2)}, u32[]{:S(2)}) collective-permute-start(bf16[128,1024]{1,0:T(8,128)(2,1)S(1)} %add_convert_fusion.1), channel_id=1, source_target_pairs={{4,0},{8,4},{12,8},{16,12},{20,16},{24,20},{28,24},{32,28},{36,32}... | collective-permute-start | bytes 786440 | tf_op jit(solution)/shard_map/ppermute | solution.py:45
  190.6 2.5 %collective-permute-done.26 = bf16[128,1024]{1,0:T(8,128)(2,1)S(1)} collective-permute-done((bf16[128,1024]{1,0:T(8,128)(2,1)S(1)}, bf16[128,1024]{1,0:T(8,128)(2,1)S(1)}, u32[]{:S(2)}, u32[]{:S(2)}) %collective-permute-start.26) | collective-permute-done | bytes 262176 | tf_op jit(solution)/shard_map/ppermute | solution.py:45
  193.8 5.9 %collective-permute-start.27 = (bf16[128,1024]{1,0:T(8,128)(2,1)}, bf16[128,1024]{1,0:T(8,128)(2,1)}, u32[]{:S(2)}, u32[]{:S(2)}) collective-permute-start(bf16[128,1024]{1,0:T(8,128)(2,1)} %add_convert_fusion), channel_id=1, source_target_pairs={{4,0},{8,4},{12,8},{16,12},{20,16},{24,20},{28,24},{32,28},{36,32}... | collective-permute-start | bytes 786440 | tf_op jit(solution)/shard_map/ppermute | solution.py:45
  201.8 2.1 %collective-permute-done.27 = bf16[128,1024]{1,0:T(8,128)(2,1)} collective-permute-done((bf16[128,1024]{1,0:T(8,128)(2,1)}, bf16[128,1024]{1,0:T(8,128)(2,1)}, u32[]{:S(2)}, u32[]{:S(2)}) %collective-permute-start.27) | collective-permute-done | bytes 262176 | tf_op jit(solution)/shard_map/ppermute | solution.py:45
  (169 shorter events, 28.6 us)
Async XLA Ops:
  0.6 132.8 %copy-start = (bf16[128,512]{1,0:T(8,128)(2,1)S(1)}, bf16[128,512]{1,0:T(8,128)(2,1)}, u32[]{:S(2)}) copy-start(bf16[128,512]{1,0:T(8,128)(2,1)} %param.15) | copy-start | bytes 393220
  0.6 16.3 %copy-start.14 = (bf16[128,512]{1,0:T(8,128)(2,1)S(1)}, bf16[128,512]{1,0:T(8,128)(2,1)}, u32[]{:S(2)}) copy-start(bf16[128,512]{1,0:T(8,128)(2,1)} %param.11) | copy-start | bytes 393220
  0.7 16.5 %copy-start.11 = (bf16[128,512]{1,0:T(8,128)(2,1)S(1)}, bf16[128,512]{1,0:T(8,128)(2,1)}, u32[]{:S(2)}) copy-start(bf16[128,512]{1,0:T(8,128)(2,1)} %param.12) | copy-start | bytes 393220
  0.7 16.2 %copy-start.37 = (s32[1,3]{1,0:T(1,128)S(1)}, s32[1,3]{1,0:T(1,128)}, u32[]{:S(2)}) copy-start(s32[1,3]{1,0:T(1,128)} %param.19) | copy-start | bytes 40
  0.7 16.2 %copy-start.9 = (bf16[128,512]{1,0:T(8,128)(2,1)S(1)}, bf16[128,512]{1,0:T(8,128)(2,1)}, u32[]{:S(2)}) copy-start(bf16[128,512]{1,0:T(8,128)(2,1)} %param.10) | copy-start | bytes 393220
  2.9 14.7 %collective-permute-start.2 = (bf16[4,128,128]{2,1,0:T(8,128)(2,1)S(1)}, bf16[4,128,128]{2,1,0:T(8,128)(2,1)S(1)}, u32[]{:S(2)}, u32[]{:S(2)}) collective-permute-start(bf16[4,128,128]{2,1,0:T(8,128)(2,1)S(1)} %get-tuple-element.44), channel_id=1, source_target_pairs={{0,12},{4,16},{8,20},{12,24},{16,28},{20,32},{24,36},{28,40},{32,4... | collective-permute-start | bytes 393224 | tf_op jit(solution)/shard_map/ppermute | solution.py:35
  6.2 16.5 %collective-permute-start.1 = (bf16[4,128,128]{2,1,0:T(8,128)(2,1)S(1)}, bf16[4,128,128]{2,1,0:T(8,128)(2,1)S(1)}, u32[]{:S(2)}, u32[]{:S(2)}) collective-permute-start(bf16[4,128,128]{2,1,0:T(8,128)(2,1)S(1)} %get-tuple-element.44), channel_id=1, source_target_pairs={{0,8},{4,12},{8,16},{12,20},{16,24},{20,28},{24,32},{28,36},{32,40... | collective-permute-start | bytes 393224 | tf_op jit(solution)/shard_map/ppermute | solution.py:35
  10.0 13.6 %collective-permute-start = (bf16[4,128,128]{2,1,0:T(8,128)(2,1)S(1)}, bf16[4,128,128]{2,1,0:T(8,128)(2,1)S(1)}, u32[]{:S(2)}, u32[]{:S(2)}) collective-permute-start(bf16[4,128,128]{2,1,0:T(8,128)(2,1)S(1)} %get-tuple-element.44), channel_id=1, source_target_pairs={{0,4},{4,8},{8,12},{12,16},{16,20},{20,24},{24,28},{28,32},{32,36}... | collective-permute-start | bytes 393224 | tf_op jit(solution)/shard_map/ppermute | solution.py:35
  14.7 72.4 %collective-permute-start.20 = (bf16[128,1024]{1,0:T(8,128)(2,1)S(1)}, bf16[128,1024]{1,0:T(8,128)(2,1)S(1)}, u32[]{:S(2)}, u32[]{:S(2)}) collective-permute-start(bf16[128,1024]{1,0:T(8,128)(2,1)S(1)} %pad_maximum_fusion), channel_id=1, source_target_pairs={{0,4},{4,8},{8,12},{12,16},{16,20},{20,24},{24,28},{28,32},{32,36}... | collective-permute-start | bytes 786440 | tf_op jit(solution)/shard_map/ppermute | solution.py:45
  17.2 34.1 %copy-start.21 = (bf16[4,128,128]{2,1,0:T(8,128)(2,1)}, bf16[4,128,128]{2,1,0:T(8,128)(2,1)S(1)}, u32[]{:S(2)}) copy-start(bf16[4,128,128]{2,1,0:T(8,128)(2,1)S(1)} %fusion.15) | copy-start | bytes 393220
  23.6 50.7 %copy-start.30 = (bf16[128,512]{1,0:T(8,128)(2,1)S(1)}, bf16[128,512]{1,0:T(8,128)(2,1)}, u32[]{:S(2)}) copy-start(bf16[128,512]{1,0:T(8,128)(2,1)} %param.14) | copy-start | bytes 393220
  23.7 10.6 %collective-permute-start.3 = (bf16[4,128,128]{2,1,0:T(8,128)(2,1)S(1)}, bf16[4,128,128]{2,1,0:T(8,128)(2,1)S(1)}, u32[]{:S(2)}, u32[]{:S(2)}) collective-permute-start(bf16[4,128,128]{2,1,0:T(8,128)(2,1)S(1)} %get-tuple-element.24), channel_id=1, source_target_pairs={{0,16},{4,20},{8,24},{12,28},{16,32},{20,36},{24,40},{28,44},{32,4... | collective-permute-start | bytes 393224 | tf_op jit(solution)/shard_map/ppermute | solution.py:35
  34.3 17.0 %collective-permute-start.4 = (bf16[4,128,128]{2,1,0:T(8,128)(2,1)S(1)}, bf16[4,128,128]{2,1,0:T(8,128)(2,1)S(1)}, u32[]{:S(2)}, u32[]{:S(2)}) collective-permute-start(bf16[4,128,128]{2,1,0:T(8,128)(2,1)S(1)} %fusion.24), channel_id=1, source_target_pairs={{0,32},{4,36},{8,40},{12,44},{16,48},{20,52},{24,56},{28,60},{32,6... | collective-permute-start | bytes 393224 | tf_op jit(solution)/shard_map/ppermute | solution.py:35
  51.3 19.1 %collective-permute-start.5 = (bf16[4,128,128]{2,1,0:T(8,128)(2,1)S(1)}, bf16[4,128,128]{2,1,0:T(8,128)(2,1)S(1)}, u32[]{:S(2)}, u32[]{:S(2)}) collective-permute-start(bf16[4,128,128]{2,1,0:T(8,128)(2,1)S(1)} %fusion.75), channel_id=1, source_target_pairs={{0,64},{4,68},{8,72},{12,76},{16,80},{20,84},{24,88},{28,92},{32,9... | collective-permute-start | bytes 393224 | tf_op jit(solution)/shard_map/ppermute | solution.py:35
  55.4 27.4 %copy-start.34 = (f32[512]{0:T(512)S(1)}, f32[512]{0:T(512)}, u32[]{:S(2)}) copy-start(f32[512]{0:T(512)} %param.13) | copy-start | bytes 6148
  70.4 10.5 %collective-permute-start.8 = (bf16[4,128,128]{2,1,0:T(8,128)(2,1)S(1)}, bf16[4,128,128]{2,1,0:T(8,128)(2,1)S(1)}, u32[]{:S(2)}, u32[]{:S(2)}) collective-permute-start(bf16[4,128,128]{2,1,0:T(8,128)(2,1)S(1)} %fusion.25), channel_id=1, source_target_pairs={{0,384},{4,388},{8,392},{12,396},{16,400},{20,404},{24,408},{28,41... | collective-permute-start | bytes 393224 | tf_op jit(solution)/shard_map/ppermute | solution.py:35
  71.7 9.2 %collective-permute-start.7 = (bf16[4,128,128]{2,1,0:T(8,128)(2,1)S(1)}, bf16[4,128,128]{2,1,0:T(8,128)(2,1)S(1)}, u32[]{:S(2)}, u32[]{:S(2)}) collective-permute-start(bf16[4,128,128]{2,1,0:T(8,128)(2,1)S(1)} %fusion.25), channel_id=1, source_target_pairs={{0,256},{4,260},{8,264},{12,268},{16,272},{20,276},{24,280},{28,28... | collective-permute-start | bytes 393224 | tf_op jit(solution)/shard_map/ppermute | solution.py:35
  73.0 9.6 %collective-permute-start.6 = (bf16[4,128,128]{2,1,0:T(8,128)(2,1)S(1)}, bf16[4,128,128]{2,1,0:T(8,128)(2,1)S(1)}, u32[]{:S(2)}, u32[]{:S(2)}) collective-permute-start(bf16[4,128,128]{2,1,0:T(8,128)(2,1)S(1)} %fusion.25), channel_id=1, source_target_pairs={{0,128},{4,132},{8,136},{12,140},{16,144},{20,148},{24,152},{28,15... | collective-permute-start | bytes 393224 | tf_op jit(solution)/shard_map/ppermute | solution.py:35
  74.5 19.9 %copy-start.31 = (bf16[128,512]{1,0:T(8,128)(2,1)S(1)}, bf16[128,512]{1,0:T(8,128)(2,1)}, u32[]{:S(2)}) copy-start(bf16[128,512]{1,0:T(8,128)(2,1)} %param.18) | copy-start | bytes 393220
  74.5 24.3 %copy-start.35 = (f32[512]{0:T(512)S(1)}, f32[512]{0:T(512)}, u32[]{:S(2)}) copy-start(f32[512]{0:T(512)} %param.13) | copy-start | bytes 6148
  83.1 5.9 %collective-permute-start.9 = (f32[2,128]{1,0:T(2,128)S(1)}, f32[2,128]{1,0:T(2,128)S(1)}, u32[]{:S(2)}, u32[]{:S(2)}) collective-permute-start(f32[2,128]{1,0:T(2,128)S(1)} %pad_maximum_fusion.2), channel_id=1, source_target_pairs={{0,1},{1,0},{2,3},{3,2},{4,5},{5,4},{6,7},{7,6},{8,9},{9,8},{10,11... | collective-permute-start | bytes 3080 | tf_op jit(solution)/shard_map/ppermute | solution.py:151
  87.1 22.2 %copy-start.26 = (bf16[128,1024]{1,0:T(8,128)(2,1)}, bf16[128,1024]{1,0:T(8,128)(2,1)S(1)}, u32[]{:S(2)}) copy-start(bf16[128,1024]{1,0:T(8,128)(2,1)S(1)} %collective-permute-done.20) | copy-start | bytes 786436
  87.1 9.8 %collective-permute-start.21 = (bf16[128,1024]{1,0:T(8,128)(2,1)S(1)}, bf16[128,1024]{1,0:T(8,128)(2,1)S(1)}, u32[]{:S(2)}, u32[]{:S(2)}) collective-permute-start(bf16[128,1024]{1,0:T(8,128)(2,1)S(1)} %collective-permute-done.20), channel_id=1, source_target_pairs={{0,4},{4,8},{8,12},{12,16},{16,20},{20,24},{24,28},{28,32},{32,36}... | collective-permute-start | bytes 786440 | tf_op jit(solution)/shard_map/ppermute | solution.py:45
  89.0 9.8 %collective-permute-start.10 = (f32[2,128]{1,0:T(2,128)S(1)}, f32[2,128]{1,0:T(2,128)S(1)}, u32[]{:S(2)}, u32[]{:S(2)}) collective-permute-start(f32[2,128]{1,0:T(2,128)S(1)} %fusion.74), channel_id=1, source_target_pairs={{0,2},{1,3},{2,0},{3,1},{4,6},{5,7},{6,4},{7,5},{8,10},{9,11},{10,... | collective-permute-start | bytes 3080 | tf_op jit(solution)/shard_map/ppermute | solution.py:151
  96.9 14.9 %copy-start.28 = (bf16[128,1024]{1,0:T(8,128)(2,1)}, bf16[128,1024]{1,0:T(8,128)(2,1)S(1)}, u32[]{:S(2)}) copy-start(bf16[128,1024]{1,0:T(8,128)(2,1)S(1)} %collective-permute-done.21) | copy-start | bytes 786436
  96.9 12.4 %collective-permute-start.22 = (bf16[128,1024]{1,0:T(8,128)(2,1)S(1)}, bf16[128,1024]{1,0:T(8,128)(2,1)S(1)}, u32[]{:S(2)}, u32[]{:S(2)}) collective-permute-start(bf16[128,1024]{1,0:T(8,128)(2,1)S(1)} %collective-permute-done.21), channel_id=1, source_target_pairs={{0,4},{4,8},{8,12},{12,16},{16,20},{20,24},{24,28},{28,32},{32,36}... | collective-permute-start | bytes 786440 | tf_op jit(solution)/shard_map/ppermute | solution.py:45
  99.0 16.6 %copy-start.5 = (bf16[128,4,128]{0,2,1:T(8,128)(2,1)}, bf16[128,4,128]{0,2,1:T(8,128)(2,1)S(1)}, u32[]{:S(2)}) copy-start(bf16[128,4,128]{0,2,1:T(8,128)(2,1)S(1)} %subtract_convert_fusion.1) | copy-start | bytes 393220
  99.4 11.9 %collective-permute-start.13 = (bf16[4,128,128]{1,2,0:T(8,128)(2,1)S(1)}, bf16[4,128,128]{1,2,0:T(8,128)(2,1)S(1)}, u32[]{:S(2)}, u32[]{:S(2)}) collective-permute-start(bf16[4,128,128]{1,2,0:T(8,128)(2,1)S(1)} %get-tuple-element.47), channel_id=1, source_target_pairs={{12,0},{16,4},{20,8},{24,12},{28,16},{32,20},{36,24},{40,28},{44,3... | collective-permute-start | bytes 393224 | tf_op jit(solution)/shard_map/ppermute | solution.py:35
  101.4 10.4 %collective-permute-start.12 = (bf16[4,128,128]{1,2,0:T(8,128)(2,1)S(1)}, bf16[4,128,128]{1,2,0:T(8,128)(2,1)S(1)}, u32[]{:S(2)}, u32[]{:S(2)}) collective-permute-start(bf16[4,128,128]{1,2,0:T(8,128)(2,1)S(1)} %get-tuple-element.47), channel_id=1, source_target_pairs={{8,0},{12,4},{16,8},{20,12},{24,16},{28,20},{32,24},{36,28},{40,32... | collective-permute-start | bytes 393224 | tf_op jit(solution)/shard_map/ppermute | solution.py:35
  104.8 6.9 %collective-permute-start.11 = (bf16[4,128,128]{1,2,0:T(8,128)(2,1)S(1)}, bf16[4,128,128]{1,2,0:T(8,128)(2,1)S(1)}, u32[]{:S(2)}, u32[]{:S(2)}) collective-permute-start(bf16[4,128,128]{1,2,0:T(8,128)(2,1)S(1)} %get-tuple-element.47), channel_id=1, source_target_pairs={{4,0},{8,4},{12,8},{16,12},{20,16},{24,20},{28,24},{32,28},{36,32}... | collective-permute-start | bytes 393224 | tf_op jit(solution)/shard_map/ppermute | solution.py:35
  109.3 20.5 %collective-permute-start.23 = (bf16[128,1024]{1,0:T(8,128)(2,1)S(1)}, bf16[128,1024]{1,0:T(8,128)(2,1)S(1)}, u32[]{:S(2)}, u32[]{:S(2)}) collective-permute-start(bf16[128,1024]{1,0:T(8,128)(2,1)S(1)} %collective-permute-done.22), channel_id=1, source_target_pairs={{0,4},{4,8},{8,12},{12,16},{16,20},{20,24},{24,28},{28,32},{32,36}... | collective-permute-start | bytes 786440 | tf_op jit(solution)/shard_map/ppermute | solution.py:45
  111.8 18.1 %copy-start.29 = (bf16[128,1024]{1,0:T(8,128)(2,1)S(1)}, bf16[128,1024]{1,0:T(8,128)(2,1)}, u32[]{:S(2)}) copy-start(bf16[128,1024]{1,0:T(8,128)(2,1)} %copy-done.28) | copy-start | bytes 786436
  111.8 18.1 %copy-start.27 = (bf16[128,1024]{1,0:T(8,128)(2,1)S(1)}, bf16[128,1024]{1,0:T(8,128)(2,1)}, u32[]{:S(2)}) copy-start(bf16[128,1024]{1,0:T(8,128)(2,1)} %copy-done.26) | copy-start | bytes 786436
  111.8 10.9 %collective-permute-start.14 = (bf16[4,128,128]{1,2,0:T(8,128)(2,1)S(1)}, bf16[4,128,128]{1,2,0:T(8,128)(2,1)S(1)}, u32[]{:S(2)}, u32[]{:S(2)}) collective-permute-start(bf16[4,128,128]{1,2,0:T(8,128)(2,1)S(1)} %get-tuple-element.20), channel_id=1, source_target_pairs={{16,0},{20,4},{24,8},{28,12},{32,16},{36,20},{40,24},{44,28},{48,3... | collective-permute-start | bytes 393224 | tf_op jit(solution)/shard_map/ppermute | solution.py:35
  123.5 30.5 %collective-permute-start.15 = (bf16[4,128,128]{1,2,0:T(8,128)(2,1)}, bf16[4,128,128]{1,2,0:T(8,128)(2,1)}, u32[]{:S(2)}, u32[]{:S(2)}) collective-permute-start(bf16[4,128,128]{1,2,0:T(8,128)(2,1)} %fusion.26), channel_id=1, source_target_pairs={{32,0},{36,4},{40,8},{44,12},{48,16},{52,20},{56,24},{60,28},{64,3... | collective-permute-start | bytes 393224 | tf_op jit(solution)/shard_map/ppermute | solution.py:35
  147.8 19.9 %collective-permute-start.24 = (bf16[128,1024]{1,0:T(8,128)(2,1)}, bf16[128,1024]{1,0:T(8,128)(2,1)}, u32[]{:S(2)}, u32[]{:S(2)}) collective-permute-start(bf16[128,1024]{1,0:T(8,128)(2,1)} %pad_maximum_fusion.1), channel_id=1, source_target_pairs={{4,0},{8,4},{12,8},{16,12},{20,16},{24,20},{28,24},{32,28},{36,32}... | collective-permute-start | bytes 786440 | tf_op jit(solution)/shard_map/ppermute | solution.py:45
  153.9 17.8 %copy-start.2 = (bf16[512,4,128]{0,2,1:T(8,128)(2,1)S(1)}, bf16[512,4,128]{0,2,1:T(8,128)(2,1)}, u32[]{:S(2)}) copy-start(bf16[512,4,128]{0,2,1:T(8,128)(2,1)} %copy-done.1) | copy-start | bytes 1572868
  153.9 17.9 %copy-start.4 = (bf16[4,128,512]{1,2,0:T(8,128)(2,1)S(1)}, bf16[4,128,512]{1,2,0:T(8,128)(2,1)}, u32[]{:S(2)}) copy-start(bf16[4,128,512]{1,2,0:T(8,128)(2,1)} %copy-done.3) | copy-start | bytes 1572868
  155.6 20.5 %collective-permute-start.16 = (bf16[4,128,128]{1,2,0:T(8,128)(2,1)}, bf16[4,128,128]{1,2,0:T(8,128)(2,1)}, u32[]{:S(2)}, u32[]{:S(2)}) collective-permute-start(bf16[4,128,128]{1,2,0:T(8,128)(2,1)} %fusion.76), channel_id=1, source_target_pairs={{64,0},{68,4},{72,8},{76,12},{80,16},{84,20},{88,24},{92,28},{96,3... | collective-permute-start | bytes 393224 | tf_op jit(solution)/shard_map/ppermute | solution.py:35
  169.4 13.7 %collective-permute-start.25 = (bf16[128,1024]{1,0:T(8,128)(2,1)}, bf16[128,1024]{1,0:T(8,128)(2,1)}, u32[]{:S(2)}, u32[]{:S(2)}) collective-permute-start(bf16[128,1024]{1,0:T(8,128)(2,1)} %add_convert_fusion.2), channel_id=1, source_target_pairs={{4,0},{8,4},{12,8},{16,12},{20,16},{24,20},{28,24},{32,28},{36,32}... | collective-permute-start | bytes 786440 | tf_op jit(solution)/shard_map/ppermute | solution.py:45
  177.1 13.2 %copy-start.13 = (f32[4,128,128]{2,1,0:T(8,128)S(1)}, f32[4,128,128]{2,1,0:T(8,128)}, u32[]{:S(2)}) copy-start(f32[4,128,128]{2,1,0:T(8,128)} %fusion.86) | copy-start | bytes 786436
  177.1 13.2 %copy-start.15 = (bf16[128,512]{1,0:T(8,128)(2,1)S(1)}, bf16[128,512]{1,0:T(8,128)(2,1)}, u32[]{:S(2)}) copy-start(bf16[128,512]{1,0:T(8,128)(2,1)} %param.11) | copy-start | bytes 393220
  177.1 12.1 %collective-permute-start.19 = (bf16[4,128,128]{1,2,0:T(8,128)(2,1)S(1)}, bf16[4,128,128]{1,2,0:T(8,128)(2,1)S(1)}, u32[]{:S(2)}, u32[]{:S(2)}) collective-permute-start(bf16[4,128,128]{1,2,0:T(8,128)(2,1)S(1)} %fusion.27), channel_id=1, source_target_pairs={{384,0},{388,4},{392,8},{396,12},{400,16},{404,20},{408,24},{412,2... | collective-permute-start | bytes 393224 | tf_op jit(solution)/shard_map/ppermute | solution.py:35
  178.6 10.7 %collective-permute-start.18 = (bf16[4,128,128]{1,2,0:T(8,128)(2,1)S(1)}, bf16[4,128,128]{1,2,0:T(8,128)(2,1)S(1)}, u32[]{:S(2)}, u32[]{:S(2)}) collective-permute-start(bf16[4,128,128]{1,2,0:T(8,128)(2,1)S(1)} %fusion.27), channel_id=1, source_target_pairs={{256,0},{260,4},{264,8},{268,12},{272,16},{276,20},{280,24},{284,2... | collective-permute-start | bytes 393224 | tf_op jit(solution)/shard_map/ppermute | solution.py:35
  181.9 7.4 %collective-permute-start.17 = (bf16[4,128,128]{1,2,0:T(8,128)(2,1)S(1)}, bf16[4,128,128]{1,2,0:T(8,128)(2,1)S(1)}, u32[]{:S(2)}, u32[]{:S(2)}) collective-permute-start(bf16[4,128,128]{1,2,0:T(8,128)(2,1)S(1)} %fusion.27), channel_id=1, source_target_pairs={{128,0},{132,4},{136,8},{140,12},{144,16},{148,20},{152,24},{156,2... | collective-permute-start | bytes 393224 | tf_op jit(solution)/shard_map/ppermute | solution.py:35
  184.4 15.4 %copy-start.12 = (bf16[128,512]{1,0:T(8,128)(2,1)S(1)}, bf16[128,512]{1,0:T(8,128)(2,1)}, u32[]{:S(2)}) copy-start(bf16[128,512]{1,0:T(8,128)(2,1)} %param.12) | copy-start | bytes 393220
  184.4 8.7 %collective-permute-start.26 = (bf16[128,1024]{1,0:T(8,128)(2,1)S(1)}, bf16[128,1024]{1,0:T(8,128)(2,1)S(1)}, u32[]{:S(2)}, u32[]{:S(2)}) collective-permute-start(bf16[128,1024]{1,0:T(8,128)(2,1)S(1)} %add_convert_fusion.1), channel_id=1, source_target_pairs={{4,0},{8,4},{12,8},{16,12},{20,16},{24,20},{28,24},{32,28},{36,32}... | collective-permute-start | bytes 786440 | tf_op jit(solution)/shard_map/ppermute | solution.py:45
  193.8 10.1 %collective-permute-start.27 = (bf16[128,1024]{1,0:T(8,128)(2,1)}, bf16[128,1024]{1,0:T(8,128)(2,1)}, u32[]{:S(2)}, u32[]{:S(2)}) collective-permute-start(bf16[128,1024]{1,0:T(8,128)(2,1)} %add_convert_fusion), channel_id=1, source_target_pairs={{4,0},{8,4},{12,8},{16,12},{20,16},{24,20},{28,24},{32,28},{36,32}... | collective-permute-start | bytes 786440 | tf_op jit(solution)/shard_map/ppermute | solution.py:45
  (19 other events, 110.8 us)

commit v8 on v7

--- a/solution.py
+++ b/solution.py
@@ -12,15 +12,17 @@
 SPAN = 4
 
 
-PLAN = (4, 2, 2, 2, 4)
-
-
-def carried_in(shard, axis, join, neutral, backward):
+CTX = ("outer", "inner")
+INNER = 8
+PLAN = (4, 4)
+
+
+def scan_over(total, axis, backward):
     count = lax.axis_size(axis)
     plan = PLAN
     if math.prod(plan) != count:
         plan = (2,) * max(1, (count - 1).bit_length())
-    total = shard.astype(jnp.float32)
+    own = total
     stride = 1
     for radix in plan:
         arrived = []
@@ -34,9 +36,24 @@
                 pairs = [(i, i + distance) for i in range(count - distance)]
             arrived.append(lax.ppermute(total.astype(jnp.bfloat16), axis, pairs))
         for part in arrived:
-            total = join(total, part.astype(jnp.float32))
+            total = total + part.astype(jnp.float32)
         stride *= radix
-    return (total - shard.astype(jnp.float32)).astype(shard.dtype)
+    return total - own
+
+
+def carried_in(shard, backward):
+    members = lax.axis_size("inner")
+    slices = shard.astype(jnp.bfloat16).reshape(members, -1)
+    mine = lax.all_to_all(slices, "inner", 0, 0, tiled=True).astype(jnp.float32)
+    if backward:
+        within = jnp.flip(jnp.cumsum(jnp.flip(mine, 0), axis=0), 0) - mine
+    else:
+        within = jnp.cumsum(mine, axis=0) - mine
+    group = jnp.sum(mine, axis=0)
+    earlier = scan_over(group, "outer", backward)
+    states = (within + earlier[None]).astype(jnp.bfloat16)
+    back = lax.all_to_all(states, "inner", 0, 0, tiled=True)
+    return back.reshape(shard.shape).astype(shard.dtype)
 
 
 def from_behind(shard, axis, by):
@@ -128,7 +145,7 @@
     key_lin = lin_key.reshape(token_count, heads_lin, HEAD)
     value_lin = lin_value.reshape(token_count, heads_lin, HEAD)
     key_value = jnp.einsum("thi,thj->hij", key_lin, value_lin, preferred_element_type=jnp.float32)
-    state_low = carried_in(key_value, "ctx", add_states, jnp.zeros_like(key_value), False)
+    state_low = carried_in(key_value, False)
     state_half = state_low.astype(jnp.bfloat16)
     causal = jnp.tril(jnp.ones((token_count, token_count), jnp.bool_))
     attn_lin = jnp.where(
@@ -159,7 +176,7 @@
     adjoint_local = jnp.einsum(
         "thi,thj->hij", query_lin, grad_out, preferred_element_type=jnp.float32
     )
-    adjoint_high = carried_in(adjoint_local, "ctx", add_states, jnp.zeros_like(adjoint_local), True)
+    adjoint_high = carried_in(adjoint_local, True)
     adjoint_half = adjoint_high.astype(jnp.bfloat16)
     grad_scores = jnp.where(
         causal[None],
@@ -183,7 +200,7 @@
     arrived = []
     moving = pair
     for distance in range(1, SPAN + 1):
-        moving = from_behind(moving, "ctx", 1)
+        moving = from_behind(moving, CTX, 1)
         arrived.append(moving)
     key_window = jnp.concatenate(
         [arrived[SPAN - 1 - place][:, :width] for place in range(SPAN)] + [sm_key], axis=0
@@ -191,7 +208,7 @@
     value_window = jnp.concatenate(
         [arrived[SPAN - 1 - place][:, width:] for place in range(SPAN)] + [sm_value], axis=0
     )
-    shard = lax.axis_index("ctx")
+    shard = lax.axis_index(CTX)
     sm_dq, key_acc, value_acc = tile_attention(
         sm_query, sm_grad, key_window, value_window, tile_lists, shard
     )
@@ -203,7 +220,7 @@
             [key_acc[SPAN - distance], value_acc[SPAN - distance]], axis=1
         ).astype(jnp.bfloat16).astype(jnp.float32)
         owed = term if owed is None else owed + term
-        owed = from_behind(owed.astype(jnp.bfloat16), "ctx", -1).astype(jnp.float32)
+        owed = from_behind(owed.astype(jnp.bfloat16), CTX, -1).astype(jnp.float32)
     key_total = key_total + owed[:, :width]
     value_total = value_total + owed[:, width:]
     return (
@@ -218,28 +235,33 @@
 
 def solution(mesh):
     placed = (
-        P("ctx", "head"),
-        P("ctx", "head"),
-        P("ctx", "head"),
+        P(CTX, "head"),
+        P(CTX, "head"),
+        P(CTX, "head"),
         P("head"),
-        P("ctx", "head"),
-        P("ctx", "head"),
-        P("ctx", "head"),
-        P("ctx", "head"),
-        P("ctx", "head"),
-        P("ctx", None),
+        P(CTX, "head"),
+        P(CTX, "head"),
+        P(CTX, "head"),
+        P(CTX, "head"),
+        P(CTX, "head"),
+        P(CTX, None),
+    )
+    count = mesh.shape["ctx"]
+    inner = INNER if count % INNER == 0 else 1
+    split = jax.sharding.Mesh(
+        mesh.devices.reshape(count // inner, inner, mesh.shape["head"]), CTX + ("head",)
     )
     return jax.shard_map(
         per_device,
-        mesh=mesh,
+        mesh=split,
         in_specs=placed,
         out_specs=(
-            P("ctx", "head"),
-            P("ctx", "head"),
-            P("ctx", "head"),
-            P("ctx", "head"),
-            P("ctx", "head"),
-            P("ctx", "head"),
+            P(CTX, "head"),
+            P(CTX, "head"),
+            P(CTX, "head"),
+            P(CTX, "head"),
+            P(CTX, "head"),
+            P(CTX, "head"),
         ),
         check_vma=False,
     )

time: 208 us -> 239 us (1.15)
  local copies, waits for them, and re-layouts: 13.7 us -> 74.9 us
  waiting for transfers between devices: 66.2 us -> 21.4 us
  other arithmetic: 18.3 us -> 26.8 us
  matrix products: 9.22 us -> 13.4 us
    rev x0 -> x2, local copies, waits for them, and re-layouts: none -> 49.5 us  [carried_in(): within = jnp.flip(jnp.cumsum(jnp.flip(mine, 0), axis=0), 0) - mine]
    ppermute x18 -> x12, waiting for transfers between devices: 59.1 us -> 10.9 us  [scan_over(): arrived.append(lax.ppermute(total.astype(jnp.bfloat16), axis, pairs))]
    all_to_all x0 -> x4, starting transfers between devices: none -> 18.4 us  [the longest x2 10.2 us: carried_in(): mine = lax.all_to_all(slices, 'inner', 0, 0, tiled=True).astype(jnp.float32)]
    ppermute x18 -> x12, starting transfers between devices: 62.9 us -> 46.5 us  [scan_over(): arrived.append(lax.ppermute(total.astype(jnp.bfloat16), axis, pairs))]
    unnamed x86 -> x79, local copies, waits for them, and re-layouts: 3.95 us -> 14.2 us
    all_to_all x0 -> x6, other arithmetic: none -> 8.14 us  [the longest x4 5.47 us: carried_in(): back = lax.all_to_all(states, 'inner', 0, 0, tiled=True)]
    all_to_all x0 -> x4, waiting for transfers between devices: none -> 7.78 us  [the longest x2 3.92 us: carried_in(): back = lax.all_to_all(states, 'inner', 0, 0, tiled=True)]
    ppermute x8, waiting for transfers between devices: 7.05 us -> 2.65 us  [from_behind(): return lax.ppermute(shard, axis, pairs)]
  transfers between devices with their start and end apart: 28 -> 26, of which waited for: 13 -> 9; matrix products, arithmetic and copies ran while one was open for 17% -> 45% of each run, Pallas kernels for 0% -> 0%
where the time goes in v8:
time: 239 us; the launch traced here: 235 us
  starting transfers between devices  97.1 us (41%)
  local copies, waits for them, and re-layouts  74.9 us (31%)
  other arithmetic  26.8 us (11%)
  waiting for transfers between devices  21.4 us (9%)
  matrix products  13.4 us (6%)
    rev x2, local copies, waits for them, and re-layouts, carried_in(): within = jnp.flip(jnp.cumsum(jnp.flip(mine, 0), axis=0), 0) - mine  49.5 us
    ppermute x12, starting transfers between devices, scan_over(): arrived.append(lax.ppermute(total.astype(jnp.bfloat16), axis, pairs))  46.5 us
    ppermute x8, starting transfers between devices, from_behind(): return lax.ppermute(shard, axis, pairs)  23.9 us
    unnamed x79, local copies, waits for them, and re-layouts  14.2 us
    ppermute x12, waiting for transfers between devices, scan_over(): arrived.append(lax.ppermute(total.astype(jnp.bfloat16), axis, pairs))  10.9 us
    all_to_all x2, starting transfers between devices, carried_in(): mine = lax.all_to_all(slices, 'inner', 0, 0, tiled=True).astype(jnp.float32)  10.2 us
    ppermute x2, starting transfers between devices, per_device(): lax.ppermute(sums, 'head', [(i, i ^ step) for i in range(heads_dev)])  8.33 us
    all_to_all x2, starting transfers between devices, carried_in(): back = lax.all_to_all(states, 'inner', 0, 0, tiled=True)  8.21 us
  transfers between devices with their start and end apart: 26, of which 9 were waited for; matrix products, arithmetic and copies ran while one was open for 45% of the time, Pallas kernels for 0%

profile of v8, /device:TPU:24, one launch (start us, length us, event | category | flops | bytes accessed | tf_op | source)
XLA Modules:
  0.0 235.3 jit_solution(15974587703048092514)
XLA Ops:
  5.6 5.9 %all-to-all-start = ((bf16[8,2,4096]{2,1,0:T(2,128)(2,1)}), bf16[8,2,4096]{2,1,0:T(2,128)(2,1)S(1)}, u32[]{:S(2)}, u32[]{:S(2)}) async-start(bf16[8,2,4096]{2,1,0:T(2,128)(2,1)} %reshape.495), calls=%async_computation | async-start | bytes 262144 | tf_op jit(solution)/shard_map/all_to_all | solution.py:47
  11.5 2.4 %collective-permute-start.14 = (bf16[128,1024]{1,0:T(8,128)(2,1)S(1)}, bf16[128,1024]{1,0:T(8,128)(2,1)S(1)}, u32[]{:S(2)}, u32[]{:S(2)}) collective-permute-start(bf16[128,1024]{1,0:T(8,128)(2,1)S(1)} %pad_maximum_fusion), channel_id=1, source_target_pairs={{0,4},{4,8},{8,12},{12,16},{16,20},{20,24},{24,28},{28,32},{32,36}... | collective-permute-start | bytes 786440 | tf_op jit(solution)/shard_map/ppermute | solution.py:62
  14.4 3.9 %all-to-all-done = bf16[8,2,4096]{2,1,0:T(2,128)(2,1)S(1)} async-done(((bf16[8,2,4096]{2,1,0:T(2,128)(2,1)}), bf16[8,2,4096]{2,1,0:T(2,128)(2,1)S(1)}, u32[]{:S(2)}, u32[]{:S(2)}) %all-to-all-start) | async-done | bytes 131104 | tf_op jit(solution)/shard_map/all_to_all | solution.py:47
  18.7 10.1 %collective-permute-start.2 = (bf16[8192]{0:T(1024)(128)(2,1)S(1)}, bf16[8192]{0:T(1024)(128)(2,1)S(1)}, u32[]{:S(2)}, u32[]{:S(2)}) collective-permute-start(bf16[8192]{0:T(1024)(128)(2,1)S(1)} %convert_element_type.205), channel_id=1, source_target_pairs={{0,96},{32,128},{64,160},{96,192},{128,224},{160,256},{192,288},{2... | collective-permute-start | bytes 49160 | tf_op jit(solution)/shard_map/ppermute | solution.py:37
  28.8 4.3 %collective-permute-start.1 = (bf16[8192]{0:T(1024)(128)(2,1)S(1)}, bf16[8192]{0:T(1024)(128)(2,1)S(1)}, u32[]{:S(2)}, u32[]{:S(2)}) collective-permute-start(bf16[8192]{0:T(1024)(128)(2,1)S(1)} %convert_element_type.205), channel_id=1, source_target_pairs={{0,64},{32,96},{64,128},{96,160},{128,192},{160,224},{192,256},{22... | collective-permute-start | bytes 49160 | tf_op jit(solution)/shard_map/ppermute | solution.py:37
  33.1 4.3 %collective-permute-start = (bf16[8192]{0:T(1024)(128)(2,1)S(1)}, bf16[8192]{0:T(1024)(128)(2,1)S(1)}, u32[]{:S(2)}, u32[]{:S(2)}) collective-permute-start(bf16[8192]{0:T(1024)(128)(2,1)S(1)} %convert_element_type.205), channel_id=1, source_target_pairs={{0,32},{32,64},{64,96},{96,128},{128,160},{160,192},{192,224},{224... | collective-permute-start | bytes 49160 | tf_op jit(solution)/shard_map/ppermute | solution.py:37
  38.3 5.8 %collective-permute-done.1 = bf16[8192]{0:T(1024)(128)(2,1)S(1)} collective-permute-done((bf16[8192]{0:T(1024)(128)(2,1)S(1)}, bf16[8192]{0:T(1024)(128)(2,1)S(1)}, u32[]{:S(2)}, u32[]{:S(2)}) %collective-permute-start.1) | collective-permute-done | bytes 16416 | tf_op jit(solution)/shard_map/ppermute | solution.py:37
  48.1 2.9 %collective-permute-done.5 = bf16[8192]{0:T(1024)(128)(2,1)S(1)} collective-permute-done((bf16[8192]{0:T(1024)(128)(2,1)S(1)}, bf16[8192]{0:T(1024)(128)(2,1)S(1)}, u32[]{:S(2)}, u32[]{:S(2)}) %collective-permute-start.5) | collective-permute-done | bytes 16416 | tf_op jit(solution)/shard_map/ppermute | solution.py:37
  51.0 1.6 collective-permute-done.4
  53.1 1.3 reduce.10
  55.2 3.4 %all-to-all-start.1 = ((bf16[8,2,4096]{2,1,0:T(2,128)(2,1)}), bf16[8,2,4096]{2,1,0:T(2,128)(2,1)S(1)}, u32[]{:S(2)}, u32[]{:S(2)}) async-start(bf16[8,2,4096]{2,1,0:T(2,128)(2,1)} %reshape.497), calls=%async_computation.1 | async-start | bytes 262144 | tf_op jit(solution)/shard_map/all_to_all | solution.py:55
  59.0 2.3 collective-permute-start.15
  61.3 3.9 %all-to-all-done.1 = bf16[8,2,4096]{2,1,0:T(2,128)(2,1)S(1)} async-done(((bf16[8,2,4096]{2,1,0:T(2,128)(2,1)}), bf16[8,2,4096]{2,1,0:T(2,128)(2,1)S(1)}, u32[]{:S(2)}, u32[]{:S(2)}) %all-to-all-start.1) | async-done | bytes 131104 | tf_op jit(solution)/shard_map/all_to_all | solution.py:55
  66.5 3.4 %collective-permute-start.6 = (f32[2,128]{1,0:T(2,128)S(1)}, f32[2,128]{1,0:T(2,128)S(1)}, u32[]{:S(2)}, u32[]{:S(2)}) collective-permute-start(f32[2,128]{1,0:T(2,128)S(1)} %pad_maximum_fusion.2), channel_id=1, source_target_pairs={{0,1},{1,0},{2,3},{3,2},{4,5},{5,4},{6,7},{7,6},{8,9},{9,8},{10,11... | collective-permute-start | bytes 3080 | tf_op jit(solution)/shard_map/ppermute | solution.py:168
  70.0 1.9 collective-permute-start.16
  72.0 4.9 %collective-permute-start.7 = (f32[2,128]{1,0:T(2,128)S(1)}, f32[2,128]{1,0:T(2,128)S(1)}, u32[]{:S(2)}, u32[]{:S(2)}) collective-permute-start(f32[2,128]{1,0:T(2,128)S(1)} %fusion.76), channel_id=1, source_target_pairs={{0,2},{1,3},{2,0},{3,1},{4,6},{5,7},{6,4},{7,5},{8,10},{9,11},{10,... | collective-permute-start | bytes 3080 | tf_op jit(solution)/shard_map/ppermute | solution.py:168
  77.1 2.6 %collective-permute-done.16 = bf16[128,1024]{1,0:T(8,128)(2,1)S(1)} collective-permute-done((bf16[128,1024]{1,0:T(8,128)(2,1)S(1)}, bf16[128,1024]{1,0:T(8,128)(2,1)S(1)}, u32[]{:S(2)}, u32[]{:S(2)}) %collective-permute-start.16) | collective-permute-done | bytes 262176 | tf_op jit(solution)/shard_map/ppermute | solution.py:62
  79.8 1.9 collective-permute-start.17
  82.9 1.3 reduce.11
  85.0 4.3 %all-to-all-start.2 = ((bf16[8,2,4096]{2,1,0:T(2,128)(2,1)}), bf16[8,2,4096]{2,1,0:T(2,128)(2,1)}, u32[]{:S(2)}, u32[]{:S(2)}) async-start(bf16[8,2,4096]{2,1,0:T(2,128)(2,1)} %reshape.499), calls=%async_computation.2 | async-start | bytes 262144 | tf_op jit(solution)/shard_map/all_to_all | solution.py:47
  95.3 1.5 fusion.79
  96.8 1.6 convolution_bitcast_fusion
  101.2 1.4 reshape.479
  104.9 2.3 scatter_fusion
  108.8 6.3 %collective-permute-start.18 = (bf16[128,1024]{1,0:T(8,128)(2,1)}, bf16[128,1024]{1,0:T(8,128)(2,1)}, u32[]{:S(2)}, u32[]{:S(2)}) collective-permute-start(bf16[128,1024]{1,0:T(8,128)(2,1)} %pad_maximum_fusion.1), channel_id=1, source_target_pairs={{4,0},{8,4},{12,8},{16,12},{20,16},{24,20},{28,24},{32,28},{36,32}... | collective-permute-start | bytes 786440 | tf_op jit(solution)/shard_map/ppermute | solution.py:62
  116.0 1.4 reshape.500
  117.7 5.4 %collective-permute-start.10 = (bf16[8192]{0:T(1024)(128)(2,1)S(1)}, bf16[8192]{0:T(1024)(128)(2,1)S(1)}, u32[]{:S(2)}, u32[]{:S(2)}) collective-permute-start(bf16[8192]{0:T(1024)(128)(2,1)S(1)} %convert_element_type.222), channel_id=1, source_target_pairs={{96,0},{128,32},{160,64},{192,96},{224,128},{256,160},{288,192},{3... | collective-permute-start | bytes 49160 | tf_op jit(solution)/shard_map/ppermute | solution.py:37
  123.2 7.4 %collective-permute-start.9 = (bf16[8192]{0:T(1024)(128)(2,1)S(1)}, bf16[8192]{0:T(1024)(128)(2,1)S(1)}, u32[]{:S(2)}, u32[]{:S(2)}) collective-permute-start(bf16[8192]{0:T(1024)(128)(2,1)S(1)} %convert_element_type.222), channel_id=1, source_target_pairs={{64,0},{96,32},{128,64},{160,96},{192,128},{224,160},{256,192},{28... | collective-permute-start | bytes 49160 | tf_op jit(solution)/shard_map/ppermute | solution.py:37
  130.6 5.5 %collective-permute-start.8 = (bf16[8192]{0:T(1024)(128)(2,1)S(1)}, bf16[8192]{0:T(1024)(128)(2,1)S(1)}, u32[]{:S(2)}, u32[]{:S(2)}) collective-permute-start(bf16[8192]{0:T(1024)(128)(2,1)S(1)} %convert_element_type.222), channel_id=1, source_target_pairs={{32,0},{64,32},{96,64},{128,96},{160,128},{192,160},{224,192},{256... | collective-permute-start | bytes 49160 | tf_op jit(solution)/shard_map/ppermute | solution.py:37
  136.1 1.8 add_convert_fusion.2
  137.9 1.9 collective-permute-start.19
  140.9 1.9 collective-permute-start.13
  142.8 1.9 collective-permute-start.12
  144.7 1.9 collective-permute-start.11
  147.4 1.7 copy.155
  150.9 21.7 %rev.7 = f32[8,8192]{1,0:T(8,128)S(1)} reverse(f32[8,8192]{1,0:T(8,128)} %bitcast.250), dimensions={0} | reverse | bytes 524288 | tf_op jit(solution)/shard_map/jit(_flip)/rev | solution.py:49
  173.5 27.9 %rev.8 = f32[8,8192]{1,0:T(8,128)} reverse(f32[8,8192]{1,0:T(8,128)} %reduce_window_sum.18), dimensions={0} | reverse | bytes 524288 | tf_op jit(solution)/shard_map/jit(_flip)/rev | solution.py:49
  202.2 1.8 add_convert_fusion.1
  204.0 1.9 collective-permute-start.20
  206.0 1.8 fusion.26
  207.7 1.5 reduce.12
  210.0 4.8 %all-to-all-start.3 = ((bf16[8,2,4096]{2,1,0:T(2,128)(2,1)}), bf16[8,2,4096]{2,1,0:T(2,128)(2,1)}, u32[]{:S(2)}, u32[]{:S(2)}) async-start(bf16[8,2,4096]{2,1,0:T(2,128)(2,1)} %reshape.501), calls=%async_computation.3 | async-start | bytes 262144 | tf_op jit(solution)/shard_map/all_to_all | solution.py:55
  216.9 1.8 add_convert_fusion
  218.8 5.2 %collective-permute-start.21 = (bf16[128,1024]{1,0:T(8,128)(2,1)}, bf16[128,1024]{1,0:T(8,128)(2,1)}, u32[]{:S(2)}, u32[]{:S(2)}) collective-permute-start(bf16[128,1024]{1,0:T(8,128)(2,1)} %add_convert_fusion), channel_id=1, source_target_pairs={{4,0},{8,4},{12,8},{16,12},{20,16},{24,20},{28,24},{32,28},{36,32}... | collective-permute-start | bytes 786440 | tf_op jit(solution)/shard_map/ppermute | solution.py:62
  224.1 1.4 reshape.502
  225.4 1.4 reduce.8
  227.8 1.8 fusion.17
  229.9 1.7 copy.157
  (174 shorter events, 42.5 us)
Async XLA Ops:
  0.6 94.6 %copy-start = (bf16[128,512]{1,0:T(8,128)(2,1)S(1)}, bf16[128,512]{1,0:T(8,128)(2,1)}, u32[]{:S(2)}) copy-start(bf16[128,512]{1,0:T(8,128)(2,1)} %param.15) | copy-start | bytes 393220
  0.6 13.5 %copy-start.14 = (bf16[128,512]{1,0:T(8,128)(2,1)S(1)}, bf16[128,512]{1,0:T(8,128)(2,1)}, u32[]{:S(2)}) copy-start(bf16[128,512]{1,0:T(8,128)(2,1)} %param.11) | copy-start | bytes 393220
  0.7 10.8 %copy-start.17 = (bf16[128,512]{1,0:T(8,128)(2,1)S(1)}, bf16[128,512]{1,0:T(8,128)(2,1)}, u32[]{:S(2)}) copy-start(bf16[128,512]{1,0:T(8,128)(2,1)} %param.17) | copy-start | bytes 393220
  0.7 10.8 %copy-start.18 = (bf16[128,512]{1,0:T(8,128)(2,1)S(1)}, bf16[128,512]{1,0:T(8,128)(2,1)}, u32[]{:S(2)}) copy-start(bf16[128,512]{1,0:T(8,128)(2,1)} %param.16) | copy-start | bytes 393220
  0.7 13.3 %copy-start.29 = (s32[1,3]{1,0:T(1,128)S(1)}, s32[1,3]{1,0:T(1,128)}, u32[]{:S(2)}) copy-start(s32[1,3]{1,0:T(1,128)} %param.19) | copy-start | bytes 40
  0.7 13.4 %copy-start.5 = (bf16[128,512]{1,0:T(8,128)(2,1)S(1)}, bf16[128,512]{1,0:T(8,128)(2,1)}, u32[]{:S(2)}) copy-start(bf16[128,512]{1,0:T(8,128)(2,1)} %param.10) | copy-start | bytes 393220
  5.6 12.7 %all-to-all-start = ((bf16[8,2,4096]{2,1,0:T(2,128)(2,1)}), bf16[8,2,4096]{2,1,0:T(2,128)(2,1)S(1)}, u32[]{:S(2)}, u32[]{:S(2)}) async-start(bf16[8,2,4096]{2,1,0:T(2,128)(2,1)} %reshape.495), calls=%async_computation | async-start | bytes 262144 | tf_op jit(solution)/shard_map/all_to_all | solution.py:47
  11.5 47.5 %collective-permute-start.14 = (bf16[128,1024]{1,0:T(8,128)(2,1)S(1)}, bf16[128,1024]{1,0:T(8,128)(2,1)S(1)}, u32[]{:S(2)}, u32[]{:S(2)}) collective-permute-start(bf16[128,1024]{1,0:T(8,128)(2,1)S(1)} %pad_maximum_fusion), channel_id=1, source_target_pairs={{0,4},{4,8},{8,12},{12,16},{16,20},{20,24},{24,28},{28,32},{32,36}... | collective-permute-start | bytes 786440 | tf_op jit(solution)/shard_map/ppermute | solution.py:62
  14.4 44.4 %copy-start.19 = (bf16[4,128,128]{2,1,0:T(8,128)(2,1)}, bf16[4,128,128]{2,1,0:T(8,128)(2,1)S(1)}, u32[]{:S(2)}) copy-start(bf16[4,128,128]{2,1,0:T(8,128)(2,1)S(1)} %fusion.15) | copy-start | bytes 393220
  14.4 44.3 %copy-start.22 = (bf16[128,512]{1,0:T(8,128)(2,1)S(1)}, bf16[128,512]{1,0:T(8,128)(2,1)}, u32[]{:S(2)}) copy-start(bf16[128,512]{1,0:T(8,128)(2,1)} %param.14) | copy-start | bytes 393220
  18.4 40.4 %copy-start.9 = (bf16[128,512]{1,0:T(8,128)(2,1)S(1)}, bf16[128,512]{1,0:T(8,128)(2,1)}, u32[]{:S(2)}) copy-start(bf16[128,512]{1,0:T(8,128)(2,1)} %param.12) | copy-start | bytes 393220
  18.7 19.6 %collective-permute-start.2 = (bf16[8192]{0:T(1024)(128)(2,1)S(1)}, bf16[8192]{0:T(1024)(128)(2,1)S(1)}, u32[]{:S(2)}, u32[]{:S(2)}) collective-permute-start(bf16[8192]{0:T(1024)(128)(2,1)S(1)} %convert_element_type.205), channel_id=1, source_target_pairs={{0,96},{32,128},{64,160},{96,192},{128,224},{160,256},{192,288},{2... | collective-permute-start | bytes 49160 | tf_op jit(solution)/shard_map/ppermute | solution.py:37
  28.8 15.3 %collective-permute-start.1 = (bf16[8192]{0:T(1024)(128)(2,1)S(1)}, bf16[8192]{0:T(1024)(128)(2,1)S(1)}, u32[]{:S(2)}, u32[]{:S(2)}) collective-permute-start(bf16[8192]{0:T(1024)(128)(2,1)S(1)} %convert_element_type.205), channel_id=1, source_target_pairs={{0,64},{32,96},{64,128},{96,160},{128,192},{160,224},{192,256},{22... | collective-permute-start | bytes 49160 | tf_op jit(solution)/shard_map/ppermute | solution.py:37
  33.1 11.1 %collective-permute-start = (bf16[8192]{0:T(1024)(128)(2,1)S(1)}, bf16[8192]{0:T(1024)(128)(2,1)S(1)}, u32[]{:S(2)}, u32[]{:S(2)}) collective-permute-start(bf16[8192]{0:T(1024)(128)(2,1)S(1)} %convert_element_type.205), channel_id=1, source_target_pairs={{0,32},{32,64},{64,96},{96,128},{128,160},{160,192},{192,224},{224... | collective-permute-start | bytes 49160 | tf_op jit(solution)/shard_map/ppermute | solution.py:37
  44.2 6.8 %collective-permute-start.5 = (bf16[8192]{0:T(1024)(128)(2,1)S(1)}, bf16[8192]{0:T(1024)(128)(2,1)S(1)}, u32[]{:S(2)}, u32[]{:S(2)}) collective-permute-start(bf16[8192]{0:T(1024)(128)(2,1)S(1)} %fusion.57), channel_id=1, source_target_pairs={{0,384},{32,416},{64,448},{96,480},{1,385},{33,417},{65,449},{97,4... | collective-permute-start | bytes 49160 | tf_op jit(solution)/shard_map/ppermute | solution.py:37
  45.5 7.1 %collective-permute-start.4 = (bf16[8192]{0:T(1024)(128)(2,1)S(1)}, bf16[8192]{0:T(1024)(128)(2,1)S(1)}, u32[]{:S(2)}, u32[]{:S(2)}) collective-permute-start(bf16[8192]{0:T(1024)(128)(2,1)S(1)} %fusion.57), channel_id=1, source_target_pairs={{0,256},{32,288},{64,320},{96,352},{128,384},{160,416},{192,448},{... | collective-permute-start | bytes 49160 | tf_op jit(solution)/shard_map/ppermute | solution.py:37
  46.8 5.8 %collective-permute-start.3 = (bf16[8192]{0:T(1024)(128)(2,1)S(1)}, bf16[8192]{0:T(1024)(128)(2,1)S(1)}, u32[]{:S(2)}, u32[]{:S(2)}) collective-permute-start(bf16[8192]{0:T(1024)(128)(2,1)S(1)} %fusion.57), channel_id=1, source_target_pairs={{0,128},{32,160},{64,192},{96,224},{128,256},{160,288},{192,320},{... | collective-permute-start | bytes 49160 | tf_op jit(solution)/shard_map/ppermute | solution.py:37
  54.4 11.8 %copy-start.28 = (f32[512]{0:T(512)S(1)}, f32[512]{0:T(512)}, u32[]{:S(2)}) copy-start(f32[512]{0:T(512)} %param.13) | copy-start | bytes 6148
  55.2 10.1 %all-to-all-start.1 = ((bf16[8,2,4096]{2,1,0:T(2,128)(2,1)}), bf16[8,2,4096]{2,1,0:T(2,128)(2,1)S(1)}, u32[]{:S(2)}, u32[]{:S(2)}) async-start(bf16[8,2,4096]{2,1,0:T(2,128)(2,1)} %reshape.497), calls=%async_computation.1 | async-start | bytes 262144 | tf_op jit(solution)/shard_map/all_to_all | solution.py:55
  58.8 18.3 %copy-start.23 = (bf16[128,512]{1,0:T(8,128)(2,1)S(1)}, bf16[128,512]{1,0:T(8,128)(2,1)}, u32[]{:S(2)}) copy-start(bf16[128,512]{1,0:T(8,128)(2,1)} %param.18) | copy-start | bytes 393220
  59.0 10.9 %collective-permute-start.15 = (bf16[128,1024]{1,0:T(8,128)(2,1)S(1)}, bf16[128,1024]{1,0:T(8,128)(2,1)S(1)}, u32[]{:S(2)}, u32[]{:S(2)}) collective-permute-start(bf16[128,1024]{1,0:T(8,128)(2,1)S(1)} %collective-permute-done.14), channel_id=1, source_target_pairs={{0,4},{4,8},{8,12},{12,16},{16,20},{20,24},{24,28},{28,32},{32,36}... | collective-permute-start | bytes 786440 | tf_op jit(solution)/shard_map/ppermute | solution.py:62
  66.2 16.5 %copy-start.7 = (bf16[4,128,128]{2,1,0:T(8,128)(2,1)}, bf16[4,128,128]{2,1,0:T(8,128)(2,1)S(1)}, u32[]{:S(2)}) copy-start(bf16[4,128,128]{2,1,0:T(8,128)(2,1)S(1)} %reshape.446) | copy-start | bytes 393220
  66.5 5.5 %collective-permute-start.6 = (f32[2,128]{1,0:T(2,128)S(1)}, f32[2,128]{1,0:T(2,128)S(1)}, u32[]{:S(2)}, u32[]{:S(2)}) collective-permute-start(f32[2,128]{1,0:T(2,128)S(1)} %pad_maximum_fusion.2), channel_id=1, source_target_pairs={{0,1},{1,0},{2,3},{3,2},{4,5},{5,4},{6,7},{7,6},{8,9},{9,8},{10,11... | collective-permute-start | bytes 3080 | tf_op jit(solution)/shard_map/ppermute | solution.py:168
  70.0 9.8 %collective-permute-start.16 = (bf16[128,1024]{1,0:T(8,128)(2,1)S(1)}, bf16[128,1024]{1,0:T(8,128)(2,1)S(1)}, u32[]{:S(2)}, u32[]{:S(2)}) collective-permute-start(bf16[128,1024]{1,0:T(8,128)(2,1)S(1)} %collective-permute-done.15), channel_id=1, source_target_pairs={{0,4},{4,8},{8,12},{12,16},{16,20},{20,24},{24,28},{28,32},{32,36}... | collective-permute-start | bytes 786440 | tf_op jit(solution)/shard_map/ppermute | solution.py:62
  72.0 9.7 %collective-permute-start.7 = (f32[2,128]{1,0:T(2,128)S(1)}, f32[2,128]{1,0:T(2,128)S(1)}, u32[]{:S(2)}, u32[]{:S(2)}) collective-permute-start(f32[2,128]{1,0:T(2,128)S(1)} %fusion.76), channel_id=1, source_target_pairs={{0,2},{1,3},{2,0},{3,1},{4,6},{5,7},{6,4},{7,5},{8,10},{9,11},{10,... | collective-permute-start | bytes 3080 | tf_op jit(solution)/shard_map/ppermute | solution.py:168
  79.8 10.4 %collective-permute-start.17 = (bf16[128,1024]{1,0:T(8,128)(2,1)S(1)}, bf16[128,1024]{1,0:T(8,128)(2,1)}, u32[]{:S(2)}, u32[]{:S(2)}) collective-permute-start(bf16[128,1024]{1,0:T(8,128)(2,1)S(1)} %collective-permute-done.16), channel_id=1, source_target_pairs={{0,4},{4,8},{8,12},{12,16},{16,20},{20,24},{24,28},{28,32},{32,36}... | collective-permute-start | bytes 786440 | tf_op jit(solution)/shard_map/ppermute | solution.py:62
  85.0 31.0 %all-to-all-start.2 = ((bf16[8,2,4096]{2,1,0:T(2,128)(2,1)}), bf16[8,2,4096]{2,1,0:T(2,128)(2,1)}, u32[]{:S(2)}, u32[]{:S(2)}) async-start(bf16[8,2,4096]{2,1,0:T(2,128)(2,1)} %reshape.499), calls=%async_computation.2 | async-start | bytes 262144 | tf_op jit(solution)/shard_map/all_to_all | solution.py:47
  107.2 7.9 %copy-start.3 = (bf16[128,4,128]{0,2,1:T(8,128)(2,1)S(1)}, bf16[128,4,128]{0,2,1:T(8,128)(2,1)}, u32[]{:S(2)}) copy-start(bf16[128,4,128]{0,2,1:T(8,128)(2,1)} %copy-done.2) | copy-start | bytes 393220
  107.3 7.9 %copy-start.8 = (bf16[4,128,128]{2,1,0:T(8,128)(2,1)S(1)}, bf16[4,128,128]{2,1,0:T(8,128)(2,1)}, u32[]{:S(2)}) copy-start(bf16[4,128,128]{2,1,0:T(8,128)(2,1)} %copy-done.7) | copy-start | bytes 393220
  107.3 7.9 %copy-start.11 = (f32[128,4,128]{0,2,1:T(8,128)S(1)}, f32[128,4,128]{0,2,1:T(8,128)}, u32[]{:S(2)}) copy-start(f32[128,4,128]{0,2,1:T(8,128)} %convolution_bitcast_fusion.6) | copy-start | bytes 786436
  108.8 27.2 %collective-permute-start.18 = (bf16[128,1024]{1,0:T(8,128)(2,1)}, bf16[128,1024]{1,0:T(8,128)(2,1)}, u32[]{:S(2)}, u32[]{:S(2)}) collective-permute-start(bf16[128,1024]{1,0:T(8,128)(2,1)} %pad_maximum_fusion.1), channel_id=1, source_target_pairs={{4,0},{8,4},{12,8},{16,12},{20,16},{24,20},{28,24},{32,28},{36,32}... | collective-permute-start | bytes 786440 | tf_op jit(solution)/shard_map/ppermute | solution.py:62
  117.4 29.2 %copy-start.4 = (bf16[128,4,128]{0,2,1:T(8,128)(2,1)S(1)}, bf16[128,4,128]{0,2,1:T(8,128)(2,1)}, u32[]{:S(2)}) copy-start(bf16[128,4,128]{0,2,1:T(8,128)(2,1)} %copy-done.2) | copy-start | bytes 393220
  117.4 29.1 %copy-start.20 = (bf16[4,128,128]{2,1,0:T(8,128)(2,1)S(1)}, bf16[4,128,128]{2,1,0:T(8,128)(2,1)}, u32[]{:S(2)}) copy-start(bf16[4,128,128]{2,1,0:T(8,128)(2,1)} %copy-done.19) | copy-start | bytes 393220
  117.7 29.7 %copy-start.13 = (f32[8192]{0:T(1024)}, f32[8192]{0:T(1024)S(1)}, u32[]{:S(2)}) copy-start(f32[8192]{0:T(1024)S(1)} %convert_reduce_fusion.1) | copy-start | bytes 98308
  117.7 22.1 %collective-permute-start.10 = (bf16[8192]{0:T(1024)(128)(2,1)S(1)}, bf16[8192]{0:T(1024)(128)(2,1)S(1)}, u32[]{:S(2)}, u32[]{:S(2)}) collective-permute-start(bf16[8192]{0:T(1024)(128)(2,1)S(1)} %convert_element_type.222), channel_id=1, source_target_pairs={{96,0},{128,32},{160,64},{192,96},{224,128},{256,160},{288,192},{3... | collective-permute-start | bytes 49160 | tf_op jit(solution)/shard_map/ppermute | solution.py:37
  123.2 16.6 %collective-permute-start.9 = (bf16[8192]{0:T(1024)(128)(2,1)S(1)}, bf16[8192]{0:T(1024)(128)(2,1)S(1)}, u32[]{:S(2)}, u32[]{:S(2)}) collective-permute-start(bf16[8192]{0:T(1024)(128)(2,1)S(1)} %convert_element_type.222), channel_id=1, source_target_pairs={{64,0},{96,32},{128,64},{160,96},{192,128},{224,160},{256,192},{28... | collective-permute-start | bytes 49160 | tf_op jit(solution)/shard_map/ppermute | solution.py:37
  130.6 9.7 %collective-permute-start.8 = (bf16[8192]{0:T(1024)(128)(2,1)S(1)}, bf16[8192]{0:T(1024)(128)(2,1)S(1)}, u32[]{:S(2)}, u32[]{:S(2)}) collective-permute-start(bf16[8192]{0:T(1024)(128)(2,1)S(1)} %convert_element_type.222), channel_id=1, source_target_pairs={{32,0},{64,32},{96,64},{128,96},{160,128},{192,160},{224,192},{256... | collective-permute-start | bytes 49160 | tf_op jit(solution)/shard_map/ppermute | solution.py:37
  137.9 64.4 %collective-permute-start.19 = (bf16[128,1024]{1,0:T(8,128)(2,1)}, bf16[128,1024]{1,0:T(8,128)(2,1)}, u32[]{:S(2)}, u32[]{:S(2)}) collective-permute-start(bf16[128,1024]{1,0:T(8,128)(2,1)} %add_convert_fusion.2), channel_id=1, source_target_pairs={{4,0},{8,4},{12,8},{16,12},{20,16},{24,20},{28,24},{32,28},{36,32}... | collective-permute-start | bytes 786440 | tf_op jit(solution)/shard_map/ppermute | solution.py:62
  140.9 60.5 %collective-permute-start.13 = (bf16[8192]{0:T(1024)(128)(2,1)}, bf16[8192]{0:T(1024)(128)(2,1)}, u32[]{:S(2)}, u32[]{:S(2)}) collective-permute-start(bf16[8192]{0:T(1024)(128)(2,1)} %fusion.58), channel_id=1, source_target_pairs={{384,0},{416,32},{448,64},{480,96},{385,1},{417,33},{449,65},{481,... | collective-permute-start | bytes 49160 | tf_op jit(solution)/shard_map/ppermute | solution.py:37
  142.8 58.6 %collective-permute-start.12 = (bf16[8192]{0:T(1024)(128)(2,1)}, bf16[8192]{0:T(1024)(128)(2,1)}, u32[]{:S(2)}, u32[]{:S(2)}) collective-permute-start(bf16[8192]{0:T(1024)(128)(2,1)} %fusion.58), channel_id=1, source_target_pairs={{256,0},{288,32},{320,64},{352,96},{384,128},{416,160},{448,192},{... | collective-permute-start | bytes 49160 | tf_op jit(solution)/shard_map/ppermute | solution.py:37
  144.7 56.7 %collective-permute-start.11 = (bf16[8192]{0:T(1024)(128)(2,1)}, bf16[8192]{0:T(1024)(128)(2,1)}, u32[]{:S(2)}, u32[]{:S(2)}) collective-permute-start(bf16[8192]{0:T(1024)(128)(2,1)} %fusion.58), channel_id=1, source_target_pairs={{128,0},{160,32},{192,64},{224,96},{256,128},{288,160},{320,192},{... | collective-permute-start | bytes 49160 | tf_op jit(solution)/shard_map/ppermute | solution.py:37
  173.5 32.5 %copy-start.12 = (f32[8,1,8192]{2,1,0:T(1,128)S(1)}, f32[8,1,8192]{2,1,0:T(1,128)}, u32[]{:S(2)}) copy-start(f32[8,1,8192]{2,1,0:T(1,128)} %convert_element_type.220) | copy-start | bytes 786436
  204.0 12.9 %collective-permute-start.20 = (bf16[128,1024]{1,0:T(8,128)(2,1)}, bf16[128,1024]{1,0:T(8,128)(2,1)}, u32[]{:S(2)}, u32[]{:S(2)}) collective-permute-start(bf16[128,1024]{1,0:T(8,128)(2,1)} %add_convert_fusion.1), channel_id=1, source_target_pairs={{4,0},{8,4},{12,8},{16,12},{20,16},{24,20},{28,24},{32,28},{36,32}... | collective-permute-start | bytes 786440 | tf_op jit(solution)/shard_map/ppermute | solution.py:62
  210.0 14.1 %all-to-all-start.3 = ((bf16[8,2,4096]{2,1,0:T(2,128)(2,1)}), bf16[8,2,4096]{2,1,0:T(2,128)(2,1)}, u32[]{:S(2)}, u32[]{:S(2)}) async-start(bf16[8,2,4096]{2,1,0:T(2,128)(2,1)} %reshape.501), calls=%async_computation.3 | async-start | bytes 262144 | tf_op jit(solution)/shard_map/all_to_all | solution.py:55
  216.2 11.7 %copy-start.15 = (bf16[128,512]{1,0:T(8,128)(2,1)S(1)}, bf16[128,512]{1,0:T(8,128)(2,1)}, u32[]{:S(2)}) copy-start(bf16[128,512]{1,0:T(8,128)(2,1)} %param.11) | copy-start | bytes 393220
  216.9 12.7 %copy-start.10 = (bf16[128,512]{1,0:T(8,128)(2,1)S(1)}, bf16[128,512]{1,0:T(8,128)(2,1)}, u32[]{:S(2)}) copy-start(bf16[128,512]{1,0:T(8,128)(2,1)} %param.12) | copy-start | bytes 393220
  218.8 12.8 %copy-start.6 = (bf16[128,512]{1,0:T(8,128)(2,1)S(1)}, bf16[128,512]{1,0:T(8,128)(2,1)}, u32[]{:S(2)}) copy-start(bf16[128,512]{1,0:T(8,128)(2,1)} %param.10) | copy-start | bytes 393220
  218.8 14.7 %collective-permute-start.21 = (bf16[128,1024]{1,0:T(8,128)(2,1)}, bf16[128,1024]{1,0:T(8,128)(2,1)}, u32[]{:S(2)}, u32[]{:S(2)}) collective-permute-start(bf16[128,1024]{1,0:T(8,128)(2,1)} %add_convert_fusion), channel_id=1, source_target_pairs={{4,0},{8,4},{12,8},{16,12},{20,16},{24,20},{28,24},{32,28},{36,32}... | collective-permute-start | bytes 786440 | tf_op jit(solution)/shard_map/ppermute | solution.py:62
  (9 other events, 33.9 us)

commit v9 on v8

--- a/solution.py
+++ b/solution.py
@@ -45,11 +45,9 @@
     members = lax.axis_size("inner")
     slices = shard.astype(jnp.bfloat16).reshape(members, -1)
     mine = lax.all_to_all(slices, "inner", 0, 0, tiled=True).astype(jnp.float32)
-    if backward:
-        within = jnp.flip(jnp.cumsum(jnp.flip(mine, 0), axis=0), 0) - mine
-    else:
-        within = jnp.cumsum(mine, axis=0) - mine
+    running = jnp.cumsum(mine, axis=0)
     group = jnp.sum(mine, axis=0)
+    within = group[None] - running if backward else running - mine
     earlier = scan_over(group, "outer", backward)
     states = (within + earlier[None]).astype(jnp.bfloat16)
     back = lax.all_to_all(states, "inner", 0, 0, tiled=True)

time: 239 us -> 187 us (0.78)
  local copies, waits for them, and re-layouts: 74.9 us -> 24.4 us
    rev x2 -> x0, local copies, waits for them, and re-layouts: 49.5 us -> none  [carried_in(): within = jnp.flip(jnp.cumsum(jnp.flip(mine, 0), axis=0), 0) - mine]
    all_to_all x4 -> x2, other arithmetic: 5.47 us -> 2.18 us  [carried_in(): back = lax.all_to_all(states, 'inner', 0, 0, tiled=True)]
    another operation x5 -> x6, other arithmetic: 2.83 us -> 5.91 us  [the longest x4 5.74 us: carried_in(): running = jnp.cumsum(mine, axis=0)]
    unnamed x79 -> x78, local copies, waits for them, and re-layouts: 14.2 us -> 13.4 us
  transfers between devices with their start and end apart: 26 -> 26, of which waited for: 9 -> 9; matrix products, arithmetic and copies ran while one was open for 45% -> 29% of each run, Pallas kernels for 0% -> 0%
where the time goes in v9:
time: 187 us; the launch traced here: 185 us
  starting transfers between devices  98.6 us (53%)
  other arithmetic  25.5 us (14%)
  local copies, waits for them, and re-layouts  24.4 us (13%)
  waiting for transfers between devices  21.4 us (11%)
  matrix products  13.4 us (7%)
    ppermute x12, starting transfers between devices, scan_over(): arrived.append(lax.ppermute(total.astype(jnp.bfloat16), axis, pairs))  46.5 us
    ppermute x8, starting transfers between devices, from_behind(): return lax.ppermute(shard, axis, pairs)  25.3 us
    unnamed x78, local copies, waits for them, and re-layouts  13.4 us
    ppermute x12, waiting for transfers between devices, scan_over(): arrived.append(lax.ppermute(total.astype(jnp.bfloat16), axis, pairs))  10.9 us
    all_to_all x2, starting transfers between devices, carried_in(): mine = lax.all_to_all(slices, 'inner', 0, 0, tiled=True).astype(jnp.float32)  10.2 us
    ppermute x2, starting transfers between devices, per_device(): lax.ppermute(sums, 'head', [(i, i ^ step) for i in range(heads_dev)])  8.33 us
    all_to_all x2, starting transfers between devices, carried_in(): back = lax.all_to_all(states, 'inner', 0, 0, tiled=True)  8.21 us
    convert_element_type x4, other arithmetic, per_device(): owed = from_behind(owed.astype(jnp.bfloat16), CTX, -1).astype(jnp.float32)  6.41 us
  transfers between devices with their start and end apart: 26, of which 9 were waited for; matrix products, arithmetic and copies ran while one was open for 29% of the time, Pallas kernels for 0%

profile of v9, /device:TPU:24, one launch (start us, length us, event | category | flops | bytes accessed | tf_op | source)
XLA Modules:
  0.0 185.0 jit_solution(9026437463701181376)
XLA Ops:
  3.4 1.3 reduce.9
  5.5 5.9 %all-to-all-start = ((bf16[8,2,4096]{2,1,0:T(2,128)(2,1)}), bf16[8,2,4096]{2,1,0:T(2,128)(2,1)S(1)}, u32[]{:S(2)}, u32[]{:S(2)}) async-start(bf16[8,2,4096]{2,1,0:T(2,128)(2,1)} %reshape.544), calls=%async_computation | async-start | bytes 262144 | tf_op jit(solution)/shard_map/all_to_all | solution.py:47
  11.4 2.4 %collective-permute-start.14 = (bf16[128,1024]{1,0:T(8,128)(2,1)S(1)}, bf16[128,1024]{1,0:T(8,128)(2,1)S(1)}, u32[]{:S(2)}, u32[]{:S(2)}) collective-permute-start(bf16[128,1024]{1,0:T(8,128)(2,1)S(1)} %pad_maximum_fusion), channel_id=1, source_target_pairs={{0,4},{4,8},{8,12},{12,16},{16,20},{20,24},{24,28},{28,32},{32,36}... | collective-permute-start | bytes 786440 | tf_op jit(solution)/shard_map/ppermute | solution.py:60
  14.3 3.9 %all-to-all-done = bf16[8,2,4096]{2,1,0:T(2,128)(2,1)S(1)} async-done(((bf16[8,2,4096]{2,1,0:T(2,128)(2,1)}), bf16[8,2,4096]{2,1,0:T(2,128)(2,1)S(1)}, u32[]{:S(2)}, u32[]{:S(2)}) %all-to-all-start) | async-done | bytes 131104 | tf_op jit(solution)/shard_map/all_to_all | solution.py:47
  18.6 10.1 %collective-permute-start.2 = (bf16[8192]{0:T(1024)(128)(2,1)S(1)}, bf16[8192]{0:T(1024)(128)(2,1)S(1)}, u32[]{:S(2)}, u32[]{:S(2)}) collective-permute-start(bf16[8192]{0:T(1024)(128)(2,1)S(1)} %convert_element_type.211), channel_id=1, source_target_pairs={{0,96},{32,128},{64,160},{96,192},{128,224},{160,256},{192,288},{2... | collective-permute-start | bytes 49160 | tf_op jit(solution)/shard_map/ppermute | solution.py:37
  28.8 4.3 %collective-permute-start.1 = (bf16[8192]{0:T(1024)(128)(2,1)S(1)}, bf16[8192]{0:T(1024)(128)(2,1)S(1)}, u32[]{:S(2)}, u32[]{:S(2)}) collective-permute-start(bf16[8192]{0:T(1024)(128)(2,1)S(1)} %convert_element_type.211), channel_id=1, source_target_pairs={{0,64},{32,96},{64,128},{96,160},{128,192},{160,224},{192,256},{22... | collective-permute-start | bytes 49160 | tf_op jit(solution)/shard_map/ppermute | solution.py:37
  33.0 4.3 %collective-permute-start = (bf16[8192]{0:T(1024)(128)(2,1)S(1)}, bf16[8192]{0:T(1024)(128)(2,1)S(1)}, u32[]{:S(2)}, u32[]{:S(2)}) collective-permute-start(bf16[8192]{0:T(1024)(128)(2,1)S(1)} %convert_element_type.211), channel_id=1, source_target_pairs={{0,32},{32,64},{64,96},{96,128},{128,160},{160,192},{192,224},{224... | collective-permute-start | bytes 49160 | tf_op jit(solution)/shard_map/ppermute | solution.py:37
  38.3 5.8 %collective-permute-done.1 = bf16[8192]{0:T(1024)(128)(2,1)S(1)} collective-permute-done((bf16[8192]{0:T(1024)(128)(2,1)S(1)}, bf16[8192]{0:T(1024)(128)(2,1)S(1)}, u32[]{:S(2)}, u32[]{:S(2)}) %collective-permute-start.1) | collective-permute-done | bytes 16416 | tf_op jit(solution)/shard_map/ppermute | solution.py:37
  48.0 2.9 %collective-permute-done.5 = bf16[8192]{0:T(1024)(128)(2,1)S(1)} collective-permute-done((bf16[8192]{0:T(1024)(128)(2,1)S(1)}, bf16[8192]{0:T(1024)(128)(2,1)S(1)}, u32[]{:S(2)}, u32[]{:S(2)}) %collective-permute-start.5) | collective-permute-done | bytes 16416 | tf_op jit(solution)/shard_map/ppermute | solution.py:37
  51.0 1.6 collective-permute-done.4
  53.0 1.3 reduce.10
  55.1 3.4 %all-to-all-start.1 = ((bf16[8,2,4096]{2,1,0:T(2,128)(2,1)}), bf16[8,2,4096]{2,1,0:T(2,128)(2,1)S(1)}, u32[]{:S(2)}, u32[]{:S(2)}) async-start(bf16[8,2,4096]{2,1,0:T(2,128)(2,1)} %reshape.546), calls=%async_computation.1 | async-start | bytes 262144 | tf_op jit(solution)/shard_map/all_to_all | solution.py:53
  58.9 2.3 %collective-permute-start.15 = (bf16[128,1024]{1,0:T(8,128)(2,1)S(1)}, bf16[128,1024]{1,0:T(8,128)(2,1)S(1)}, u32[]{:S(2)}, u32[]{:S(2)}) collective-permute-start(bf16[128,1024]{1,0:T(8,128)(2,1)S(1)} %collective-permute-done.14), channel_id=1, source_target_pairs={{0,4},{4,8},{8,12},{12,16},{16,20},{20,24},{24,28},{28,32},{32,36}... | collective-permute-start | bytes 786440 | tf_op jit(solution)/shard_map/ppermute | solution.py:60
  61.2 3.9 %all-to-all-done.1 = bf16[8,2,4096]{2,1,0:T(2,128)(2,1)S(1)} async-done(((bf16[8,2,4096]{2,1,0:T(2,128)(2,1)}), bf16[8,2,4096]{2,1,0:T(2,128)(2,1)S(1)}, u32[]{:S(2)}, u32[]{:S(2)}) %all-to-all-start.1) | async-done | bytes 131104 | tf_op jit(solution)/shard_map/all_to_all | solution.py:53
  66.4 3.4 %collective-permute-start.6 = (f32[2,128]{1,0:T(2,128)S(1)}, f32[2,128]{1,0:T(2,128)S(1)}, u32[]{:S(2)}, u32[]{:S(2)}) collective-permute-start(f32[2,128]{1,0:T(2,128)S(1)} %pad_maximum_fusion.2), channel_id=1, source_target_pairs={{0,1},{1,0},{2,3},{3,2},{4,5},{5,4},{6,7},{7,6},{8,9},{9,8},{10,11... | collective-permute-start | bytes 3080 | tf_op jit(solution)/shard_map/ppermute | solution.py:166
  69.9 1.9 %collective-permute-start.16 = (bf16[128,1024]{1,0:T(8,128)(2,1)S(1)}, bf16[128,1024]{1,0:T(8,128)(2,1)S(1)}, u32[]{:S(2)}, u32[]{:S(2)}) collective-permute-start(bf16[128,1024]{1,0:T(8,128)(2,1)S(1)} %collective-permute-done.15), channel_id=1, source_target_pairs={{0,4},{4,8},{8,12},{12,16},{16,20},{20,24},{24,28},{28,32},{32,36}... | collective-permute-start | bytes 786440 | tf_op jit(solution)/shard_map/ppermute | solution.py:60
  71.9 4.9 %collective-permute-start.7 = (f32[2,128]{1,0:T(2,128)S(1)}, f32[2,128]{1,0:T(2,128)S(1)}, u32[]{:S(2)}, u32[]{:S(2)}) collective-permute-start(f32[2,128]{1,0:T(2,128)S(1)} %fusion.78), channel_id=1, source_target_pairs={{0,2},{1,3},{2,0},{3,1},{4,6},{5,7},{6,4},{7,5},{8,10},{9,11},{10,... | collective-permute-start | bytes 3080 | tf_op jit(solution)/shard_map/ppermute | solution.py:166
  77.0 2.6 %collective-permute-done.16 = bf16[128,1024]{1,0:T(8,128)(2,1)S(1)} collective-permute-done((bf16[128,1024]{1,0:T(8,128)(2,1)S(1)}, bf16[128,1024]{1,0:T(8,128)(2,1)S(1)}, u32[]{:S(2)}, u32[]{:S(2)}) %collective-permute-start.16) | collective-permute-done | bytes 262176 | tf_op jit(solution)/shard_map/ppermute | solution.py:60
  79.7 1.9 %collective-permute-start.17 = (bf16[128,1024]{1,0:T(8,128)(2,1)S(1)}, bf16[128,1024]{1,0:T(8,128)(2,1)}, u32[]{:S(2)}, u32[]{:S(2)}) collective-permute-start(bf16[128,1024]{1,0:T(8,128)(2,1)S(1)} %collective-permute-done.16), channel_id=1, source_target_pairs={{0,4},{4,8},{8,12},{12,16},{16,20},{20,24},{24,28},{28,32},{32,36}... | collective-permute-start | bytes 786440 | tf_op jit(solution)/shard_map/ppermute | solution.py:60
  82.8 1.3 reduce.11
  84.9 4.3 %all-to-all-start.2 = ((bf16[8,2,4096]{2,1,0:T(2,128)(2,1)}), bf16[8,2,4096]{2,1,0:T(2,128)(2,1)}, u32[]{:S(2)}, u32[]{:S(2)}) async-start(bf16[8,2,4096]{2,1,0:T(2,128)(2,1)} %reshape.548), calls=%async_computation.2 | async-start | bytes 262144 | tf_op jit(solution)/shard_map/all_to_all | solution.py:47
  95.2 1.5 fusion.81
  96.7 1.6 convolution_bitcast_fusion
  101.1 1.4 reshape.528
  104.8 2.3 %scatter_fusion = f32[5,128,512]{2,1,0:T(8,128)S(1)} fusion(f32[5,128,512]{2,1,0:T(8,128)S(1)} %broadcast.249.clone.1, s32[4]{0:T(128)S(1)} %fusion.70, f32[4,128,512]{2,1,0:T(8,128)} %reshape.528), kind=kCustom, calls=%fused_computation.2 | custom fusion | flops 262144 | bytes 3145744 | tf_op jit(solution)/shard_map/scatter-add | solution.py:122
  108.7 6.3 %collective-permute-start.18 = (bf16[128,1024]{1,0:T(8,128)(2,1)}, bf16[128,1024]{1,0:T(8,128)(2,1)}, u32[]{:S(2)}, u32[]{:S(2)}) collective-permute-start(bf16[128,1024]{1,0:T(8,128)(2,1)} %pad_maximum_fusion.1), channel_id=1, source_target_pairs={{4,0},{8,4},{12,8},{16,12},{20,16},{24,20},{28,24},{32,28},{36,32}... | collective-permute-start | bytes 786440 | tf_op jit(solution)/shard_map/ppermute | solution.py:60
  115.9 1.4 reshape.549
  117.6 5.4 %collective-permute-start.10 = (bf16[8192]{0:T(1024)(128)(2,1)S(1)}, bf16[8192]{0:T(1024)(128)(2,1)S(1)}, u32[]{:S(2)}, u32[]{:S(2)}) collective-permute-start(bf16[8192]{0:T(1024)(128)(2,1)S(1)} %convert_element_type.227), channel_id=1, source_target_pairs={{96,0},{128,32},{160,64},{192,96},{224,128},{256,160},{288,192},{3... | collective-permute-start | bytes 49160 | tf_op jit(solution)/shard_map/ppermute | solution.py:37
  123.0 7.4 %collective-permute-start.9 = (bf16[8192]{0:T(1024)(128)(2,1)S(1)}, bf16[8192]{0:T(1024)(128)(2,1)S(1)}, u32[]{:S(2)}, u32[]{:S(2)}) collective-permute-start(bf16[8192]{0:T(1024)(128)(2,1)S(1)} %convert_element_type.227), channel_id=1, source_target_pairs={{64,0},{96,32},{128,64},{160,96},{192,128},{224,160},{256,192},{28... | collective-permute-start | bytes 49160 | tf_op jit(solution)/shard_map/ppermute | solution.py:37
  130.4 5.5 %collective-permute-start.8 = (bf16[8192]{0:T(1024)(128)(2,1)S(1)}, bf16[8192]{0:T(1024)(128)(2,1)S(1)}, u32[]{:S(2)}, u32[]{:S(2)}) collective-permute-start(bf16[8192]{0:T(1024)(128)(2,1)S(1)} %convert_element_type.227), channel_id=1, source_target_pairs={{32,0},{64,32},{96,64},{128,96},{160,128},{192,160},{224,192},{256... | collective-permute-start | bytes 49160 | tf_op jit(solution)/shard_map/ppermute | solution.py:37
  135.9 1.8 add_convert_fusion.2
  137.7 1.9 %collective-permute-start.19 = (bf16[128,1024]{1,0:T(8,128)(2,1)}, bf16[128,1024]{1,0:T(8,128)(2,1)}, u32[]{:S(2)}, u32[]{:S(2)}) collective-permute-start(bf16[128,1024]{1,0:T(8,128)(2,1)} %add_convert_fusion.2), channel_id=1, source_target_pairs={{4,0},{8,4},{12,8},{16,12},{20,16},{24,20},{28,24},{32,28},{36,32}... | collective-permute-start | bytes 786440 | tf_op jit(solution)/shard_map/ppermute | solution.py:60
  140.8 1.9 %collective-permute-start.13 = (bf16[8192]{0:T(1024)(128)(2,1)}, bf16[8192]{0:T(1024)(128)(2,1)}, u32[]{:S(2)}, u32[]{:S(2)}) collective-permute-start(bf16[8192]{0:T(1024)(128)(2,1)} %fusion.60), channel_id=1, source_target_pairs={{384,0},{416,32},{448,64},{480,96},{385,1},{417,33},{449,65},{481,... | collective-permute-start | bytes 49160 | tf_op jit(solution)/shard_map/ppermute | solution.py:37
  142.7 1.9 %collective-permute-start.12 = (bf16[8192]{0:T(1024)(128)(2,1)}, bf16[8192]{0:T(1024)(128)(2,1)}, u32[]{:S(2)}, u32[]{:S(2)}) collective-permute-start(bf16[8192]{0:T(1024)(128)(2,1)} %fusion.60), channel_id=1, source_target_pairs={{256,0},{288,32},{320,64},{352,96},{384,128},{416,160},{448,192},{... | collective-permute-start | bytes 49160 | tf_op jit(solution)/shard_map/ppermute | solution.py:37
  144.5 1.9 %collective-permute-start.11 = (bf16[8192]{0:T(1024)(128)(2,1)}, bf16[8192]{0:T(1024)(128)(2,1)}, u32[]{:S(2)}, u32[]{:S(2)}) collective-permute-start(bf16[8192]{0:T(1024)(128)(2,1)} %fusion.60), channel_id=1, source_target_pairs={{128,0},{160,32},{192,64},{224,96},{256,128},{288,160},{320,192},{... | collective-permute-start | bytes 49160 | tf_op jit(solution)/shard_map/ppermute | solution.py:37
  147.3 1.7 copy.153
  149.8 1.8 add_convert_fusion.1
  151.6 1.9 %collective-permute-start.20 = (bf16[128,1024]{1,0:T(8,128)(2,1)}, bf16[128,1024]{1,0:T(8,128)(2,1)}, u32[]{:S(2)}, u32[]{:S(2)}) collective-permute-start(bf16[128,1024]{1,0:T(8,128)(2,1)} %add_convert_fusion.1), channel_id=1, source_target_pairs={{4,0},{8,4},{12,8},{16,12},{20,16},{24,20},{28,24},{32,28},{36,32}... | collective-permute-start | bytes 786440 | tf_op jit(solution)/shard_map/ppermute | solution.py:60
  153.5 1.7 add_convert_fusion.3
  155.3 2.3 %reduce.12 = bf16[8,8192]{1,0:T(8,128)(2,1)S(1)} reduce(bf16[8,1,8192]{2,1,0:T(2,128)(2,1)} %add_convert_fusion.3, bf16[]{:T(256)} %broadcast.281), dimensions={1}, to_apply=%add_convert_fusion.3.reduce_sub_computation | reduce | bytes 262146 | tf_op jit(solution)/shard_map/jit(cumsum)/reduce_window_sum | solution.py:48
  158.3 4.8 %all-to-all-start.3 = ((bf16[8,2,4096]{2,1,0:T(2,128)(2,1)}), bf16[8,2,4096]{2,1,0:T(2,128)(2,1)}, u32[]{:S(2)}, u32[]{:S(2)}) async-start(bf16[8,2,4096]{2,1,0:T(2,128)(2,1)} %reshape.550), calls=%async_computation.3 | async-start | bytes 262144 | tf_op jit(solution)/shard_map/all_to_all | solution.py:53
  163.1 1.3 convolution_convert_fusion
  165.3 1.8 add_convert_fusion
  167.1 6.7 %collective-permute-start.21 = (bf16[128,1024]{1,0:T(8,128)(2,1)}, bf16[128,1024]{1,0:T(8,128)(2,1)}, u32[]{:S(2)}, u32[]{:S(2)}) collective-permute-start(bf16[128,1024]{1,0:T(8,128)(2,1)} %add_convert_fusion), channel_id=1, source_target_pairs={{4,0},{8,4},{12,8},{16,12},{20,16},{24,20},{28,24},{32,28},{36,32}... | collective-permute-start | bytes 786440 | tf_op jit(solution)/shard_map/ppermute | solution.py:60
  173.8 1.4 reshape.551
  175.1 1.4 reduce.8
  177.5 1.8 fusion.17
  179.6 1.7 copy.155
  (169 shorter events, 37.1 us)
Async XLA Ops:
  0.6 94.5 %copy-start = (bf16[128,512]{1,0:T(8,128)(2,1)S(1)}, bf16[128,512]{1,0:T(8,128)(2,1)}, u32[]{:S(2)}) copy-start(bf16[128,512]{1,0:T(8,128)(2,1)} %param.15) | copy-start | bytes 393220
  0.6 13.4 %copy-start.13 = (bf16[128,512]{1,0:T(8,128)(2,1)S(1)}, bf16[128,512]{1,0:T(8,128)(2,1)}, u32[]{:S(2)}) copy-start(bf16[128,512]{1,0:T(8,128)(2,1)} %param.11) | copy-start | bytes 393220
  0.7 10.7 %copy-start.16 = (bf16[128,512]{1,0:T(8,128)(2,1)S(1)}, bf16[128,512]{1,0:T(8,128)(2,1)}, u32[]{:S(2)}) copy-start(bf16[128,512]{1,0:T(8,128)(2,1)} %param.17) | copy-start | bytes 393220
  0.7 10.7 %copy-start.17 = (bf16[128,512]{1,0:T(8,128)(2,1)S(1)}, bf16[128,512]{1,0:T(8,128)(2,1)}, u32[]{:S(2)}) copy-start(bf16[128,512]{1,0:T(8,128)(2,1)} %param.16) | copy-start | bytes 393220
  0.7 13.2 %copy-start.29 = (s32[1,3]{1,0:T(1,128)S(1)}, s32[1,3]{1,0:T(1,128)}, u32[]{:S(2)}) copy-start(s32[1,3]{1,0:T(1,128)} %param.19) | copy-start | bytes 40
  0.7 13.4 %copy-start.5 = (bf16[128,512]{1,0:T(8,128)(2,1)S(1)}, bf16[128,512]{1,0:T(8,128)(2,1)}, u32[]{:S(2)}) copy-start(bf16[128,512]{1,0:T(8,128)(2,1)} %param.10) | copy-start | bytes 393220
  5.5 12.7 %all-to-all-start = ((bf16[8,2,4096]{2,1,0:T(2,128)(2,1)}), bf16[8,2,4096]{2,1,0:T(2,128)(2,1)S(1)}, u32[]{:S(2)}, u32[]{:S(2)}) async-start(bf16[8,2,4096]{2,1,0:T(2,128)(2,1)} %reshape.544), calls=%async_computation | async-start | bytes 262144 | tf_op jit(solution)/shard_map/all_to_all | solution.py:47
  11.4 47.5 %collective-permute-start.14 = (bf16[128,1024]{1,0:T(8,128)(2,1)S(1)}, bf16[128,1024]{1,0:T(8,128)(2,1)S(1)}, u32[]{:S(2)}, u32[]{:S(2)}) collective-permute-start(bf16[128,1024]{1,0:T(8,128)(2,1)S(1)} %pad_maximum_fusion), channel_id=1, source_target_pairs={{0,4},{4,8},{8,12},{12,16},{16,20},{20,24},{24,28},{28,32},{32,36}... | collective-permute-start | bytes 786440 | tf_op jit(solution)/shard_map/ppermute | solution.py:60
  14.3 44.4 %copy-start.18 = (bf16[4,128,128]{2,1,0:T(8,128)(2,1)}, bf16[4,128,128]{2,1,0:T(8,128)(2,1)S(1)}, u32[]{:S(2)}) copy-start(bf16[4,128,128]{2,1,0:T(8,128)(2,1)S(1)} %fusion.15) | copy-start | bytes 393220
  14.3 44.2 %copy-start.22 = (bf16[128,512]{1,0:T(8,128)(2,1)S(1)}, bf16[128,512]{1,0:T(8,128)(2,1)}, u32[]{:S(2)}) copy-start(bf16[128,512]{1,0:T(8,128)(2,1)} %param.14) | copy-start | bytes 393220
  18.3 40.4 %copy-start.9 = (bf16[128,512]{1,0:T(8,128)(2,1)S(1)}, bf16[128,512]{1,0:T(8,128)(2,1)}, u32[]{:S(2)}) copy-start(bf16[128,512]{1,0:T(8,128)(2,1)} %param.12) | copy-start | bytes 393220
  18.6 19.6 %collective-permute-start.2 = (bf16[8192]{0:T(1024)(128)(2,1)S(1)}, bf16[8192]{0:T(1024)(128)(2,1)S(1)}, u32[]{:S(2)}, u32[]{:S(2)}) collective-permute-start(bf16[8192]{0:T(1024)(128)(2,1)S(1)} %convert_element_type.211), channel_id=1, source_target_pairs={{0,96},{32,128},{64,160},{96,192},{128,224},{160,256},{192,288},{2... | collective-permute-start | bytes 49160 | tf_op jit(solution)/shard_map/ppermute | solution.py:37
  28.8 15.3 %collective-permute-start.1 = (bf16[8192]{0:T(1024)(128)(2,1)S(1)}, bf16[8192]{0:T(1024)(128)(2,1)S(1)}, u32[]{:S(2)}, u32[]{:S(2)}) collective-permute-start(bf16[8192]{0:T(1024)(128)(2,1)S(1)} %convert_element_type.211), channel_id=1, source_target_pairs={{0,64},{32,96},{64,128},{96,160},{128,192},{160,224},{192,256},{22... | collective-permute-start | bytes 49160 | tf_op jit(solution)/shard_map/ppermute | solution.py:37
  33.0 11.1 %collective-permute-start = (bf16[8192]{0:T(1024)(128)(2,1)S(1)}, bf16[8192]{0:T(1024)(128)(2,1)S(1)}, u32[]{:S(2)}, u32[]{:S(2)}) collective-permute-start(bf16[8192]{0:T(1024)(128)(2,1)S(1)} %convert_element_type.211), channel_id=1, source_target_pairs={{0,32},{32,64},{64,96},{96,128},{128,160},{160,192},{192,224},{224... | collective-permute-start | bytes 49160 | tf_op jit(solution)/shard_map/ppermute | solution.py:37
  44.1 6.8 %collective-permute-start.5 = (bf16[8192]{0:T(1024)(128)(2,1)S(1)}, bf16[8192]{0:T(1024)(128)(2,1)S(1)}, u32[]{:S(2)}, u32[]{:S(2)}) collective-permute-start(bf16[8192]{0:T(1024)(128)(2,1)S(1)} %fusion.59), channel_id=1, source_target_pairs={{0,384},{32,416},{64,448},{96,480},{1,385},{33,417},{65,449},{97,4... | collective-permute-start | bytes 49160 | tf_op jit(solution)/shard_map/ppermute | solution.py:37
  45.4 7.1 %collective-permute-start.4 = (bf16[8192]{0:T(1024)(128)(2,1)S(1)}, bf16[8192]{0:T(1024)(128)(2,1)S(1)}, u32[]{:S(2)}, u32[]{:S(2)}) collective-permute-start(bf16[8192]{0:T(1024)(128)(2,1)S(1)} %fusion.59), channel_id=1, source_target_pairs={{0,256},{32,288},{64,320},{96,352},{128,384},{160,416},{192,448},{... | collective-permute-start | bytes 49160 | tf_op jit(solution)/shard_map/ppermute | solution.py:37
  46.7 5.8 %collective-permute-start.3 = (bf16[8192]{0:T(1024)(128)(2,1)S(1)}, bf16[8192]{0:T(1024)(128)(2,1)S(1)}, u32[]{:S(2)}, u32[]{:S(2)}) collective-permute-start(bf16[8192]{0:T(1024)(128)(2,1)S(1)} %fusion.59), channel_id=1, source_target_pairs={{0,128},{32,160},{64,192},{96,224},{128,256},{160,288},{192,320},{... | collective-permute-start | bytes 49160 | tf_op jit(solution)/shard_map/ppermute | solution.py:37
  54.3 11.8 %copy-start.28 = (f32[512]{0:T(512)S(1)}, f32[512]{0:T(512)}, u32[]{:S(2)}) copy-start(f32[512]{0:T(512)} %param.13) | copy-start | bytes 6148
  55.1 10.1 %all-to-all-start.1 = ((bf16[8,2,4096]{2,1,0:T(2,128)(2,1)}), bf16[8,2,4096]{2,1,0:T(2,128)(2,1)S(1)}, u32[]{:S(2)}, u32[]{:S(2)}) async-start(bf16[8,2,4096]{2,1,0:T(2,128)(2,1)} %reshape.546), calls=%async_computation.1 | async-start | bytes 262144 | tf_op jit(solution)/shard_map/all_to_all | solution.py:53
  58.7 18.3 %copy-start.23 = (bf16[128,512]{1,0:T(8,128)(2,1)S(1)}, bf16[128,512]{1,0:T(8,128)(2,1)}, u32[]{:S(2)}) copy-start(bf16[128,512]{1,0:T(8,128)(2,1)} %param.18) | copy-start | bytes 393220
  58.9 10.9 %collective-permute-start.15 = (bf16[128,1024]{1,0:T(8,128)(2,1)S(1)}, bf16[128,1024]{1,0:T(8,128)(2,1)S(1)}, u32[]{:S(2)}, u32[]{:S(2)}) collective-permute-start(bf16[128,1024]{1,0:T(8,128)(2,1)S(1)} %collective-permute-done.14), channel_id=1, source_target_pairs={{0,4},{4,8},{8,12},{12,16},{16,20},{20,24},{24,28},{28,32},{32,36}... | collective-permute-start | bytes 786440 | tf_op jit(solution)/shard_map/ppermute | solution.py:60
  66.1 16.5 %copy-start.7 = (bf16[4,128,128]{2,1,0:T(8,128)(2,1)}, bf16[4,128,128]{2,1,0:T(8,128)(2,1)S(1)}, u32[]{:S(2)}) copy-start(bf16[4,128,128]{2,1,0:T(8,128)(2,1)S(1)} %reshape.495) | copy-start | bytes 393220
  66.4 5.5 %collective-permute-start.6 = (f32[2,128]{1,0:T(2,128)S(1)}, f32[2,128]{1,0:T(2,128)S(1)}, u32[]{:S(2)}, u32[]{:S(2)}) collective-permute-start(f32[2,128]{1,0:T(2,128)S(1)} %pad_maximum_fusion.2), channel_id=1, source_target_pairs={{0,1},{1,0},{2,3},{3,2},{4,5},{5,4},{6,7},{7,6},{8,9},{9,8},{10,11... | collective-permute-start | bytes 3080 | tf_op jit(solution)/shard_map/ppermute | solution.py:166
  69.9 9.8 %collective-permute-start.16 = (bf16[128,1024]{1,0:T(8,128)(2,1)S(1)}, bf16[128,1024]{1,0:T(8,128)(2,1)S(1)}, u32[]{:S(2)}, u32[]{:S(2)}) collective-permute-start(bf16[128,1024]{1,0:T(8,128)(2,1)S(1)} %collective-permute-done.15), channel_id=1, source_target_pairs={{0,4},{4,8},{8,12},{12,16},{16,20},{20,24},{24,28},{28,32},{32,36}... | collective-permute-start | bytes 786440 | tf_op jit(solution)/shard_map/ppermute | solution.py:60
  71.9 9.7 %collective-permute-start.7 = (f32[2,128]{1,0:T(2,128)S(1)}, f32[2,128]{1,0:T(2,128)S(1)}, u32[]{:S(2)}, u32[]{:S(2)}) collective-permute-start(f32[2,128]{1,0:T(2,128)S(1)} %fusion.78), channel_id=1, source_target_pairs={{0,2},{1,3},{2,0},{3,1},{4,6},{5,7},{6,4},{7,5},{8,10},{9,11},{10,... | collective-permute-start | bytes 3080 | tf_op jit(solution)/shard_map/ppermute | solution.py:166
  79.7 10.4 %collective-permute-start.17 = (bf16[128,1024]{1,0:T(8,128)(2,1)S(1)}, bf16[128,1024]{1,0:T(8,128)(2,1)}, u32[]{:S(2)}, u32[]{:S(2)}) collective-permute-start(bf16[128,1024]{1,0:T(8,128)(2,1)S(1)} %collective-permute-done.16), channel_id=1, source_target_pairs={{0,4},{4,8},{8,12},{12,16},{16,20},{20,24},{24,28},{28,32},{32,36}... | collective-permute-start | bytes 786440 | tf_op jit(solution)/shard_map/ppermute | solution.py:60
  84.9 31.0 %all-to-all-start.2 = ((bf16[8,2,4096]{2,1,0:T(2,128)(2,1)}), bf16[8,2,4096]{2,1,0:T(2,128)(2,1)}, u32[]{:S(2)}, u32[]{:S(2)}) async-start(bf16[8,2,4096]{2,1,0:T(2,128)(2,1)} %reshape.548), calls=%async_computation.2 | async-start | bytes 262144 | tf_op jit(solution)/shard_map/all_to_all | solution.py:47
  107.1 7.9 %copy-start.3 = (bf16[128,4,128]{0,2,1:T(8,128)(2,1)S(1)}, bf16[128,4,128]{0,2,1:T(8,128)(2,1)}, u32[]{:S(2)}) copy-start(bf16[128,4,128]{0,2,1:T(8,128)(2,1)} %copy-done.2) | copy-start | bytes 393220
  107.1 7.9 %copy-start.8 = (bf16[4,128,128]{2,1,0:T(8,128)(2,1)S(1)}, bf16[4,128,128]{2,1,0:T(8,128)(2,1)}, u32[]{:S(2)}) copy-start(bf16[4,128,128]{2,1,0:T(8,128)(2,1)} %copy-done.7) | copy-start | bytes 393220
  107.1 7.9 %copy-start.11 = (f32[128,4,128]{0,2,1:T(8,128)S(1)}, f32[128,4,128]{0,2,1:T(8,128)}, u32[]{:S(2)}) copy-start(f32[128,4,128]{0,2,1:T(8,128)} %convolution_bitcast_fusion.6) | copy-start | bytes 786436
  108.7 27.2 %collective-permute-start.18 = (bf16[128,1024]{1,0:T(8,128)(2,1)}, bf16[128,1024]{1,0:T(8,128)(2,1)}, u32[]{:S(2)}, u32[]{:S(2)}) collective-permute-start(bf16[128,1024]{1,0:T(8,128)(2,1)} %pad_maximum_fusion.1), channel_id=1, source_target_pairs={{4,0},{8,4},{12,8},{16,12},{20,16},{24,20},{28,24},{32,28},{36,32}... | collective-permute-start | bytes 786440 | tf_op jit(solution)/shard_map/ppermute | solution.py:60
  117.3 29.1 %copy-start.4 = (bf16[128,4,128]{0,2,1:T(8,128)(2,1)S(1)}, bf16[128,4,128]{0,2,1:T(8,128)(2,1)}, u32[]{:S(2)}) copy-start(bf16[128,4,128]{0,2,1:T(8,128)(2,1)} %copy-done.2) | copy-start | bytes 393220
  117.3 29.1 %copy-start.19 = (bf16[4,128,128]{2,1,0:T(8,128)(2,1)S(1)}, bf16[4,128,128]{2,1,0:T(8,128)(2,1)}, u32[]{:S(2)}) copy-start(bf16[4,128,128]{2,1,0:T(8,128)(2,1)} %copy-done.18) | copy-start | bytes 393220
  117.6 29.7 %copy-start.12 = (f32[8192]{0:T(1024)}, f32[8192]{0:T(1024)S(1)}, u32[]{:S(2)}) copy-start(f32[8192]{0:T(1024)S(1)} %convert_reduce_fusion) | copy-start | bytes 98308
  117.6 22.0 %collective-permute-start.10 = (bf16[8192]{0:T(1024)(128)(2,1)S(1)}, bf16[8192]{0:T(1024)(128)(2,1)S(1)}, u32[]{:S(2)}, u32[]{:S(2)}) collective-permute-start(bf16[8192]{0:T(1024)(128)(2,1)S(1)} %convert_element_type.227), channel_id=1, source_target_pairs={{96,0},{128,32},{160,64},{192,96},{224,128},{256,160},{288,192},{3... | collective-permute-start | bytes 49160 | tf_op jit(solution)/shard_map/ppermute | solution.py:37
  123.0 16.6 %collective-permute-start.9 = (bf16[8192]{0:T(1024)(128)(2,1)S(1)}, bf16[8192]{0:T(1024)(128)(2,1)S(1)}, u32[]{:S(2)}, u32[]{:S(2)}) collective-permute-start(bf16[8192]{0:T(1024)(128)(2,1)S(1)} %convert_element_type.227), channel_id=1, source_target_pairs={{64,0},{96,32},{128,64},{160,96},{192,128},{224,160},{256,192},{28... | collective-permute-start | bytes 49160 | tf_op jit(solution)/shard_map/ppermute | solution.py:37
  130.4 9.7 %collective-permute-start.8 = (bf16[8192]{0:T(1024)(128)(2,1)S(1)}, bf16[8192]{0:T(1024)(128)(2,1)S(1)}, u32[]{:S(2)}, u32[]{:S(2)}) collective-permute-start(bf16[8192]{0:T(1024)(128)(2,1)S(1)} %convert_element_type.227), channel_id=1, source_target_pairs={{32,0},{64,32},{96,64},{128,96},{160,128},{192,160},{224,192},{256... | collective-permute-start | bytes 49160 | tf_op jit(solution)/shard_map/ppermute | solution.py:37
  137.7 12.1 %collective-permute-start.19 = (bf16[128,1024]{1,0:T(8,128)(2,1)}, bf16[128,1024]{1,0:T(8,128)(2,1)}, u32[]{:S(2)}, u32[]{:S(2)}) collective-permute-start(bf16[128,1024]{1,0:T(8,128)(2,1)} %add_convert_fusion.2), channel_id=1, source_target_pairs={{4,0},{8,4},{12,8},{16,12},{20,16},{24,20},{28,24},{32,28},{36,32}... | collective-permute-start | bytes 786440 | tf_op jit(solution)/shard_map/ppermute | solution.py:60
  140.8 8.2 %collective-permute-start.13 = (bf16[8192]{0:T(1024)(128)(2,1)}, bf16[8192]{0:T(1024)(128)(2,1)}, u32[]{:S(2)}, u32[]{:S(2)}) collective-permute-start(bf16[8192]{0:T(1024)(128)(2,1)} %fusion.60), channel_id=1, source_target_pairs={{384,0},{416,32},{448,64},{480,96},{385,1},{417,33},{449,65},{481,... | collective-permute-start | bytes 49160 | tf_op jit(solution)/shard_map/ppermute | solution.py:37
  142.7 6.3 %collective-permute-start.12 = (bf16[8192]{0:T(1024)(128)(2,1)}, bf16[8192]{0:T(1024)(128)(2,1)}, u32[]{:S(2)}, u32[]{:S(2)}) collective-permute-start(bf16[8192]{0:T(1024)(128)(2,1)} %fusion.60), channel_id=1, source_target_pairs={{256,0},{288,32},{320,64},{352,96},{384,128},{416,160},{448,192},{... | collective-permute-start | bytes 49160 | tf_op jit(solution)/shard_map/ppermute | solution.py:37
  144.5 4.4 %collective-permute-start.11 = (bf16[8192]{0:T(1024)(128)(2,1)}, bf16[8192]{0:T(1024)(128)(2,1)}, u32[]{:S(2)}, u32[]{:S(2)}) collective-permute-start(bf16[8192]{0:T(1024)(128)(2,1)} %fusion.60), channel_id=1, source_target_pairs={{128,0},{160,32},{192,64},{224,96},{256,128},{288,160},{320,192},{... | collective-permute-start | bytes 49160 | tf_op jit(solution)/shard_map/ppermute | solution.py:37
  151.6 13.6 %collective-permute-start.20 = (bf16[128,1024]{1,0:T(8,128)(2,1)}, bf16[128,1024]{1,0:T(8,128)(2,1)}, u32[]{:S(2)}, u32[]{:S(2)}) collective-permute-start(bf16[128,1024]{1,0:T(8,128)(2,1)} %add_convert_fusion.1), channel_id=1, source_target_pairs={{4,0},{8,4},{12,8},{16,12},{20,16},{24,20},{28,24},{32,28},{36,32}... | collective-permute-start | bytes 786440 | tf_op jit(solution)/shard_map/ppermute | solution.py:60
  155.3 10.0 %copy-start.20 = (bf16[128,512]{1,0:T(8,128)(2,1)S(1)}, bf16[128,512]{1,0:T(8,128)(2,1)}, u32[]{:S(2)}) copy-start(bf16[128,512]{1,0:T(8,128)(2,1)} %get-tuple-element.38) | copy-start | bytes 393220
  158.3 15.4 %all-to-all-start.3 = ((bf16[8,2,4096]{2,1,0:T(2,128)(2,1)}), bf16[8,2,4096]{2,1,0:T(2,128)(2,1)}, u32[]{:S(2)}, u32[]{:S(2)}) async-start(bf16[8,2,4096]{2,1,0:T(2,128)(2,1)} %reshape.550), calls=%async_computation.3 | async-start | bytes 262144 | tf_op jit(solution)/shard_map/all_to_all | solution.py:53
  164.5 13.1 %copy-start.14 = (bf16[128,512]{1,0:T(8,128)(2,1)S(1)}, bf16[128,512]{1,0:T(8,128)(2,1)}, u32[]{:S(2)}) copy-start(bf16[128,512]{1,0:T(8,128)(2,1)} %param.11) | copy-start | bytes 393220
  165.3 14.1 %copy-start.10 = (bf16[128,512]{1,0:T(8,128)(2,1)S(1)}, bf16[128,512]{1,0:T(8,128)(2,1)}, u32[]{:S(2)}) copy-start(bf16[128,512]{1,0:T(8,128)(2,1)} %param.12) | copy-start | bytes 393220
  167.1 14.2 %copy-start.6 = (bf16[128,512]{1,0:T(8,128)(2,1)S(1)}, bf16[128,512]{1,0:T(8,128)(2,1)}, u32[]{:S(2)}) copy-start(bf16[128,512]{1,0:T(8,128)(2,1)} %param.10) | copy-start | bytes 393220
  167.1 16.1 %collective-permute-start.21 = (bf16[128,1024]{1,0:T(8,128)(2,1)}, bf16[128,1024]{1,0:T(8,128)(2,1)}, u32[]{:S(2)}, u32[]{:S(2)}) collective-permute-start(bf16[128,1024]{1,0:T(8,128)(2,1)} %add_convert_fusion), channel_id=1, source_target_pairs={{4,0},{8,4},{12,8},{16,12},{20,16},{24,20},{28,24},{32,28},{36,32}... | collective-permute-start | bytes 786440 | tf_op jit(solution)/shard_map/ppermute | solution.py:60
  (9 other events, 33.9 us)

commit v10 on v9

--- a/solution.py
+++ b/solution.py
@@ -41,6 +41,16 @@
     return total - own
 
 
+def gathered_before(total, axis, backward):
+    count = lax.axis_size(axis)
+    sent = jnp.broadcast_to(total.astype(jnp.bfloat16)[None], (count,) + total.shape)
+    got = lax.all_to_all(sent, axis, 0, 0, tiled=True).astype(jnp.float32)
+    index = jnp.arange(count)
+    place = lax.axis_index(axis)
+    mask = index > place if backward else index < place
+    return jnp.sum(jnp.where(mask.reshape((-1,) + (1,) * total.ndim), got, 0.0), axis=0)
+
+
 def carried_in(shard, backward):
     members = lax.axis_size("inner")
     slices = shard.astype(jnp.bfloat16).reshape(members, -1)
@@ -48,7 +58,7 @@
     running = jnp.cumsum(mine, axis=0)
     group = jnp.sum(mine, axis=0)
     within = group[None] - running if backward else running - mine
-    earlier = scan_over(group, "outer", backward)
+    earlier = gathered_before(group, "outer", backward)
     states = (within + earlier[None]).astype(jnp.bfloat16)
     back = lax.all_to_all(states, "inner", 0, 0, tiled=True)
     return back.reshape(shard.shape).astype(shard.dtype)
@@ -161,10 +171,8 @@
     cross_sum = jnp.sum(gain_grad * output_lin, axis=(1, 2))
     sums = jnp.stack([square_sum, cross_sum])
     heads_dev = lax.axis_size("head")
-    step = 1
-    while step < heads_dev:
-        sums = sums + lax.ppermute(sums, "head", [(i, i ^ step) for i in range(heads_dev)])
-        step *= 2
+    spread = jnp.broadcast_to(sums[None], (heads_dev,) + sums.shape)
+    sums = jnp.sum(lax.all_to_all(spread, "head", 0, 0, tiled=True), axis=0)
     square_sum, cross_sum = sums[0], sums[1]
     full_width = LIN_HEADS * HEAD
     inv_rms = lax.rsqrt(square_sum / full_width + 1e-06)[:, None, None]

time: 187 us -> 209 us (1.12)
  the two profiles are of different devices: /device:TPU:24 before, /device:TPU:1 now
where the time goes in v10:
time: 209 us; the launch traced here: 207 us
  starting transfers between devices  89.4 us (43%)
  local copies, waits for them, and re-layouts  45.3 us (22%)
  other arithmetic  38.8 us (19%)
  waiting for transfers between devices  18.9 us (9%)
  matrix products  13.2 us (6%)
    unnamed x90, local copies, waits for them, and re-layouts  26.4 us
    ppermute x8, starting transfers between devices, from_behind(): return lax.ppermute(shard, axis, pairs)  25.8 us
    all_to_all x2, starting transfers between devices, gathered_before(): got = lax.all_to_all(sent, axis, 0, 0, tiled=True).astype(jnp.float32)  21.4 us
    all_to_all x2, starting transfers between devices, carried_in(): back = lax.all_to_all(states, 'inner', 0, 0, tiled=True)  21.2 us
    all_to_all x2, starting transfers between devices, carried_in(): mine = lax.all_to_all(slices, 'inner', 0, 0, tiled=True).astype(jnp.float32)  17 us
    ppermute x8, waiting for transfers between devices, from_behind(): return lax.ppermute(shard, axis, pairs)  7.29 us
    all_to_all x2, waiting for transfers between devices, gathered_before(): got = lax.all_to_all(sent, axis, 0, 0, tiled=True).astype(jnp.float32)  7.07 us
    convert_element_type x4, other arithmetic, per_device(): owed = from_behind(owed.astype(jnp.bfloat16), CTX, -1).astype(jnp.float32)  6.41 us
  transfers between devices with their start and end apart: 15, of which 8 were waited for; matrix products, arithmetic and copies ran while one was open for 37% of the time, Pallas kernels for 0%

profile of v10, /device:TPU:1, one launch (start us, length us, event | category | flops | bytes accessed | tf_op | source)
XLA Modules:
  0.0 207.1 jit_solution(8341160028636032877)
XLA Ops:
  3.6 1.4 reduce.10
  5.7 10.2 %all-to-all-start = ((bf16[8,2,4096]{2,1,0:T(2,128)(2,1)}), bf16[8,2,4096]{2,1,0:T(2,128)(2,1)S(1)}, u32[]{:S(2)}, u32[]{:S(2)}) async-start(bf16[8,2,4096]{2,1,0:T(2,128)(2,1)} %reshape.575), calls=%async_computation | async-start | bytes 262144 | tf_op jit(solution)/shard_map/all_to_all | solution.py:57
  15.9 3.5 %collective-permute-start = (bf16[128,1024]{1,0:T(8,128)(2,1)S(1)}, bf16[128,1024]{1,0:T(8,128)(2,1)S(1)}, u32[]{:S(2)}, u32[]{:S(2)}) collective-permute-start(bf16[128,1024]{1,0:T(8,128)(2,1)S(1)} %pad_maximum_fusion), channel_id=1, source_target_pairs={{0,4},{4,8},{8,12},{12,16},{16,20},{20,24},{24,28},{28,32},{32,36}... | collective-permute-start | bytes 786440 | tf_op jit(solution)/shard_map/ppermute | solution.py:70
  20.6 2.2 %collective-permute-done = bf16[128,1024]{1,0:T(8,128)(2,1)S(1)} collective-permute-done((bf16[128,1024]{1,0:T(8,128)(2,1)S(1)}, bf16[128,1024]{1,0:T(8,128)(2,1)S(1)}, u32[]{:S(2)}, u32[]{:S(2)}) %collective-permute-start) | collective-permute-done | bytes 262176 | tf_op jit(solution)/shard_map/ppermute | solution.py:70
  22.8 4.4 %collective-permute-start.1 = (bf16[128,1024]{1,0:T(8,128)(2,1)S(1)}, bf16[128,1024]{1,0:T(8,128)(2,1)S(1)}, u32[]{:S(2)}, u32[]{:S(2)}) collective-permute-start(bf16[128,1024]{1,0:T(8,128)(2,1)S(1)} %collective-permute-done), channel_id=1, source_target_pairs={{0,4},{4,8},{8,12},{12,16},{16,20},{20,24},{24,28},{28,32},{32,36}... | collective-permute-start | bytes 786440 | tf_op jit(solution)/shard_map/ppermute | solution.py:70
  27.4 3.0 %collective-permute-done.1 = bf16[128,1024]{1,0:T(8,128)(2,1)S(1)} collective-permute-done((bf16[128,1024]{1,0:T(8,128)(2,1)S(1)}, bf16[128,1024]{1,0:T(8,128)(2,1)S(1)}, u32[]{:S(2)}, u32[]{:S(2)}) %collective-permute-start.1) | collective-permute-done | bytes 262176 | tf_op jit(solution)/shard_map/ppermute | solution.py:70
  30.4 4.4 %collective-permute-start.2 = (bf16[128,1024]{1,0:T(8,128)(2,1)S(1)}, bf16[128,1024]{1,0:T(8,128)(2,1)S(1)}, u32[]{:S(2)}, u32[]{:S(2)}) collective-permute-start(bf16[128,1024]{1,0:T(8,128)(2,1)S(1)} %collective-permute-done.1), channel_id=1, source_target_pairs={{0,4},{4,8},{8,12},{12,16},{16,20},{20,24},{24,28},{28,32},{32,36}... | collective-permute-start | bytes 786440 | tf_op jit(solution)/shard_map/ppermute | solution.py:70
  36.0 2.1 %collective-permute-done.2 = bf16[128,1024]{1,0:T(8,128)(2,1)S(1)} collective-permute-done((bf16[128,1024]{1,0:T(8,128)(2,1)S(1)}, bf16[128,1024]{1,0:T(8,128)(2,1)S(1)}, u32[]{:S(2)}, u32[]{:S(2)}) %collective-permute-start.2) | collective-permute-done | bytes 262176 | tf_op jit(solution)/shard_map/ppermute | solution.py:70
  38.1 4.4 %collective-permute-start.3 = (bf16[128,1024]{1,0:T(8,128)(2,1)S(1)}, bf16[128,1024]{1,0:T(8,128)(2,1)}, u32[]{:S(2)}, u32[]{:S(2)}) collective-permute-start(bf16[128,1024]{1,0:T(8,128)(2,1)S(1)} %collective-permute-done.2), channel_id=1, source_target_pairs={{0,4},{4,8},{8,12},{12,16},{16,20},{20,24},{24,28},{28,32},{32,36}... | collective-permute-start | bytes 786440 | tf_op jit(solution)/shard_map/ppermute | solution.py:70
  45.8 2.2 %reduce.11 = bf16[16,8192]{1,0:T(8,128)(2,1)S(1)} reduce(bf16[16,1,8192]{2,1,0:T(2,128)(2,1)S(1)} %broadcast_in_dim.106, bf16[]{:T(256)} %broadcast.298), dimensions={1}, to_apply=%broadcast_in_dim.106.reduce_sub_computation | reduce | bytes 524290 | tf_op jit(solution)/shard_map/broadcast_in_dim | solution.py:46
  48.9 12.2 %all-to-all-start.1 = ((bf16[16,2,4096]{2,1,0:T(2,128)(2,1)}), bf16[16,2,4096]{2,1,0:T(2,128)(2,1)}, u32[]{:S(2)}, u32[]{:S(2)}) async-start(bf16[16,2,4096]{2,1,0:T(2,128)(2,1)} %reshape.577), calls=%async_computation.1 | async-start | bytes 524288 | tf_op jit(solution)/shard_map/all_to_all | solution.py:47
  64.0 1.6 reshape.526
  72.8 1.3 scatter_fusion.1
  77.0 1.7 all-to-all-done.1
  78.7 2.2 %reshape.578 = bf16[16,1,8192]{2,1,0:T(2,128)(2,1)S(1)} reshape(bf16[16,2,4096]{2,1,0:T(2,128)(2,1)} %all-to-all-done.1) | data formatting | bytes 524288
  82.9 1.4 reduce.12
  85.0 10.0 %all-to-all-start.2 = ((bf16[8,2,4096]{2,1,0:T(2,128)(2,1)}), bf16[8,2,4096]{2,1,0:T(2,128)(2,1)}, u32[]{:S(2)}, u32[]{:S(2)}) async-start(bf16[8,2,4096]{2,1,0:T(2,128)(2,1)} %reshape.579), calls=%async_computation.2 | async-start | bytes 262144 | tf_op jit(solution)/shard_map/all_to_all | solution.py:63
  96.0 1.4 reshape.559
  97.5 2.4 %scatter_fusion = f32[5,128,512]{2,1,0:T(8,128)S(1)} fusion(f32[5,128,512]{2,1,0:T(8,128)S(1)} %broadcast.265.clone.1, s32[4]{0:T(128)} %fusion.72, f32[4,128,512]{2,1,0:T(8,128)} %reshape.559), kind=kCustom, calls=%fused_computation.2 | custom fusion | flops 262144 | bytes 3145744 | tf_op jit(solution)/shard_map/scatter-add | solution.py:132
  101.6 2.1 %collective-permute-start.4 = (bf16[128,1024]{1,0:T(8,128)(2,1)}, bf16[128,1024]{1,0:T(8,128)(2,1)}, u32[]{:S(2)}, u32[]{:S(2)}) collective-permute-start(bf16[128,1024]{1,0:T(8,128)(2,1)} %pad_maximum_fusion.1), channel_id=1, source_target_pairs={{4,0},{8,4},{12,8},{16,12},{20,16},{24,20},{28,24},{32,28},{36,32}... | collective-permute-start | bytes 786440 | tf_op jit(solution)/shard_map/ppermute | solution.py:70
  103.7 2.0 reshape.580
  105.7 2.4 %reduce.8 = bf16[8,8192]{1,0:T(8,128)(2,1)} reduce(bf16[8,1,8192]{2,1,0:T(2,128)(2,1)} %reshape.580, bf16[]{:T(256)} %constant.89), dimensions={1}, to_apply=%all_to_all.34.reduce_sub_computation | reduce | bytes 262146 | tf_op jit(solution)/shard_map/all_to_all | solution.py:63
  108.1 1.6 reshape.524
  109.7 2.1 multiply_reduce_fusion.1
  112.4 4.0 %all-to-all-start.3 = ((f32[4,2,128]{2,1,0:T(2,128)}), f32[4,2,128]{2,1,0:T(2,128)}, u32[]{:S(2)}, u32[]{:S(2)}) async-start(f32[4,2,128]{2,1,0:T(2,128)} %broadcast_in_dim.108), calls=%async_computation.3 | async-start | bytes 8192 | tf_op jit(solution)/shard_map/all_to_all | solution.py:175
  116.4 1.8 add_convert_fusion.2
  118.2 1.9 collective-permute-start.5
  127.8 2.0 reduce.13
  129.9 1.6 reshape.581
  131.5 6.8 %all-to-all-start.4 = ((bf16[8,2,4096]{2,1,0:T(2,128)(2,1)}), bf16[8,2,4096]{2,1,0:T(2,128)(2,1)}, u32[]{:S(2)}, u32[]{:S(2)}) async-start(bf16[8,2,4096]{2,1,0:T(2,128)(2,1)} %reshape.581), calls=%async_computation.4 | async-start | bytes 262144 | tf_op jit(solution)/shard_map/all_to_all | solution.py:57
  138.8 1.8 add_convert_fusion.1
  140.6 1.9 collective-permute-start.6
  142.6 1.7 all-to-all-done.4
  144.3 1.4 reshape.582
  147.7 3.9 %reduce.14 = bf16[16,8192]{1,0:T(8,128)(2,1)} reduce(bf16[16,1,8192]{2,1,0:T(2,128)(2,1)} %broadcast_in_dim.110, bf16[]{:T(256)} %broadcast.298), dimensions={1}, to_apply=%broadcast_in_dim.110.reduce_sub_computation | reduce | bytes 524290 | tf_op jit(solution)/shard_map/broadcast_in_dim | solution.py:46
  151.6 1.8 reshape.583
  153.5 9.2 %all-to-all-start.5 = ((bf16[16,2,4096]{2,1,0:T(2,128)(2,1)}), bf16[16,2,4096]{2,1,0:T(2,128)(2,1)}, u32[]{:S(2)}, u32[]{:S(2)}) async-start(bf16[16,2,4096]{2,1,0:T(2,128)(2,1)} %reshape.583), calls=%async_computation.5 | async-start | bytes 524288 | tf_op jit(solution)/shard_map/all_to_all | solution.py:47
  162.7 2.0 convolution_convert_fusion
  164.7 1.7 copy.235
  166.4 1.8 add_convert_fusion
  168.2 3.2 %collective-permute-start.7 = (bf16[128,1024]{1,0:T(8,128)(2,1)}, bf16[128,1024]{1,0:T(8,128)(2,1)}, u32[]{:S(2)}, u32[]{:S(2)}) collective-permute-start(bf16[128,1024]{1,0:T(8,128)(2,1)} %add_convert_fusion), channel_id=1, source_target_pairs={{4,0},{8,4},{12,8},{16,12},{20,16},{24,20},{28,24},{32,28},{36,32}... | collective-permute-start | bytes 786440 | tf_op jit(solution)/shard_map/ppermute | solution.py:70
  173.8 5.4 %all-to-all-done.5 = bf16[16,2,4096]{2,1,0:T(2,128)(2,1)} async-done(((bf16[16,2,4096]{2,1,0:T(2,128)(2,1)}), bf16[16,2,4096]{2,1,0:T(2,128)(2,1)}, u32[]{:S(2)}, u32[]{:S(2)}) %all-to-all-start.5) | async-done | bytes 262176 | tf_op jit(solution)/shard_map/all_to_all | solution.py:47
  179.2 2.2 %reshape.584 = bf16[16,1,8192]{2,1,0:T(2,128)(2,1)S(1)} reshape(bf16[16,2,4096]{2,1,0:T(2,128)(2,1)} %all-to-all-done.5) | data formatting | bytes 524288
  183.4 1.4 reduce.15
  185.5 11.2 %all-to-all-start.6 = ((bf16[8,2,4096]{2,1,0:T(2,128)(2,1)}), bf16[8,2,4096]{2,1,0:T(2,128)(2,1)}, u32[]{:S(2)}, u32[]{:S(2)}) async-start(bf16[8,2,4096]{2,1,0:T(2,128)(2,1)} %reshape.585), calls=%async_computation.6 | async-start | bytes 262144 | tf_op jit(solution)/shard_map/all_to_all | solution.py:63
  196.7 1.8 fusion.83
  200.2 2.3 %all-to-all-done.6 = bf16[8,2,4096]{2,1,0:T(2,128)(2,1)} async-done(((bf16[8,2,4096]{2,1,0:T(2,128)(2,1)}), bf16[8,2,4096]{2,1,0:T(2,128)(2,1)}, u32[]{:S(2)}, u32[]{:S(2)}) %all-to-all-start.6) | async-done | bytes 131104 | tf_op jit(solution)/shard_map/all_to_all | solution.py:63
  202.6 1.4 reshape.586
  (163 shorter events, 49.3 us)
Async XLA Ops:
  0.6 69.0 %copy-start = (bf16[128,512]{1,0:T(8,128)(2,1)S(1)}, bf16[128,512]{1,0:T(8,128)(2,1)}, u32[]{:S(2)}) copy-start(bf16[128,512]{1,0:T(8,128)(2,1)} %param.15) | copy-start | bytes 393220
  0.6 26.5 %copy-start.14 = (bf16[128,512]{1,0:T(8,128)(2,1)S(1)}, bf16[128,512]{1,0:T(8,128)(2,1)}, u32[]{:S(2)}) copy-start(bf16[128,512]{1,0:T(8,128)(2,1)} %param.11) | copy-start | bytes 393220
  0.7 15.2 %copy-start.19 = (bf16[128,512]{1,0:T(8,128)(2,1)S(1)}, bf16[128,512]{1,0:T(8,128)(2,1)}, u32[]{:S(2)}) copy-start(bf16[128,512]{1,0:T(8,128)(2,1)} %param.17) | copy-start | bytes 393220
  0.7 15.2 %copy-start.20 = (bf16[128,512]{1,0:T(8,128)(2,1)S(1)}, bf16[128,512]{1,0:T(8,128)(2,1)}, u32[]{:S(2)}) copy-start(bf16[128,512]{1,0:T(8,128)(2,1)} %param.16) | copy-start | bytes 393220
  0.7 18.8 %copy-start.30 = (s32[1,3]{1,0:T(1,128)S(1)}, s32[1,3]{1,0:T(1,128)}, u32[]{:S(2)}) copy-start(s32[1,3]{1,0:T(1,128)} %param.19) | copy-start | bytes 40
  0.7 26.5 %copy-start.5 = (bf16[128,512]{1,0:T(8,128)(2,1)S(1)}, bf16[128,512]{1,0:T(8,128)(2,1)}, u32[]{:S(2)}) copy-start(bf16[128,512]{1,0:T(8,128)(2,1)} %param.10) | copy-start | bytes 393220
  1.8 25.6 %copy-start.8 = (bf16[128,512]{0,1:T(8,128)(2,1)}, bf16[128,512]{0,1:T(8,128)(2,1)S(1)}, u32[]{:S(2)}) copy-start(bf16[128,512]{0,1:T(8,128)(2,1)S(1)} %copy.321) | copy-start | bytes 393220
  3.0 40.1 %copy-start.26 = (bf16[128,512]{1,0:T(8,128)(2,1)S(1)}, bf16[128,512]{1,0:T(8,128)(2,1)}, u32[]{:S(2)}) copy-start(bf16[128,512]{1,0:T(8,128)(2,1)} %param.14) | copy-start | bytes 393220
  3.0 40.2 %copy-start.27 = (bf16[128,512]{1,0:T(8,128)(2,1)S(1)}, bf16[128,512]{1,0:T(8,128)(2,1)}, u32[]{:S(2)}) copy-start(bf16[128,512]{1,0:T(8,128)(2,1)} %param.18) | copy-start | bytes 393220
  5.0 39.0 %copy-start.10 = (bf16[128,512]{1,0:T(8,128)(2,1)S(1)}, bf16[128,512]{1,0:T(8,128)(2,1)}, u32[]{:S(2)}) copy-start(bf16[128,512]{1,0:T(8,128)(2,1)} %param.12) | copy-start | bytes 393220
  5.7 39.2 %all-to-all-start = ((bf16[8,2,4096]{2,1,0:T(2,128)(2,1)}), bf16[8,2,4096]{2,1,0:T(2,128)(2,1)S(1)}, u32[]{:S(2)}, u32[]{:S(2)}) async-start(bf16[8,2,4096]{2,1,0:T(2,128)(2,1)} %reshape.575), calls=%async_computation | async-start | bytes 262144 | tf_op jit(solution)/shard_map/all_to_all | solution.py:57
  15.9 6.8 %collective-permute-start = (bf16[128,1024]{1,0:T(8,128)(2,1)S(1)}, bf16[128,1024]{1,0:T(8,128)(2,1)S(1)}, u32[]{:S(2)}, u32[]{:S(2)}) collective-permute-start(bf16[128,1024]{1,0:T(8,128)(2,1)S(1)} %pad_maximum_fusion), channel_id=1, source_target_pairs={{0,4},{4,8},{8,12},{12,16},{16,20},{20,24},{24,28},{28,32},{32,36}... | collective-permute-start | bytes 786440 | tf_op jit(solution)/shard_map/ppermute | solution.py:70
  22.8 7.7 %collective-permute-start.1 = (bf16[128,1024]{1,0:T(8,128)(2,1)S(1)}, bf16[128,1024]{1,0:T(8,128)(2,1)S(1)}, u32[]{:S(2)}, u32[]{:S(2)}) collective-permute-start(bf16[128,1024]{1,0:T(8,128)(2,1)S(1)} %collective-permute-done), channel_id=1, source_target_pairs={{0,4},{4,8},{8,12},{12,16},{16,20},{20,24},{24,28},{28,32},{32,36}... | collective-permute-start | bytes 786440 | tf_op jit(solution)/shard_map/ppermute | solution.py:70
  27.4 20.5 %copy-start.21 = (bf16[4,128,128]{2,1,0:T(8,128)(2,1)}, bf16[4,128,128]{2,1,0:T(8,128)(2,1)S(1)}, u32[]{:S(2)}) copy-start(bf16[4,128,128]{2,1,0:T(8,128)(2,1)S(1)} %fusion.19) | copy-start | bytes 393220
  30.4 7.7 %collective-permute-start.2 = (bf16[128,1024]{1,0:T(8,128)(2,1)S(1)}, bf16[128,1024]{1,0:T(8,128)(2,1)S(1)}, u32[]{:S(2)}, u32[]{:S(2)}) collective-permute-start(bf16[128,1024]{1,0:T(8,128)(2,1)S(1)} %collective-permute-done.1), channel_id=1, source_target_pairs={{0,4},{4,8},{8,12},{12,16},{16,20},{20,24},{24,28},{28,32},{32,36}... | collective-permute-start | bytes 786440 | tf_op jit(solution)/shard_map/ppermute | solution.py:70
  38.1 9.8 %copy-start.25 = (bf16[128,1024]{1,0:T(8,128)(2,1)}, bf16[128,1024]{1,0:T(8,128)(2,1)S(1)}, u32[]{:S(2)}) copy-start(bf16[128,1024]{1,0:T(8,128)(2,1)S(1)} %collective-permute-done.2) | copy-start | bytes 786436
  38.1 23.0 %collective-permute-start.3 = (bf16[128,1024]{1,0:T(8,128)(2,1)S(1)}, bf16[128,1024]{1,0:T(8,128)(2,1)}, u32[]{:S(2)}, u32[]{:S(2)}) collective-permute-start(bf16[128,1024]{1,0:T(8,128)(2,1)S(1)} %collective-permute-done.2), channel_id=1, source_target_pairs={{0,4},{4,8},{8,12},{12,16},{16,20},{20,24},{24,28},{28,32},{32,36}... | collective-permute-start | bytes 786440 | tf_op jit(solution)/shard_map/ppermute | solution.py:70
  48.9 29.8 %all-to-all-start.1 = ((bf16[16,2,4096]{2,1,0:T(2,128)(2,1)}), bf16[16,2,4096]{2,1,0:T(2,128)(2,1)}, u32[]{:S(2)}, u32[]{:S(2)}) async-start(bf16[16,2,4096]{2,1,0:T(2,128)(2,1)} %reshape.577), calls=%async_computation.1 | async-start | bytes 524288 | tf_op jit(solution)/shard_map/all_to_all | solution.py:47
  63.2 0.8 copy-start.13
  67.3 2.4 %copy-start.29 = (pred[128,512]{0,1:T(8,128)(4,1)S(1)}, pred[128,512]{0,1:T(8,128)(4,1)}, u32[]{:S(2)}) copy-start(pred[128,512]{0,1:T(8,128)(4,1)} %fusion.32) | copy-start | bytes 196612
  70.2 1.0 copy-start.31
  70.2 1.3 copy-start.33
  74.1 1.0 copy-start.16
  74.1 1.3 copy-start.24
  74.1 1.6 copy-start.32
  74.1 1.6 copy-start.34
  75.7 0.9 copy-start.28
  77.0 18.0 %copy-start.1 = (bf16[4,128,512]{1,2,0:T(8,128)(2,1)}, bf16[4,128,512]{1,2,0:T(8,128)(2,1)S(1)}, u32[]{:S(2)}) copy-start(bf16[4,128,512]{1,2,0:T(8,128)(2,1)S(1)} %fusion.12) | copy-start | bytes 1572868
  85.0 18.7 %all-to-all-start.2 = ((bf16[8,2,4096]{2,1,0:T(2,128)(2,1)}), bf16[8,2,4096]{2,1,0:T(2,128)(2,1)}, u32[]{:S(2)}, u32[]{:S(2)}) async-start(bf16[8,2,4096]{2,1,0:T(2,128)(2,1)} %reshape.579), calls=%async_computation.2 | async-start | bytes 262144 | tf_op jit(solution)/shard_map/all_to_all | solution.py:63
  100.0 0.9 copy-start.22
  101.6 14.8 %collective-permute-start.4 = (bf16[128,1024]{1,0:T(8,128)(2,1)}, bf16[128,1024]{1,0:T(8,128)(2,1)}, u32[]{:S(2)}, u32[]{:S(2)}) collective-permute-start(bf16[128,1024]{1,0:T(8,128)(2,1)} %pad_maximum_fusion.1), channel_id=1, source_target_pairs={{4,0},{8,4},{12,8},{16,12},{20,16},{24,20},{28,24},{32,28},{36,32}... | collective-permute-start | bytes 786440 | tf_op jit(solution)/shard_map/ppermute | solution.py:70
  112.4 8.3 %all-to-all-start.3 = ((f32[4,2,128]{2,1,0:T(2,128)}), f32[4,2,128]{2,1,0:T(2,128)}, u32[]{:S(2)}, u32[]{:S(2)}) async-start(f32[4,2,128]{2,1,0:T(2,128)} %broadcast_in_dim.108), calls=%async_computation.3 | async-start | bytes 8192 | tf_op jit(solution)/shard_map/all_to_all | solution.py:175
  118.2 20.6 %collective-permute-start.5 = (bf16[128,1024]{1,0:T(8,128)(2,1)}, bf16[128,1024]{1,0:T(8,128)(2,1)}, u32[]{:S(2)}, u32[]{:S(2)}) collective-permute-start(bf16[128,1024]{1,0:T(8,128)(2,1)} %add_convert_fusion.2), channel_id=1, source_target_pairs={{4,0},{8,4},{12,8},{16,12},{20,16},{24,20},{28,24},{32,28},{36,32}... | collective-permute-start | bytes 786440 | tf_op jit(solution)/shard_map/ppermute | solution.py:70
  131.5 12.8 %all-to-all-start.4 = ((bf16[8,2,4096]{2,1,0:T(2,128)(2,1)}), bf16[8,2,4096]{2,1,0:T(2,128)(2,1)}, u32[]{:S(2)}, u32[]{:S(2)}) async-start(bf16[8,2,4096]{2,1,0:T(2,128)(2,1)} %reshape.581), calls=%async_computation.4 | async-start | bytes 262144 | tf_op jit(solution)/shard_map/all_to_all | solution.py:57
  140.6 25.7 %collective-permute-start.6 = (bf16[128,1024]{1,0:T(8,128)(2,1)}, bf16[128,1024]{1,0:T(8,128)(2,1)}, u32[]{:S(2)}, u32[]{:S(2)}) collective-permute-start(bf16[128,1024]{1,0:T(8,128)(2,1)} %add_convert_fusion.1), channel_id=1, source_target_pairs={{4,0},{8,4},{12,8},{16,12},{20,16},{24,20},{28,24},{32,28},{36,32}... | collective-permute-start | bytes 786440 | tf_op jit(solution)/shard_map/ppermute | solution.py:70
  153.5 25.7 %all-to-all-start.5 = ((bf16[16,2,4096]{2,1,0:T(2,128)(2,1)}), bf16[16,2,4096]{2,1,0:T(2,128)(2,1)}, u32[]{:S(2)}, u32[]{:S(2)}) async-start(bf16[16,2,4096]{2,1,0:T(2,128)(2,1)} %reshape.583), calls=%async_computation.5 | async-start | bytes 524288 | tf_op jit(solution)/shard_map/all_to_all | solution.py:47
  164.7 7.9 %copy-start.9 = (bf16[128,512]{0,1:T(8,128)(2,1)S(1)}, bf16[128,512]{0,1:T(8,128)(2,1)}, u32[]{:S(2)}) copy-start(bf16[128,512]{0,1:T(8,128)(2,1)} %copy-done.8) | copy-start | bytes 393220
  164.7 8.1 %copy-start.3 = (bf16[128,4,128]{0,2,1:T(8,128)(2,1)S(1)}, bf16[128,4,128]{0,2,1:T(8,128)(2,1)}, u32[]{:S(2)}) copy-start(bf16[128,4,128]{0,2,1:T(8,128)(2,1)} %copy-done.2) | copy-start | bytes 393220
  164.7 8.1 %copy-start.7 = (bf16[4,128,128]{2,1,0:T(8,128)(2,1)S(1)}, bf16[4,128,128]{2,1,0:T(8,128)(2,1)}, u32[]{:S(2)}) copy-start(bf16[4,128,128]{2,1,0:T(8,128)(2,1)} %reshape.524) | copy-start | bytes 393220
  168.2 30.3 %collective-permute-start.7 = (bf16[128,1024]{1,0:T(8,128)(2,1)}, bf16[128,1024]{1,0:T(8,128)(2,1)}, u32[]{:S(2)}, u32[]{:S(2)}) collective-permute-start(bf16[128,1024]{1,0:T(8,128)(2,1)} %add_convert_fusion), channel_id=1, source_target_pairs={{4,0},{8,4},{12,8},{16,12},{20,16},{24,20},{28,24},{32,28},{36,32}... | collective-permute-start | bytes 786440 | tf_op jit(solution)/shard_map/ppermute | solution.py:70
  172.6 1.2 copy-start.17
  182.3 14.4 %copy-start.4 = (bf16[128,4,128]{0,2,1:T(8,128)(2,1)S(1)}, bf16[128,4,128]{0,2,1:T(8,128)(2,1)}, u32[]{:S(2)}) copy-start(bf16[128,4,128]{0,2,1:T(8,128)(2,1)} %copy-done.2) | copy-start | bytes 393220
  185.5 17.1 %all-to-all-start.6 = ((bf16[8,2,4096]{2,1,0:T(2,128)(2,1)}), bf16[8,2,4096]{2,1,0:T(2,128)(2,1)}, u32[]{:S(2)}, u32[]{:S(2)}) async-start(bf16[8,2,4096]{2,1,0:T(2,128)(2,1)} %reshape.585), calls=%async_computation.6 | async-start | bytes 262144 | tf_op jit(solution)/shard_map/all_to_all | solution.py:63
  199.4 5.4 %copy-start.11 = (bf16[128,512]{1,0:T(8,128)(2,1)S(1)}, bf16[128,512]{1,0:T(8,128)(2,1)}, u32[]{:S(2)}) copy-start(bf16[128,512]{1,0:T(8,128)(2,1)} %param.12) | copy-start | bytes 393220
  199.5 5.6 %copy-start.15 = (bf16[128,512]{1,0:T(8,128)(2,1)S(1)}, bf16[128,512]{1,0:T(8,128)(2,1)}, u32[]{:S(2)}) copy-start(bf16[128,512]{1,0:T(8,128)(2,1)} %param.11) | copy-start | bytes 393220
  200.2 4.8 %copy-start.12 = (f32[4,128,128]{2,1,0:T(8,128)S(1)}, f32[4,128,128]{2,1,0:T(8,128)}, u32[]{:S(2)}) copy-start(f32[4,128,128]{2,1,0:T(8,128)} %fusion.83) | copy-start | bytes 786436
  200.2 5.8 %copy-start.6 = (bf16[128,512]{1,0:T(8,128)(2,1)S(1)}, bf16[128,512]{1,0:T(8,128)(2,1)}, u32[]{:S(2)}) copy-start(bf16[128,512]{1,0:T(8,128)(2,1)} %param.10) | copy-start | bytes 393220
  200.2 5.8 %copy-start.18 = (bf16[4,128,128]{2,1,0:T(8,128)(2,1)S(1)}, bf16[4,128,128]{2,1,0:T(8,128)(2,1)}, u32[]{:S(2)}) copy-start(bf16[4,128,128]{2,1,0:T(8,128)(2,1)} %copy-done.17) | copy-start | bytes 393220
  (2 other events, 1.3 us)

commit v11 on v9

--- a/solution.py
+++ b/solution.py
@@ -161,10 +161,8 @@
     cross_sum = jnp.sum(gain_grad * output_lin, axis=(1, 2))
     sums = jnp.stack([square_sum, cross_sum])
     heads_dev = lax.axis_size("head")
-    step = 1
-    while step < heads_dev:
-        sums = sums + lax.ppermute(sums, "head", [(i, i ^ step) for i in range(heads_dev)])
-        step *= 2
+    spread = jnp.broadcast_to(sums[None], (heads_dev,) + sums.shape)
+    sums = jnp.sum(lax.all_to_all(spread, "head", 0, 0, tiled=True), axis=0)
     square_sum, cross_sum = sums[0], sums[1]
     full_width = LIN_HEADS * HEAD
     inv_rms = lax.rsqrt(square_sum / full_width + 1e-06)[:, None, None]

time: 187 us -> 187 us (level)
  starting transfers between devices: 98.6 us -> 93.7 us
  waiting for transfers between devices: 21.4 us -> 25.7 us
    ppermute x2 -> x0, starting transfers between devices: 8.33 us -> none  [per_device(): lax.ppermute(sums, 'head', [(i, i ^ step) for i in range(heads_dev)])]
    ppermute x8, waiting for transfers between devices: 2.65 us -> 8.59 us  [from_behind(): return lax.ppermute(shard, axis, pairs)]
    all_to_all x0 -> x1, starting transfers between devices: none -> 4.29 us  [per_device(): sums = jnp.sum(lax.all_to_all(spread, 'head', 0, 0, tiled=True), axis=0)]
    all_to_all x2, waiting for transfers between devices: 3.92 us -> 0.01 us  [carried_in(): back = lax.all_to_all(states, 'inner', 0, 0, tiled=True)]
  transfers between devices with their start and end apart: 26 -> 25, of which waited for: 9 -> 8; matrix products, arithmetic and copies ran while one was open for 29% -> 30% of each run, Pallas kernels for 0% -> 0%
where the time goes in v11:
time: 187 us; the launch traced here: 185 us
  starting transfers between devices  93.7 us (50%)
  other arithmetic  25.7 us (14%)
  waiting for transfers between devices  25.7 us (14%)
  local copies, waits for them, and re-layouts  25.1 us (13%)
  matrix products  13.4 us (7%)
    ppermute x12, starting transfers between devices, scan_over(): arrived.append(lax.ppermute(total.astype(jnp.bfloat16), axis, pairs))  46.9 us
    ppermute x8, starting transfers between devices, from_behind(): return lax.ppermute(shard, axis, pairs)  25.1 us
    unnamed x78, local copies, waits for them, and re-layouts  13.4 us
    ppermute x12, waiting for transfers between devices, scan_over(): arrived.append(lax.ppermute(total.astype(jnp.bfloat16), axis, pairs))  12.5 us
    all_to_all x2, starting transfers between devices, carried_in(): mine = lax.all_to_all(slices, 'inner', 0, 0, tiled=True).astype(jnp.float32)  10.1 us
    ppermute x8, waiting for transfers between devices, from_behind(): return lax.ppermute(shard, axis, pairs)  8.59 us
    all_to_all x2, starting transfers between devices, carried_in(): back = lax.all_to_all(states, 'inner', 0, 0, tiled=True)  7.37 us
    convert_element_type x4, other arithmetic, per_device(): owed = from_behind(owed.astype(jnp.bfloat16), CTX, -1).astype(jnp.float32)  6.4 us
  transfers between devices with their start and end apart: 25, of which 8 were waited for; matrix products, arithmetic and copies ran while one was open for 30% of the time, Pallas kernels for 0%

profile of v11, /device:TPU:24, one launch (start us, length us, event | category | flops | bytes accessed | tf_op | source)
XLA Modules:
  0.0 185.2 jit_solution(2571650949364213568)
XLA Ops:
  3.5 1.3 reduce.9
  5.6 5.9 %all-to-all-start = ((bf16[8,2,4096]{2,1,0:T(2,128)(2,1)}), bf16[8,2,4096]{2,1,0:T(2,128)(2,1)S(1)}, u32[]{:S(2)}, u32[]{:S(2)}) async-start(bf16[8,2,4096]{2,1,0:T(2,128)(2,1)} %reshape.545), calls=%async_computation | async-start | bytes 262144 | tf_op jit(solution)/shard_map/all_to_all | solution.py:47
  11.5 2.4 %collective-permute-start.12 = (bf16[128,1024]{1,0:T(8,128)(2,1)S(1)}, bf16[128,1024]{1,0:T(8,128)(2,1)S(1)}, u32[]{:S(2)}, u32[]{:S(2)}) collective-permute-start(bf16[128,1024]{1,0:T(8,128)(2,1)S(1)} %pad_maximum_fusion), channel_id=1, source_target_pairs={{0,4},{4,8},{8,12},{12,16},{16,20},{20,24},{24,28},{28,32},{32,36}... | collective-permute-start | bytes 786440 | tf_op jit(solution)/shard_map/ppermute | solution.py:60
  15.3 2.9 %all-to-all-done = bf16[8,2,4096]{2,1,0:T(2,128)(2,1)S(1)} async-done(((bf16[8,2,4096]{2,1,0:T(2,128)(2,1)}), bf16[8,2,4096]{2,1,0:T(2,128)(2,1)S(1)}, u32[]{:S(2)}, u32[]{:S(2)}) %all-to-all-start) | async-done | bytes 131104 | tf_op jit(solution)/shard_map/all_to_all | solution.py:47
  18.7 10.1 %collective-permute-start.2 = (bf16[8192]{0:T(1024)(128)(2,1)S(1)}, bf16[8192]{0:T(1024)(128)(2,1)S(1)}, u32[]{:S(2)}, u32[]{:S(2)}) collective-permute-start(bf16[8192]{0:T(1024)(128)(2,1)S(1)} %convert_element_type.211), channel_id=1, source_target_pairs={{0,96},{32,128},{64,160},{96,192},{128,224},{160,256},{192,288},{2... | collective-permute-start | bytes 49160 | tf_op jit(solution)/shard_map/ppermute | solution.py:37
  28.8 4.3 %collective-permute-start.1 = (bf16[8192]{0:T(1024)(128)(2,1)S(1)}, bf16[8192]{0:T(1024)(128)(2,1)S(1)}, u32[]{:S(2)}, u32[]{:S(2)}) collective-permute-start(bf16[8192]{0:T(1024)(128)(2,1)S(1)} %convert_element_type.211), channel_id=1, source_target_pairs={{0,64},{32,96},{64,128},{96,160},{128,192},{160,224},{192,256},{22... | collective-permute-start | bytes 49160 | tf_op jit(solution)/shard_map/ppermute | solution.py:37
  33.1 4.3 %collective-permute-start = (bf16[8192]{0:T(1024)(128)(2,1)S(1)}, bf16[8192]{0:T(1024)(128)(2,1)S(1)}, u32[]{:S(2)}, u32[]{:S(2)}) collective-permute-start(bf16[8192]{0:T(1024)(128)(2,1)S(1)} %convert_element_type.211), channel_id=1, source_target_pairs={{0,32},{32,64},{64,96},{96,128},{128,160},{160,192},{192,224},{224... | collective-permute-start | bytes 49160 | tf_op jit(solution)/shard_map/ppermute | solution.py:37
  37.4 6.7 %collective-permute-done.1 = bf16[8192]{0:T(1024)(128)(2,1)S(1)} collective-permute-done((bf16[8192]{0:T(1024)(128)(2,1)S(1)}, bf16[8192]{0:T(1024)(128)(2,1)S(1)}, u32[]{:S(2)}, u32[]{:S(2)}) %collective-permute-start.1) | collective-permute-done | bytes 16416 | tf_op jit(solution)/shard_map/ppermute | solution.py:37
  48.0 2.9 %collective-permute-done.5 = bf16[8192]{0:T(1024)(128)(2,1)S(1)} collective-permute-done((bf16[8192]{0:T(1024)(128)(2,1)S(1)}, bf16[8192]{0:T(1024)(128)(2,1)S(1)}, u32[]{:S(2)}, u32[]{:S(2)}) %collective-permute-start.5) | collective-permute-done | bytes 16416 | tf_op jit(solution)/shard_map/ppermute | solution.py:37
  51.0 1.6 collective-permute-done.4
  53.0 1.3 reduce.10
  55.1 3.4 %all-to-all-start.1 = ((bf16[8,2,4096]{2,1,0:T(2,128)(2,1)}), bf16[8,2,4096]{2,1,0:T(2,128)(2,1)S(1)}, u32[]{:S(2)}, u32[]{:S(2)}) async-start(bf16[8,2,4096]{2,1,0:T(2,128)(2,1)} %reshape.547), calls=%async_computation.1 | async-start | bytes 262144 | tf_op jit(solution)/shard_map/all_to_all | solution.py:53
  58.6 2.3 %collective-permute-start.13 = (bf16[128,1024]{1,0:T(8,128)(2,1)S(1)}, bf16[128,1024]{1,0:T(8,128)(2,1)S(1)}, u32[]{:S(2)}, u32[]{:S(2)}) collective-permute-start(bf16[128,1024]{1,0:T(8,128)(2,1)S(1)} %collective-permute-done.12), channel_id=1, source_target_pairs={{0,4},{4,8},{8,12},{12,16},{16,20},{20,24},{24,28},{28,32},{32,36}... | collective-permute-start | bytes 786440 | tf_op jit(solution)/shard_map/ppermute | solution.py:60
  61.3 7.1 %collective-permute-done.13 = bf16[128,1024]{1,0:T(8,128)(2,1)S(1)} collective-permute-done((bf16[128,1024]{1,0:T(8,128)(2,1)S(1)}, bf16[128,1024]{1,0:T(8,128)(2,1)S(1)}, u32[]{:S(2)}, u32[]{:S(2)}) %collective-permute-start.13) | collective-permute-done | bytes 262176 | tf_op jit(solution)/shard_map/ppermute | solution.py:60
  68.3 1.9 %collective-permute-start.14 = (bf16[128,1024]{1,0:T(8,128)(2,1)S(1)}, bf16[128,1024]{1,0:T(8,128)(2,1)S(1)}, u32[]{:S(2)}, u32[]{:S(2)}) collective-permute-start(bf16[128,1024]{1,0:T(8,128)(2,1)S(1)} %collective-permute-done.13), channel_id=1, source_target_pairs={{0,4},{4,8},{8,12},{12,16},{16,20},{20,24},{24,28},{28,32},{32,36}... | collective-permute-start | bytes 786440 | tf_op jit(solution)/shard_map/ppermute | solution.py:60
  72.2 4.3 %all-to-all-start.2 = ((f32[4,2,128]{2,1,0:T(2,128)}), f32[4,2,128]{2,1,0:T(2,128)S(1)}, u32[]{:S(2)}, u32[]{:S(2)}) async-start(f32[4,2,128]{2,1,0:T(2,128)} %broadcast_in_dim.75), calls=%async_computation.2 | async-start | bytes 8192 | tf_op jit(solution)/shard_map/all_to_all | solution.py:165
  76.6 1.5 collective-permute-done.14
  78.1 1.9 %collective-permute-start.15 = (bf16[128,1024]{1,0:T(8,128)(2,1)S(1)}, bf16[128,1024]{1,0:T(8,128)(2,1)}, u32[]{:S(2)}, u32[]{:S(2)}) collective-permute-start(bf16[128,1024]{1,0:T(8,128)(2,1)S(1)} %collective-permute-done.14), channel_id=1, source_target_pairs={{0,4},{4,8},{8,12},{12,16},{16,20},{20,24},{24,28},{28,32},{32,36}... | collective-permute-start | bytes 786440 | tf_op jit(solution)/shard_map/ppermute | solution.py:60
  80.1 1.7 all-to-all-done.2
  83.0 1.3 reduce.11
  85.1 4.2 %all-to-all-start.3 = ((bf16[8,2,4096]{2,1,0:T(2,128)(2,1)}), bf16[8,2,4096]{2,1,0:T(2,128)(2,1)}, u32[]{:S(2)}, u32[]{:S(2)}) async-start(bf16[8,2,4096]{2,1,0:T(2,128)(2,1)} %reshape.549), calls=%async_computation.3 | async-start | bytes 262144 | tf_op jit(solution)/shard_map/all_to_all | solution.py:47
  95.2 1.5 fusion.80
  96.8 1.6 convolution_bitcast_fusion
  101.2 1.4 reshape.529
  104.9 2.3 %scatter_fusion = f32[5,128,512]{2,1,0:T(8,128)S(1)} fusion(f32[5,128,512]{2,1,0:T(8,128)S(1)} %broadcast.250.clone.1, s32[4]{0:T(128)S(1)} %fusion.70, f32[4,128,512]{2,1,0:T(8,128)} %reshape.529), kind=kCustom, calls=%fused_computation.2 | custom fusion | flops 262144 | bytes 3145744 | tf_op jit(solution)/shard_map/scatter-add | solution.py:122
  108.8 6.1 %collective-permute-start.16 = (bf16[128,1024]{1,0:T(8,128)(2,1)}, bf16[128,1024]{1,0:T(8,128)(2,1)}, u32[]{:S(2)}, u32[]{:S(2)}) collective-permute-start(bf16[128,1024]{1,0:T(8,128)(2,1)} %pad_maximum_fusion.1), channel_id=1, source_target_pairs={{4,0},{8,4},{12,8},{16,12},{20,16},{24,20},{28,24},{32,28},{36,32}... | collective-permute-start | bytes 786440 | tf_op jit(solution)/shard_map/ppermute | solution.py:60
  115.8 1.4 reshape.550
  117.5 5.3 %collective-permute-start.8 = (bf16[8192]{0:T(1024)(128)(2,1)S(1)}, bf16[8192]{0:T(1024)(128)(2,1)S(1)}, u32[]{:S(2)}, u32[]{:S(2)}) collective-permute-start(bf16[8192]{0:T(1024)(128)(2,1)S(1)} %convert_element_type.227), channel_id=1, source_target_pairs={{96,0},{128,32},{160,64},{192,96},{224,128},{256,160},{288,192},{3... | collective-permute-start | bytes 49160 | tf_op jit(solution)/shard_map/ppermute | solution.py:37
  122.9 8.7 %collective-permute-start.7 = (bf16[8192]{0:T(1024)(128)(2,1)S(1)}, bf16[8192]{0:T(1024)(128)(2,1)S(1)}, u32[]{:S(2)}, u32[]{:S(2)}) collective-permute-start(bf16[8192]{0:T(1024)(128)(2,1)S(1)} %convert_element_type.227), channel_id=1, source_target_pairs={{64,0},{96,32},{128,64},{160,96},{192,128},{224,160},{256,192},{28... | collective-permute-start | bytes 49160 | tf_op jit(solution)/shard_map/ppermute | solution.py:37
  131.6 4.6 %collective-permute-start.6 = (bf16[8192]{0:T(1024)(128)(2,1)S(1)}, bf16[8192]{0:T(1024)(128)(2,1)S(1)}, u32[]{:S(2)}, u32[]{:S(2)}) collective-permute-start(bf16[8192]{0:T(1024)(128)(2,1)S(1)} %convert_element_type.227), channel_id=1, source_target_pairs={{32,0},{64,32},{96,64},{128,96},{160,128},{192,160},{224,192},{256... | collective-permute-start | bytes 49160 | tf_op jit(solution)/shard_map/ppermute | solution.py:37
  136.2 1.8 add_convert_fusion.2
  138.0 1.9 %collective-permute-start.17 = (bf16[128,1024]{1,0:T(8,128)(2,1)}, bf16[128,1024]{1,0:T(8,128)(2,1)}, u32[]{:S(2)}, u32[]{:S(2)}) collective-permute-start(bf16[128,1024]{1,0:T(8,128)(2,1)} %add_convert_fusion.2), channel_id=1, source_target_pairs={{4,0},{8,4},{12,8},{16,12},{20,16},{24,20},{28,24},{32,28},{36,32}... | collective-permute-start | bytes 786440 | tf_op jit(solution)/shard_map/ppermute | solution.py:60
  141.8 1.9 %collective-permute-start.11 = (bf16[8192]{0:T(1024)(128)(2,1)}, bf16[8192]{0:T(1024)(128)(2,1)}, u32[]{:S(2)}, u32[]{:S(2)}) collective-permute-start(bf16[8192]{0:T(1024)(128)(2,1)} %fusion.60), channel_id=1, source_target_pairs={{384,0},{416,32},{448,64},{480,96},{385,1},{417,33},{449,65},{481,... | collective-permute-start | bytes 49160 | tf_op jit(solution)/shard_map/ppermute | solution.py:37
  143.7 1.9 %collective-permute-start.10 = (bf16[8192]{0:T(1024)(128)(2,1)}, bf16[8192]{0:T(1024)(128)(2,1)}, u32[]{:S(2)}, u32[]{:S(2)}) collective-permute-start(bf16[8192]{0:T(1024)(128)(2,1)} %fusion.60), channel_id=1, source_target_pairs={{256,0},{288,32},{320,64},{352,96},{384,128},{416,160},{448,192},{... | collective-permute-start | bytes 49160 | tf_op jit(solution)/shard_map/ppermute | solution.py:37
  145.6 1.9 %collective-permute-start.9 = (bf16[8192]{0:T(1024)(128)(2,1)}, bf16[8192]{0:T(1024)(128)(2,1)}, u32[]{:S(2)}, u32[]{:S(2)}) collective-permute-start(bf16[8192]{0:T(1024)(128)(2,1)} %fusion.60), channel_id=1, source_target_pairs={{128,0},{160,32},{192,64},{224,96},{256,128},{288,160},{320,192},{... | collective-permute-start | bytes 49160 | tf_op jit(solution)/shard_map/ppermute | solution.py:37
  148.4 1.7 copy.228
  150.9 1.8 add_convert_fusion.1
  152.7 1.9 %collective-permute-start.18 = (bf16[128,1024]{1,0:T(8,128)(2,1)}, bf16[128,1024]{1,0:T(8,128)(2,1)}, u32[]{:S(2)}, u32[]{:S(2)}) collective-permute-start(bf16[128,1024]{1,0:T(8,128)(2,1)} %add_convert_fusion.1), channel_id=1, source_target_pairs={{4,0},{8,4},{12,8},{16,12},{20,16},{24,20},{28,24},{32,28},{36,32}... | collective-permute-start | bytes 786440 | tf_op jit(solution)/shard_map/ppermute | solution.py:60
  154.6 1.8 add_convert_fusion.3
  156.4 2.3 %reduce.12 = bf16[8,8192]{1,0:T(8,128)(2,1)S(1)} reduce(bf16[8,1,8192]{2,1,0:T(2,128)(2,1)} %add_convert_fusion.3, bf16[]{:T(256)} %broadcast.282), dimensions={1}, to_apply=%add_convert_fusion.3.reduce_sub_computation | reduce | bytes 262146 | tf_op jit(solution)/shard_map/jit(cumsum)/reduce_window_sum | solution.py:48
  159.4 4.0 %all-to-all-start.4 = ((bf16[8,2,4096]{2,1,0:T(2,128)(2,1)}), bf16[8,2,4096]{2,1,0:T(2,128)(2,1)}, u32[]{:S(2)}, u32[]{:S(2)}) async-start(bf16[8,2,4096]{2,1,0:T(2,128)(2,1)} %reshape.551), calls=%async_computation.4 | async-start | bytes 262144 | tf_op jit(solution)/shard_map/all_to_all | solution.py:53
  163.4 1.3 convolution_convert_fusion
  165.5 1.8 add_convert_fusion
  167.3 6.7 %collective-permute-start.19 = (bf16[128,1024]{1,0:T(8,128)(2,1)}, bf16[128,1024]{1,0:T(8,128)(2,1)}, u32[]{:S(2)}, u32[]{:S(2)}) collective-permute-start(bf16[128,1024]{1,0:T(8,128)(2,1)} %add_convert_fusion), channel_id=1, source_target_pairs={{4,0},{8,4},{12,8},{16,12},{20,16},{24,20},{28,24},{32,28},{36,32}... | collective-permute-start | bytes 786440 | tf_op jit(solution)/shard_map/ppermute | solution.py:60
  174.0 1.4 reshape.552
  175.4 1.4 reduce.8
  177.8 1.8 fusion.17
  179.9 1.7 copy.230
  (167 shorter events, 38.4 us)
Async XLA Ops:
  0.6 94.6 %copy-start = (bf16[128,512]{1,0:T(8,128)(2,1)S(1)}, bf16[128,512]{1,0:T(8,128)(2,1)}, u32[]{:S(2)}) copy-start(bf16[128,512]{1,0:T(8,128)(2,1)} %param.15) | copy-start | bytes 393220
  0.6 14.4 %copy-start.13 = (bf16[128,512]{1,0:T(8,128)(2,1)S(1)}, bf16[128,512]{1,0:T(8,128)(2,1)}, u32[]{:S(2)}) copy-start(bf16[128,512]{1,0:T(8,128)(2,1)} %param.11) | copy-start | bytes 393220
  0.7 10.8 %copy-start.16 = (bf16[128,512]{1,0:T(8,128)(2,1)S(1)}, bf16[128,512]{1,0:T(8,128)(2,1)}, u32[]{:S(2)}) copy-start(bf16[128,512]{1,0:T(8,128)(2,1)} %param.17) | copy-start | bytes 393220
  0.7 10.8 %copy-start.17 = (bf16[128,512]{1,0:T(8,128)(2,1)S(1)}, bf16[128,512]{1,0:T(8,128)(2,1)}, u32[]{:S(2)}) copy-start(bf16[128,512]{1,0:T(8,128)(2,1)} %param.16) | copy-start | bytes 393220
  0.7 13.3 %copy-start.29 = (s32[1,3]{1,0:T(1,128)S(1)}, s32[1,3]{1,0:T(1,128)}, u32[]{:S(2)}) copy-start(s32[1,3]{1,0:T(1,128)} %param.19) | copy-start | bytes 40
  0.7 14.4 %copy-start.5 = (bf16[128,512]{1,0:T(8,128)(2,1)S(1)}, bf16[128,512]{1,0:T(8,128)(2,1)}, u32[]{:S(2)}) copy-start(bf16[128,512]{1,0:T(8,128)(2,1)} %param.10) | copy-start | bytes 393220
  5.6 12.7 %all-to-all-start = ((bf16[8,2,4096]{2,1,0:T(2,128)(2,1)}), bf16[8,2,4096]{2,1,0:T(2,128)(2,1)S(1)}, u32[]{:S(2)}, u32[]{:S(2)}) async-start(bf16[8,2,4096]{2,1,0:T(2,128)(2,1)} %reshape.545), calls=%async_computation | async-start | bytes 262144 | tf_op jit(solution)/shard_map/all_to_all | solution.py:47
  11.5 47.1 %collective-permute-start.12 = (bf16[128,1024]{1,0:T(8,128)(2,1)S(1)}, bf16[128,1024]{1,0:T(8,128)(2,1)S(1)}, u32[]{:S(2)}, u32[]{:S(2)}) collective-permute-start(bf16[128,1024]{1,0:T(8,128)(2,1)S(1)} %pad_maximum_fusion), channel_id=1, source_target_pairs={{0,4},{4,8},{8,12},{12,16},{16,20},{20,24},{24,28},{28,32},{32,36}... | collective-permute-start | bytes 786440 | tf_op jit(solution)/shard_map/ppermute | solution.py:60
  15.3 45.7 %copy-start.18 = (bf16[4,128,128]{2,1,0:T(8,128)(2,1)}, bf16[4,128,128]{2,1,0:T(8,128)(2,1)S(1)}, u32[]{:S(2)}) copy-start(bf16[4,128,128]{2,1,0:T(8,128)(2,1)S(1)} %fusion.15) | copy-start | bytes 393220
  15.3 45.6 %copy-start.22 = (bf16[128,512]{1,0:T(8,128)(2,1)S(1)}, bf16[128,512]{1,0:T(8,128)(2,1)}, u32[]{:S(2)}) copy-start(bf16[128,512]{1,0:T(8,128)(2,1)} %param.14) | copy-start | bytes 393220
  18.4 42.6 %copy-start.9 = (bf16[128,512]{1,0:T(8,128)(2,1)S(1)}, bf16[128,512]{1,0:T(8,128)(2,1)}, u32[]{:S(2)}) copy-start(bf16[128,512]{1,0:T(8,128)(2,1)} %param.12) | copy-start | bytes 393220
  18.7 18.8 %collective-permute-start.2 = (bf16[8192]{0:T(1024)(128)(2,1)S(1)}, bf16[8192]{0:T(1024)(128)(2,1)S(1)}, u32[]{:S(2)}, u32[]{:S(2)}) collective-permute-start(bf16[8192]{0:T(1024)(128)(2,1)S(1)} %convert_element_type.211), channel_id=1, source_target_pairs={{0,96},{32,128},{64,160},{96,192},{128,224},{160,256},{192,288},{2... | collective-permute-start | bytes 49160 | tf_op jit(solution)/shard_map/ppermute | solution.py:37
  28.8 15.3 %collective-permute-start.1 = (bf16[8192]{0:T(1024)(128)(2,1)S(1)}, bf16[8192]{0:T(1024)(128)(2,1)S(1)}, u32[]{:S(2)}, u32[]{:S(2)}) collective-permute-start(bf16[8192]{0:T(1024)(128)(2,1)S(1)} %convert_element_type.211), channel_id=1, source_target_pairs={{0,64},{32,96},{64,128},{96,160},{128,192},{160,224},{192,256},{22... | collective-permute-start | bytes 49160 | tf_op jit(solution)/shard_map/ppermute | solution.py:37
  33.1 11.0 %collective-permute-start = (bf16[8192]{0:T(1024)(128)(2,1)S(1)}, bf16[8192]{0:T(1024)(128)(2,1)S(1)}, u32[]{:S(2)}, u32[]{:S(2)}) collective-permute-start(bf16[8192]{0:T(1024)(128)(2,1)S(1)} %convert_element_type.211), channel_id=1, source_target_pairs={{0,32},{32,64},{64,96},{96,128},{128,160},{160,192},{192,224},{224... | collective-permute-start | bytes 49160 | tf_op jit(solution)/shard_map/ppermute | solution.py:37
  44.1 6.8 %collective-permute-start.5 = (bf16[8192]{0:T(1024)(128)(2,1)S(1)}, bf16[8192]{0:T(1024)(128)(2,1)S(1)}, u32[]{:S(2)}, u32[]{:S(2)}) collective-permute-start(bf16[8192]{0:T(1024)(128)(2,1)S(1)} %fusion.59), channel_id=1, source_target_pairs={{0,384},{32,416},{64,448},{96,480},{1,385},{33,417},{65,449},{97,4... | collective-permute-start | bytes 49160 | tf_op jit(solution)/shard_map/ppermute | solution.py:37
  45.4 7.1 %collective-permute-start.4 = (bf16[8192]{0:T(1024)(128)(2,1)S(1)}, bf16[8192]{0:T(1024)(128)(2,1)S(1)}, u32[]{:S(2)}, u32[]{:S(2)}) collective-permute-start(bf16[8192]{0:T(1024)(128)(2,1)S(1)} %fusion.59), channel_id=1, source_target_pairs={{0,256},{32,288},{64,320},{96,352},{128,384},{160,416},{192,448},{... | collective-permute-start | bytes 49160 | tf_op jit(solution)/shard_map/ppermute | solution.py:37
  46.7 5.9 %collective-permute-start.3 = (bf16[8192]{0:T(1024)(128)(2,1)S(1)}, bf16[8192]{0:T(1024)(128)(2,1)S(1)}, u32[]{:S(2)}, u32[]{:S(2)}) collective-permute-start(bf16[8192]{0:T(1024)(128)(2,1)S(1)} %fusion.59), channel_id=1, source_target_pairs={{0,128},{32,160},{64,192},{96,224},{128,256},{160,288},{192,320},{... | collective-permute-start | bytes 49160 | tf_op jit(solution)/shard_map/ppermute | solution.py:37
  54.4 16.9 %copy-start.28 = (f32[512]{0:T(512)S(1)}, f32[512]{0:T(512)}, u32[]{:S(2)}) copy-start(f32[512]{0:T(512)} %param.13) | copy-start | bytes 6148
  55.1 15.2 %all-to-all-start.1 = ((bf16[8,2,4096]{2,1,0:T(2,128)(2,1)}), bf16[8,2,4096]{2,1,0:T(2,128)(2,1)S(1)}, u32[]{:S(2)}, u32[]{:S(2)}) async-start(bf16[8,2,4096]{2,1,0:T(2,128)(2,1)} %reshape.547), calls=%async_computation.1 | async-start | bytes 262144 | tf_op jit(solution)/shard_map/all_to_all | solution.py:53
  58.6 9.8 %collective-permute-start.13 = (bf16[128,1024]{1,0:T(8,128)(2,1)S(1)}, bf16[128,1024]{1,0:T(8,128)(2,1)S(1)}, u32[]{:S(2)}, u32[]{:S(2)}) collective-permute-start(bf16[128,1024]{1,0:T(8,128)(2,1)S(1)} %collective-permute-done.12), channel_id=1, source_target_pairs={{0,4},{4,8},{8,12},{12,16},{16,20},{20,24},{24,28},{28,32},{32,36}... | collective-permute-start | bytes 786440 | tf_op jit(solution)/shard_map/ppermute | solution.py:60
  61.0 15.5 %copy-start.23 = (bf16[128,512]{1,0:T(8,128)(2,1)S(1)}, bf16[128,512]{1,0:T(8,128)(2,1)}, u32[]{:S(2)}) copy-start(bf16[128,512]{1,0:T(8,128)(2,1)} %param.18) | copy-start | bytes 393220
  68.3 9.8 %collective-permute-start.14 = (bf16[128,1024]{1,0:T(8,128)(2,1)S(1)}, bf16[128,1024]{1,0:T(8,128)(2,1)S(1)}, u32[]{:S(2)}, u32[]{:S(2)}) collective-permute-start(bf16[128,1024]{1,0:T(8,128)(2,1)S(1)} %collective-permute-done.13), channel_id=1, source_target_pairs={{0,4},{4,8},{8,12},{12,16},{16,20},{20,24},{24,28},{28,32},{32,36}... | collective-permute-start | bytes 786440 | tf_op jit(solution)/shard_map/ppermute | solution.py:60
  71.2 11.5 %copy-start.7 = (bf16[4,128,128]{2,1,0:T(8,128)(2,1)}, bf16[4,128,128]{2,1,0:T(8,128)(2,1)S(1)}, u32[]{:S(2)}) copy-start(bf16[4,128,128]{2,1,0:T(8,128)(2,1)S(1)} %reshape.496) | copy-start | bytes 393220
  72.2 9.6 %all-to-all-start.2 = ((f32[4,2,128]{2,1,0:T(2,128)}), f32[4,2,128]{2,1,0:T(2,128)S(1)}, u32[]{:S(2)}, u32[]{:S(2)}) async-start(f32[4,2,128]{2,1,0:T(2,128)} %broadcast_in_dim.75), calls=%async_computation.2 | async-start | bytes 8192 | tf_op jit(solution)/shard_map/all_to_all | solution.py:165
  78.1 12.0 %collective-permute-start.15 = (bf16[128,1024]{1,0:T(8,128)(2,1)S(1)}, bf16[128,1024]{1,0:T(8,128)(2,1)}, u32[]{:S(2)}, u32[]{:S(2)}) collective-permute-start(bf16[128,1024]{1,0:T(8,128)(2,1)S(1)} %collective-permute-done.14), channel_id=1, source_target_pairs={{0,4},{4,8},{8,12},{12,16},{16,20},{20,24},{24,28},{28,32},{32,36}... | collective-permute-start | bytes 786440 | tf_op jit(solution)/shard_map/ppermute | solution.py:60
  85.1 30.7 %all-to-all-start.3 = ((bf16[8,2,4096]{2,1,0:T(2,128)(2,1)}), bf16[8,2,4096]{2,1,0:T(2,128)(2,1)}, u32[]{:S(2)}, u32[]{:S(2)}) async-start(bf16[8,2,4096]{2,1,0:T(2,128)(2,1)} %reshape.549), calls=%async_computation.3 | async-start | bytes 262144 | tf_op jit(solution)/shard_map/all_to_all | solution.py:47
  107.2 7.7 %copy-start.3 = (bf16[128,4,128]{0,2,1:T(8,128)(2,1)S(1)}, bf16[128,4,128]{0,2,1:T(8,128)(2,1)}, u32[]{:S(2)}) copy-start(bf16[128,4,128]{0,2,1:T(8,128)(2,1)} %copy-done.2) | copy-start | bytes 393220
  107.2 7.7 %copy-start.8 = (bf16[4,128,128]{2,1,0:T(8,128)(2,1)S(1)}, bf16[4,128,128]{2,1,0:T(8,128)(2,1)}, u32[]{:S(2)}) copy-start(bf16[4,128,128]{2,1,0:T(8,128)(2,1)} %copy-done.7) | copy-start | bytes 393220
  107.2 7.7 %copy-start.11 = (f32[128,4,128]{0,2,1:T(8,128)S(1)}, f32[128,4,128]{0,2,1:T(8,128)}, u32[]{:S(2)}) copy-start(f32[128,4,128]{0,2,1:T(8,128)} %convolution_bitcast_fusion.6) | copy-start | bytes 786436
  108.8 27.3 %collective-permute-start.16 = (bf16[128,1024]{1,0:T(8,128)(2,1)}, bf16[128,1024]{1,0:T(8,128)(2,1)}, u32[]{:S(2)}, u32[]{:S(2)}) collective-permute-start(bf16[128,1024]{1,0:T(8,128)(2,1)} %pad_maximum_fusion.1), channel_id=1, source_target_pairs={{4,0},{8,4},{12,8},{16,12},{20,16},{24,20},{28,24},{32,28},{36,32}... | collective-permute-start | bytes 786440 | tf_op jit(solution)/shard_map/ppermute | solution.py:60
  117.2 30.3 %copy-start.4 = (bf16[128,4,128]{0,2,1:T(8,128)(2,1)S(1)}, bf16[128,4,128]{0,2,1:T(8,128)(2,1)}, u32[]{:S(2)}) copy-start(bf16[128,4,128]{0,2,1:T(8,128)(2,1)} %copy-done.2) | copy-start | bytes 393220
  117.2 30.3 %copy-start.19 = (bf16[4,128,128]{2,1,0:T(8,128)(2,1)S(1)}, bf16[4,128,128]{2,1,0:T(8,128)(2,1)}, u32[]{:S(2)}) copy-start(bf16[4,128,128]{2,1,0:T(8,128)(2,1)} %copy-done.18) | copy-start | bytes 393220
  117.5 30.9 %copy-start.12 = (f32[8192]{0:T(1024)}, f32[8192]{0:T(1024)S(1)}, u32[]{:S(2)}) copy-start(f32[8192]{0:T(1024)S(1)} %convert_reduce_fusion) | copy-start | bytes 98308
  117.5 22.4 %collective-permute-start.8 = (bf16[8192]{0:T(1024)(128)(2,1)S(1)}, bf16[8192]{0:T(1024)(128)(2,1)S(1)}, u32[]{:S(2)}, u32[]{:S(2)}) collective-permute-start(bf16[8192]{0:T(1024)(128)(2,1)S(1)} %convert_element_type.227), channel_id=1, source_target_pairs={{96,0},{128,32},{160,64},{192,96},{224,128},{256,160},{288,192},{3... | collective-permute-start | bytes 49160 | tf_op jit(solution)/shard_map/ppermute | solution.py:37
  122.9 17.1 %collective-permute-start.7 = (bf16[8192]{0:T(1024)(128)(2,1)S(1)}, bf16[8192]{0:T(1024)(128)(2,1)S(1)}, u32[]{:S(2)}, u32[]{:S(2)}) collective-permute-start(bf16[8192]{0:T(1024)(128)(2,1)S(1)} %convert_element_type.227), channel_id=1, source_target_pairs={{64,0},{96,32},{128,64},{160,96},{192,128},{224,160},{256,192},{28... | collective-permute-start | bytes 49160 | tf_op jit(solution)/shard_map/ppermute | solution.py:37
  131.6 9.6 %collective-permute-start.6 = (bf16[8192]{0:T(1024)(128)(2,1)S(1)}, bf16[8192]{0:T(1024)(128)(2,1)S(1)}, u32[]{:S(2)}, u32[]{:S(2)}) collective-permute-start(bf16[8192]{0:T(1024)(128)(2,1)S(1)} %convert_element_type.227), channel_id=1, source_target_pairs={{32,0},{64,32},{96,64},{128,96},{160,128},{192,160},{224,192},{256... | collective-permute-start | bytes 49160 | tf_op jit(solution)/shard_map/ppermute | solution.py:37
  138.0 12.9 %collective-permute-start.17 = (bf16[128,1024]{1,0:T(8,128)(2,1)}, bf16[128,1024]{1,0:T(8,128)(2,1)}, u32[]{:S(2)}, u32[]{:S(2)}) collective-permute-start(bf16[128,1024]{1,0:T(8,128)(2,1)} %add_convert_fusion.2), channel_id=1, source_target_pairs={{4,0},{8,4},{12,8},{16,12},{20,16},{24,20},{28,24},{32,28},{36,32}... | collective-permute-start | bytes 786440 | tf_op jit(solution)/shard_map/ppermute | solution.py:60
  139.9 8.4 %copy-start.26 = (bf16[8192]{0:T(1024)(128)(2,1)}, bf16[8192]{0:T(1024)(128)(2,1)S(1)}, u32[]{:S(2)}) copy-start(bf16[8192]{0:T(1024)(128)(2,1)S(1)} %collective-permute-done.7) | copy-start | bytes 49156
  141.8 8.2 %collective-permute-start.11 = (bf16[8192]{0:T(1024)(128)(2,1)}, bf16[8192]{0:T(1024)(128)(2,1)}, u32[]{:S(2)}, u32[]{:S(2)}) collective-permute-start(bf16[8192]{0:T(1024)(128)(2,1)} %fusion.60), channel_id=1, source_target_pairs={{384,0},{416,32},{448,64},{480,96},{385,1},{417,33},{449,65},{481,... | collective-permute-start | bytes 49160 | tf_op jit(solution)/shard_map/ppermute | solution.py:37
  143.7 6.3 %collective-permute-start.10 = (bf16[8192]{0:T(1024)(128)(2,1)}, bf16[8192]{0:T(1024)(128)(2,1)}, u32[]{:S(2)}, u32[]{:S(2)}) collective-permute-start(bf16[8192]{0:T(1024)(128)(2,1)} %fusion.60), channel_id=1, source_target_pairs={{256,0},{288,32},{320,64},{352,96},{384,128},{416,160},{448,192},{... | collective-permute-start | bytes 49160 | tf_op jit(solution)/shard_map/ppermute | solution.py:37
  145.6 4.4 %collective-permute-start.9 = (bf16[8192]{0:T(1024)(128)(2,1)}, bf16[8192]{0:T(1024)(128)(2,1)}, u32[]{:S(2)}, u32[]{:S(2)}) collective-permute-start(bf16[8192]{0:T(1024)(128)(2,1)} %fusion.60), channel_id=1, source_target_pairs={{128,0},{160,32},{192,64},{224,96},{256,128},{288,160},{320,192},{... | collective-permute-start | bytes 49160 | tf_op jit(solution)/shard_map/ppermute | solution.py:37
  152.7 12.8 %collective-permute-start.18 = (bf16[128,1024]{1,0:T(8,128)(2,1)}, bf16[128,1024]{1,0:T(8,128)(2,1)}, u32[]{:S(2)}, u32[]{:S(2)}) collective-permute-start(bf16[128,1024]{1,0:T(8,128)(2,1)} %add_convert_fusion.1), channel_id=1, source_target_pairs={{4,0},{8,4},{12,8},{16,12},{20,16},{24,20},{28,24},{32,28},{36,32}... | collective-permute-start | bytes 786440 | tf_op jit(solution)/shard_map/ppermute | solution.py:60
  156.4 9.2 %copy-start.20 = (bf16[128,512]{1,0:T(8,128)(2,1)S(1)}, bf16[128,512]{1,0:T(8,128)(2,1)}, u32[]{:S(2)}) copy-start(bf16[128,512]{1,0:T(8,128)(2,1)} %get-tuple-element.50) | copy-start | bytes 393220
  159.4 14.6 %all-to-all-start.4 = ((bf16[8,2,4096]{2,1,0:T(2,128)(2,1)}), bf16[8,2,4096]{2,1,0:T(2,128)(2,1)}, u32[]{:S(2)}, u32[]{:S(2)}) async-start(bf16[8,2,4096]{2,1,0:T(2,128)(2,1)} %reshape.551), calls=%async_computation.4 | async-start | bytes 262144 | tf_op jit(solution)/shard_map/all_to_all | solution.py:53
  164.7 13.1 %copy-start.14 = (bf16[128,512]{1,0:T(8,128)(2,1)S(1)}, bf16[128,512]{1,0:T(8,128)(2,1)}, u32[]{:S(2)}) copy-start(bf16[128,512]{1,0:T(8,128)(2,1)} %param.11) | copy-start | bytes 393220
  165.5 14.2 %copy-start.10 = (bf16[128,512]{1,0:T(8,128)(2,1)S(1)}, bf16[128,512]{1,0:T(8,128)(2,1)}, u32[]{:S(2)}) copy-start(bf16[128,512]{1,0:T(8,128)(2,1)} %param.12) | copy-start | bytes 393220
  167.3 14.2 %copy-start.6 = (bf16[128,512]{1,0:T(8,128)(2,1)S(1)}, bf16[128,512]{1,0:T(8,128)(2,1)}, u32[]{:S(2)}) copy-start(bf16[128,512]{1,0:T(8,128)(2,1)} %param.10) | copy-start | bytes 393220
  167.3 16.2 %collective-permute-start.19 = (bf16[128,1024]{1,0:T(8,128)(2,1)}, bf16[128,1024]{1,0:T(8,128)(2,1)}, u32[]{:S(2)}, u32[]{:S(2)}) collective-permute-start(bf16[128,1024]{1,0:T(8,128)(2,1)} %add_convert_fusion), channel_id=1, source_target_pairs={{4,0},{8,4},{12,8},{16,12},{20,16},{24,20},{28,24},{32,28},{36,32}... | collective-permute-start | bytes 786440 | tf_op jit(solution)/shard_map/ppermute | solution.py:60
  (8 other events, 27.9 us)

commit v12 on v10

--- a/solution.py
+++ b/solution.py
@@ -12,8 +12,9 @@
 SPAN = 4
 
 
-CTX = ("outer", "inner")
+CTX = ("upper", "lower", "inner")
 INNER = 8
+LOWER = 4
 PLAN = (4, 4)
 
 
@@ -48,7 +49,8 @@
     index = jnp.arange(count)
     place = lax.axis_index(axis)
     mask = index > place if backward else index < place
-    return jnp.sum(jnp.where(mask.reshape((-1,) + (1,) * total.ndim), got, 0.0), axis=0)
+    picked = jnp.where(mask.reshape((-1,) + (1,) * total.ndim), got, 0.0)
+    return jnp.sum(picked, axis=0), jnp.sum(got, axis=0)
 
 
 def carried_in(shard, backward):
@@ -58,7 +60,9 @@
     running = jnp.cumsum(mine, axis=0)
     group = jnp.sum(mine, axis=0)
     within = group[None] - running if backward else running - mine
-    earlier = gathered_before(group, "outer", backward)
+    near, lower = gathered_before(group, "lower", backward)
+    far, _ = gathered_before(lower, "upper", backward)
+    earlier = near + far
     states = (within + earlier[None]).astype(jnp.bfloat16)
     back = lax.all_to_all(states, "inner", 0, 0, tiled=True)
     return back.reshape(shard.shape).astype(shard.dtype)
@@ -171,8 +175,10 @@
     cross_sum = jnp.sum(gain_grad * output_lin, axis=(1, 2))
     sums = jnp.stack([square_sum, cross_sum])
     heads_dev = lax.axis_size("head")
-    spread = jnp.broadcast_to(sums[None], (heads_dev,) + sums.shape)
-    sums = jnp.sum(lax.all_to_all(spread, "head", 0, 0, tiled=True), axis=0)
+    step = 1
+    while step < heads_dev:
+        sums = sums + lax.ppermute(sums, "head", [(i, i ^ step) for i in range(heads_dev)])
+        step *= 2
     square_sum, cross_sum = sums[0], sums[1]
     full_width = LIN_HEADS * HEAD
     inv_rms = lax.rsqrt(square_sum / full_width + 1e-06)[:, None, None]
@@ -254,8 +260,10 @@
     )
     count = mesh.shape["ctx"]
     inner = INNER if count % INNER == 0 else 1
+    outer = count // inner
+    lower = LOWER if outer % LOWER == 0 else 1
     split = jax.sharding.Mesh(
-        mesh.devices.reshape(count // inner, inner, mesh.shape["head"]), CTX + ("head",)
+        mesh.devices.reshape(outer // lower, lower, inner, mesh.shape["head"]), CTX + ("head",)
     )
     return jax.shard_map(
         per_device,

time: 209 us -> 214 us (1.024)
  the two profiles are of different devices: /device:TPU:1 before, /device:TPU:24 now
where the time goes in v12:
time: 214 us; the launch traced here: 211 us
  starting transfers between devices  74.9 us (35%)
  other arithmetic  41.9 us (20%)
  waiting for transfers between devices  40.5 us (19%)
  local copies, waits for them, and re-layouts  34.2 us (16%)
  matrix products  18.1 us (8%)
    all_to_all x4, starting transfers between devices, gathered_before(): got = lax.all_to_all(sent, axis, 0, 0, tiled=True).astype(jnp.float32)  24.6 us
    all_to_all x4, waiting for transfers between devices, gathered_before(): got = lax.all_to_all(sent, axis, 0, 0, tiled=True).astype(jnp.float32)  23.3 us
    ppermute x8, starting transfers between devices, from_behind(): return lax.ppermute(shard, axis, pairs)  23.1 us
    unnamed x90, local copies, waits for them, and re-layouts  19.7 us
    ppermute x8, waiting for transfers between devices, from_behind(): return lax.ppermute(shard, axis, pairs)  11.6 us
    all_to_all x2, starting transfers between devices, carried_in(): mine = lax.all_to_all(slices, 'inner', 0, 0, tiled=True).astype(jnp.float32)  9.9 us
    all_to_all x2, starting transfers between devices, carried_in(): back = lax.all_to_all(states, 'inner', 0, 0, tiled=True)  8.8 us
    ppermute x2, starting transfers between devices, per_device(): lax.ppermute(sums, 'head', [(i, i ^ step) for i in range(heads_dev)])  8.45 us
  transfers between devices with their start and end apart: 18, of which 9 were waited for; matrix products, arithmetic and copies ran while one was open for 36% of the time, Pallas kernels for 0%

profile of v12, /device:TPU:24, one launch (start us, length us, event | category | flops | bytes accessed | tf_op | source)
XLA Modules:
  0.0 211.2 jit_solution(10956013329036027685)
XLA Ops:
  3.6 1.4 reduce.14
  5.8 5.9 %all-to-all-start = ((bf16[8,2,4096]{2,1,0:T(2,128)(2,1)}), bf16[8,2,4096]{2,1,0:T(2,128)(2,1)S(1)}, u32[]{:S(2)}, u32[]{:S(2)}) async-start(bf16[8,2,4096]{2,1,0:T(2,128)(2,1)} %reshape.612), calls=%async_computation | async-start | bytes 262144 | tf_op jit(solution)/shard_map/all_to_all | solution.py:59
  11.8 2.4 %collective-permute-start.2 = (bf16[128,1024]{1,0:T(8,128)(2,1)S(1)}, bf16[128,1024]{1,0:T(8,128)(2,1)S(1)}, u32[]{:S(2)}, u32[]{:S(2)}) collective-permute-start(bf16[128,1024]{1,0:T(8,128)(2,1)S(1)} %pad_maximum_fusion), channel_id=1, source_target_pairs={{0,4},{4,8},{8,12},{12,16},{16,20},{20,24},{24,28},{28,32},{32,36}... | collective-permute-start | bytes 786440 | tf_op jit(solution)/shard_map/ppermute | solution.py:74
  16.9 9.6 %collective-permute-done.2 = bf16[128,1024]{1,0:T(8,128)(2,1)S(1)} collective-permute-done((bf16[128,1024]{1,0:T(8,128)(2,1)S(1)}, bf16[128,1024]{1,0:T(8,128)(2,1)S(1)}, u32[]{:S(2)}, u32[]{:S(2)}) %collective-permute-start.2) | collective-permute-done | bytes 262176 | tf_op jit(solution)/shard_map/ppermute | solution.py:74
  26.5 1.9 collective-permute-start.3
  32.2 6.8 %all-to-all-start.1 = ((bf16[4,2,4096]{2,1,0:T(2,128)(2,1)}), bf16[4,2,4096]{2,1,0:T(2,128)(2,1)S(1)}, u32[]{:S(2)}, u32[]{:S(2)}) async-start(bf16[4,2,4096]{2,1,0:T(2,128)(2,1)} %reshape.614), calls=%async_computation.1 | async-start | bytes 131072 | tf_op jit(solution)/shard_map/all_to_all | solution.py:48
  39.9 2.4 %collective-permute-start.4 = (bf16[128,1024]{1,0:T(8,128)(2,1)S(1)}, bf16[128,1024]{1,0:T(8,128)(2,1)S(1)}, u32[]{:S(2)}, u32[]{:S(2)}) collective-permute-start(bf16[128,1024]{1,0:T(8,128)(2,1)S(1)} %collective-permute-done.3), channel_id=1, source_target_pairs={{0,4},{4,8},{8,12},{12,16},{16,20},{20,24},{24,28},{28,32},{32,36}... | collective-permute-start | bytes 786440 | tf_op jit(solution)/shard_map/ppermute | solution.py:74
  42.3 10.3 %all-to-all-done.1 = bf16[4,2,4096]{2,1,0:T(2,128)(2,1)S(1)} async-done(((bf16[4,2,4096]{2,1,0:T(2,128)(2,1)}), bf16[4,2,4096]{2,1,0:T(2,128)(2,1)S(1)}, u32[]{:S(2)}, u32[]{:S(2)}) %all-to-all-start.1) | async-done | bytes 65568 | tf_op jit(solution)/shard_map/all_to_all | solution.py:48
  54.8 4.7 %all-to-all-start.2 = ((bf16[4,2,4096]{2,1,0:T(2,128)(2,1)}), bf16[4,2,4096]{2,1,0:T(2,128)(2,1)S(1)}, u32[]{:S(2)}, u32[]{:S(2)}) async-start(bf16[4,2,4096]{2,1,0:T(2,128)(2,1)} %reshape.616), calls=%async_computation.2 | async-start | bytes 131072 | tf_op jit(solution)/shard_map/all_to_all | solution.py:48
  59.7 3.4 %all-to-all-done.2 = bf16[4,2,4096]{2,1,0:T(2,128)(2,1)S(1)} async-done(((bf16[4,2,4096]{2,1,0:T(2,128)(2,1)}), bf16[4,2,4096]{2,1,0:T(2,128)(2,1)S(1)}, u32[]{:S(2)}, u32[]{:S(2)}) %all-to-all-start.2) | async-done | bytes 65568 | tf_op jit(solution)/shard_map/all_to_all | solution.py:48
  63.3 1.9 collective-permute-start.5
  65.6 1.4 reduce.17
  67.8 4.8 %all-to-all-start.3 = ((bf16[8,2,4096]{2,1,0:T(2,128)(2,1)}), bf16[8,2,4096]{2,1,0:T(2,128)(2,1)}, u32[]{:S(2)}, u32[]{:S(2)}) async-start(bf16[8,2,4096]{2,1,0:T(2,128)(2,1)} %reshape.618), calls=%async_computation.3 | async-start | bytes 262144 | tf_op jit(solution)/shard_map/all_to_all | solution.py:67
  77.6 1.5 fusion.84
  79.1 1.6 convolution_bitcast_fusion
  85.3 1.4 reshape.596
  89.2 2.4 %scatter_fusion = f32[5,128,512]{2,1,0:T(8,128)S(1)} fusion(f32[5,128,512]{2,1,0:T(8,128)S(1)} %broadcast.280.clone.1, s32[4]{0:T(128)} %fusion.74, f32[4,128,512]{2,1,0:T(8,128)} %reshape.596), kind=kCustom, calls=%fused_computation.2 | custom fusion | flops 262144 | bytes 3145744 | tf_op jit(solution)/shard_map/scatter-add | solution.py:136
  94.7 1.4 reshape.619
  96.9 2.0 multiply_reduce_fusion.1
  99.0 3.5 %collective-permute-start = (f32[2,128]{1,0:T(2,128)S(1)}, f32[2,128]{1,0:T(2,128)S(1)}, u32[]{:S(2)}, u32[]{:S(2)}) collective-permute-start(f32[2,128]{1,0:T(2,128)S(1)} %pad_maximum_fusion.2), channel_id=1, source_target_pairs={{0,1},{1,0},{2,3},{3,2},{4,5},{5,4},{6,7},{7,6},{8,9},{9,8},{10,11... | collective-permute-start | bytes 3080 | tf_op jit(solution)/shard_map/ppermute | solution.py:180
  105.1 4.9 %collective-permute-start.1 = (f32[2,128]{1,0:T(2,128)}, f32[2,128]{1,0:T(2,128)}, u32[]{:S(2)}, u32[]{:S(2)}) collective-permute-start(f32[2,128]{1,0:T(2,128)} %fusion.80), channel_id=1, source_target_pairs={{0,2},{1,3},{2,0},{3,1},{4,6},{5,7},{6,4},{7,5},{8,10},{9,11},{10,... | collective-permute-start | bytes 3080 | tf_op jit(solution)/shard_map/ppermute | solution.py:180
  110.1 1.7 pad_maximum_fusion.1
  112.5 3.8 %collective-permute-start.6 = (bf16[128,1024]{1,0:T(8,128)(2,1)}, bf16[128,1024]{1,0:T(8,128)(2,1)S(1)}, u32[]{:S(2)}, u32[]{:S(2)}) collective-permute-start(bf16[128,1024]{1,0:T(8,128)(2,1)} %pad_maximum_fusion.1), channel_id=1, source_target_pairs={{4,0},{8,4},{12,8},{16,12},{20,16},{24,20},{28,24},{32,28},{36,32}... | collective-permute-start | bytes 786440 | tf_op jit(solution)/shard_map/ppermute | solution.py:74
  119.1 1.5 collective-permute-done.6
  120.5 1.8 add_convert_fusion.2
  122.3 5.8 %collective-permute-start.7 = (bf16[128,1024]{1,0:T(8,128)(2,1)}, bf16[128,1024]{1,0:T(8,128)(2,1)}, u32[]{:S(2)}, u32[]{:S(2)}) collective-permute-start(bf16[128,1024]{1,0:T(8,128)(2,1)} %add_convert_fusion.2), channel_id=1, source_target_pairs={{4,0},{8,4},{12,8},{16,12},{20,16},{24,20},{28,24},{32,28},{36,32}... | collective-permute-start | bytes 786440 | tf_op jit(solution)/shard_map/ppermute | solution.py:74
  130.7 2.4 %reduce.18 = bf16[8,8192]{1,0:T(8,128)(2,1)S(1)} reduce(bf16[8,1,8192]{2,1,0:T(2,128)(2,1)} %all_to_all.47, bf16[]{:T(256)} %broadcast.313), dimensions={1}, to_apply=%all_to_all.47.reduce_sub_computation | reduce | bytes 262146 | tf_op jit(solution)/shard_map/all_to_all | solution.py:59
  133.8 4.0 %all-to-all-start.4 = ((bf16[8,2,4096]{2,1,0:T(2,128)(2,1)}), bf16[8,2,4096]{2,1,0:T(2,128)(2,1)}, u32[]{:S(2)}, u32[]{:S(2)}) async-start(bf16[8,2,4096]{2,1,0:T(2,128)(2,1)} %reshape.620), calls=%async_computation.4 | async-start | bytes 262144 | tf_op jit(solution)/shard_map/all_to_all | solution.py:59
  137.9 1.8 convolution_bitcast_fusion.6
  139.7 1.8 add_convert_fusion.1
  141.5 3.0 %collective-permute-start.8 = (bf16[128,1024]{1,0:T(8,128)(2,1)}, bf16[128,1024]{1,0:T(8,128)(2,1)}, u32[]{:S(2)}, u32[]{:S(2)}) collective-permute-start(bf16[128,1024]{1,0:T(8,128)(2,1)} %add_convert_fusion.1), channel_id=1, source_target_pairs={{4,0},{8,4},{12,8},{16,12},{20,16},{24,20},{28,24},{32,28},{36,32}... | collective-permute-start | bytes 786440 | tf_op jit(solution)/shard_map/ppermute | solution.py:74
  144.6 1.4 reshape.621
  147.6 2.6 %reduce.19 = bf16[4,8192]{1,0:T(4,128)(2,1)} reduce(bf16[4,1,8192]{2,1,0:T(2,128)(2,1)} %broadcast_in_dim.129, bf16[]{:T(256)} %broadcast.313), dimensions={1}, to_apply=%broadcast_in_dim.129.reduce_sub_computation | reduce | bytes 131074 | tf_op jit(solution)/shard_map/broadcast_in_dim | solution.py:47
  150.2 1.6 reshape.622
  151.8 7.3 %all-to-all-start.5 = ((bf16[4,2,4096]{2,1,0:T(2,128)(2,1)}), bf16[4,2,4096]{2,1,0:T(2,128)(2,1)}, u32[]{:S(2)}, u32[]{:S(2)}) async-start(bf16[4,2,4096]{2,1,0:T(2,128)(2,1)} %reshape.622), calls=%async_computation.5 | async-start | bytes 131072 | tf_op jit(solution)/shard_map/all_to_all | solution.py:48
  159.1 1.8 fusion.17
  160.8 1.7 copy.159
  162.5 9.7 %all-to-all-done.5 = bf16[4,2,4096]{2,1,0:T(2,128)(2,1)} async-done(((bf16[4,2,4096]{2,1,0:T(2,128)(2,1)}), bf16[4,2,4096]{2,1,0:T(2,128)(2,1)}, u32[]{:S(2)}, u32[]{:S(2)}) %all-to-all-start.5) | async-done | bytes 65568 | tf_op jit(solution)/shard_map/all_to_all | solution.py:48
  174.0 2.6 %reduce.20 = bf16[4,8192]{1,0:T(4,128)(2,1)} reduce(bf16[4,1,8192]{2,1,0:T(2,128)(2,1)} %broadcast_in_dim.131, bf16[]{:T(256)} %broadcast.313), dimensions={1}, to_apply=%broadcast_in_dim.131.reduce_sub_computation | reduce | bytes 131074 | tf_op jit(solution)/shard_map/broadcast_in_dim | solution.py:47
  176.6 1.5 reshape.624
  178.1 5.8 %all-to-all-start.6 = ((bf16[4,2,4096]{2,1,0:T(2,128)(2,1)}), bf16[4,2,4096]{2,1,0:T(2,128)(2,1)}, u32[]{:S(2)}, u32[]{:S(2)}) async-start(bf16[4,2,4096]{2,1,0:T(2,128)(2,1)} %reshape.624), calls=%async_computation.6 | async-start | bytes 131072 | tf_op jit(solution)/shard_map/all_to_all | solution.py:48
  184.0 1.4 fusion.47
  185.4 1.8 add_convert_fusion
  187.2 1.9 collective-permute-start.9
  191.0 1.8 fusion.4
  192.8 2.4 %reduce.21 = bf16[8,8192]{1,0:T(8,128)(2,1)S(1)} reduce(bf16[8,1,8192]{2,1,0:T(2,128)(2,1)} %fusion.4, bf16[]{:T(256)} %broadcast.313), dimensions={1}, to_apply=%fusion.4.reduce_sub_computation | reduce | bytes 262146 | tf_op jit(solution)/shard_map/jit(cumsum)/reduce_window_sum | solution.py:60
  195.9 4.0 %all-to-all-start.7 = ((bf16[8,2,4096]{2,1,0:T(2,128)(2,1)}), bf16[8,2,4096]{2,1,0:T(2,128)(2,1)}, u32[]{:S(2)}, u32[]{:S(2)}) async-start(bf16[8,2,4096]{2,1,0:T(2,128)(2,1)} %reshape.626), calls=%async_computation.7 | async-start | bytes 262144 | tf_op jit(solution)/shard_map/all_to_all | solution.py:67
  202.6 4.1 %all-to-all-done.7 = bf16[8,2,4096]{2,1,0:T(2,128)(2,1)} async-done(((bf16[8,2,4096]{2,1,0:T(2,128)(2,1)}), bf16[8,2,4096]{2,1,0:T(2,128)(2,1)}, u32[]{:S(2)}, u32[]{:S(2)}) %all-to-all-start.7) | async-done | bytes 131104 | tf_op jit(solution)/shard_map/all_to_all | solution.py:67
  (180 shorter events, 53.1 us)
Async XLA Ops:
  0.6 76.9 %copy-start = (bf16[128,512]{1,0:T(8,128)(2,1)S(1)}, bf16[128,512]{1,0:T(8,128)(2,1)}, u32[]{:S(2)}) copy-start(bf16[128,512]{1,0:T(8,128)(2,1)} %param.15) | copy-start | bytes 393220
  0.6 15.0 %copy-start.11 = (bf16[128,512]{1,0:T(8,128)(2,1)S(1)}, bf16[128,512]{1,0:T(8,128)(2,1)}, u32[]{:S(2)}) copy-start(bf16[128,512]{1,0:T(8,128)(2,1)} %param.11) | copy-start | bytes 393220
  0.7 11.1 %copy-start.15 = (bf16[128,512]{1,0:T(8,128)(2,1)S(1)}, bf16[128,512]{1,0:T(8,128)(2,1)}, u32[]{:S(2)}) copy-start(bf16[128,512]{1,0:T(8,128)(2,1)} %param.17) | copy-start | bytes 393220
  0.7 11.1 %copy-start.16 = (bf16[128,512]{1,0:T(8,128)(2,1)S(1)}, bf16[128,512]{1,0:T(8,128)(2,1)}, u32[]{:S(2)}) copy-start(bf16[128,512]{1,0:T(8,128)(2,1)} %param.16) | copy-start | bytes 393220
  0.7 13.5 %copy-start.31 = (s32[1,3]{1,0:T(1,128)S(1)}, s32[1,3]{1,0:T(1,128)}, u32[]{:S(2)}) copy-start(s32[1,3]{1,0:T(1,128)} %param.19) | copy-start | bytes 40
  0.7 15.0 %copy-start.4 = (bf16[128,512]{1,0:T(8,128)(2,1)S(1)}, bf16[128,512]{1,0:T(8,128)(2,1)}, u32[]{:S(2)}) copy-start(bf16[128,512]{1,0:T(8,128)(2,1)} %param.10) | copy-start | bytes 393220
  1.8 14.1 %copy-start.6 = (bf16[128,512]{0,1:T(8,128)(2,1)}, bf16[128,512]{0,1:T(8,128)(2,1)S(1)}, u32[]{:S(2)}) copy-start(bf16[128,512]{0,1:T(8,128)(2,1)S(1)} %copy.247) | copy-start | bytes 393220
  1.8 14.1 %copy-start.8 = (bf16[128,512]{1,0:T(8,128)(2,1)S(1)}, bf16[128,512]{1,0:T(8,128)(2,1)}, u32[]{:S(2)}) copy-start(bf16[128,512]{1,0:T(8,128)(2,1)} %param.12) | copy-start | bytes 393220
  3.0 25.9 %copy-start.21 = (bf16[128,512]{1,0:T(8,128)(2,1)S(1)}, bf16[128,512]{1,0:T(8,128)(2,1)}, u32[]{:S(2)}) copy-start(bf16[128,512]{1,0:T(8,128)(2,1)} %param.14) | copy-start | bytes 393220
  5.1 24.0 %copy-start.22 = (bf16[128,512]{1,0:T(8,128)(2,1)S(1)}, bf16[128,512]{1,0:T(8,128)(2,1)}, u32[]{:S(2)}) copy-start(bf16[128,512]{1,0:T(8,128)(2,1)} %param.18) | copy-start | bytes 393220
  5.8 24.1 %all-to-all-start = ((bf16[8,2,4096]{2,1,0:T(2,128)(2,1)}), bf16[8,2,4096]{2,1,0:T(2,128)(2,1)S(1)}, u32[]{:S(2)}, u32[]{:S(2)}) async-start(bf16[8,2,4096]{2,1,0:T(2,128)(2,1)} %reshape.612), calls=%async_computation | async-start | bytes 262144 | tf_op jit(solution)/shard_map/all_to_all | solution.py:59
  11.8 14.7 %collective-permute-start.2 = (bf16[128,1024]{1,0:T(8,128)(2,1)S(1)}, bf16[128,1024]{1,0:T(8,128)(2,1)S(1)}, u32[]{:S(2)}, u32[]{:S(2)}) collective-permute-start(bf16[128,1024]{1,0:T(8,128)(2,1)S(1)} %pad_maximum_fusion), channel_id=1, source_target_pairs={{0,4},{4,8},{8,12},{12,16},{16,20},{20,24},{24,28},{28,32},{32,36}... | collective-permute-start | bytes 786440 | tf_op jit(solution)/shard_map/ppermute | solution.py:74
  15.7 58.8 %copy-start.27 = (s32[1024]{0:T(1024)}, s32[1024]{0:T(1024)S(1)}, u32[]{:S(2)}) copy-start(s32[1024]{0:T(1024)S(1)} %pad_clamp_fusion) | copy-start | bytes 12292
  15.9 14.0 %copy-start.17 = (bf16[4,128,128]{2,1,0:T(8,128)(2,1)}, bf16[4,128,128]{2,1,0:T(8,128)(2,1)S(1)}, u32[]{:S(2)}) copy-start(bf16[4,128,128]{2,1,0:T(8,128)(2,1)S(1)} %fusion.19) | copy-start | bytes 393220
  26.5 13.4 %collective-permute-start.3 = (bf16[128,1024]{1,0:T(8,128)(2,1)S(1)}, bf16[128,1024]{1,0:T(8,128)(2,1)S(1)}, u32[]{:S(2)}, u32[]{:S(2)}) collective-permute-start(bf16[128,1024]{1,0:T(8,128)(2,1)S(1)} %collective-permute-done.2), channel_id=1, source_target_pairs={{0,4},{4,8},{8,12},{12,16},{16,20},{20,24},{24,28},{28,32},{32,36}... | collective-permute-start | bytes 786440 | tf_op jit(solution)/shard_map/ppermute | solution.py:74
  32.2 20.4 %all-to-all-start.1 = ((bf16[4,2,4096]{2,1,0:T(2,128)(2,1)}), bf16[4,2,4096]{2,1,0:T(2,128)(2,1)S(1)}, u32[]{:S(2)}, u32[]{:S(2)}) async-start(bf16[4,2,4096]{2,1,0:T(2,128)(2,1)} %reshape.614), calls=%async_computation.1 | async-start | bytes 131072 | tf_op jit(solution)/shard_map/all_to_all | solution.py:48
  39.9 23.4 %collective-permute-start.4 = (bf16[128,1024]{1,0:T(8,128)(2,1)S(1)}, bf16[128,1024]{1,0:T(8,128)(2,1)S(1)}, u32[]{:S(2)}, u32[]{:S(2)}) collective-permute-start(bf16[128,1024]{1,0:T(8,128)(2,1)S(1)} %collective-permute-done.3), channel_id=1, source_target_pairs={{0,4},{4,8},{8,12},{12,16},{16,20},{20,24},{24,28},{28,32},{32,36}... | collective-permute-start | bytes 786440 | tf_op jit(solution)/shard_map/ppermute | solution.py:74
  54.8 8.2 %all-to-all-start.2 = ((bf16[4,2,4096]{2,1,0:T(2,128)(2,1)}), bf16[4,2,4096]{2,1,0:T(2,128)(2,1)S(1)}, u32[]{:S(2)}, u32[]{:S(2)}) async-start(bf16[4,2,4096]{2,1,0:T(2,128)(2,1)} %reshape.616), calls=%async_computation.2 | async-start | bytes 131072 | tf_op jit(solution)/shard_map/all_to_all | solution.py:48
  63.3 9.9 %collective-permute-start.5 = (bf16[128,1024]{1,0:T(8,128)(2,1)S(1)}, bf16[128,1024]{1,0:T(8,128)(2,1)}, u32[]{:S(2)}, u32[]{:S(2)}) collective-permute-start(bf16[128,1024]{1,0:T(8,128)(2,1)S(1)} %collective-permute-done.4), channel_id=1, source_target_pairs={{0,4},{4,8},{8,12},{12,16},{16,20},{20,24},{24,28},{28,32},{32,36}... | collective-permute-start | bytes 786440 | tf_op jit(solution)/shard_map/ppermute | solution.py:74
  67.8 26.8 %all-to-all-start.3 = ((bf16[8,2,4096]{2,1,0:T(2,128)(2,1)}), bf16[8,2,4096]{2,1,0:T(2,128)(2,1)}, u32[]{:S(2)}, u32[]{:S(2)}) async-start(bf16[8,2,4096]{2,1,0:T(2,128)(2,1)} %reshape.618), calls=%async_computation.3 | async-start | bytes 262144 | tf_op jit(solution)/shard_map/all_to_all | solution.py:67
  76.0 1.6 copy-start.24
  79.1 1.6 copy-start.20
  79.1 1.6 copy-start.32
  85.3 1.6 copy-start.29
  91.6 2.1 copy-start.3
  96.9 5.6 %copy-start.1 = (bf16[5,128,512]{2,1,0:T(8,128)(2,1)S(1)}, bf16[5,128,512]{2,1,0:T(8,128)(2,1)}, u32[]{:S(2)}) copy-start(bf16[5,128,512]{2,1,0:T(8,128)(2,1)} %convert.37) | copy-start | bytes 1966084
  96.9 14.9 %copy-start.13 = (bf16[4,128,128]{2,1,0:T(8,128)(2,1)S(1)}, bf16[4,128,128]{2,1,0:T(8,128)(2,1)}, u32[]{:S(2)}) copy-start(bf16[4,128,128]{2,1,0:T(8,128)(2,1)} %convolution_convert_fusion) | copy-start | bytes 393220
  98.9 11.1 %copy-start.25 = (f32[128]{0:T(128)}, f32[128]{0:T(128)S(1)}, u32[]{:S(2)}) copy-start(f32[128]{0:T(128)S(1)} %get-tuple-element.30) | copy-start | bytes 1540
  98.9 11.1 %copy-start.26 = (f32[128]{0:T(128)}, f32[128]{0:T(128)S(1)}, u32[]{:S(2)}) copy-start(f32[128]{0:T(128)S(1)} %get-tuple-element.31) | copy-start | bytes 1540
  98.9 19.2 %copy-start.9 = (bf16[128,512]{1,0:T(8,128)(2,1)S(1)}, bf16[128,512]{1,0:T(8,128)(2,1)}, u32[]{:S(2)}) copy-start(bf16[128,512]{1,0:T(8,128)(2,1)} %param.12) | copy-start | bytes 393220
  99.0 5.6 %collective-permute-start = (f32[2,128]{1,0:T(2,128)S(1)}, f32[2,128]{1,0:T(2,128)S(1)}, u32[]{:S(2)}, u32[]{:S(2)}) collective-permute-start(f32[2,128]{1,0:T(2,128)S(1)} %pad_maximum_fusion.2), channel_id=1, source_target_pairs={{0,1},{1,0},{2,3},{3,2},{4,5},{5,4},{6,7},{7,6},{8,9},{9,8},{10,11... | collective-permute-start | bytes 3080 | tf_op jit(solution)/shard_map/ppermute | solution.py:180
  104.6 5.5 %copy-start.28 = (f32[2,128]{1,0:T(2,128)}, f32[2,128]{1,0:T(2,128)S(1)}, u32[]{:S(2)}) copy-start(f32[2,128]{1,0:T(2,128)S(1)} %collective-permute-done) | copy-start | bytes 3076
  105.1 11.2 %collective-permute-start.1 = (f32[2,128]{1,0:T(2,128)}, f32[2,128]{1,0:T(2,128)}, u32[]{:S(2)}, u32[]{:S(2)}) collective-permute-start(f32[2,128]{1,0:T(2,128)} %fusion.80), channel_id=1, source_target_pairs={{0,2},{1,3},{2,0},{3,1},{4,6},{5,7},{6,4},{7,5},{8,10},{9,11},{10,... | collective-permute-start | bytes 3080 | tf_op jit(solution)/shard_map/ppermute | solution.py:180
  110.1 18.0 %copy-start.5 = (bf16[128,512]{1,0:T(8,128)(2,1)S(1)}, bf16[128,512]{1,0:T(8,128)(2,1)}, u32[]{:S(2)}) copy-start(bf16[128,512]{1,0:T(8,128)(2,1)} %param.10) | copy-start | bytes 393220
  112.5 8.0 %collective-permute-start.6 = (bf16[128,1024]{1,0:T(8,128)(2,1)}, bf16[128,1024]{1,0:T(8,128)(2,1)S(1)}, u32[]{:S(2)}, u32[]{:S(2)}) collective-permute-start(bf16[128,1024]{1,0:T(8,128)(2,1)} %pad_maximum_fusion.1), channel_id=1, source_target_pairs={{4,0},{8,4},{12,8},{16,12},{20,16},{24,20},{28,24},{32,28},{36,32}... | collective-permute-start | bytes 786440 | tf_op jit(solution)/shard_map/ppermute | solution.py:74
  120.5 17.3 %copy-start.7 = (bf16[128,512]{0,1:T(8,128)(2,1)S(1)}, bf16[128,512]{0,1:T(8,128)(2,1)}, u32[]{:S(2)}) copy-start(bf16[128,512]{0,1:T(8,128)(2,1)} %copy-done.6) | copy-start | bytes 393220
  122.3 17.4 %collective-permute-start.7 = (bf16[128,1024]{1,0:T(8,128)(2,1)}, bf16[128,1024]{1,0:T(8,128)(2,1)}, u32[]{:S(2)}, u32[]{:S(2)}) collective-permute-start(bf16[128,1024]{1,0:T(8,128)(2,1)} %add_convert_fusion.2), channel_id=1, source_target_pairs={{4,0},{8,4},{12,8},{16,12},{20,16},{24,20},{28,24},{32,28},{36,32}... | collective-permute-start | bytes 786440 | tf_op jit(solution)/shard_map/ppermute | solution.py:74
  133.8 10.8 %all-to-all-start.4 = ((bf16[8,2,4096]{2,1,0:T(2,128)(2,1)}), bf16[8,2,4096]{2,1,0:T(2,128)(2,1)}, u32[]{:S(2)}, u32[]{:S(2)}) async-start(bf16[8,2,4096]{2,1,0:T(2,128)(2,1)} %reshape.620), calls=%async_computation.4 | async-start | bytes 262144 | tf_op jit(solution)/shard_map/all_to_all | solution.py:59
  141.5 43.9 %collective-permute-start.8 = (bf16[128,1024]{1,0:T(8,128)(2,1)}, bf16[128,1024]{1,0:T(8,128)(2,1)}, u32[]{:S(2)}, u32[]{:S(2)}) collective-permute-start(bf16[128,1024]{1,0:T(8,128)(2,1)} %add_convert_fusion.1), channel_id=1, source_target_pairs={{4,0},{8,4},{12,8},{16,12},{20,16},{24,20},{28,24},{32,28},{36,32}... | collective-permute-start | bytes 786440 | tf_op jit(solution)/shard_map/ppermute | solution.py:74
  151.8 20.4 %all-to-all-start.5 = ((bf16[4,2,4096]{2,1,0:T(2,128)(2,1)}), bf16[4,2,4096]{2,1,0:T(2,128)(2,1)}, u32[]{:S(2)}, u32[]{:S(2)}) async-start(bf16[4,2,4096]{2,1,0:T(2,128)(2,1)} %reshape.622), calls=%async_computation.5 | async-start | bytes 131072 | tf_op jit(solution)/shard_map/all_to_all | solution.py:48
  174.0 16.1 %copy-start.30 = (pred[4]{0:T(512)(128)(4,1)S(1)}, pred[4]{0:T(512)(128)(4,1)}, u32[]{:S(2)}) copy-start(pred[4]{0:T(512)(128)(4,1)} %iota_compare_fusion.2) | copy-start | bytes 16
  178.1 11.0 %all-to-all-start.6 = ((bf16[4,2,4096]{2,1,0:T(2,128)(2,1)}), bf16[4,2,4096]{2,1,0:T(2,128)(2,1)}, u32[]{:S(2)}, u32[]{:S(2)}) async-start(bf16[4,2,4096]{2,1,0:T(2,128)(2,1)} %reshape.624), calls=%async_computation.6 | async-start | bytes 131072 | tf_op jit(solution)/shard_map/all_to_all | solution.py:48
  187.2 13.6 %collective-permute-start.9 = (bf16[128,1024]{1,0:T(8,128)(2,1)}, bf16[128,1024]{1,0:T(8,128)(2,1)}, u32[]{:S(2)}, u32[]{:S(2)}) collective-permute-start(bf16[128,1024]{1,0:T(8,128)(2,1)} %add_convert_fusion), channel_id=1, source_target_pairs={{4,0},{8,4},{12,8},{16,12},{20,16},{24,20},{28,24},{32,28},{36,32}... | collective-permute-start | bytes 786440 | tf_op jit(solution)/shard_map/ppermute | solution.py:74
  190.2 9.7 %copy-start.18 = (bf16[4,128,128]{2,1,0:T(8,128)(2,1)S(1)}, bf16[4,128,128]{2,1,0:T(8,128)(2,1)}, u32[]{:S(2)}) copy-start(bf16[4,128,128]{2,1,0:T(8,128)(2,1)} %copy-done.17) | copy-start | bytes 393220
  195.9 10.8 %all-to-all-start.7 = ((bf16[8,2,4096]{2,1,0:T(2,128)(2,1)}), bf16[8,2,4096]{2,1,0:T(2,128)(2,1)}, u32[]{:S(2)}, u32[]{:S(2)}) async-start(bf16[8,2,4096]{2,1,0:T(2,128)(2,1)} %reshape.626), calls=%async_computation.7 | async-start | bytes 262144 | tf_op jit(solution)/shard_map/all_to_all | solution.py:67
  201.8 7.3 %copy-start.10 = (f32[4,128,128]{2,1,0:T(8,128)S(1)}, f32[4,128,128]{2,1,0:T(8,128)}, u32[]{:S(2)}) copy-start(f32[4,128,128]{2,1,0:T(8,128)} %fusion.87) | copy-start | bytes 786436
  202.6 6.5 %copy-start.12 = (bf16[128,512]{1,0:T(8,128)(2,1)S(1)}, bf16[128,512]{1,0:T(8,128)(2,1)}, u32[]{:S(2)}) copy-start(bf16[128,512]{1,0:T(8,128)(2,1)} %param.11) | copy-start | bytes 393220
  202.6 7.6 %copy-start.14 = (bf16[4,128,128]{2,1,0:T(8,128)(2,1)S(1)}, bf16[4,128,128]{2,1,0:T(8,128)(2,1)}, u32[]{:S(2)}) copy-start(bf16[4,128,128]{2,1,0:T(8,128)(2,1)} %fusion.20) | copy-start | bytes 393220
  (3 other events, 3.4 us)

commit v13 on v9

--- a/solution.py
+++ b/solution.py
@@ -13,8 +13,8 @@
 
 
 CTX = ("outer", "inner")
-INNER = 8
-PLAN = (4, 4)
+INNER = 32
+PLAN = (4,)
 
 
 def scan_over(total, axis, backward):

time: 187 us -> 181 us (0.968)
  starting transfers between devices: 98.6 us -> 81 us
  waiting for transfers between devices: 21.4 us -> 35.9 us
  other arithmetic: 25.5 us -> 23.5 us
    ppermute x12 -> x6, starting transfers between devices: 46.5 us -> 11.4 us  [scan_over(): arrived.append(lax.ppermute(total.astype(jnp.bfloat16), axis, pairs))]
    all_to_all x2, waiting for transfers between devices: 3.92 us -> 14.8 us  [carried_in(): back = lax.all_to_all(states, 'inner', 0, 0, tiled=True)]
    all_to_all x2, starting transfers between devices: 10.2 us -> 20.2 us  [carried_in(): mine = lax.all_to_all(slices, 'inner', 0, 0, tiled=True).astype(jnp.float32)]
    all_to_all x2, waiting for transfers between devices: 3.86 us -> 13.8 us  [carried_in(): mine = lax.all_to_all(slices, 'inner', 0, 0, tiled=True).astype(jnp.float32)]
    ppermute x12 -> x6, waiting for transfers between devices: 10.9 us -> 4.4 us  [scan_over(): arrived.append(lax.ppermute(total.astype(jnp.bfloat16), axis, pairs))]
    all_to_all x2, starting transfers between devices: 8.21 us -> 14.2 us  [carried_in(): back = lax.all_to_all(states, 'inner', 0, 0, tiled=True)]
    unnamed x78 -> x70, local copies, waits for them, and re-layouts: 13.4 us -> 12.4 us
  transfers between devices with their start and end apart: 26 -> 20, of which waited for: 9 -> 7; matrix products, arithmetic and copies ran while one was open for 29% -> 30% of each run, Pallas kernels for 0% -> 0%
where the time goes in v13:
time: 181 us; the launch traced here: 180 us
  starting transfers between devices  81 us (45%)
  waiting for transfers between devices  35.9 us (20%)
  local copies, waits for them, and re-layouts  23.6 us (13%)
  other arithmetic  23.5 us (13%)
  matrix products  14.4 us (8%)
    ppermute x8, starting transfers between devices, from_behind(): return lax.ppermute(shard, axis, pairs)  26.8 us
    all_to_all x2, starting transfers between devices, carried_in(): mine = lax.all_to_all(slices, 'inner', 0, 0, tiled=True).astype(jnp.float32)  20.2 us
    all_to_all x2, waiting for transfers between devices, carried_in(): back = lax.all_to_all(states, 'inner', 0, 0, tiled=True)  14.8 us
    all_to_all x2, starting transfers between devices, carried_in(): back = lax.all_to_all(states, 'inner', 0, 0, tiled=True)  14.2 us
    all_to_all x2, waiting for transfers between devices, carried_in(): mine = lax.all_to_all(slices, 'inner', 0, 0, tiled=True).astype(jnp.float32)  13.8 us
    unnamed x70, local copies, waits for them, and re-layouts  12.4 us
    ppermute x6, starting transfers between devices, scan_over(): arrived.append(lax.ppermute(total.astype(jnp.bfloat16), axis, pairs))  11.4 us
    ppermute x2, starting transfers between devices, per_device(): lax.ppermute(sums, 'head', [(i, i ^ step) for i in range(heads_dev)])  8.33 us
  transfers between devices with their start and end apart: 20, of which 7 were waited for; matrix products, arithmetic and copies ran while one was open for 30% of the time, Pallas kernels for 0%

profile of v13, /device:TPU:24, one launch (start us, length us, event | category | flops | bytes accessed | tf_op | source)
XLA Modules:
  0.0 180.0 jit_solution(693365717816904572)
XLA Ops:
  0.7 1.1 copy.202
  1.8 1.1 convolution_convert_fusion.2
  3.5 1.4 reduce.9
  5.7 15.5 %all-to-all-start = ((bf16[32,2,1024]{2,1,0:T(2,128)(2,1)}), bf16[32,2,1024]{2,1,0:T(2,128)(2,1)S(1)}, u32[]{:S(2)}, u32[]{:S(2)}) async-start(bf16[32,2,1024]{2,1,0:T(2,128)(2,1)} %reshape.544), calls=%async_computation | async-start | bytes 262144 | tf_op jit(solution)/shard_map/all_to_all | solution.py:47
  21.2 2.2 %collective-permute-start.8 = (bf16[128,1024]{1,0:T(8,128)(2,1)S(1)}, bf16[128,1024]{1,0:T(8,128)(2,1)S(1)}, u32[]{:S(2)}, u32[]{:S(2)}) collective-permute-start(bf16[128,1024]{1,0:T(8,128)(2,1)S(1)} %pad_maximum_fusion), channel_id=1, source_target_pairs={{0,4},{4,8},{8,12},{12,16},{16,20},{20,24},{24,28},{28,32},{32,36}... | collective-permute-start | bytes 786440 | tf_op jit(solution)/shard_map/ppermute | solution.py:60
  24.8 13.8 %all-to-all-done = bf16[32,2,1024]{2,1,0:T(2,128)(2,1)S(1)} async-done(((bf16[32,2,1024]{2,1,0:T(2,128)(2,1)}), bf16[32,2,1024]{2,1,0:T(2,128)(2,1)S(1)}, u32[]{:S(2)}, u32[]{:S(2)}) %all-to-all-start) | async-done | bytes 131104 | tf_op jit(solution)/shard_map/all_to_all | solution.py:47
  38.9 1.3 collective-permute-start.2
  40.2 1.3 collective-permute-start.1
  41.5 1.3 collective-permute-start
  42.9 2.8 %collective-permute-done.2 = bf16[2048]{0:T(1024)(128)(2,1)S(1)} collective-permute-done((bf16[2048]{0:T(1024)(128)(2,1)S(1)}, bf16[2048]{0:T(1024)(128)(2,1)S(1)}, u32[]{:S(2)}, u32[]{:S(2)}) %collective-permute-start.2) | collective-permute-done | bytes 4128 | tf_op jit(solution)/shard_map/ppermute | solution.py:37
  45.6 1.6 collective-permute-done.1
  47.7 1.4 reduce.10
  49.8 3.9 %all-to-all-start.1 = ((bf16[32,2,1024]{2,1,0:T(2,128)(2,1)}), bf16[32,2,1024]{2,1,0:T(2,128)(2,1)S(1)}, u32[]{:S(2)}, u32[]{:S(2)}) async-start(bf16[32,2,1024]{2,1,0:T(2,128)(2,1)} %reshape.546), calls=%async_computation.1 | async-start | bytes 262144 | tf_op jit(solution)/shard_map/all_to_all | solution.py:53
  54.2 2.1 %collective-permute-start.9 = (bf16[128,1024]{1,0:T(8,128)(2,1)S(1)}, bf16[128,1024]{1,0:T(8,128)(2,1)S(1)}, u32[]{:S(2)}, u32[]{:S(2)}) collective-permute-start(bf16[128,1024]{1,0:T(8,128)(2,1)S(1)} %collective-permute-done.8), channel_id=1, source_target_pairs={{0,4},{4,8},{8,12},{12,16},{16,20},{20,24},{24,28},{28,32},{32,36}... | collective-permute-start | bytes 786440 | tf_op jit(solution)/shard_map/ppermute | solution.py:60
  56.3 14.8 %all-to-all-done.1 = bf16[32,2,1024]{2,1,0:T(2,128)(2,1)S(1)} async-done(((bf16[32,2,1024]{2,1,0:T(2,128)(2,1)}), bf16[32,2,1024]{2,1,0:T(2,128)(2,1)S(1)}, u32[]{:S(2)}, u32[]{:S(2)}) %all-to-all-start.1) | async-done | bytes 131104 | tf_op jit(solution)/shard_map/all_to_all | solution.py:53
  72.3 3.4 %collective-permute-start.3 = (f32[2,128]{1,0:T(2,128)S(1)}, f32[2,128]{1,0:T(2,128)S(1)}, u32[]{:S(2)}, u32[]{:S(2)}) collective-permute-start(f32[2,128]{1,0:T(2,128)S(1)} %pad_maximum_fusion.2), channel_id=1, source_target_pairs={{0,1},{1,0},{2,3},{3,2},{4,5},{5,4},{6,7},{7,6},{8,9},{9,8},{10,11... | collective-permute-start | bytes 3080 | tf_op jit(solution)/shard_map/ppermute | solution.py:166
  75.7 1.9 %collective-permute-start.10 = (bf16[128,1024]{1,0:T(8,128)(2,1)S(1)}, bf16[128,1024]{1,0:T(8,128)(2,1)S(1)}, u32[]{:S(2)}, u32[]{:S(2)}) collective-permute-start(bf16[128,1024]{1,0:T(8,128)(2,1)S(1)} %collective-permute-done.9), channel_id=1, source_target_pairs={{0,4},{4,8},{8,12},{12,16},{16,20},{20,24},{24,28},{28,32},{32,36}... | collective-permute-start | bytes 786440 | tf_op jit(solution)/shard_map/ppermute | solution.py:60
  77.7 4.9 %collective-permute-start.4 = (f32[2,128]{1,0:T(2,128)S(1)}, f32[2,128]{1,0:T(2,128)S(1)}, u32[]{:S(2)}, u32[]{:S(2)}) collective-permute-start(f32[2,128]{1,0:T(2,128)S(1)} %fusion.78), channel_id=1, source_target_pairs={{0,2},{1,3},{2,0},{3,1},{4,6},{5,7},{6,4},{7,5},{8,10},{9,11},{10,... | collective-permute-start | bytes 3080 | tf_op jit(solution)/shard_map/ppermute | solution.py:166
  82.9 2.6 %collective-permute-done.10 = bf16[128,1024]{1,0:T(8,128)(2,1)S(1)} collective-permute-done((bf16[128,1024]{1,0:T(8,128)(2,1)S(1)}, bf16[128,1024]{1,0:T(8,128)(2,1)S(1)}, u32[]{:S(2)}, u32[]{:S(2)}) %collective-permute-start.10) | collective-permute-done | bytes 262176 | tf_op jit(solution)/shard_map/ppermute | solution.py:60
  85.5 1.9 %collective-permute-start.11 = (bf16[128,1024]{1,0:T(8,128)(2,1)S(1)}, bf16[128,1024]{1,0:T(8,128)(2,1)}, u32[]{:S(2)}, u32[]{:S(2)}) collective-permute-start(bf16[128,1024]{1,0:T(8,128)(2,1)S(1)} %collective-permute-done.10), channel_id=1, source_target_pairs={{0,4},{4,8},{8,12},{12,16},{16,20},{20,24},{24,28},{28,32},{32,36}... | collective-permute-start | bytes 786440 | tf_op jit(solution)/shard_map/ppermute | solution.py:60
  88.7 1.4 reduce.11
  90.8 4.8 %all-to-all-start.2 = ((bf16[32,2,1024]{2,1,0:T(2,128)(2,1)}), bf16[32,2,1024]{2,1,0:T(2,128)(2,1)}, u32[]{:S(2)}, u32[]{:S(2)}) async-start(bf16[32,2,1024]{2,1,0:T(2,128)(2,1)} %reshape.548), calls=%async_computation.2 | async-start | bytes 262144 | tf_op jit(solution)/shard_map/all_to_all | solution.py:47
  101.6 1.5 fusion.81
  103.1 1.6 convolution_bitcast_fusion
  107.5 1.4 reshape.528
  109.0 1.2 scatter_fusion.1
  111.2 2.3 %scatter_fusion = f32[5,128,512]{2,1,0:T(8,128)S(1)} fusion(f32[5,128,512]{2,1,0:T(8,128)S(1)} %broadcast.249.clone.1, s32[4]{0:T(128)S(1)} %fusion.68, f32[4,128,512]{2,1,0:T(8,128)} %reshape.528), kind=kCustom, calls=%fused_computation.2 | custom fusion | flops 262144 | bytes 3145744 | tf_op jit(solution)/shard_map/scatter-add | solution.py:122
  115.1 5.8 %collective-permute-start.12 = (bf16[128,1024]{1,0:T(8,128)(2,1)}, bf16[128,1024]{1,0:T(8,128)(2,1)}, u32[]{:S(2)}, u32[]{:S(2)}) collective-permute-start(bf16[128,1024]{1,0:T(8,128)(2,1)} %pad_maximum_fusion.1), channel_id=1, source_target_pairs={{4,0},{8,4},{12,8},{16,12},{20,16},{24,20},{28,24},{32,28},{36,32}... | collective-permute-start | bytes 786440 | tf_op jit(solution)/shard_map/ppermute | solution.py:60
  121.8 1.4 reshape.549
  123.4 1.4 collective-permute-start.7
  124.8 4.8 %collective-permute-start.6 = (bf16[2048]{0:T(1024)(128)(2,1)S(1)}, bf16[2048]{0:T(1024)(128)(2,1)S(1)}, u32[]{:S(2)}, u32[]{:S(2)}) collective-permute-start(bf16[2048]{0:T(1024)(128)(2,1)S(1)} %convert_element_type.195), channel_id=1, source_target_pairs={{256,0},{384,128},{257,1},{385,129},{258,2},{386,130},{259,3},{387... | collective-permute-start | bytes 12296 | tf_op jit(solution)/shard_map/ppermute | solution.py:37
  129.7 1.3 collective-permute-start.5
  131.0 1.8 %add_convert_fusion.2 = bf16[128,1024]{1,0:T(8,128)(2,1)} fusion(bf16[128,1024]{1,0:T(8,128)(2,1)} %collective-permute-done.12, bf16[128,512]{1,0:T(8,128)(2,1)} %get-tuple-element.34, bf16[128,512]{1,0:T(8,128)(2,1)} %get-tuple-element.30), kind=kLoop, calls=%fused_computation.43 | loop fusion | flops 917504 | bytes 786432 | tf_op jit(solution)/shard_map/convert_element_type | solution.py:221
  132.8 2.6 %collective-permute-start.13 = (bf16[128,1024]{1,0:T(8,128)(2,1)}, bf16[128,1024]{1,0:T(8,128)(2,1)}, u32[]{:S(2)}, u32[]{:S(2)}) collective-permute-start(bf16[128,1024]{1,0:T(8,128)(2,1)} %add_convert_fusion.2), channel_id=1, source_target_pairs={{4,0},{8,4},{12,8},{16,12},{20,16},{24,20},{28,24},{32,28},{36,32}... | collective-permute-start | bytes 786440 | tf_op jit(solution)/shard_map/ppermute | solution.py:60
  135.5 1.0 add_convert_fusion.3
  136.5 2.4 %reduce.12 = bf16[32,2048]{1,0:T(8,128)(2,1)S(1)} reduce(bf16[32,1,2048]{2,1,0:T(2,128)(2,1)} %add_convert_fusion.3, bf16[]{:T(256)} %broadcast.281), dimensions={1}, to_apply=%add_convert_fusion.3.reduce_sub_computation | reduce | bytes 262146 | tf_op jit(solution)/shard_map/jit(cumsum)/reduce_window_sum | solution.py:48
  139.6 10.4 %all-to-all-start.3 = ((bf16[32,2,1024]{2,1,0:T(2,128)(2,1)}), bf16[32,2,1024]{2,1,0:T(2,128)(2,1)}, u32[]{:S(2)}, u32[]{:S(2)}) async-start(bf16[32,2,1024]{2,1,0:T(2,128)(2,1)} %reshape.550), calls=%async_computation.3 | async-start | bytes 262144 | tf_op jit(solution)/shard_map/all_to_all | solution.py:53
  150.0 1.8 %add_convert_fusion.1 = bf16[128,1024]{1,0:T(8,128)(2,1)} fusion(bf16[128,1024]{1,0:T(8,128)(2,1)} %collective-permute-done.13, bf16[128,512]{1,0:T(8,128)(2,1)} %get-tuple-element.33, bf16[128,512]{1,0:T(8,128)(2,1)} %get-tuple-element.29), kind=kLoop, calls=%fused_computation.42 | loop fusion | flops 917504 | bytes 786432 | tf_op jit(solution)/shard_map/convert_element_type | solution.py:221
  151.8 4.3 %collective-permute-start.14 = (bf16[128,1024]{1,0:T(8,128)(2,1)}, bf16[128,1024]{1,0:T(8,128)(2,1)}, u32[]{:S(2)}, u32[]{:S(2)}) collective-permute-start(bf16[128,1024]{1,0:T(8,128)(2,1)} %add_convert_fusion.1), channel_id=1, source_target_pairs={{4,0},{8,4},{12,8},{16,12},{20,16},{24,20},{28,24},{32,28},{36,32}... | collective-permute-start | bytes 786440 | tf_op jit(solution)/shard_map/ppermute | solution.py:60
  156.1 1.9 %fusion.84 = f32[4,128,128]{2,1,0:T(8,128)} fusion(bf16[128,4,128]{0,2,1:T(8,128)(2,1)} %copy-done.2, bf16[4,128,128]{2,1,0:T(8,128)(2,1)} %copy-done.17), kind=kOutput, calls=%fused_computation.148 | convolution fusion | flops 16777216 | bytes 524288 | tf_op jit(solution)/shard_map/hts,thd->shd/dot_general | solution.py:190
  158.7 1.3 convolution_convert_fusion
  161.0 1.7 add_convert_fusion
  162.8 6.0 %collective-permute-start.15 = (bf16[128,1024]{1,0:T(8,128)(2,1)}, bf16[128,1024]{1,0:T(8,128)(2,1)}, u32[]{:S(2)}, u32[]{:S(2)}) collective-permute-start(bf16[128,1024]{1,0:T(8,128)(2,1)} %add_convert_fusion), channel_id=1, source_target_pairs={{4,0},{8,4},{12,8},{16,12},{20,16},{24,20},{28,24},{32,28},{36,32}... | collective-permute-start | bytes 786440 | tf_op jit(solution)/shard_map/ppermute | solution.py:60
  168.8 1.4 reshape.551
  170.2 1.4 reduce.8
  172.5 1.8 %fusion.17 = bf16[4,128,128]{2,1,0:T(8,128)(2,1)} fusion(f32[4,128,128]{2,1,0:T(8,128)} %fusion.84, bf16[4,128,128]{2,1,0:T(8,128)(2,1)S(1)} %reshape.496, bf16[128,512]{1,0:T(8,128)(2,1)S(1)} %copy-done.12), kind=kOutput, calls=%fused_computation.35 | convolution fusion | flops 16908288 | bytes 655360 | tf_op jit(solution)/shard_map/shi,hij->shj/dot_general | solution.py:192
  174.6 1.7 copy.121
  176.3 1.1 fusion.14
  (147 shorter events, 26.7 us)
Async XLA Ops:
  0.6 100.9 %copy-start = (bf16[128,512]{1,0:T(8,128)(2,1)S(1)}, bf16[128,512]{1,0:T(8,128)(2,1)}, u32[]{:S(2)}) copy-start(bf16[128,512]{1,0:T(8,128)(2,1)} %param.15) | copy-start | bytes 393220
  0.6 23.9 %copy-start.11 = (bf16[128,512]{1,0:T(8,128)(2,1)S(1)}, bf16[128,512]{1,0:T(8,128)(2,1)}, u32[]{:S(2)}) copy-start(bf16[128,512]{1,0:T(8,128)(2,1)} %param.11) | copy-start | bytes 393220
  0.7 20.5 %copy-start.15 = (bf16[128,512]{1,0:T(8,128)(2,1)S(1)}, bf16[128,512]{1,0:T(8,128)(2,1)}, u32[]{:S(2)}) copy-start(bf16[128,512]{1,0:T(8,128)(2,1)} %param.17) | copy-start | bytes 393220
  0.7 20.5 %copy-start.16 = (bf16[128,512]{1,0:T(8,128)(2,1)S(1)}, bf16[128,512]{1,0:T(8,128)(2,1)}, u32[]{:S(2)}) copy-start(bf16[128,512]{1,0:T(8,128)(2,1)} %param.16) | copy-start | bytes 393220
  0.7 22.8 %copy-start.25 = (s32[1,3]{1,0:T(1,128)S(1)}, s32[1,3]{1,0:T(1,128)}, u32[]{:S(2)}) copy-start(s32[1,3]{1,0:T(1,128)} %param.19) | copy-start | bytes 40
  0.7 23.9 %copy-start.4 = (bf16[128,512]{1,0:T(8,128)(2,1)S(1)}, bf16[128,512]{1,0:T(8,128)(2,1)}, u32[]{:S(2)}) copy-start(bf16[128,512]{1,0:T(8,128)(2,1)} %param.10) | copy-start | bytes 393220
  5.7 32.9 %all-to-all-start = ((bf16[32,2,1024]{2,1,0:T(2,128)(2,1)}), bf16[32,2,1024]{2,1,0:T(2,128)(2,1)S(1)}, u32[]{:S(2)}, u32[]{:S(2)}) async-start(bf16[32,2,1024]{2,1,0:T(2,128)(2,1)} %reshape.544), calls=%async_computation | async-start | bytes 262144 | tf_op jit(solution)/shard_map/all_to_all | solution.py:47
  21.2 33.0 %collective-permute-start.8 = (bf16[128,1024]{1,0:T(8,128)(2,1)S(1)}, bf16[128,1024]{1,0:T(8,128)(2,1)S(1)}, u32[]{:S(2)}, u32[]{:S(2)}) collective-permute-start(bf16[128,1024]{1,0:T(8,128)(2,1)S(1)} %pad_maximum_fusion), channel_id=1, source_target_pairs={{0,4},{4,8},{8,12},{12,16},{16,20},{20,24},{24,28},{28,32},{32,36}... | collective-permute-start | bytes 786440 | tf_op jit(solution)/shard_map/ppermute | solution.py:60
  24.8 29.2 %copy-start.17 = (bf16[4,128,128]{2,1,0:T(8,128)(2,1)}, bf16[4,128,128]{2,1,0:T(8,128)(2,1)S(1)}, u32[]{:S(2)}) copy-start(bf16[4,128,128]{2,1,0:T(8,128)(2,1)S(1)} %fusion.15) | copy-start | bytes 393220
  24.8 29.0 %copy-start.20 = (bf16[128,512]{1,0:T(8,128)(2,1)S(1)}, bf16[128,512]{1,0:T(8,128)(2,1)}, u32[]{:S(2)}) copy-start(bf16[128,512]{1,0:T(8,128)(2,1)} %param.14) | copy-start | bytes 393220
  24.8 29.1 %copy-start.8 = (bf16[128,512]{1,0:T(8,128)(2,1)S(1)}, bf16[128,512]{1,0:T(8,128)(2,1)}, u32[]{:S(2)}) copy-start(bf16[128,512]{1,0:T(8,128)(2,1)} %param.12) | copy-start | bytes 393220
  38.9 6.7 %collective-permute-start.2 = (bf16[2048]{0:T(1024)(128)(2,1)S(1)}, bf16[2048]{0:T(1024)(128)(2,1)S(1)}, u32[]{:S(2)}, u32[]{:S(2)}) collective-permute-start(bf16[2048]{0:T(1024)(128)(2,1)S(1)} %convert_element_type.183), channel_id=1, source_target_pairs={{0,384},{1,385},{2,386},{3,387},{4,388},{5,389},{6,390},{7,391},{8... | collective-permute-start | bytes 12296 | tf_op jit(solution)/shard_map/ppermute | solution.py:37
  40.2 7.0 %collective-permute-start.1 = (bf16[2048]{0:T(1024)(128)(2,1)S(1)}, bf16[2048]{0:T(1024)(128)(2,1)S(1)}, u32[]{:S(2)}, u32[]{:S(2)}) collective-permute-start(bf16[2048]{0:T(1024)(128)(2,1)S(1)} %convert_element_type.183), channel_id=1, source_target_pairs={{0,256},{128,384},{1,257},{129,385},{2,258},{130,386},{3,259},{131... | collective-permute-start | bytes 12296 | tf_op jit(solution)/shard_map/ppermute | solution.py:37
  41.5 5.7 %collective-permute-start = (bf16[2048]{0:T(1024)(128)(2,1)S(1)}, bf16[2048]{0:T(1024)(128)(2,1)S(1)}, u32[]{:S(2)}, u32[]{:S(2)}) collective-permute-start(bf16[2048]{0:T(1024)(128)(2,1)S(1)} %convert_element_type.183), channel_id=1, source_target_pairs={{0,128},{128,256},{256,384},{1,129},{129,257},{257,385},{2,130},{1... | collective-permute-start | bytes 12296 | tf_op jit(solution)/shard_map/ppermute | solution.py:37
  49.1 22.9 %copy-start.24 = (f32[512]{0:T(512)S(1)}, f32[512]{0:T(512)}, u32[]{:S(2)}) copy-start(f32[512]{0:T(512)} %param.13) | copy-start | bytes 6148
  49.8 21.2 %all-to-all-start.1 = ((bf16[32,2,1024]{2,1,0:T(2,128)(2,1)}), bf16[32,2,1024]{2,1,0:T(2,128)(2,1)S(1)}, u32[]{:S(2)}, u32[]{:S(2)}) async-start(bf16[32,2,1024]{2,1,0:T(2,128)(2,1)} %reshape.546), calls=%async_computation.1 | async-start | bytes 262144 | tf_op jit(solution)/shard_map/all_to_all | solution.py:53
  53.9 28.8 %copy-start.21 = (bf16[128,512]{1,0:T(8,128)(2,1)S(1)}, bf16[128,512]{1,0:T(8,128)(2,1)}, u32[]{:S(2)}) copy-start(bf16[128,512]{1,0:T(8,128)(2,1)} %param.18) | copy-start | bytes 393220
  54.2 21.5 %collective-permute-start.9 = (bf16[128,1024]{1,0:T(8,128)(2,1)S(1)}, bf16[128,1024]{1,0:T(8,128)(2,1)S(1)}, u32[]{:S(2)}, u32[]{:S(2)}) collective-permute-start(bf16[128,1024]{1,0:T(8,128)(2,1)S(1)} %collective-permute-done.8), channel_id=1, source_target_pairs={{0,4},{4,8},{8,12},{12,16},{16,20},{20,24},{24,28},{28,32},{32,36}... | collective-permute-start | bytes 786440 | tf_op jit(solution)/shard_map/ppermute | solution.py:60
  72.0 16.5 %copy-start.6 = (bf16[4,128,128]{2,1,0:T(8,128)(2,1)}, bf16[4,128,128]{2,1,0:T(8,128)(2,1)S(1)}, u32[]{:S(2)}) copy-start(bf16[4,128,128]{2,1,0:T(8,128)(2,1)S(1)} %reshape.495) | copy-start | bytes 393220
  72.3 5.5 %collective-permute-start.3 = (f32[2,128]{1,0:T(2,128)S(1)}, f32[2,128]{1,0:T(2,128)S(1)}, u32[]{:S(2)}, u32[]{:S(2)}) collective-permute-start(f32[2,128]{1,0:T(2,128)S(1)} %pad_maximum_fusion.2), channel_id=1, source_target_pairs={{0,1},{1,0},{2,3},{3,2},{4,5},{5,4},{6,7},{7,6},{8,9},{9,8},{10,11... | collective-permute-start | bytes 3080 | tf_op jit(solution)/shard_map/ppermute | solution.py:166
  75.7 9.8 %collective-permute-start.10 = (bf16[128,1024]{1,0:T(8,128)(2,1)S(1)}, bf16[128,1024]{1,0:T(8,128)(2,1)S(1)}, u32[]{:S(2)}, u32[]{:S(2)}) collective-permute-start(bf16[128,1024]{1,0:T(8,128)(2,1)S(1)} %collective-permute-done.9), channel_id=1, source_target_pairs={{0,4},{4,8},{8,12},{12,16},{16,20},{20,24},{24,28},{28,32},{32,36}... | collective-permute-start | bytes 786440 | tf_op jit(solution)/shard_map/ppermute | solution.py:60
  77.7 9.7 %collective-permute-start.4 = (f32[2,128]{1,0:T(2,128)S(1)}, f32[2,128]{1,0:T(2,128)S(1)}, u32[]{:S(2)}, u32[]{:S(2)}) collective-permute-start(f32[2,128]{1,0:T(2,128)S(1)} %fusion.78), channel_id=1, source_target_pairs={{0,2},{1,3},{2,0},{3,1},{4,6},{5,7},{6,4},{7,5},{8,10},{9,11},{10,... | collective-permute-start | bytes 3080 | tf_op jit(solution)/shard_map/ppermute | solution.py:166
  85.5 5.3 %copy-start.19 = (bf16[128,1024]{1,0:T(8,128)(2,1)}, bf16[128,1024]{1,0:T(8,128)(2,1)S(1)}, u32[]{:S(2)}) copy-start(bf16[128,1024]{1,0:T(8,128)(2,1)S(1)} %collective-permute-done.10) | copy-start | bytes 786436
  85.5 11.0 %collective-permute-start.11 = (bf16[128,1024]{1,0:T(8,128)(2,1)S(1)}, bf16[128,1024]{1,0:T(8,128)(2,1)}, u32[]{:S(2)}, u32[]{:S(2)}) collective-permute-start(bf16[128,1024]{1,0:T(8,128)(2,1)S(1)} %collective-permute-done.10), channel_id=1, source_target_pairs={{0,4},{4,8},{8,12},{12,16},{16,20},{20,24},{24,28},{28,32},{32,36}... | collective-permute-start | bytes 786440 | tf_op jit(solution)/shard_map/ppermute | solution.py:60
  87.6 0.7 copy-start.2
  88.3 8.2 %copy-start.14 = (bf16[4,128,128]{2,1,0:T(8,128)(2,1)}, bf16[4,128,128]{2,1,0:T(8,128)(2,1)S(1)}, u32[]{:S(2)}) copy-start(bf16[4,128,128]{2,1,0:T(8,128)(2,1)S(1)} %fusion.16) | copy-start | bytes 393220
  90.8 31.0 %all-to-all-start.2 = ((bf16[32,2,1024]{2,1,0:T(2,128)(2,1)}), bf16[32,2,1024]{2,1,0:T(2,128)(2,1)}, u32[]{:S(2)}, u32[]{:S(2)}) async-start(bf16[32,2,1024]{2,1,0:T(2,128)(2,1)} %reshape.548), calls=%async_computation.2 | async-start | bytes 262144 | tf_op jit(solution)/shard_map/all_to_all | solution.py:47
  100.2 1.3 copy-start.23
  101.6 1.5 copy-start.22
  103.1 1.6 copy-start.26
  105.4 1.1 copy-start.1
  113.5 7.4 %copy-start.3 = (bf16[128,4,128]{0,2,1:T(8,128)(2,1)S(1)}, bf16[128,4,128]{0,2,1:T(8,128)(2,1)}, u32[]{:S(2)}) copy-start(bf16[128,4,128]{0,2,1:T(8,128)(2,1)} %copy-done.2) | copy-start | bytes 393220
  113.5 7.4 %copy-start.7 = (bf16[4,128,128]{2,1,0:T(8,128)(2,1)S(1)}, bf16[4,128,128]{2,1,0:T(8,128)(2,1)}, u32[]{:S(2)}) copy-start(bf16[4,128,128]{2,1,0:T(8,128)(2,1)} %copy-done.6) | copy-start | bytes 393220
  113.5 7.4 %copy-start.10 = (f32[128,4,128]{0,2,1:T(8,128)S(1)}, f32[128,4,128]{0,2,1:T(8,128)}, u32[]{:S(2)}) copy-start(f32[128,4,128]{0,2,1:T(8,128)} %convolution_bitcast_fusion.6) | copy-start | bytes 786436
  115.1 15.9 %collective-permute-start.12 = (bf16[128,1024]{1,0:T(8,128)(2,1)}, bf16[128,1024]{1,0:T(8,128)(2,1)}, u32[]{:S(2)}, u32[]{:S(2)}) collective-permute-start(bf16[128,1024]{1,0:T(8,128)(2,1)} %pad_maximum_fusion.1), channel_id=1, source_target_pairs={{4,0},{8,4},{12,8},{16,12},{20,16},{24,20},{28,24},{32,28},{36,32}... | collective-permute-start | bytes 786440 | tf_op jit(solution)/shard_map/ppermute | solution.py:60
  123.4 12.0 %collective-permute-start.7 = (bf16[2048]{0:T(1024)(128)(2,1)S(1)}, bf16[2048]{0:T(1024)(128)(2,1)S(1)}, u32[]{:S(2)}, u32[]{:S(2)}) collective-permute-start(bf16[2048]{0:T(1024)(128)(2,1)S(1)} %convert_element_type.195), channel_id=1, source_target_pairs={{384,0},{385,1},{386,2},{387,3},{388,4},{389,5},{390,6},{391,7},{3... | collective-permute-start | bytes 12296 | tf_op jit(solution)/shard_map/ppermute | solution.py:37
  124.8 10.6 %collective-permute-start.6 = (bf16[2048]{0:T(1024)(128)(2,1)S(1)}, bf16[2048]{0:T(1024)(128)(2,1)S(1)}, u32[]{:S(2)}, u32[]{:S(2)}) collective-permute-start(bf16[2048]{0:T(1024)(128)(2,1)S(1)} %convert_element_type.195), channel_id=1, source_target_pairs={{256,0},{384,128},{257,1},{385,129},{258,2},{386,130},{259,3},{387... | collective-permute-start | bytes 12296 | tf_op jit(solution)/shard_map/ppermute | solution.py:37
  129.7 5.8 %collective-permute-start.5 = (bf16[2048]{0:T(1024)(128)(2,1)S(1)}, bf16[2048]{0:T(1024)(128)(2,1)S(1)}, u32[]{:S(2)}, u32[]{:S(2)}) collective-permute-start(bf16[2048]{0:T(1024)(128)(2,1)S(1)} %convert_element_type.195), channel_id=1, source_target_pairs={{128,0},{256,128},{384,256},{129,1},{257,129},{385,257},{130,2},{2... | collective-permute-start | bytes 12296 | tf_op jit(solution)/shard_map/ppermute | solution.py:37
  132.8 17.2 %collective-permute-start.13 = (bf16[128,1024]{1,0:T(8,128)(2,1)}, bf16[128,1024]{1,0:T(8,128)(2,1)}, u32[]{:S(2)}, u32[]{:S(2)}) collective-permute-start(bf16[128,1024]{1,0:T(8,128)(2,1)} %add_convert_fusion.2), channel_id=1, source_target_pairs={{4,0},{8,4},{12,8},{16,12},{20,16},{24,20},{28,24},{32,28},{36,32}... | collective-permute-start | bytes 786440 | tf_op jit(solution)/shard_map/ppermute | solution.py:60
  136.5 21.4 %copy-start.13 = (bf16[128,4,128]{0,2,1:T(8,128)(2,1)S(1)}, bf16[128,4,128]{0,2,1:T(8,128)(2,1)}, u32[]{:S(2)}) copy-start(bf16[128,4,128]{0,2,1:T(8,128)(2,1)} %fusion.13) | copy-start | bytes 393220
  139.6 29.2 %all-to-all-start.3 = ((bf16[32,2,1024]{2,1,0:T(2,128)(2,1)}), bf16[32,2,1024]{2,1,0:T(2,128)(2,1)}, u32[]{:S(2)}, u32[]{:S(2)}) async-start(bf16[32,2,1024]{2,1,0:T(2,128)(2,1)} %reshape.550), calls=%async_computation.3 | async-start | bytes 262144 | tf_op jit(solution)/shard_map/all_to_all | solution.py:53
  151.8 9.2 %copy-start.18 = (bf16[128,512]{1,0:T(8,128)(2,1)S(1)}, bf16[128,512]{1,0:T(8,128)(2,1)}, u32[]{:S(2)}) copy-start(bf16[128,512]{1,0:T(8,128)(2,1)} %get-tuple-element.32) | copy-start | bytes 393220
  151.8 9.2 %collective-permute-start.14 = (bf16[128,1024]{1,0:T(8,128)(2,1)}, bf16[128,1024]{1,0:T(8,128)(2,1)}, u32[]{:S(2)}, u32[]{:S(2)}) collective-permute-start(bf16[128,1024]{1,0:T(8,128)(2,1)} %add_convert_fusion.1), channel_id=1, source_target_pairs={{4,0},{8,4},{12,8},{16,12},{20,16},{24,20},{28,24},{32,28},{36,32}... | collective-permute-start | bytes 786440 | tf_op jit(solution)/shard_map/ppermute | solution.py:60
  160.0 12.5 %copy-start.12 = (bf16[128,512]{1,0:T(8,128)(2,1)S(1)}, bf16[128,512]{1,0:T(8,128)(2,1)}, u32[]{:S(2)}) copy-start(bf16[128,512]{1,0:T(8,128)(2,1)} %param.11) | copy-start | bytes 393220
  160.8 13.6 %copy-start.9 = (bf16[128,512]{1,0:T(8,128)(2,1)S(1)}, bf16[128,512]{1,0:T(8,128)(2,1)}, u32[]{:S(2)}) copy-start(bf16[128,512]{1,0:T(8,128)(2,1)} %param.12) | copy-start | bytes 393220
  162.8 13.5 %copy-start.5 = (bf16[128,512]{1,0:T(8,128)(2,1)S(1)}, bf16[128,512]{1,0:T(8,128)(2,1)}, u32[]{:S(2)}) copy-start(bf16[128,512]{1,0:T(8,128)(2,1)} %param.10) | copy-start | bytes 393220
  162.8 15.4 %collective-permute-start.15 = (bf16[128,1024]{1,0:T(8,128)(2,1)}, bf16[128,1024]{1,0:T(8,128)(2,1)}, u32[]{:S(2)}, u32[]{:S(2)}) collective-permute-start(bf16[128,1024]{1,0:T(8,128)(2,1)} %add_convert_fusion), channel_id=1, source_target_pairs={{4,0},{8,4},{12,8},{16,12},{20,16},{24,20},{28,24},{32,28},{36,32}... | collective-permute-start | bytes 786440 | tf_op jit(solution)/shard_map/ppermute | solution.py:60

commit v14 on v13

--- a/solution.py
+++ b/solution.py
@@ -41,7 +41,7 @@
     return total - own
 
 
-def carried_in(shard, backward):
+def carried_in(shard, backward, tied=None):
     members = lax.axis_size("inner")
     slices = shard.astype(jnp.bfloat16).reshape(members, -1)
     mine = lax.all_to_all(slices, "inner", 0, 0, tiled=True).astype(jnp.float32)
@@ -50,8 +50,10 @@
     within = group[None] - running if backward else running - mine
     earlier = scan_over(group, "outer", backward)
     states = (within + earlier[None]).astype(jnp.bfloat16)
+    if tied is not None:
+        states, tied = lax.optimization_barrier((states, tied))
     back = lax.all_to_all(states, "inner", 0, 0, tiled=True)
-    return back.reshape(shard.shape).astype(shard.dtype)
+    return back.reshape(shard.shape).astype(shard.dtype), tied
 
 
 def from_behind(shard, axis, by):
@@ -143,7 +145,26 @@
     key_lin = lin_key.reshape(token_count, heads_lin, HEAD)
     value_lin = lin_value.reshape(token_count, heads_lin, HEAD)
     key_value = jnp.einsum("thi,thj->hij", key_lin, value_lin, preferred_element_type=jnp.float32)
-    state_low = carried_in(key_value, False)
+    width = sm_key.shape[1]
+    pair = jnp.concatenate([sm_key, sm_value], axis=1)
+    arrived = []
+    moving = pair
+    for distance in range(1, SPAN + 1):
+        moving = from_behind(moving, CTX, 1)
+        arrived.append(moving)
+    key_window = jnp.concatenate(
+        [arrived[SPAN - 1 - place][:, :width] for place in range(SPAN)] + [sm_key], axis=0
+    )
+    value_window = jnp.concatenate(
+        [arrived[SPAN - 1 - place][:, width:] for place in range(SPAN)] + [sm_value], axis=0
+    )
+    shard = lax.axis_index(CTX)
+    sm_dq, key_acc, value_acc = tile_attention(
+        sm_query, sm_grad, key_window, value_window, tile_lists, shard
+    )
+    state_low, (sm_dq, key_acc, value_acc) = carried_in(
+        key_value, False, (sm_dq, key_acc, value_acc)
+    )
     state_half = state_low.astype(jnp.bfloat16)
     causal = jnp.tril(jnp.ones((token_count, token_count), jnp.bool_))
     attn_lin = jnp.where(
@@ -174,7 +195,7 @@
     adjoint_local = jnp.einsum(
         "thi,thj->hij", query_lin, grad_out, preferred_element_type=jnp.float32
     )
-    adjoint_high = carried_in(adjoint_local, True)
+    adjoint_high, _ = carried_in(adjoint_local, True)
     adjoint_half = adjoint_high.astype(jnp.bfloat16)
     grad_scores = jnp.where(
         causal[None],
@@ -193,23 +214,6 @@
     lin_dq = lin_dq.reshape(token_count, lin_width).astype(jnp.bfloat16)
     lin_dk = lin_dk.reshape(token_count, lin_width).astype(jnp.bfloat16)
     lin_dv = lin_dv.reshape(token_count, lin_width).astype(jnp.bfloat16)
-    width = sm_key.shape[1]
-    pair = jnp.concatenate([sm_key, sm_value], axis=1)
-    arrived = []
-    moving = pair
-    for distance in range(1, SPAN + 1):
-        moving = from_behind(moving, CTX, 1)
-        arrived.append(moving)
-    key_window = jnp.concatenate(
-        [arrived[SPAN - 1 - place][:, :width] for place in range(SPAN)] + [sm_key], axis=0
-    )
-    value_window = jnp.concatenate(
-        [arrived[SPAN - 1 - place][:, width:] for place in range(SPAN)] + [sm_value], axis=0
-    )
-    shard = lax.axis_index(CTX)
-    sm_dq, key_acc, value_acc = tile_attention(
-        sm_query, sm_grad, key_window, value_window, tile_lists, shard
-    )
     key_total = key_acc[SPAN]
     value_total = value_acc[SPAN]
     owed = None

time: 181 us -> 201 us (1.11)
  waiting for transfers between devices: 35.9 us -> 55.4 us
  other arithmetic: 23.5 us -> 30.2 us
  starting transfers between devices: 81 us -> 74.4 us
    ppermute x8, waiting for transfers between devices: 2.83 us -> 9.43 us  [from_behind(): return lax.ppermute(shard, axis, pairs)]
    all_to_all x2, waiting for transfers between devices: 13.8 us -> 19.9 us  [carried_in(): mine = lax.all_to_all(slices, 'inner', 0, 0, tiled=True).astype(jnp.float32)]
    all_to_all x2, waiting for transfers between devices: 14.8 us -> 20.5 us  [carried_in(): back = lax.all_to_all(states, 'inner', 0, 0, tiled=True)]
    all_to_all x2, starting transfers between devices: 14.2 us -> 9.15 us  [carried_in(): back = lax.all_to_all(states, 'inner', 0, 0, tiled=True)]
    ppermute x8, starting transfers between devices: 26.8 us -> 24.3 us  [from_behind(): return lax.ppermute(shard, axis, pairs)]
    all_to_all x2 -> x3, other arithmetic: 2.12 us -> 4.63 us  [carried_in(): back = lax.all_to_all(states, 'inner', 0, 0, tiled=True)]
    another operation x4 -> x3, other arithmetic: 5.22 us -> 3.56 us  [carried_in(): running = jnp.cumsum(mine, axis=0)]
    unnamed x70 -> x64, local copies, waits for them, and re-layouts: 12.4 us -> 12.9 us
  transfers between devices with their start and end apart: 20 -> 20, of which waited for: 7 -> 9; matrix products, arithmetic and copies ran while one was open for 30% -> 22% of each run, Pallas kernels for 0% -> 0%
where the time goes in v14:
time: 201 us; the launch traced here: 200 us
  starting transfers between devices  74.4 us (37%)
  waiting for transfers between devices  55.4 us (28%)
  other arithmetic  30.2 us (15%)
  local copies, waits for them, and re-layouts  25.4 us (13%)
  matrix products  13.1 us (7%)
    ppermute x8, starting transfers between devices, from_behind(): return lax.ppermute(shard, axis, pairs)  24.3 us
    all_to_all x2, starting transfers between devices, carried_in(): mine = lax.all_to_all(slices, 'inner', 0, 0, tiled=True).astype(jnp.float32)  20.8 us
    all_to_all x2, waiting for transfers between devices, carried_in(): back = lax.all_to_all(states, 'inner', 0, 0, tiled=True)  20.5 us
    all_to_all x2, waiting for transfers between devices, carried_in(): mine = lax.all_to_all(slices, 'inner', 0, 0, tiled=True).astype(jnp.float32)  19.9 us
    unnamed x64, local copies, waits for them, and re-layouts  12.9 us
    ppermute x6, starting transfers between devices, scan_over(): arrived.append(lax.ppermute(total.astype(jnp.bfloat16), axis, pairs))  11.9 us
    ppermute x8, waiting for transfers between devices, from_behind(): return lax.ppermute(shard, axis, pairs)  9.43 us
    all_to_all x2, starting transfers between devices, carried_in(): back = lax.all_to_all(states, 'inner', 0, 0, tiled=True)  9.15 us
  transfers between devices with their start and end apart: 20, of which 9 were waited for; matrix products, arithmetic and copies ran while one was open for 22% of the time, Pallas kernels for 0%

profile of v14, /device:TPU:24, one launch (start us, length us, event | category | flops | bytes accessed | tf_op | source)
XLA Modules:
  0.0 200.0 jit_solution(5969102873299882254)
XLA Ops:
  1.8 2.1 %collective-permute-start.3 = (bf16[128,1024]{1,0:T(8,128)(2,1)S(1)}, bf16[128,1024]{1,0:T(8,128)(2,1)S(1)}, u32[]{:S(2)}, u32[]{:S(2)}) collective-permute-start(bf16[128,1024]{1,0:T(8,128)(2,1)S(1)} %pad_maximum_fusion), channel_id=1, source_target_pairs={{0,4},{4,8},{8,12},{12,16},{16,20},{20,24},{24,28},{28,32},{32,36}... | collective-permute-start | bytes 786440 | tf_op jit(solution)/shard_map/ppermute | solution.py:62
  6.7 1.4 reduce.9
  8.8 16.2 %all-to-all-start = ((bf16[32,2,1024]{2,1,0:T(2,128)(2,1)}), bf16[32,2,1024]{2,1,0:T(2,128)(2,1)S(1)}, u32[]{:S(2)}, u32[]{:S(2)}) async-start(bf16[32,2,1024]{2,1,0:T(2,128)(2,1)} %reshape.537), calls=%async_computation | async-start | bytes 262144 | tf_op jit(solution)/shard_map/all_to_all | solution.py:47
  26.8 2.2 %collective-permute-start.4 = (bf16[128,1024]{1,0:T(8,128)(2,1)S(1)}, bf16[128,1024]{1,0:T(8,128)(2,1)S(1)}, u32[]{:S(2)}, u32[]{:S(2)}) collective-permute-start(bf16[128,1024]{1,0:T(8,128)(2,1)S(1)} %collective-permute-done.3), channel_id=1, source_target_pairs={{0,4},{4,8},{8,12},{12,16},{16,20},{20,24},{24,28},{28,32},{32,36}... | collective-permute-start | bytes 786440 | tf_op jit(solution)/shard_map/ppermute | solution.py:62
  30.5 11.9 %all-to-all-done = bf16[32,2,1024]{2,1,0:T(2,128)(2,1)S(1)} async-done(((bf16[32,2,1024]{2,1,0:T(2,128)(2,1)}), bf16[32,2,1024]{2,1,0:T(2,128)(2,1)S(1)}, u32[]{:S(2)}, u32[]{:S(2)}) %all-to-all-start) | async-done | bytes 131104 | tf_op jit(solution)/shard_map/all_to_all | solution.py:47
  42.6 1.3 collective-permute-start
  43.9 1.3 collective-permute-start.1
  45.2 1.3 collective-permute-start.2
  46.5 1.9 collective-permute-start.5
  48.8 2.1 %collective-permute-done.1 = bf16[2048]{0:T(1024)(128)(2,1)S(1)} collective-permute-done((bf16[2048]{0:T(1024)(128)(2,1)S(1)}, bf16[2048]{0:T(1024)(128)(2,1)S(1)}, u32[]{:S(2)}, u32[]{:S(2)}) %collective-permute-start.1) | collective-permute-done | bytes 4128 | tf_op jit(solution)/shard_map/ppermute | solution.py:37
  50.9 3.1 %collective-permute-done.2 = bf16[2048]{0:T(1024)(128)(2,1)S(1)} collective-permute-done((bf16[2048]{0:T(1024)(128)(2,1)S(1)}, bf16[2048]{0:T(1024)(128)(2,1)S(1)}, u32[]{:S(2)}, u32[]{:S(2)}) %collective-permute-start.2) | collective-permute-done | bytes 4128 | tf_op jit(solution)/shard_map/ppermute | solution.py:37
  54.0 2.3 %collective-permute-done.5 = bf16[128,1024]{1,0:T(8,128)(2,1)S(1)} collective-permute-done((bf16[128,1024]{1,0:T(8,128)(2,1)S(1)}, bf16[128,1024]{1,0:T(8,128)(2,1)S(1)}, u32[]{:S(2)}, u32[]{:S(2)}) %collective-permute-start.5) | collective-permute-done | bytes 262176 | tf_op jit(solution)/shard_map/ppermute | solution.py:62
  56.3 1.9 collective-permute-start.6
  59.0 7.1 %collective-permute-done.6 = bf16[128,1024]{1,0:T(8,128)(2,1)S(1)} collective-permute-done((bf16[128,1024]{1,0:T(8,128)(2,1)S(1)}, bf16[128,1024]{1,0:T(8,128)(2,1)S(1)}, u32[]{:S(2)}, u32[]{:S(2)}) %collective-permute-start.6) | collective-permute-done | bytes 262176 | tf_op jit(solution)/shard_map/ppermute | solution.py:62
  69.2 1.5 fusion.77
  70.7 1.6 convolution_bitcast_fusion
  76.0 1.4 reshape.521
  77.6 1.2 scatter_fusion.1
  78.9 2.3 %scatter_fusion = f32[5,128,512]{2,1,0:T(8,128)S(1)} fusion(f32[5,128,512]{2,1,0:T(8,128)S(1)} %broadcast.246.clone, s32[4]{0:T(128)S(1)} %copy-done.21, f32[4,128,512]{2,1,0:T(8,128)} %reshape.521), kind=kCustom, calls=%fused_computation.2 | custom fusion | flops 262144 | bytes 3145744 | tf_op jit(solution)/shard_map/scatter-add | solution.py:124
  82.3 1.6 reduce.10
  84.6 4.6 %all-to-all-start.1 = ((bf16[32,2,1024]{2,1,0:T(2,128)(2,1)}), bf16[32,2,1024]{2,1,0:T(2,128)(2,1)}, u32[]{:S(2)}, u32[]{:S(2)}) async-start(bf16[32,2,1024]{2,1,0:T(2,128)(2,1)} %reshape.539), calls=%async_computation.1 | async-start | bytes 262144 | tf_op jit(solution)/shard_map/all_to_all | solution.py:55
  91.9 6.3 %collective-permute-start.12 = (bf16[128,1024]{1,0:T(8,128)(2,1)}, bf16[128,1024]{1,0:T(8,128)(2,1)}, u32[]{:S(2)}, u32[]{:S(2)}) collective-permute-start(bf16[128,1024]{1,0:T(8,128)(2,1)} %pad_maximum_fusion.1), channel_id=1, source_target_pairs={{4,0},{8,4},{12,8},{16,12},{20,16},{24,20},{28,24},{32,28},{36,32}... | collective-permute-start | bytes 786440 | tf_op jit(solution)/shard_map/ppermute | solution.py:62
  98.2 8.1 %all-to-all-done.1 = bf16[32,2,1024]{2,1,0:T(2,128)(2,1)} async-done(((bf16[32,2,1024]{2,1,0:T(2,128)(2,1)}), bf16[32,2,1024]{2,1,0:T(2,128)(2,1)}, u32[]{:S(2)}, u32[]{:S(2)}) %all-to-all-start.1) | async-done | bytes 131104 | tf_op jit(solution)/shard_map/all_to_all | solution.py:55
  106.3 2.0 reshape.540
  108.3 2.3 %reduce.7 = bf16[32,2048]{1,0:T(8,128)(2,1)} reduce(bf16[32,1,2048]{2,1,0:T(2,128)(2,1)} %reshape.540, bf16[]{:T(256)} %constant.86), dimensions={1}, to_apply=%all_to_all.25.reduce_sub_computation | reduce | bytes 262146 | tf_op jit(solution)/shard_map/all_to_all | solution.py:55
  111.6 1.6 multiply_reduce_fusion.1
  113.8 3.4 %collective-permute-start.7 = (f32[2,128]{1,0:T(2,128)S(1)}, f32[2,128]{1,0:T(2,128)S(1)}, u32[]{:S(2)}, u32[]{:S(2)}) collective-permute-start(f32[2,128]{1,0:T(2,128)S(1)} %pad_maximum_fusion.2), channel_id=1, source_target_pairs={{0,1},{1,0},{2,3},{3,2},{4,5},{5,4},{6,7},{7,6},{8,9},{9,8},{10,11... | collective-permute-start | bytes 3080 | tf_op jit(solution)/shard_map/ppermute | solution.py:187
  117.2 1.7 copy.122
  120.0 4.9 %collective-permute-start.8 = (f32[2,128]{1,0:T(2,128)S(1)}, f32[2,128]{1,0:T(2,128)S(1)}, u32[]{:S(2)}, u32[]{:S(2)}) collective-permute-start(f32[2,128]{1,0:T(2,128)S(1)} %fusion.74), channel_id=1, source_target_pairs={{0,2},{1,3},{2,0},{3,1},{4,6},{5,7},{6,4},{7,5},{8,10},{9,11},{10,... | collective-permute-start | bytes 3080 | tf_op jit(solution)/shard_map/ppermute | solution.py:187
  124.9 1.8 add_convert_fusion.2
  126.7 1.9 collective-permute-start.13
  129.4 1.1 subtract_convert_fusion
  131.6 2.3 %reduce.11 = bf16[32,2048]{1,0:T(8,128)(2,1)S(1)} reduce(bf16[32,1,2048]{2,1,0:T(2,128)(2,1)} %all_to_all.30, bf16[]{:T(256)} %broadcast.279), dimensions={1}, to_apply=%all_to_all.30.reduce_sub_computation | reduce | bytes 262146 | tf_op jit(solution)/shard_map/all_to_all | solution.py:47
  134.6 4.6 %all-to-all-start.2 = ((bf16[32,2,1024]{2,1,0:T(2,128)(2,1)}), bf16[32,2,1024]{2,1,0:T(2,128)(2,1)}, u32[]{:S(2)}, u32[]{:S(2)}) async-start(bf16[32,2,1024]{2,1,0:T(2,128)(2,1)} %reshape.541), calls=%async_computation.2 | async-start | bytes 262144 | tf_op jit(solution)/shard_map/all_to_all | solution.py:47
  139.5 1.9 add_convert_fusion.1
  141.4 6.1 %collective-permute-start.14 = (bf16[128,1024]{1,0:T(8,128)(2,1)}, bf16[128,1024]{1,0:T(8,128)(2,1)}, u32[]{:S(2)}, u32[]{:S(2)}) collective-permute-start(bf16[128,1024]{1,0:T(8,128)(2,1)} %add_convert_fusion.1), channel_id=1, source_target_pairs={{4,0},{8,4},{12,8},{16,12},{20,16},{24,20},{28,24},{32,28},{36,32}... | collective-permute-start | bytes 786440 | tf_op jit(solution)/shard_map/ppermute | solution.py:62
  148.4 8.0 %all-to-all-done.2 = bf16[32,2,1024]{2,1,0:T(2,128)(2,1)} async-done(((bf16[32,2,1024]{2,1,0:T(2,128)(2,1)}), bf16[32,2,1024]{2,1,0:T(2,128)(2,1)}, u32[]{:S(2)}, u32[]{:S(2)}) %all-to-all-start.2) | async-done | bytes 131104 | tf_op jit(solution)/shard_map/all_to_all | solution.py:47
  156.4 1.4 reshape.542
  158.0 5.4 %collective-permute-start.10 = (bf16[2048]{0:T(1024)(128)(2,1)S(1)}, bf16[2048]{0:T(1024)(128)(2,1)S(1)}, u32[]{:S(2)}, u32[]{:S(2)}) collective-permute-start(bf16[2048]{0:T(1024)(128)(2,1)S(1)} %convert_element_type.203), channel_id=1, source_target_pairs={{256,0},{384,128},{257,1},{385,129},{258,2},{386,130},{259,3},{387... | collective-permute-start | bytes 12296 | tf_op jit(solution)/shard_map/ppermute | solution.py:37
  163.4 1.3 collective-permute-start.11
  164.7 1.3 collective-permute-start.9
  166.0 1.8 add_convert_fusion
  167.8 1.9 collective-permute-start.15
  170.8 2.3 %reduce.12 = bf16[32,2048]{1,0:T(8,128)(2,1)S(1)} reduce(bf16[32,1,2048]{2,1,0:T(2,128)(2,1)} %add_convert_fusion.3, bf16[]{:T(256)} %broadcast.279), dimensions={1}, to_apply=%add_convert_fusion.3.reduce_sub_computation | reduce | bytes 262146 | tf_op jit(solution)/shard_map/jit(cumsum)/reduce_window_sum | solution.py:48
  173.9 4.6 %all-to-all-start.3 = ((bf16[32,2,1024]{2,1,0:T(2,128)(2,1)}), bf16[32,2,1024]{2,1,0:T(2,128)(2,1)}, u32[]{:S(2)}, u32[]{:S(2)}) async-start(bf16[32,2,1024]{2,1,0:T(2,128)(2,1)} %reshape.543), calls=%async_computation.3 | async-start | bytes 262144 | tf_op jit(solution)/shard_map/all_to_all | solution.py:55
  178.4 1.1 fusion.13
  183.2 12.4 %all-to-all-done.3 = bf16[32,2,1024]{2,1,0:T(2,128)(2,1)} async-done(((bf16[32,2,1024]{2,1,0:T(2,128)(2,1)}), bf16[32,2,1024]{2,1,0:T(2,128)(2,1)}, u32[]{:S(2)}, u32[]{:S(2)}) %all-to-all-start.3) | async-done | bytes 131104 | tf_op jit(solution)/shard_map/all_to_all | solution.py:55
  195.6 1.4 reshape.544
  (143 shorter events, 35.5 us)
Async XLA Ops:
  0.6 68.6 %copy-start = (bf16[128,512]{1,0:T(8,128)(2,1)S(1)}, bf16[128,512]{1,0:T(8,128)(2,1)}, u32[]{:S(2)}) copy-start(bf16[128,512]{1,0:T(8,128)(2,1)} %param.15) | copy-start | bytes 393220
  0.6 24.6 %copy-start.10 = (bf16[128,512]{1,0:T(8,128)(2,1)S(1)}, bf16[128,512]{1,0:T(8,128)(2,1)}, u32[]{:S(2)}) copy-start(bf16[128,512]{1,0:T(8,128)(2,1)} %param.11) | copy-start | bytes 393220
  0.7 24.4 %copy-start.22 = (s32[1,3]{1,0:T(1,128)S(1)}, s32[1,3]{1,0:T(1,128)}, u32[]{:S(2)}) copy-start(s32[1,3]{1,0:T(1,128)} %param.19) | copy-start | bytes 40
  0.7 24.6 %copy-start.3 = (bf16[128,512]{1,0:T(8,128)(2,1)S(1)}, bf16[128,512]{1,0:T(8,128)(2,1)}, u32[]{:S(2)}) copy-start(bf16[128,512]{1,0:T(8,128)(2,1)} %param.10) | copy-start | bytes 393220
  1.8 24.1 %copy-start.7 = (bf16[128,512]{1,0:T(8,128)(2,1)S(1)}, bf16[128,512]{1,0:T(8,128)(2,1)}, u32[]{:S(2)}) copy-start(bf16[128,512]{1,0:T(8,128)(2,1)} %param.12) | copy-start | bytes 393220
  1.8 25.0 %collective-permute-start.3 = (bf16[128,1024]{1,0:T(8,128)(2,1)S(1)}, bf16[128,1024]{1,0:T(8,128)(2,1)S(1)}, u32[]{:S(2)}, u32[]{:S(2)}) collective-permute-start(bf16[128,1024]{1,0:T(8,128)(2,1)S(1)} %pad_maximum_fusion), channel_id=1, source_target_pairs={{0,4},{4,8},{8,12},{12,16},{16,20},{20,24},{24,28},{28,32},{32,36}... | collective-permute-start | bytes 786440 | tf_op jit(solution)/shard_map/ppermute | solution.py:62
  4.9 21.9 %copy-start.5 = (bf16[128,512]{0,1:T(8,128)(2,1)}, bf16[128,512]{0,1:T(8,128)(2,1)S(1)}, u32[]{:S(2)}) copy-start(bf16[128,512]{0,1:T(8,128)(2,1)S(1)} %copy.205) | copy-start | bytes 393220
  6.0 23.6 %copy-start.18 = (bf16[128,512]{1,0:T(8,128)(2,1)S(1)}, bf16[128,512]{1,0:T(8,128)(2,1)}, u32[]{:S(2)}) copy-start(bf16[128,512]{1,0:T(8,128)(2,1)} %param.18) | copy-start | bytes 393220
  6.1 23.6 %copy-start.17 = (bf16[128,512]{1,0:T(8,128)(2,1)S(1)}, bf16[128,512]{1,0:T(8,128)(2,1)}, u32[]{:S(2)}) copy-start(bf16[128,512]{1,0:T(8,128)(2,1)} %param.14) | copy-start | bytes 393220
  8.8 33.6 %all-to-all-start = ((bf16[32,2,1024]{2,1,0:T(2,128)(2,1)}), bf16[32,2,1024]{2,1,0:T(2,128)(2,1)S(1)}, u32[]{:S(2)}, u32[]{:S(2)}) async-start(bf16[32,2,1024]{2,1,0:T(2,128)(2,1)} %reshape.537), calls=%async_computation | async-start | bytes 262144 | tf_op jit(solution)/shard_map/all_to_all | solution.py:47
  25.5 23.0 %copy-start.16 = (bf16[4,128,128]{2,1,0:T(8,128)(2,1)}, bf16[4,128,128]{2,1,0:T(8,128)(2,1)S(1)}, u32[]{:S(2)}) copy-start(bf16[4,128,128]{2,1,0:T(8,128)(2,1)S(1)} %fusion.15) | copy-start | bytes 393220
  26.8 19.7 %collective-permute-start.4 = (bf16[128,1024]{1,0:T(8,128)(2,1)S(1)}, bf16[128,1024]{1,0:T(8,128)(2,1)S(1)}, u32[]{:S(2)}, u32[]{:S(2)}) collective-permute-start(bf16[128,1024]{1,0:T(8,128)(2,1)S(1)} %collective-permute-done.3), channel_id=1, source_target_pairs={{0,4},{4,8},{8,12},{12,16},{16,20},{20,24},{24,28},{28,32},{32,36}... | collective-permute-start | bytes 786440 | tf_op jit(solution)/shard_map/ppermute | solution.py:62
  42.6 6.2 %collective-permute-start = (bf16[2048]{0:T(1024)(128)(2,1)S(1)}, bf16[2048]{0:T(1024)(128)(2,1)S(1)}, u32[]{:S(2)}, u32[]{:S(2)}) collective-permute-start(bf16[2048]{0:T(1024)(128)(2,1)S(1)} %convert_element_type.183), channel_id=1, source_target_pairs={{0,128},{128,256},{256,384},{1,129},{129,257},{257,385},{2,130},{1... | collective-permute-start | bytes 12296 | tf_op jit(solution)/shard_map/ppermute | solution.py:37
  43.9 7.0 %collective-permute-start.1 = (bf16[2048]{0:T(1024)(128)(2,1)S(1)}, bf16[2048]{0:T(1024)(128)(2,1)S(1)}, u32[]{:S(2)}, u32[]{:S(2)}) collective-permute-start(bf16[2048]{0:T(1024)(128)(2,1)S(1)} %convert_element_type.183), channel_id=1, source_target_pairs={{0,256},{128,384},{1,257},{129,385},{2,258},{130,386},{3,259},{131... | collective-permute-start | bytes 12296 | tf_op jit(solution)/shard_map/ppermute | solution.py:37
  45.2 8.8 %collective-permute-start.2 = (bf16[2048]{0:T(1024)(128)(2,1)S(1)}, bf16[2048]{0:T(1024)(128)(2,1)S(1)}, u32[]{:S(2)}, u32[]{:S(2)}) collective-permute-start(bf16[2048]{0:T(1024)(128)(2,1)S(1)} %convert_element_type.183), channel_id=1, source_target_pairs={{0,384},{1,385},{2,386},{3,387},{4,388},{5,389},{6,390},{7,391},{8... | collective-permute-start | bytes 12296 | tf_op jit(solution)/shard_map/ppermute | solution.py:37
  46.5 9.8 %collective-permute-start.5 = (bf16[128,1024]{1,0:T(8,128)(2,1)S(1)}, bf16[128,1024]{1,0:T(8,128)(2,1)S(1)}, u32[]{:S(2)}, u32[]{:S(2)}) collective-permute-start(bf16[128,1024]{1,0:T(8,128)(2,1)S(1)} %collective-permute-done.4), channel_id=1, source_target_pairs={{0,4},{4,8},{8,12},{12,16},{16,20},{20,24},{24,28},{28,32},{32,36}... | collective-permute-start | bytes 786440 | tf_op jit(solution)/shard_map/ppermute | solution.py:62
  54.0 12.2 %copy-start.14 = (bf16[128,512]{1,0:T(8,128)(2,1)S(1)}, bf16[128,512]{1,0:T(8,128)(2,1)}, u32[]{:S(2)}) copy-start(bf16[128,512]{1,0:T(8,128)(2,1)} %param.17) | copy-start | bytes 393220
  54.0 12.2 %copy-start.15 = (bf16[128,512]{1,0:T(8,128)(2,1)S(1)}, bf16[128,512]{1,0:T(8,128)(2,1)}, u32[]{:S(2)}) copy-start(bf16[128,512]{1,0:T(8,128)(2,1)} %param.16) | copy-start | bytes 393220
  56.3 9.8 %collective-permute-start.6 = (bf16[128,1024]{1,0:T(8,128)(2,1)S(1)}, bf16[128,1024]{1,0:T(8,128)(2,1)S(1)}, u32[]{:S(2)}, u32[]{:S(2)}) collective-permute-start(bf16[128,1024]{1,0:T(8,128)(2,1)S(1)} %collective-permute-done.5), channel_id=1, source_target_pairs={{0,4},{4,8},{8,12},{12,16},{16,20},{20,24},{24,28},{28,32},{32,36}... | collective-permute-start | bytes 786440 | tf_op jit(solution)/shard_map/ppermute | solution.py:62
  70.7 1.6 copy-start.23
  76.0 1.6 copy-start.21
  84.6 21.7 %all-to-all-start.1 = ((bf16[32,2,1024]{2,1,0:T(2,128)(2,1)}), bf16[32,2,1024]{2,1,0:T(2,128)(2,1)}, u32[]{:S(2)}, u32[]{:S(2)}) async-start(bf16[32,2,1024]{2,1,0:T(2,128)(2,1)} %reshape.539), calls=%async_computation.1 | async-start | bytes 262144 | tf_op jit(solution)/shard_map/all_to_all | solution.py:55
  89.1 1.2 copy-start.2
  90.4 21.2 %copy-start.1 = (f32[128,512]{0,1:T(8,128)S(1)}, f32[128,512]{0,1:T(8,128)}, u32[]{:S(2)}) copy-start(f32[128,512]{0,1:T(8,128)} %copy.84) | copy-start | bytes 786436
  90.4 21.2 %copy-start.4 = (bf16[128,512]{1,0:T(8,128)(2,1)S(1)}, bf16[128,512]{1,0:T(8,128)(2,1)}, u32[]{:S(2)}) copy-start(bf16[128,512]{1,0:T(8,128)(2,1)} %param.10) | copy-start | bytes 393220
  90.4 21.2 %copy-start.9 = (f32[128,4,128]{0,2,1:T(8,128)S(1)}, f32[128,4,128]{0,2,1:T(8,128)}, u32[]{:S(2)}) copy-start(f32[128,4,128]{0,2,1:T(8,128)} %convolution_bitcast_fusion.8) | copy-start | bytes 786436
  91.9 33.0 %collective-permute-start.12 = (bf16[128,1024]{1,0:T(8,128)(2,1)}, bf16[128,1024]{1,0:T(8,128)(2,1)}, u32[]{:S(2)}, u32[]{:S(2)}) collective-permute-start(bf16[128,1024]{1,0:T(8,128)(2,1)} %pad_maximum_fusion.1), channel_id=1, source_target_pairs={{4,0},{8,4},{12,8},{16,12},{20,16},{24,20},{28,24},{32,28},{36,32}... | collective-permute-start | bytes 786440 | tf_op jit(solution)/shard_map/ppermute | solution.py:62
  113.3 0.5 copy-start.19
  113.3 0.6 copy-start.20
  113.8 5.5 %collective-permute-start.7 = (f32[2,128]{1,0:T(2,128)S(1)}, f32[2,128]{1,0:T(2,128)S(1)}, u32[]{:S(2)}, u32[]{:S(2)}) collective-permute-start(f32[2,128]{1,0:T(2,128)S(1)} %pad_maximum_fusion.2), channel_id=1, source_target_pairs={{0,1},{1,0},{2,3},{3,2},{4,5},{5,4},{6,7},{7,6},{8,9},{9,8},{10,11... | collective-permute-start | bytes 3080 | tf_op jit(solution)/shard_map/ppermute | solution.py:187
  120.0 8.7 %collective-permute-start.8 = (f32[2,128]{1,0:T(2,128)S(1)}, f32[2,128]{1,0:T(2,128)S(1)}, u32[]{:S(2)}, u32[]{:S(2)}) collective-permute-start(f32[2,128]{1,0:T(2,128)S(1)} %fusion.74), channel_id=1, source_target_pairs={{0,2},{1,3},{2,0},{3,1},{4,6},{5,7},{6,4},{7,5},{8,10},{9,11},{10,... | collective-permute-start | bytes 3080 | tf_op jit(solution)/shard_map/ppermute | solution.py:187
  126.7 12.8 %collective-permute-start.13 = (bf16[128,1024]{1,0:T(8,128)(2,1)}, bf16[128,1024]{1,0:T(8,128)(2,1)}, u32[]{:S(2)}, u32[]{:S(2)}) collective-permute-start(bf16[128,1024]{1,0:T(8,128)(2,1)} %add_convert_fusion.2), channel_id=1, source_target_pairs={{4,0},{8,4},{12,8},{16,12},{20,16},{24,20},{28,24},{32,28},{36,32}... | collective-permute-start | bytes 786440 | tf_op jit(solution)/shard_map/ppermute | solution.py:62
  129.4 9.9 %copy-start.8 = (bf16[128,512]{1,0:T(8,128)(2,1)S(1)}, bf16[128,512]{1,0:T(8,128)(2,1)}, u32[]{:S(2)}) copy-start(bf16[128,512]{1,0:T(8,128)(2,1)} %param.12) | copy-start | bytes 393220
  130.8 16.7 %copy-start.6 = (bf16[128,512]{0,1:T(8,128)(2,1)S(1)}, bf16[128,512]{0,1:T(8,128)(2,1)}, u32[]{:S(2)}) copy-start(bf16[128,512]{0,1:T(8,128)(2,1)} %copy-done.5) | copy-start | bytes 393220
  134.6 21.7 %all-to-all-start.2 = ((bf16[32,2,1024]{2,1,0:T(2,128)(2,1)}), bf16[32,2,1024]{2,1,0:T(2,128)(2,1)}, u32[]{:S(2)}, u32[]{:S(2)}) async-start(bf16[32,2,1024]{2,1,0:T(2,128)(2,1)} %reshape.541), calls=%async_computation.2 | async-start | bytes 262144 | tf_op jit(solution)/shard_map/all_to_all | solution.py:47
  139.5 8.0 %copy-start.12 = (bf16[4,128,128]{2,1,0:T(8,128)(2,1)}, bf16[4,128,128]{2,1,0:T(8,128)(2,1)S(1)}, u32[]{:S(2)}) copy-start(bf16[4,128,128]{2,1,0:T(8,128)(2,1)S(1)} %fusion.16) | copy-start | bytes 393220
  141.4 24.6 %collective-permute-start.14 = (bf16[128,1024]{1,0:T(8,128)(2,1)}, bf16[128,1024]{1,0:T(8,128)(2,1)}, u32[]{:S(2)}, u32[]{:S(2)}) collective-permute-start(bf16[128,1024]{1,0:T(8,128)(2,1)} %add_convert_fusion.1), channel_id=1, source_target_pairs={{4,0},{8,4},{12,8},{16,12},{20,16},{24,20},{28,24},{32,28},{36,32}... | collective-permute-start | bytes 786440 | tf_op jit(solution)/shard_map/ppermute | solution.py:62
  158.0 11.8 %collective-permute-start.10 = (bf16[2048]{0:T(1024)(128)(2,1)S(1)}, bf16[2048]{0:T(1024)(128)(2,1)S(1)}, u32[]{:S(2)}, u32[]{:S(2)}) collective-permute-start(bf16[2048]{0:T(1024)(128)(2,1)S(1)} %convert_element_type.203), channel_id=1, source_target_pairs={{256,0},{384,128},{257,1},{385,129},{258,2},{386,130},{259,3},{387... | collective-permute-start | bytes 12296 | tf_op jit(solution)/shard_map/ppermute | solution.py:37
  163.4 6.4 %collective-permute-start.11 = (bf16[2048]{0:T(1024)(128)(2,1)S(1)}, bf16[2048]{0:T(1024)(128)(2,1)S(1)}, u32[]{:S(2)}, u32[]{:S(2)}) collective-permute-start(bf16[2048]{0:T(1024)(128)(2,1)S(1)} %convert_element_type.203), channel_id=1, source_target_pairs={{384,0},{385,1},{386,2},{387,3},{388,4},{389,5},{390,6},{391,7},{3... | collective-permute-start | bytes 12296 | tf_op jit(solution)/shard_map/ppermute | solution.py:37
  164.7 5.1 %collective-permute-start.9 = (bf16[2048]{0:T(1024)(128)(2,1)S(1)}, bf16[2048]{0:T(1024)(128)(2,1)S(1)}, u32[]{:S(2)}, u32[]{:S(2)}) collective-permute-start(bf16[2048]{0:T(1024)(128)(2,1)S(1)} %convert_element_type.203), channel_id=1, source_target_pairs={{128,0},{256,128},{384,256},{129,1},{257,129},{385,257},{130,2},{2... | collective-permute-start | bytes 12296 | tf_op jit(solution)/shard_map/ppermute | solution.py:37
  167.8 13.6 %collective-permute-start.15 = (bf16[128,1024]{1,0:T(8,128)(2,1)}, bf16[128,1024]{1,0:T(8,128)(2,1)}, u32[]{:S(2)}, u32[]{:S(2)}) collective-permute-start(bf16[128,1024]{1,0:T(8,128)(2,1)} %add_convert_fusion), channel_id=1, source_target_pairs={{4,0},{8,4},{12,8},{16,12},{20,16},{24,20},{28,24},{32,28},{36,32}... | collective-permute-start | bytes 786440 | tf_op jit(solution)/shard_map/ppermute | solution.py:62
  173.9 21.7 %all-to-all-start.3 = ((bf16[32,2,1024]{2,1,0:T(2,128)(2,1)}), bf16[32,2,1024]{2,1,0:T(2,128)(2,1)}, u32[]{:S(2)}, u32[]{:S(2)}) async-start(bf16[32,2,1024]{2,1,0:T(2,128)(2,1)} %reshape.543), calls=%async_computation.3 | async-start | bytes 262144 | tf_op jit(solution)/shard_map/all_to_all | solution.py:55
  182.4 15.6 %copy-start.11 = (bf16[128,512]{1,0:T(8,128)(2,1)S(1)}, bf16[128,512]{1,0:T(8,128)(2,1)}, u32[]{:S(2)}) copy-start(bf16[128,512]{1,0:T(8,128)(2,1)} %param.11) | copy-start | bytes 393220
  183.2 15.8 %copy-start.13 = (bf16[4,128,128]{2,1,0:T(8,128)(2,1)S(1)}, bf16[4,128,128]{2,1,0:T(8,128)(2,1)}, u32[]{:S(2)}) copy-start(bf16[4,128,128]{2,1,0:T(8,128)(2,1)} %copy-done.12) | copy-start | bytes 393220

commit v15 on v13

--- a/solution.py
+++ b/solution.py
@@ -13,8 +13,8 @@
 
 
 CTX = ("outer", "inner")
-INNER = 32
-PLAN = (4,)
+INNER = 16
+PLAN = (2, 4)
 
 
 def scan_over(total, axis, backward):

time: 181 us -> 198 us (1.094)
  starting transfers between devices: 81 us -> 95 us
    ppermute x6 -> x8, starting transfers between devices: 11.4 us -> 28.5 us  [scan_over(): arrived.append(lax.ppermute(total.astype(jnp.bfloat16), axis, pairs))]
    ppermute x6 -> x8, waiting for transfers between devices: 4.4 us -> 14.3 us  [scan_over(): arrived.append(lax.ppermute(total.astype(jnp.bfloat16), axis, pairs))]
    all_to_all x2, waiting for transfers between devices: 14.8 us -> 9.4 us  [carried_in(): back = lax.all_to_all(states, 'inner', 0, 0, tiled=True)]
    all_to_all x2, starting transfers between devices: 14.2 us -> 8.99 us  [carried_in(): back = lax.all_to_all(states, 'inner', 0, 0, tiled=True)]
    all_to_all x2, waiting for transfers between devices: 13.8 us -> 9.37 us  [carried_in(): mine = lax.all_to_all(slices, 'inner', 0, 0, tiled=True).astype(jnp.float32)]
    ppermute x8, starting transfers between devices: 26.8 us -> 30.4 us  [from_behind(): return lax.ppermute(shard, axis, pairs)]
  transfers between devices with their start and end apart: 20 -> 22, of which waited for: 7 -> 8; matrix products, arithmetic and copies ran while one was open for 30% -> 28% of each run, Pallas kernels for 0% -> 0%
where the time goes in v15:
time: 198 us; the launch traced here: 197 us
  starting transfers between devices  95 us (48%)
  waiting for transfers between devices  35.8 us (18%)
  local copies, waits for them, and re-layouts  25.1 us (13%)
  other arithmetic  24.8 us (13%)
  matrix products  14.4 us (7%)
    ppermute x8, starting transfers between devices, from_behind(): return lax.ppermute(shard, axis, pairs)  30.4 us
    ppermute x8, starting transfers between devices, scan_over(): arrived.append(lax.ppermute(total.astype(jnp.bfloat16), axis, pairs))  28.5 us
    all_to_all x2, starting transfers between devices, carried_in(): mine = lax.all_to_all(slices, 'inner', 0, 0, tiled=True).astype(jnp.float32)  18.9 us
    ppermute x8, waiting for transfers between devices, scan_over(): arrived.append(lax.ppermute(total.astype(jnp.bfloat16), axis, pairs))  14.3 us
    unnamed x70, local copies, waits for them, and re-layouts  13.9 us
    all_to_all x2, waiting for transfers between devices, carried_in(): back = lax.all_to_all(states, 'inner', 0, 0, tiled=True)  9.4 us
    all_to_all x2, waiting for transfers between devices, carried_in(): mine = lax.all_to_all(slices, 'inner', 0, 0, tiled=True).astype(jnp.float32)  9.37 us
    all_to_all x2, starting transfers between devices, carried_in(): back = lax.all_to_all(states, 'inner', 0, 0, tiled=True)  8.99 us
  transfers between devices with their start and end apart: 22, of which 8 were waited for; matrix products, arithmetic and copies ran while one was open for 28% of the time, Pallas kernels for 0%

profile of v15, /device:TPU:24, one launch (start us, length us, event | category | flops | bytes accessed | tf_op | source)
XLA Modules:
  0.0 196.7 jit_solution(6923013714559948973)
XLA Ops:
  3.5 1.4 reduce.9
  5.6 12.6 %all-to-all-start = ((bf16[16,2,2048]{2,1,0:T(2,128)(2,1)}), bf16[16,2,2048]{2,1,0:T(2,128)(2,1)S(1)}, u32[]{:S(2)}, u32[]{:S(2)}) async-start(bf16[16,2,2048]{2,1,0:T(2,128)(2,1)} %reshape.544), calls=%async_computation | async-start | bytes 262144 | tf_op jit(solution)/shard_map/all_to_all | solution.py:47
  18.3 2.3 %collective-permute-start.10 = (bf16[128,1024]{1,0:T(8,128)(2,1)S(1)}, bf16[128,1024]{1,0:T(8,128)(2,1)S(1)}, u32[]{:S(2)}, u32[]{:S(2)}) collective-permute-start(bf16[128,1024]{1,0:T(8,128)(2,1)S(1)} %pad_maximum_fusion), channel_id=1, source_target_pairs={{0,4},{4,8},{8,12},{12,16},{16,20},{20,24},{24,28},{28,32},{32,36}... | collective-permute-start | bytes 786440 | tf_op jit(solution)/shard_map/ppermute | solution.py:60
  21.1 9.4 %all-to-all-done = bf16[16,2,2048]{2,1,0:T(2,128)(2,1)S(1)} async-done(((bf16[16,2,2048]{2,1,0:T(2,128)(2,1)}), bf16[16,2,2048]{2,1,0:T(2,128)(2,1)S(1)}, u32[]{:S(2)}, u32[]{:S(2)}) %all-to-all-start) | async-done | bytes 131104 | tf_op jit(solution)/shard_map/all_to_all | solution.py:47
  30.9 8.2 %collective-permute-start = (bf16[4096]{0:T(1024)(128)(2,1)S(1)}, bf16[4096]{0:T(1024)(128)(2,1)S(1)}, u32[]{:S(2)}, u32[]{:S(2)}) collective-permute-start(bf16[4096]{0:T(1024)(128)(2,1)S(1)} %convert_element_type.195), channel_id=1, source_target_pairs={{0,64},{64,128},{128,192},{192,256},{256,320},{320,384},{384,448},... | collective-permute-start | bytes 24584 | tf_op jit(solution)/shard_map/ppermute | solution.py:37
  40.0 6.0 %collective-permute-done = bf16[4096]{0:T(1024)(128)(2,1)S(1)} collective-permute-done((bf16[4096]{0:T(1024)(128)(2,1)S(1)}, bf16[4096]{0:T(1024)(128)(2,1)S(1)}, u32[]{:S(2)}, u32[]{:S(2)}) %collective-permute-start) | collective-permute-done | bytes 8224 | tf_op jit(solution)/shard_map/ppermute | solution.py:37
  46.1 1.3 collective-permute-start.3
  47.3 1.3 collective-permute-start.2
  48.6 1.3 collective-permute-start.1
  50.0 2.8 %collective-permute-done.3 = bf16[4096]{0:T(1024)(128)(2,1)S(1)} collective-permute-done((bf16[4096]{0:T(1024)(128)(2,1)S(1)}, bf16[4096]{0:T(1024)(128)(2,1)S(1)}, u32[]{:S(2)}, u32[]{:S(2)}) %collective-permute-start.3) | collective-permute-done | bytes 8224 | tf_op jit(solution)/shard_map/ppermute | solution.py:37
  52.8 1.6 collective-permute-done.2
  54.8 1.4 reduce.10
  56.9 4.8 %all-to-all-start.1 = ((bf16[16,2,2048]{2,1,0:T(2,128)(2,1)}), bf16[16,2,2048]{2,1,0:T(2,128)(2,1)S(1)}, u32[]{:S(2)}, u32[]{:S(2)}) async-start(bf16[16,2,2048]{2,1,0:T(2,128)(2,1)} %reshape.546), calls=%async_computation.1 | async-start | bytes 262144 | tf_op jit(solution)/shard_map/all_to_all | solution.py:53
  62.3 2.3 %collective-permute-start.11 = (bf16[128,1024]{1,0:T(8,128)(2,1)S(1)}, bf16[128,1024]{1,0:T(8,128)(2,1)S(1)}, u32[]{:S(2)}, u32[]{:S(2)}) collective-permute-start(bf16[128,1024]{1,0:T(8,128)(2,1)S(1)} %collective-permute-done.10), channel_id=1, source_target_pairs={{0,4},{4,8},{8,12},{12,16},{16,20},{20,24},{24,28},{28,32},{32,36}... | collective-permute-start | bytes 786440 | tf_op jit(solution)/shard_map/ppermute | solution.py:60
  64.6 9.4 %all-to-all-done.1 = bf16[16,2,2048]{2,1,0:T(2,128)(2,1)S(1)} async-done(((bf16[16,2,2048]{2,1,0:T(2,128)(2,1)}), bf16[16,2,2048]{2,1,0:T(2,128)(2,1)S(1)}, u32[]{:S(2)}, u32[]{:S(2)}) %all-to-all-start.1) | async-done | bytes 131104 | tf_op jit(solution)/shard_map/all_to_all | solution.py:53
  75.2 3.4 %collective-permute-start.4 = (f32[2,128]{1,0:T(2,128)S(1)}, f32[2,128]{1,0:T(2,128)S(1)}, u32[]{:S(2)}, u32[]{:S(2)}) collective-permute-start(f32[2,128]{1,0:T(2,128)S(1)} %pad_maximum_fusion.2), channel_id=1, source_target_pairs={{0,1},{1,0},{2,3},{3,2},{4,5},{5,4},{6,7},{7,6},{8,9},{9,8},{10,11... | collective-permute-start | bytes 3080 | tf_op jit(solution)/shard_map/ppermute | solution.py:166
  78.7 1.9 collective-permute-start.12
  80.7 4.9 %collective-permute-start.5 = (f32[2,128]{1,0:T(2,128)S(1)}, f32[2,128]{1,0:T(2,128)S(1)}, u32[]{:S(2)}, u32[]{:S(2)}) collective-permute-start(f32[2,128]{1,0:T(2,128)S(1)} %fusion.78), channel_id=1, source_target_pairs={{0,2},{1,3},{2,0},{3,1},{4,6},{5,7},{6,4},{7,5},{8,10},{9,11},{10,... | collective-permute-start | bytes 3080 | tf_op jit(solution)/shard_map/ppermute | solution.py:166
  85.8 2.6 %collective-permute-done.12 = bf16[128,1024]{1,0:T(8,128)(2,1)S(1)} collective-permute-done((bf16[128,1024]{1,0:T(8,128)(2,1)S(1)}, bf16[128,1024]{1,0:T(8,128)(2,1)S(1)}, u32[]{:S(2)}, u32[]{:S(2)}) %collective-permute-start.12) | collective-permute-done | bytes 262176 | tf_op jit(solution)/shard_map/ppermute | solution.py:60
  88.5 1.9 collective-permute-start.13
  91.6 1.4 reduce.11
  93.7 6.2 %all-to-all-start.2 = ((bf16[16,2,2048]{2,1,0:T(2,128)(2,1)}), bf16[16,2,2048]{2,1,0:T(2,128)(2,1)}, u32[]{:S(2)}, u32[]{:S(2)}) async-start(bf16[16,2,2048]{2,1,0:T(2,128)(2,1)} %reshape.548), calls=%async_computation.2 | async-start | bytes 262144 | tf_op jit(solution)/shard_map/all_to_all | solution.py:47
  106.0 1.5 fusion.81
  107.5 1.6 convolution_bitcast_fusion
  111.9 1.4 reshape.528
  115.6 2.3 %scatter_fusion = f32[5,128,512]{2,1,0:T(8,128)S(1)} fusion(f32[5,128,512]{2,1,0:T(8,128)S(1)} %broadcast.249.clone.1, s32[4]{0:T(128)S(1)} %fusion.70, f32[4,128,512]{2,1,0:T(8,128)} %reshape.528), kind=kCustom, calls=%fused_computation.2 | custom fusion | flops 262144 | bytes 3145744 | tf_op jit(solution)/shard_map/scatter-add | solution.py:122
  119.5 9.2 %collective-permute-start.14 = (bf16[128,1024]{1,0:T(8,128)(2,1)}, bf16[128,1024]{1,0:T(8,128)(2,1)}, u32[]{:S(2)}, u32[]{:S(2)}) collective-permute-start(bf16[128,1024]{1,0:T(8,128)(2,1)} %pad_maximum_fusion.1), channel_id=1, source_target_pairs={{4,0},{8,4},{12,8},{16,12},{20,16},{24,20},{28,24},{32,28},{36,32}... | collective-permute-start | bytes 786440 | tf_op jit(solution)/shard_map/ppermute | solution.py:60
  129.6 1.4 reshape.549
  131.2 6.8 %collective-permute-start.6 = (bf16[4096]{0:T(1024)(128)(2,1)S(1)}, bf16[4096]{0:T(1024)(128)(2,1)S(1)}, u32[]{:S(2)}, u32[]{:S(2)}) collective-permute-start(bf16[4096]{0:T(1024)(128)(2,1)S(1)} %convert_element_type.209), channel_id=1, source_target_pairs={{64,0},{128,64},{192,128},{256,192},{320,256},{384,320},{448,384},... | collective-permute-start | bytes 24584 | tf_op jit(solution)/shard_map/ppermute | solution.py:37
  138.1 1.8 add_convert_fusion.2
  139.9 2.0 %collective-permute-start.15 = (bf16[128,1024]{1,0:T(8,128)(2,1)}, bf16[128,1024]{1,0:T(8,128)(2,1)}, u32[]{:S(2)}, u32[]{:S(2)}) collective-permute-start(bf16[128,1024]{1,0:T(8,128)(2,1)} %add_convert_fusion.2), channel_id=1, source_target_pairs={{4,0},{8,4},{12,8},{16,12},{20,16},{24,20},{28,24},{32,28},{36,32}... | collective-permute-start | bytes 786440 | tf_op jit(solution)/shard_map/ppermute | solution.py:60
  141.9 3.9 %collective-permute-done.6 = bf16[4096]{0:T(1024)(128)(2,1)S(1)} collective-permute-done((bf16[4096]{0:T(1024)(128)(2,1)S(1)}, bf16[4096]{0:T(1024)(128)(2,1)S(1)}, u32[]{:S(2)}, u32[]{:S(2)}) %collective-permute-start.6) | collective-permute-done | bytes 8224 | tf_op jit(solution)/shard_map/ppermute | solution.py:37
  146.9 1.9 collective-permute-start.9
  148.8 5.8 %collective-permute-start.8 = (bf16[4096]{0:T(1024)(128)(2,1)}, bf16[4096]{0:T(1024)(128)(2,1)}, u32[]{:S(2)}, u32[]{:S(2)}) collective-permute-start(bf16[4096]{0:T(1024)(128)(2,1)} %fusion.59), channel_id=1, source_target_pairs={{256,0},{320,64},{384,128},{448,192},{257,1},{321,65},{385,129},{4... | collective-permute-start | bytes 24584 | tf_op jit(solution)/shard_map/ppermute | solution.py:37
  154.6 1.9 collective-permute-start.7
  156.5 1.8 fusion.84
  158.3 1.7 copy.119
  160.8 1.8 add_convert_fusion.1
  162.6 1.9 collective-permute-start.16
  165.5 2.4 %reduce.12 = bf16[16,4096]{1,0:T(8,128)(2,1)S(1)} reduce(bf16[16,1,4096]{2,1,0:T(2,128)(2,1)} %add_convert_fusion.3, bf16[]{:T(256)} %broadcast.281), dimensions={1}, to_apply=%add_convert_fusion.3.reduce_sub_computation | reduce | bytes 262146 | tf_op jit(solution)/shard_map/jit(cumsum)/reduce_window_sum | solution.py:48
  168.6 4.2 %all-to-all-start.3 = ((bf16[16,2,2048]{2,1,0:T(2,128)(2,1)}), bf16[16,2,2048]{2,1,0:T(2,128)(2,1)}, u32[]{:S(2)}, u32[]{:S(2)}) async-start(bf16[16,2,2048]{2,1,0:T(2,128)(2,1)} %reshape.550), calls=%async_computation.3 | async-start | bytes 262144 | tf_op jit(solution)/shard_map/all_to_all | solution.py:53
  172.8 1.3 convolution_convert_fusion
  174.9 1.8 add_convert_fusion
  176.7 8.8 %collective-permute-start.17 = (bf16[128,1024]{1,0:T(8,128)(2,1)}, bf16[128,1024]{1,0:T(8,128)(2,1)}, u32[]{:S(2)}, u32[]{:S(2)}) collective-permute-start(bf16[128,1024]{1,0:T(8,128)(2,1)} %add_convert_fusion), channel_id=1, source_target_pairs={{4,0},{8,4},{12,8},{16,12},{20,16},{24,20},{28,24},{32,28},{36,32}... | collective-permute-start | bytes 786440 | tf_op jit(solution)/shard_map/ppermute | solution.py:60
  185.6 1.4 reshape.551
  187.0 1.4 reduce.8
  189.3 1.8 fusion.17
  191.4 1.7 copy.121
  (153 shorter events, 33.3 us)
Async XLA Ops:
  0.6 105.3 %copy-start = (bf16[128,512]{1,0:T(8,128)(2,1)S(1)}, bf16[128,512]{1,0:T(8,128)(2,1)}, u32[]{:S(2)}) copy-start(bf16[128,512]{1,0:T(8,128)(2,1)} %param.15) | copy-start | bytes 393220
  0.6 20.2 %copy-start.11 = (bf16[128,512]{1,0:T(8,128)(2,1)S(1)}, bf16[128,512]{1,0:T(8,128)(2,1)}, u32[]{:S(2)}) copy-start(bf16[128,512]{1,0:T(8,128)(2,1)} %param.11) | copy-start | bytes 393220
  0.7 17.6 %copy-start.14 = (bf16[128,512]{1,0:T(8,128)(2,1)S(1)}, bf16[128,512]{1,0:T(8,128)(2,1)}, u32[]{:S(2)}) copy-start(bf16[128,512]{1,0:T(8,128)(2,1)} %param.17) | copy-start | bytes 393220
  0.7 17.6 %copy-start.15 = (bf16[128,512]{1,0:T(8,128)(2,1)S(1)}, bf16[128,512]{1,0:T(8,128)(2,1)}, u32[]{:S(2)}) copy-start(bf16[128,512]{1,0:T(8,128)(2,1)} %param.16) | copy-start | bytes 393220
  0.7 20.0 %copy-start.25 = (s32[1,3]{1,0:T(1,128)S(1)}, s32[1,3]{1,0:T(1,128)}, u32[]{:S(2)}) copy-start(s32[1,3]{1,0:T(1,128)} %param.19) | copy-start | bytes 40
  0.7 20.2 %copy-start.4 = (bf16[128,512]{1,0:T(8,128)(2,1)S(1)}, bf16[128,512]{1,0:T(8,128)(2,1)}, u32[]{:S(2)}) copy-start(bf16[128,512]{1,0:T(8,128)(2,1)} %param.10) | copy-start | bytes 393220
  5.6 24.8 %all-to-all-start = ((bf16[16,2,2048]{2,1,0:T(2,128)(2,1)}), bf16[16,2,2048]{2,1,0:T(2,128)(2,1)S(1)}, u32[]{:S(2)}, u32[]{:S(2)}) async-start(bf16[16,2,2048]{2,1,0:T(2,128)(2,1)} %reshape.544), calls=%async_computation | async-start | bytes 262144 | tf_op jit(solution)/shard_map/all_to_all | solution.py:47
  18.3 43.9 %collective-permute-start.10 = (bf16[128,1024]{1,0:T(8,128)(2,1)S(1)}, bf16[128,1024]{1,0:T(8,128)(2,1)S(1)}, u32[]{:S(2)}, u32[]{:S(2)}) collective-permute-start(bf16[128,1024]{1,0:T(8,128)(2,1)S(1)} %pad_maximum_fusion), channel_id=1, source_target_pairs={{0,4},{4,8},{8,12},{12,16},{16,20},{20,24},{24,28},{28,32},{32,36}... | collective-permute-start | bytes 786440 | tf_op jit(solution)/shard_map/ppermute | solution.py:60
  20.9 41.0 %copy-start.19 = (bf16[128,512]{1,0:T(8,128)(2,1)S(1)}, bf16[128,512]{1,0:T(8,128)(2,1)}, u32[]{:S(2)}) copy-start(bf16[128,512]{1,0:T(8,128)(2,1)} %param.14) | copy-start | bytes 393220
  21.1 40.9 %copy-start.16 = (bf16[4,128,128]{2,1,0:T(8,128)(2,1)}, bf16[4,128,128]{2,1,0:T(8,128)(2,1)S(1)}, u32[]{:S(2)}) copy-start(bf16[4,128,128]{2,1,0:T(8,128)(2,1)S(1)} %fusion.15) | copy-start | bytes 393220
  21.1 40.9 %copy-start.8 = (bf16[128,512]{1,0:T(8,128)(2,1)S(1)}, bf16[128,512]{1,0:T(8,128)(2,1)}, u32[]{:S(2)}) copy-start(bf16[128,512]{1,0:T(8,128)(2,1)} %param.12) | copy-start | bytes 393220
  30.9 15.2 %collective-permute-start = (bf16[4096]{0:T(1024)(128)(2,1)S(1)}, bf16[4096]{0:T(1024)(128)(2,1)S(1)}, u32[]{:S(2)}, u32[]{:S(2)}) collective-permute-start(bf16[4096]{0:T(1024)(128)(2,1)S(1)} %convert_element_type.195), channel_id=1, source_target_pairs={{0,64},{64,128},{128,192},{192,256},{256,320},{320,384},{384,448},... | collective-permute-start | bytes 24584 | tf_op jit(solution)/shard_map/ppermute | solution.py:37
  46.1 6.7 %collective-permute-start.3 = (bf16[4096]{0:T(1024)(128)(2,1)S(1)}, bf16[4096]{0:T(1024)(128)(2,1)S(1)}, u32[]{:S(2)}, u32[]{:S(2)}) collective-permute-start(bf16[4096]{0:T(1024)(128)(2,1)S(1)} %fusion.60), channel_id=1, source_target_pairs={{0,384},{64,448},{1,385},{65,449},{2,386},{66,450},{3,387},{67,451... | collective-permute-start | bytes 24584 | tf_op jit(solution)/shard_map/ppermute | solution.py:37
  47.3 7.0 %collective-permute-start.2 = (bf16[4096]{0:T(1024)(128)(2,1)S(1)}, bf16[4096]{0:T(1024)(128)(2,1)S(1)}, u32[]{:S(2)}, u32[]{:S(2)}) collective-permute-start(bf16[4096]{0:T(1024)(128)(2,1)S(1)} %fusion.60), channel_id=1, source_target_pairs={{0,256},{64,320},{128,384},{192,448},{1,257},{65,321},{129,385},{1... | collective-permute-start | bytes 24584 | tf_op jit(solution)/shard_map/ppermute | solution.py:37
  48.6 5.8 %collective-permute-start.1 = (bf16[4096]{0:T(1024)(128)(2,1)S(1)}, bf16[4096]{0:T(1024)(128)(2,1)S(1)}, u32[]{:S(2)}, u32[]{:S(2)}) collective-permute-start(bf16[4096]{0:T(1024)(128)(2,1)S(1)} %fusion.60), channel_id=1, source_target_pairs={{0,128},{64,192},{128,256},{192,320},{256,384},{320,448},{1,129},{... | collective-permute-start | bytes 24584 | tf_op jit(solution)/shard_map/ppermute | solution.py:37
  56.2 18.7 %copy-start.24 = (f32[512]{0:T(512)S(1)}, f32[512]{0:T(512)}, u32[]{:S(2)}) copy-start(f32[512]{0:T(512)} %param.13) | copy-start | bytes 6148
  56.9 17.0 %all-to-all-start.1 = ((bf16[16,2,2048]{2,1,0:T(2,128)(2,1)}), bf16[16,2,2048]{2,1,0:T(2,128)(2,1)S(1)}, u32[]{:S(2)}, u32[]{:S(2)}) async-start(bf16[16,2,2048]{2,1,0:T(2,128)(2,1)} %reshape.546), calls=%async_computation.1 | async-start | bytes 262144 | tf_op jit(solution)/shard_map/all_to_all | solution.py:53
  62.0 23.7 %copy-start.20 = (bf16[128,512]{1,0:T(8,128)(2,1)S(1)}, bf16[128,512]{1,0:T(8,128)(2,1)}, u32[]{:S(2)}) copy-start(bf16[128,512]{1,0:T(8,128)(2,1)} %param.18) | copy-start | bytes 393220
  62.3 16.4 %collective-permute-start.11 = (bf16[128,1024]{1,0:T(8,128)(2,1)S(1)}, bf16[128,1024]{1,0:T(8,128)(2,1)S(1)}, u32[]{:S(2)}, u32[]{:S(2)}) collective-permute-start(bf16[128,1024]{1,0:T(8,128)(2,1)S(1)} %collective-permute-done.10), channel_id=1, source_target_pairs={{0,4},{4,8},{8,12},{12,16},{16,20},{20,24},{24,28},{28,32},{32,36}... | collective-permute-start | bytes 786440 | tf_op jit(solution)/shard_map/ppermute | solution.py:60
  74.9 16.5 %copy-start.6 = (bf16[4,128,128]{2,1,0:T(8,128)(2,1)}, bf16[4,128,128]{2,1,0:T(8,128)(2,1)S(1)}, u32[]{:S(2)}) copy-start(bf16[4,128,128]{2,1,0:T(8,128)(2,1)S(1)} %reshape.495) | copy-start | bytes 393220
  75.2 5.5 %collective-permute-start.4 = (f32[2,128]{1,0:T(2,128)S(1)}, f32[2,128]{1,0:T(2,128)S(1)}, u32[]{:S(2)}, u32[]{:S(2)}) collective-permute-start(f32[2,128]{1,0:T(2,128)S(1)} %pad_maximum_fusion.2), channel_id=1, source_target_pairs={{0,1},{1,0},{2,3},{3,2},{4,5},{5,4},{6,7},{7,6},{8,9},{9,8},{10,11... | collective-permute-start | bytes 3080 | tf_op jit(solution)/shard_map/ppermute | solution.py:166
  78.7 9.8 %collective-permute-start.12 = (bf16[128,1024]{1,0:T(8,128)(2,1)S(1)}, bf16[128,1024]{1,0:T(8,128)(2,1)S(1)}, u32[]{:S(2)}, u32[]{:S(2)}) collective-permute-start(bf16[128,1024]{1,0:T(8,128)(2,1)S(1)} %collective-permute-done.11), channel_id=1, source_target_pairs={{0,4},{4,8},{8,12},{12,16},{16,20},{20,24},{24,28},{28,32},{32,36}... | collective-permute-start | bytes 786440 | tf_op jit(solution)/shard_map/ppermute | solution.py:60
  80.7 9.7 %collective-permute-start.5 = (f32[2,128]{1,0:T(2,128)S(1)}, f32[2,128]{1,0:T(2,128)S(1)}, u32[]{:S(2)}, u32[]{:S(2)}) collective-permute-start(f32[2,128]{1,0:T(2,128)S(1)} %fusion.78), channel_id=1, source_target_pairs={{0,2},{1,3},{2,0},{3,1},{4,6},{5,7},{6,4},{7,5},{8,10},{9,11},{10,... | collective-permute-start | bytes 3080 | tf_op jit(solution)/shard_map/ppermute | solution.py:166
  88.5 5.3 %copy-start.18 = (bf16[128,1024]{1,0:T(8,128)(2,1)}, bf16[128,1024]{1,0:T(8,128)(2,1)S(1)}, u32[]{:S(2)}) copy-start(bf16[128,1024]{1,0:T(8,128)(2,1)S(1)} %collective-permute-done.12) | copy-start | bytes 786436
  88.5 12.4 %collective-permute-start.13 = (bf16[128,1024]{1,0:T(8,128)(2,1)S(1)}, bf16[128,1024]{1,0:T(8,128)(2,1)}, u32[]{:S(2)}, u32[]{:S(2)}) collective-permute-start(bf16[128,1024]{1,0:T(8,128)(2,1)S(1)} %collective-permute-done.12), channel_id=1, source_target_pairs={{0,4},{4,8},{8,12},{12,16},{16,20},{20,24},{24,28},{28,32},{32,36}... | collective-permute-start | bytes 786440 | tf_op jit(solution)/shard_map/ppermute | solution.py:60
  90.6 0.7 copy-start.2
  91.2 9.6 %copy-start.13 = (bf16[4,128,128]{2,1,0:T(8,128)(2,1)}, bf16[4,128,128]{2,1,0:T(8,128)(2,1)S(1)}, u32[]{:S(2)}) copy-start(bf16[4,128,128]{2,1,0:T(8,128)(2,1)S(1)} %fusion.16) | copy-start | bytes 393220
  93.7 35.8 %all-to-all-start.2 = ((bf16[16,2,2048]{2,1,0:T(2,128)(2,1)}), bf16[16,2,2048]{2,1,0:T(2,128)(2,1)}, u32[]{:S(2)}, u32[]{:S(2)}) async-start(bf16[16,2,2048]{2,1,0:T(2,128)(2,1)} %reshape.548), calls=%async_computation.2 | async-start | bytes 262144 | tf_op jit(solution)/shard_map/all_to_all | solution.py:47
  104.6 1.3 copy-start.22
  105.9 1.5 copy-start.21
  107.5 1.6 copy-start.26
  109.8 1.1 copy-start.1
  117.9 10.8 %copy-start.3 = (bf16[128,4,128]{0,2,1:T(8,128)(2,1)S(1)}, bf16[128,4,128]{0,2,1:T(8,128)(2,1)}, u32[]{:S(2)}) copy-start(bf16[128,4,128]{0,2,1:T(8,128)(2,1)} %copy-done.2) | copy-start | bytes 393220
  117.9 10.8 %copy-start.7 = (bf16[4,128,128]{2,1,0:T(8,128)(2,1)S(1)}, bf16[4,128,128]{2,1,0:T(8,128)(2,1)}, u32[]{:S(2)}) copy-start(bf16[4,128,128]{2,1,0:T(8,128)(2,1)} %copy-done.6) | copy-start | bytes 393220
  117.9 10.8 %copy-start.10 = (f32[128,4,128]{0,2,1:T(8,128)S(1)}, f32[128,4,128]{0,2,1:T(8,128)}, u32[]{:S(2)}) copy-start(f32[128,4,128]{0,2,1:T(8,128)} %convolution_bitcast_fusion.6) | copy-start | bytes 786436
  119.5 18.6 %collective-permute-start.14 = (bf16[128,1024]{1,0:T(8,128)(2,1)}, bf16[128,1024]{1,0:T(8,128)(2,1)}, u32[]{:S(2)}, u32[]{:S(2)}) collective-permute-start(bf16[128,1024]{1,0:T(8,128)(2,1)} %pad_maximum_fusion.1), channel_id=1, source_target_pairs={{4,0},{8,4},{12,8},{16,12},{20,16},{24,20},{28,24},{32,28},{36,32}... | collective-permute-start | bytes 786440 | tf_op jit(solution)/shard_map/ppermute | solution.py:60
  131.2 14.5 %collective-permute-start.6 = (bf16[4096]{0:T(1024)(128)(2,1)S(1)}, bf16[4096]{0:T(1024)(128)(2,1)S(1)}, u32[]{:S(2)}, u32[]{:S(2)}) collective-permute-start(bf16[4096]{0:T(1024)(128)(2,1)S(1)} %convert_element_type.209), channel_id=1, source_target_pairs={{64,0},{128,64},{192,128},{256,192},{320,256},{384,320},{448,384},... | collective-permute-start | bytes 24584 | tf_op jit(solution)/shard_map/ppermute | solution.py:37
  139.9 20.9 %collective-permute-start.15 = (bf16[128,1024]{1,0:T(8,128)(2,1)}, bf16[128,1024]{1,0:T(8,128)(2,1)}, u32[]{:S(2)}, u32[]{:S(2)}) collective-permute-start(bf16[128,1024]{1,0:T(8,128)(2,1)} %add_convert_fusion.2), channel_id=1, source_target_pairs={{4,0},{8,4},{12,8},{16,12},{20,16},{24,20},{28,24},{32,28},{36,32}... | collective-permute-start | bytes 786440 | tf_op jit(solution)/shard_map/ppermute | solution.py:60
  146.9 13.1 %collective-permute-start.9 = (bf16[4096]{0:T(1024)(128)(2,1)}, bf16[4096]{0:T(1024)(128)(2,1)}, u32[]{:S(2)}, u32[]{:S(2)}) collective-permute-start(bf16[4096]{0:T(1024)(128)(2,1)} %fusion.59), channel_id=1, source_target_pairs={{384,0},{448,64},{385,1},{449,65},{386,2},{450,66},{387,3},{451,67... | collective-permute-start | bytes 24584 | tf_op jit(solution)/shard_map/ppermute | solution.py:37
  148.8 11.2 %collective-permute-start.8 = (bf16[4096]{0:T(1024)(128)(2,1)}, bf16[4096]{0:T(1024)(128)(2,1)}, u32[]{:S(2)}, u32[]{:S(2)}) collective-permute-start(bf16[4096]{0:T(1024)(128)(2,1)} %fusion.59), channel_id=1, source_target_pairs={{256,0},{320,64},{384,128},{448,192},{257,1},{321,65},{385,129},{4... | collective-permute-start | bytes 24584 | tf_op jit(solution)/shard_map/ppermute | solution.py:37
  154.6 5.4 %collective-permute-start.7 = (bf16[4096]{0:T(1024)(128)(2,1)}, bf16[4096]{0:T(1024)(128)(2,1)}, u32[]{:S(2)}, u32[]{:S(2)}) collective-permute-start(bf16[4096]{0:T(1024)(128)(2,1)} %fusion.59), channel_id=1, source_target_pairs={{128,0},{192,64},{256,128},{320,192},{384,256},{448,320},{129,1},{... | collective-permute-start | bytes 24584 | tf_op jit(solution)/shard_map/ppermute | solution.py:37
  162.6 12.3 %collective-permute-start.16 = (bf16[128,1024]{1,0:T(8,128)(2,1)}, bf16[128,1024]{1,0:T(8,128)(2,1)}, u32[]{:S(2)}, u32[]{:S(2)}) collective-permute-start(bf16[128,1024]{1,0:T(8,128)(2,1)} %add_convert_fusion.1), channel_id=1, source_target_pairs={{4,0},{8,4},{12,8},{16,12},{20,16},{24,20},{28,24},{32,28},{36,32}... | collective-permute-start | bytes 786440 | tf_op jit(solution)/shard_map/ppermute | solution.py:60
  165.5 9.4 %copy-start.17 = (bf16[128,512]{1,0:T(8,128)(2,1)S(1)}, bf16[128,512]{1,0:T(8,128)(2,1)}, u32[]{:S(2)}) copy-start(bf16[128,512]{1,0:T(8,128)(2,1)} %get-tuple-element.32) | copy-start | bytes 393220
  168.6 17.0 %all-to-all-start.3 = ((bf16[16,2,2048]{2,1,0:T(2,128)(2,1)}), bf16[16,2,2048]{2,1,0:T(2,128)(2,1)}, u32[]{:S(2)}, u32[]{:S(2)}) async-start(bf16[16,2,2048]{2,1,0:T(2,128)(2,1)} %reshape.550), calls=%async_computation.3 | async-start | bytes 262144 | tf_op jit(solution)/shard_map/all_to_all | solution.py:53
  174.1 15.2 %copy-start.12 = (bf16[128,512]{1,0:T(8,128)(2,1)S(1)}, bf16[128,512]{1,0:T(8,128)(2,1)}, u32[]{:S(2)}) copy-start(bf16[128,512]{1,0:T(8,128)(2,1)} %param.11) | copy-start | bytes 393220
  174.9 16.3 %copy-start.9 = (bf16[128,512]{1,0:T(8,128)(2,1)S(1)}, bf16[128,512]{1,0:T(8,128)(2,1)}, u32[]{:S(2)}) copy-start(bf16[128,512]{1,0:T(8,128)(2,1)} %param.12) | copy-start | bytes 393220
  176.7 16.3 %copy-start.5 = (bf16[128,512]{1,0:T(8,128)(2,1)S(1)}, bf16[128,512]{1,0:T(8,128)(2,1)}, u32[]{:S(2)}) copy-start(bf16[128,512]{1,0:T(8,128)(2,1)} %param.10) | copy-start | bytes 393220
  176.7 18.3 %collective-permute-start.17 = (bf16[128,1024]{1,0:T(8,128)(2,1)}, bf16[128,1024]{1,0:T(8,128)(2,1)}, u32[]{:S(2)}, u32[]{:S(2)}) collective-permute-start(bf16[128,1024]{1,0:T(8,128)(2,1)} %add_convert_fusion), channel_id=1, source_target_pairs={{4,0},{8,4},{12,8},{16,12},{20,16},{24,20},{28,24},{32,28},{36,32}... | collective-permute-start | bytes 786440 | tf_op jit(solution)/shard_map/ppermute | solution.py:60
  (1 other events, 0.6 us)

commit v16 on v13

--- a/solution.py
+++ b/solution.py
@@ -195,11 +195,7 @@
     lin_dv = lin_dv.reshape(token_count, lin_width).astype(jnp.bfloat16)
     width = sm_key.shape[1]
     pair = jnp.concatenate([sm_key, sm_value], axis=1)
-    arrived = []
-    moving = pair
-    for distance in range(1, SPAN + 1):
-        moving = from_behind(moving, CTX, 1)
-        arrived.append(moving)
+    arrived = [from_behind(pair, CTX, distance) for distance in range(1, SPAN + 1)]
     key_window = jnp.concatenate(
         [arrived[SPAN - 1 - place][:, :width] for place in range(SPAN)] + [sm_key], axis=0
     )
@@ -212,15 +208,16 @@
     )
     key_total = key_acc[SPAN]
     value_total = value_acc[SPAN]
-    owed = None
-    for distance in range(SPAN, 0, -1):
-        term = jnp.concatenate(
-            [key_acc[SPAN - distance], value_acc[SPAN - distance]], axis=1
-        ).astype(jnp.bfloat16).astype(jnp.float32)
-        owed = term if owed is None else owed + term
-        owed = from_behind(owed.astype(jnp.bfloat16), CTX, -1).astype(jnp.float32)
-    key_total = key_total + owed[:, :width]
-    value_total = value_total + owed[:, width:]
+    for distance in range(1, SPAN + 1):
+        back = from_behind(
+            jnp.concatenate(
+                [key_acc[SPAN - distance], value_acc[SPAN - distance]], axis=1
+            ).astype(jnp.bfloat16),
+            CTX,
+            -distance,
+        ).astype(jnp.float32)
+        key_total = key_total + back[:, :width]
+        value_total = value_total + back[:, width:]
     return (
         lin_dq,
         lin_dk,

time: 181 us -> 193 us (1.066)
  local copies, waits for them, and re-layouts: 23.6 us -> 32.2 us
  starting transfers between devices: 81 us -> 87.6 us
  matrix products: 14.4 us -> 10.3 us
  waiting for transfers between devices: 35.9 us -> 32.8 us
  other arithmetic: 23.5 us -> 25.6 us
    ppermute x8, starting transfers between devices: 26.8 us -> 34.5 us  [from_behind(): return lax.ppermute(shard, axis, pairs)]
    all_to_all x2, starting transfers between devices: 20.2 us -> 14.3 us  [carried_in(): mine = lax.all_to_all(slices, 'inner', 0, 0, tiled=True).astype(jnp.float32)]
    all_to_all x2, starting transfers between devices: 14.2 us -> 19.3 us  [carried_in(): back = lax.all_to_all(states, 'inner', 0, 0, tiled=True)]
    concatenate x1 -> x4, other arithmetic: 0.72 us -> 3.9 us  [per_device(): jnp.concatenate([key_acc[SPAN - distance], value_acc[SPAN - distance]], a...]
    unnamed x70 -> x81, local copies, waits for them, and re-layouts: 12.4 us -> 15.1 us
    ppermute x8, waiting for transfers between devices: 2.83 us -> 0.18 us  [from_behind(): return lax.ppermute(shard, axis, pairs)]
    convert_element_type x4, other arithmetic: 6.35 us -> 3.96 us  [per_device(): back = from_behind(jnp.concatenate([key_acc[SPAN - distance], value_acc[S...]
  transfers between devices with their start and end apart: 20 -> 20, of which waited for: 7 -> 7; matrix products, arithmetic and copies ran while one was open for 30% -> 27% of each run, Pallas kernels for 0% -> 0%
where the time goes in v16:
time: 193 us; the launch traced here: 190 us
  starting transfers between devices  87.6 us (45%)
  waiting for transfers between devices  32.8 us (17%)
  local copies, waits for them, and re-layouts  32.2 us (17%)
  other arithmetic  25.6 us (13%)
  matrix products  10.3 us (5%)
    ppermute x8, starting transfers between devices, from_behind(): return lax.ppermute(shard, axis, pairs)  34.5 us
    all_to_all x2, starting transfers between devices, carried_in(): back = lax.all_to_all(states, 'inner', 0, 0, tiled=True)  19.3 us
    all_to_all x2, waiting for transfers between devices, carried_in(): back = lax.all_to_all(states, 'inner', 0, 0, tiled=True)  15.8 us
    unnamed x81, local copies, waits for them, and re-layouts  15.1 us
    all_to_all x2, starting transfers between devices, carried_in(): mine = lax.all_to_all(slices, 'inner', 0, 0, tiled=True).astype(jnp.float32)  14.3 us
    all_to_all x2, waiting for transfers between devices, carried_in(): mine = lax.all_to_all(slices, 'inner', 0, 0, tiled=True).astype(jnp.float32)  12.1 us
    ppermute x6, starting transfers between devices, scan_over(): arrived.append(lax.ppermute(total.astype(jnp.bfloat16), axis, pairs))  11.4 us
    ppermute x2, starting transfers between devices, per_device(): lax.ppermute(sums, 'head', [(i, i ^ step) for i in range(heads_dev)])  8.04 us
  transfers between devices with their start and end apart: 20, of which 7 were waited for; matrix products, arithmetic and copies ran while one was open for 27% of the time, Pallas kernels for 0%

profile of v16, /device:TPU:24, one launch (start us, length us, event | category | flops | bytes accessed | tf_op | source)
XLA Modules:
  0.0 190.1 jit_solution(5707456238392043154)
XLA Ops:
  0.7 1.6 constant_dynamic-update-slice_fusion.1
  2.3 1.6 constant_dynamic-update-slice_fusion
  3.9 2.0 %collective-permute-start.11 = (bf16[128,1024]{1,0:T(8,128)(2,1)}, bf16[128,1024]{1,0:T(8,128)(2,1)S(1)}, u32[]{:S(2)}, u32[]{:S(2)}) collective-permute-start(bf16[128,1024]{1,0:T(8,128)(2,1)} %constant_dynamic-update-slice_fusion), channel_id=1, source_target_pairs={{0,4},{4,8},{8,12},{12,16},{16,20},{20,24},{24,28},{28,32},{32,36}... | collective-permute-start | bytes 786440 | tf_op jit(solution)/shard_map/ppermute | solution.py:60
  6.0 3.8 %collective-permute-start.10 = (bf16[128,1024]{1,0:T(8,128)(2,1)}, bf16[128,1024]{1,0:T(8,128)(2,1)S(1)}, u32[]{:S(2)}, u32[]{:S(2)}) collective-permute-start(bf16[128,1024]{1,0:T(8,128)(2,1)} %constant_dynamic-update-slice_fusion), channel_id=1, source_target_pairs={{0,8},{4,12},{8,16},{12,20},{16,24},{20,28},{24,32},{28,36},{32,40... | collective-permute-start | bytes 786440 | tf_op jit(solution)/shard_map/ppermute | solution.py:60
  9.8 5.2 %collective-permute-start.9 = (bf16[128,1024]{1,0:T(8,128)(2,1)}, bf16[128,1024]{1,0:T(8,128)(2,1)S(1)}, u32[]{:S(2)}, u32[]{:S(2)}) collective-permute-start(bf16[128,1024]{1,0:T(8,128)(2,1)} %constant_dynamic-update-slice_fusion), channel_id=1, source_target_pairs={{0,12},{4,16},{8,20},{12,24},{16,28},{20,32},{24,36},{28,40},{32,4... | collective-permute-start | bytes 786440 | tf_op jit(solution)/shard_map/ppermute | solution.py:60
  15.0 6.4 %collective-permute-start.8 = (bf16[128,1024]{1,0:T(8,128)(2,1)}, bf16[128,1024]{1,0:T(8,128)(2,1)S(1)}, u32[]{:S(2)}, u32[]{:S(2)}) collective-permute-start(bf16[128,1024]{1,0:T(8,128)(2,1)} %constant_dynamic-update-slice_fusion), channel_id=1, source_target_pairs={{0,16},{4,20},{8,24},{12,28},{16,32},{20,36},{24,40},{28,44},{32,4... | collective-permute-start | bytes 786440 | tf_op jit(solution)/shard_map/ppermute | solution.py:60
  22.4 1.1 convolution_convert_fusion.2
  24.2 1.4 reduce.9
  26.3 9.8 %all-to-all-start = ((bf16[32,2,1024]{2,1,0:T(2,128)(2,1)}), bf16[32,2,1024]{2,1,0:T(2,128)(2,1)S(1)}, u32[]{:S(2)}, u32[]{:S(2)}) async-start(bf16[32,2,1024]{2,1,0:T(2,128)(2,1)} %reshape.544), calls=%async_computation | async-start | bytes 262144 | tf_op jit(solution)/shard_map/all_to_all | solution.py:47
  42.8 1.2 gather_fusion.1
  44.0 1.1 copy.128
  48.0 1.3 scatter_fusion.1
  51.1 1.2 fusion.8
  52.3 2.1 %all-to-all-done = bf16[32,2,1024]{2,1,0:T(2,128)(2,1)S(1)} async-done(((bf16[32,2,1024]{2,1,0:T(2,128)(2,1)}), bf16[32,2,1024]{2,1,0:T(2,128)(2,1)S(1)}, u32[]{:S(2)}, u32[]{:S(2)}) %all-to-all-start) | async-done | bytes 131104 | tf_op jit(solution)/shard_map/all_to_all | solution.py:47
  54.7 1.3 collective-permute-start.2
  56.0 1.3 collective-permute-start.1
  57.3 1.3 collective-permute-start
  59.4 2.0 %collective-permute-done.2 = bf16[2048]{0:T(1024)(128)(2,1)S(1)} collective-permute-done((bf16[2048]{0:T(1024)(128)(2,1)S(1)}, bf16[2048]{0:T(1024)(128)(2,1)S(1)}, u32[]{:S(2)}, u32[]{:S(2)}) %collective-permute-start.2) | collective-permute-done | bytes 4128 | tf_op jit(solution)/shard_map/ppermute | solution.py:37
  61.4 1.6 collective-permute-done.1
  63.5 1.4 reduce.10
  65.6 15.5 %all-to-all-start.1 = ((bf16[32,2,1024]{2,1,0:T(2,128)(2,1)}), bf16[32,2,1024]{2,1,0:T(2,128)(2,1)}, u32[]{:S(2)}, u32[]{:S(2)}) async-start(bf16[32,2,1024]{2,1,0:T(2,128)(2,1)} %reshape.546), calls=%async_computation.1 | async-start | bytes 262144 | tf_op jit(solution)/shard_map/all_to_all | solution.py:53
  81.0 1.3 convolution_bitcast_fusion.1
  83.0 1.4 reshape.528
  84.6 2.4 %scatter_fusion = f32[5,128,512]{2,1,0:T(8,128)S(1)} fusion(f32[5,128,512]{2,1,0:T(8,128)S(1)} %broadcast.249.clone.1, s32[4]{0:T(128)} %fusion.68, f32[4,128,512]{2,1,0:T(8,128)} %reshape.528), kind=kCustom, calls=%fused_computation.2 | custom fusion | flops 262144 | bytes 3145744 | tf_op jit(solution)/shard_map/scatter-add | solution.py:122
  88.7 6.1 %collective-permute-start.13 = (bf16[128,1024]{1,0:T(8,128)(2,1)}, bf16[128,1024]{1,0:T(8,128)(2,1)}, u32[]{:S(2)}, u32[]{:S(2)}) collective-permute-start(bf16[128,1024]{1,0:T(8,128)(2,1)} %pad_maximum_fusion.1), channel_id=1, source_target_pairs={{8,0},{12,4},{16,8},{20,12},{24,16},{28,20},{32,24},{36,28},{40,32... | collective-permute-start | bytes 786440 | tf_op jit(solution)/shard_map/ppermute | solution.py:60
  95.5 3.7 %collective-permute-start.14 = (bf16[128,1024]{1,0:T(8,128)(2,1)}, bf16[128,1024]{1,0:T(8,128)(2,1)}, u32[]{:S(2)}, u32[]{:S(2)}) collective-permute-start(bf16[128,1024]{1,0:T(8,128)(2,1)} %pad_maximum_fusion.2), channel_id=1, source_target_pairs={{12,0},{16,4},{20,8},{24,12},{28,16},{32,20},{36,24},{40,28},{44,3... | collective-permute-start | bytes 786440 | tf_op jit(solution)/shard_map/ppermute | solution.py:60
  99.2 2.0 %reshape.547 = bf16[32,1,2048]{2,1,0:T(2,128)(2,1)} reshape(bf16[32,2,1024]{2,1,0:T(2,128)(2,1)} %all-to-all-done.1) | data formatting | bytes 262144
  101.2 2.3 %reduce.7 = bf16[32,2048]{1,0:T(8,128)(2,1)} reduce(bf16[32,1,2048]{2,1,0:T(2,128)(2,1)} %reshape.547, bf16[]{:T(256)} %constant.86), dimensions={1}, to_apply=%all_to_all.22.reduce_sub_computation | reduce | bytes 262146 | tf_op jit(solution)/shard_map/all_to_all | solution.py:53
  103.6 1.6 reshape.495
  105.2 1.4 multiply_reduce_fusion.1
  106.6 3.4 %collective-permute-start.3 = (f32[2,128]{1,0:T(2,128)S(1)}, f32[2,128]{1,0:T(2,128)S(1)}, u32[]{:S(2)}, u32[]{:S(2)}) collective-permute-start(f32[2,128]{1,0:T(2,128)S(1)} %pad_maximum_fusion.4), channel_id=1, source_target_pairs={{0,1},{1,0},{2,3},{3,2},{4,5},{5,4},{6,7},{7,6},{8,9},{9,8},{10,11... | collective-permute-start | bytes 3080 | tf_op jit(solution)/shard_map/ppermute | solution.py:166
  110.0 1.7 pad_maximum_fusion.3
  111.7 5.4 %collective-permute-start.15 = (bf16[128,1024]{1,0:T(8,128)(2,1)}, bf16[128,1024]{1,0:T(8,128)(2,1)}, u32[]{:S(2)}, u32[]{:S(2)}) collective-permute-start(bf16[128,1024]{1,0:T(8,128)(2,1)} %pad_maximum_fusion.3), channel_id=1, source_target_pairs={{16,0},{20,4},{24,8},{28,12},{32,16},{36,20},{40,24},{44,28},{48,3... | collective-permute-start | bytes 786440 | tf_op jit(solution)/shard_map/ppermute | solution.py:60
  117.2 4.6 %collective-permute-start.4 = (f32[2,128]{1,0:T(2,128)S(1)}, f32[2,128]{1,0:T(2,128)S(1)}, u32[]{:S(2)}, u32[]{:S(2)}) collective-permute-start(f32[2,128]{1,0:T(2,128)S(1)} %fusion.78), channel_id=1, source_target_pairs={{0,2},{1,3},{2,0},{3,1},{4,6},{5,7},{6,4},{7,5},{8,10},{9,11},{10,... | collective-permute-start | bytes 3080 | tf_op jit(solution)/shard_map/ppermute | solution.py:166
  122.6 1.9 %collective-permute-start.12 = (bf16[128,1024]{1,0:T(8,128)(2,1)}, bf16[128,1024]{1,0:T(8,128)(2,1)}, u32[]{:S(2)}, u32[]{:S(2)}) collective-permute-start(bf16[128,1024]{1,0:T(8,128)(2,1)} %pad_maximum_fusion), channel_id=1, source_target_pairs={{4,0},{8,4},{12,8},{16,12},{20,16},{24,20},{28,24},{32,28},{36,32}... | collective-permute-start | bytes 786440 | tf_op jit(solution)/shard_map/ppermute | solution.py:60
  126.4 1.2 all_to_all.27
  127.6 2.0 %reduce.11 = bf16[32,2048]{1,0:T(8,128)(2,1)} reduce(bf16[32,1,2048]{2,1,0:T(2,128)(2,1)S(1)} %all_to_all.27, bf16[]{:T(256)} %broadcast.281), dimensions={1}, to_apply=%all_to_all.27.reduce_sub_computation | reduce | bytes 262146 | tf_op jit(solution)/shard_map/all_to_all | solution.py:47
  129.6 1.6 reshape.548
  131.2 4.6 %all-to-all-start.2 = ((bf16[32,2,1024]{2,1,0:T(2,128)(2,1)}), bf16[32,2,1024]{2,1,0:T(2,128)(2,1)}, u32[]{:S(2)}, u32[]{:S(2)}) async-start(bf16[32,2,1024]{2,1,0:T(2,128)(2,1)} %reshape.548), calls=%async_computation.2 | async-start | bytes 262144 | tf_op jit(solution)/shard_map/all_to_all | solution.py:47
  135.8 1.3 convolution_convert_fusion
  142.9 10.1 %all-to-all-done.2 = bf16[32,2,1024]{2,1,0:T(2,128)(2,1)} async-done(((bf16[32,2,1024]{2,1,0:T(2,128)(2,1)}), bf16[32,2,1024]{2,1,0:T(2,128)(2,1)}, u32[]{:S(2)}, u32[]{:S(2)}) %all-to-all-start.2) | async-done | bytes 131104 | tf_op jit(solution)/shard_map/all_to_all | solution.py:47
  153.0 1.4 reshape.549
  154.6 3.4 %collective-permute-start.7 = (bf16[2048]{0:T(1024)(128)(2,1)S(1)}, bf16[2048]{0:T(1024)(128)(2,1)S(1)}, u32[]{:S(2)}, u32[]{:S(2)}) collective-permute-start(bf16[2048]{0:T(1024)(128)(2,1)S(1)} %convert_element_type.175), channel_id=1, source_target_pairs={{384,0},{385,1},{386,2},{387,3},{388,4},{389,5},{390,6},{391,7},{3... | collective-permute-start | bytes 12296 | tf_op jit(solution)/shard_map/ppermute | solution.py:37
  158.0 2.4 %collective-permute-start.6 = (bf16[2048]{0:T(1024)(128)(2,1)S(1)}, bf16[2048]{0:T(1024)(128)(2,1)S(1)}, u32[]{:S(2)}, u32[]{:S(2)}) collective-permute-start(bf16[2048]{0:T(1024)(128)(2,1)S(1)} %convert_element_type.175), channel_id=1, source_target_pairs={{256,0},{384,128},{257,1},{385,129},{258,2},{386,130},{259,3},{387... | collective-permute-start | bytes 12296 | tf_op jit(solution)/shard_map/ppermute | solution.py:37
  160.4 1.7 collective-permute-start.5
  163.7 1.4 reduce.12
  165.9 3.9 %all-to-all-start.3 = ((bf16[32,2,1024]{2,1,0:T(2,128)(2,1)}), bf16[32,2,1024]{2,1,0:T(2,128)(2,1)S(1)}, u32[]{:S(2)}, u32[]{:S(2)}) async-start(bf16[32,2,1024]{2,1,0:T(2,128)(2,1)} %reshape.550), calls=%async_computation.3 | async-start | bytes 262144 | tf_op jit(solution)/shard_map/all_to_all | solution.py:53
  171.1 15.8 %all-to-all-done.3 = bf16[32,2,1024]{2,1,0:T(2,128)(2,1)S(1)} async-done(((bf16[32,2,1024]{2,1,0:T(2,128)(2,1)}), bf16[32,2,1024]{2,1,0:T(2,128)(2,1)S(1)}, u32[]{:S(2)}, u32[]{:S(2)}) %all-to-all-start.3) | async-done | bytes 131104 | tf_op jit(solution)/shard_map/all_to_all | solution.py:53
  (161 shorter events, 34.1 us)
Async XLA Ops:
  0.6 44.6 %copy-start = (bf16[128,512]{1,0:T(8,128)(2,1)S(1)}, bf16[128,512]{1,0:T(8,128)(2,1)}, u32[]{:S(2)}) copy-start(bf16[128,512]{1,0:T(8,128)(2,1)} %param.15) | copy-start | bytes 393220
  0.6 35.7 %copy-start.11 = (bf16[128,512]{1,0:T(8,128)(2,1)S(1)}, bf16[128,512]{1,0:T(8,128)(2,1)}, u32[]{:S(2)}) copy-start(bf16[128,512]{1,0:T(8,128)(2,1)} %param.11) | copy-start | bytes 393220
  0.7 35.4 %copy-start.27 = (s32[1,3]{1,0:T(1,128)S(1)}, s32[1,3]{1,0:T(1,128)}, u32[]{:S(2)}) copy-start(s32[1,3]{1,0:T(1,128)} %param.19) | copy-start | bytes 40
  0.7 35.6 %copy-start.3 = (bf16[128,512]{1,0:T(8,128)(2,1)S(1)}, bf16[128,512]{1,0:T(8,128)(2,1)}, u32[]{:S(2)}) copy-start(bf16[128,512]{1,0:T(8,128)(2,1)} %param.10) | copy-start | bytes 393220
  3.9 32.6 %copy-start.9 = (bf16[128,512]{1,0:T(8,128)(2,1)S(1)}, bf16[128,512]{1,0:T(8,128)(2,1)}, u32[]{:S(2)}) copy-start(bf16[128,512]{1,0:T(8,128)(2,1)} %param.12) | copy-start | bytes 393220
  3.9 37.0 %collective-permute-start.11 = (bf16[128,1024]{1,0:T(8,128)(2,1)}, bf16[128,1024]{1,0:T(8,128)(2,1)S(1)}, u32[]{:S(2)}, u32[]{:S(2)}) collective-permute-start(bf16[128,1024]{1,0:T(8,128)(2,1)} %constant_dynamic-update-slice_fusion), channel_id=1, source_target_pairs={{0,4},{4,8},{8,12},{12,16},{16,20},{20,24},{24,28},{28,32},{32,36}... | collective-permute-start | bytes 786440 | tf_op jit(solution)/shard_map/ppermute | solution.py:60
  6.0 34.9 %collective-permute-start.10 = (bf16[128,1024]{1,0:T(8,128)(2,1)}, bf16[128,1024]{1,0:T(8,128)(2,1)S(1)}, u32[]{:S(2)}, u32[]{:S(2)}) collective-permute-start(bf16[128,1024]{1,0:T(8,128)(2,1)} %constant_dynamic-update-slice_fusion), channel_id=1, source_target_pairs={{0,8},{4,12},{8,16},{12,20},{16,24},{20,28},{24,32},{28,36},{32,40... | collective-permute-start | bytes 786440 | tf_op jit(solution)/shard_map/ppermute | solution.py:60
  9.8 31.1 %collective-permute-start.9 = (bf16[128,1024]{1,0:T(8,128)(2,1)}, bf16[128,1024]{1,0:T(8,128)(2,1)S(1)}, u32[]{:S(2)}, u32[]{:S(2)}) collective-permute-start(bf16[128,1024]{1,0:T(8,128)(2,1)} %constant_dynamic-update-slice_fusion), channel_id=1, source_target_pairs={{0,12},{4,16},{8,20},{12,24},{16,28},{20,32},{24,36},{28,40},{32,4... | collective-permute-start | bytes 786440 | tf_op jit(solution)/shard_map/ppermute | solution.py:60
  15.0 25.8 %collective-permute-start.8 = (bf16[128,1024]{1,0:T(8,128)(2,1)}, bf16[128,1024]{1,0:T(8,128)(2,1)S(1)}, u32[]{:S(2)}, u32[]{:S(2)}) collective-permute-start(bf16[128,1024]{1,0:T(8,128)(2,1)} %constant_dynamic-update-slice_fusion), channel_id=1, source_target_pairs={{0,16},{4,20},{8,24},{12,28},{16,32},{20,36},{24,40},{28,44},{32,4... | collective-permute-start | bytes 786440 | tf_op jit(solution)/shard_map/ppermute | solution.py:60
  22.4 15.1 %copy-start.7 = (bf16[128,512]{0,1:T(8,128)(2,1)}, bf16[128,512]{0,1:T(8,128)(2,1)S(1)}, u32[]{:S(2)}) copy-start(bf16[128,512]{0,1:T(8,128)(2,1)S(1)} %copy.202) | copy-start | bytes 393220
  23.5 16.1 %copy-start.23 = (bf16[128,512]{1,0:T(8,128)(2,1)S(1)}, bf16[128,512]{1,0:T(8,128)(2,1)}, u32[]{:S(2)}) copy-start(bf16[128,512]{1,0:T(8,128)(2,1)} %param.14) | copy-start | bytes 393220
  23.6 16.2 %copy-start.24 = (bf16[128,512]{1,0:T(8,128)(2,1)S(1)}, bf16[128,512]{1,0:T(8,128)(2,1)}, u32[]{:S(2)}) copy-start(bf16[128,512]{1,0:T(8,128)(2,1)} %param.18) | copy-start | bytes 393220
  26.3 28.1 %all-to-all-start = ((bf16[32,2,1024]{2,1,0:T(2,128)(2,1)}), bf16[32,2,1024]{2,1,0:T(2,128)(2,1)S(1)}, u32[]{:S(2)}, u32[]{:S(2)}) async-start(bf16[32,2,1024]{2,1,0:T(2,128)(2,1)} %reshape.544), calls=%async_computation | async-start | bytes 262144 | tf_op jit(solution)/shard_map/all_to_all | solution.py:47
  36.5 4.1 %copy-start.16 = (bf16[4,128,128]{2,1,0:T(8,128)(2,1)}, bf16[4,128,128]{2,1,0:T(8,128)(2,1)S(1)}, u32[]{:S(2)}) copy-start(bf16[4,128,128]{2,1,0:T(8,128)(2,1)S(1)} %fusion.15) | copy-start | bytes 393220
  39.8 1.2 copy-start.14
  39.8 1.2 copy-start.15
  42.8 2.4 %copy-start.25 = (pred[128,512]{0,1:T(8,128)(4,1)S(1)}, pred[128,512]{0,1:T(8,128)(4,1)}, u32[]{:S(2)}) copy-start(pred[128,512]{0,1:T(8,128)(4,1)} %fusion.28) | copy-start | bytes 196612
  49.3 1.0 copy-start.13
  49.3 1.1 copy-start.22
  49.3 1.5 copy-start.29
  49.3 1.4 copy-start.31
  54.7 6.7 %collective-permute-start.2 = (bf16[2048]{0:T(1024)(128)(2,1)S(1)}, bf16[2048]{0:T(1024)(128)(2,1)S(1)}, u32[]{:S(2)}, u32[]{:S(2)}) collective-permute-start(bf16[2048]{0:T(1024)(128)(2,1)S(1)} %convert_element_type.163), channel_id=1, source_target_pairs={{0,384},{1,385},{2,386},{3,387},{4,388},{5,389},{6,390},{7,391},{8... | collective-permute-start | bytes 12296 | tf_op jit(solution)/shard_map/ppermute | solution.py:37
  56.0 7.0 %collective-permute-start.1 = (bf16[2048]{0:T(1024)(128)(2,1)S(1)}, bf16[2048]{0:T(1024)(128)(2,1)S(1)}, u32[]{:S(2)}, u32[]{:S(2)}) collective-permute-start(bf16[2048]{0:T(1024)(128)(2,1)S(1)} %convert_element_type.163), channel_id=1, source_target_pairs={{0,256},{128,384},{1,257},{129,385},{2,258},{130,386},{3,259},{131... | collective-permute-start | bytes 12296 | tf_op jit(solution)/shard_map/ppermute | solution.py:37
  57.3 5.7 %collective-permute-start = (bf16[2048]{0:T(1024)(128)(2,1)S(1)}, bf16[2048]{0:T(1024)(128)(2,1)S(1)}, u32[]{:S(2)}, u32[]{:S(2)}) collective-permute-start(bf16[2048]{0:T(1024)(128)(2,1)S(1)} %convert_element_type.163), channel_id=1, source_target_pairs={{0,128},{128,256},{256,384},{1,129},{129,257},{257,385},{2,130},{1... | collective-permute-start | bytes 12296 | tf_op jit(solution)/shard_map/ppermute | solution.py:37
  65.6 33.6 %all-to-all-start.1 = ((bf16[32,2,1024]{2,1,0:T(2,128)(2,1)}), bf16[32,2,1024]{2,1,0:T(2,128)(2,1)}, u32[]{:S(2)}, u32[]{:S(2)}) async-start(bf16[32,2,1024]{2,1,0:T(2,128)(2,1)} %reshape.546), calls=%async_computation.1 | async-start | bytes 262144 | tf_op jit(solution)/shard_map/all_to_all | solution.py:53
  87.0 7.7 %copy-start.19 = (bf16[128,512]{1,0:T(8,128)(2,1)S(1)}, bf16[128,512]{1,0:T(8,128)(2,1)}, u32[]{:S(2)}) copy-start(bf16[128,512]{1,0:T(8,128)(2,1)} %get-tuple-element.36) | copy-start | bytes 393220
  88.7 49.2 %collective-permute-start.13 = (bf16[128,1024]{1,0:T(8,128)(2,1)}, bf16[128,1024]{1,0:T(8,128)(2,1)}, u32[]{:S(2)}, u32[]{:S(2)}) collective-permute-start(bf16[128,1024]{1,0:T(8,128)(2,1)} %pad_maximum_fusion.1), channel_id=1, source_target_pairs={{8,0},{12,4},{16,8},{20,12},{24,16},{28,20},{32,24},{36,28},{40,32... | collective-permute-start | bytes 786440 | tf_op jit(solution)/shard_map/ppermute | solution.py:60
  95.5 43.5 %collective-permute-start.14 = (bf16[128,1024]{1,0:T(8,128)(2,1)}, bf16[128,1024]{1,0:T(8,128)(2,1)}, u32[]{:S(2)}, u32[]{:S(2)}) collective-permute-start(bf16[128,1024]{1,0:T(8,128)(2,1)} %pad_maximum_fusion.2), channel_id=1, source_target_pairs={{12,0},{16,4},{20,8},{24,12},{28,16},{32,20},{36,24},{40,28},{44,3... | collective-permute-start | bytes 786440 | tf_op jit(solution)/shard_map/ppermute | solution.py:60
  105.2 16.7 %copy-start.18 = (bf16[128,512]{1,0:T(8,128)(2,1)S(1)}, bf16[128,512]{1,0:T(8,128)(2,1)}, u32[]{:S(2)}) copy-start(bf16[128,512]{1,0:T(8,128)(2,1)} %get-tuple-element.34) | copy-start | bytes 393220
  105.2 16.7 %copy-start.20 = (bf16[128,512]{1,0:T(8,128)(2,1)S(1)}, bf16[128,512]{1,0:T(8,128)(2,1)}, u32[]{:S(2)}) copy-start(bf16[128,512]{1,0:T(8,128)(2,1)} %get-tuple-element.30) | copy-start | bytes 393220
  105.2 19.4 %copy-start.26 = (f32[512]{0:T(512)S(1)}, f32[512]{0:T(512)}, u32[]{:S(2)}) copy-start(f32[512]{0:T(512)} %param.13) | copy-start | bytes 6148
  105.2 20.2 %copy-start.4 = (bf16[128,512]{1,0:T(8,128)(2,1)S(1)}, bf16[128,512]{1,0:T(8,128)(2,1)}, u32[]{:S(2)}) copy-start(bf16[128,512]{1,0:T(8,128)(2,1)} %param.10) | copy-start | bytes 393220
  106.6 10.6 %collective-permute-start.3 = (f32[2,128]{1,0:T(2,128)S(1)}, f32[2,128]{1,0:T(2,128)S(1)}, u32[]{:S(2)}, u32[]{:S(2)}) collective-permute-start(f32[2,128]{1,0:T(2,128)S(1)} %pad_maximum_fusion.4), channel_id=1, source_target_pairs={{0,1},{1,0},{2,3},{3,2},{4,5},{5,4},{6,7},{7,6},{8,9},{9,8},{10,11... | collective-permute-start | bytes 3080 | tf_op jit(solution)/shard_map/ppermute | solution.py:166
  111.7 28.2 %collective-permute-start.15 = (bf16[128,1024]{1,0:T(8,128)(2,1)}, bf16[128,1024]{1,0:T(8,128)(2,1)}, u32[]{:S(2)}, u32[]{:S(2)}) collective-permute-start(bf16[128,1024]{1,0:T(8,128)(2,1)} %pad_maximum_fusion.3), channel_id=1, source_target_pairs={{16,0},{20,4},{24,8},{28,12},{32,16},{36,20},{40,24},{44,28},{48,3... | collective-permute-start | bytes 786440 | tf_op jit(solution)/shard_map/ppermute | solution.py:60
  117.2 7.3 %collective-permute-start.4 = (f32[2,128]{1,0:T(2,128)S(1)}, f32[2,128]{1,0:T(2,128)S(1)}, u32[]{:S(2)}, u32[]{:S(2)}) collective-permute-start(f32[2,128]{1,0:T(2,128)S(1)} %fusion.78), channel_id=1, source_target_pairs={{0,2},{1,3},{2,0},{3,1},{4,6},{5,7},{6,4},{7,5},{8,10},{9,11},{10,... | collective-permute-start | bytes 3080 | tf_op jit(solution)/shard_map/ppermute | solution.py:166
  122.6 18.3 %collective-permute-start.12 = (bf16[128,1024]{1,0:T(8,128)(2,1)}, bf16[128,1024]{1,0:T(8,128)(2,1)}, u32[]{:S(2)}, u32[]{:S(2)}) collective-permute-start(bf16[128,1024]{1,0:T(8,128)(2,1)} %pad_maximum_fusion), channel_id=1, source_target_pairs={{4,0},{8,4},{12,8},{16,12},{20,16},{24,20},{28,24},{32,28},{36,32}... | collective-permute-start | bytes 786440 | tf_op jit(solution)/shard_map/ppermute | solution.py:60
  131.2 21.7 %all-to-all-start.2 = ((bf16[32,2,1024]{2,1,0:T(2,128)(2,1)}), bf16[32,2,1024]{2,1,0:T(2,128)(2,1)}, u32[]{:S(2)}, u32[]{:S(2)}) async-start(bf16[32,2,1024]{2,1,0:T(2,128)(2,1)} %reshape.548), calls=%async_computation.2 | async-start | bytes 262144 | tf_op jit(solution)/shard_map/all_to_all | solution.py:47
  142.0 20.2 %copy-start.2 = (bf16[128,4,128]{0,2,1:T(8,128)(2,1)S(1)}, bf16[128,4,128]{0,2,1:T(8,128)(2,1)}, u32[]{:S(2)}) copy-start(bf16[128,4,128]{0,2,1:T(8,128)(2,1)} %copy-done.1) | copy-start | bytes 393220
  142.0 20.2 %copy-start.10 = (bf16[128,512]{1,0:T(8,128)(2,1)S(1)}, bf16[128,512]{1,0:T(8,128)(2,1)}, u32[]{:S(2)}) copy-start(bf16[128,512]{1,0:T(8,128)(2,1)} %param.12) | copy-start | bytes 393220
  142.9 26.9 %copy-start.8 = (bf16[128,512]{0,1:T(8,128)(2,1)S(1)}, bf16[128,512]{0,1:T(8,128)(2,1)}, u32[]{:S(2)}) copy-start(bf16[128,512]{0,1:T(8,128)(2,1)} %copy-done.7) | copy-start | bytes 393220
  154.3 15.6 %copy-start.6 = (bf16[4,128,128]{2,1,0:T(8,128)(2,1)S(1)}, bf16[4,128,128]{2,1,0:T(8,128)(2,1)}, u32[]{:S(2)}) copy-start(bf16[4,128,128]{2,1,0:T(8,128)(2,1)} %reshape.495) | copy-start | bytes 393220
  154.6 7.8 %collective-permute-start.7 = (bf16[2048]{0:T(1024)(128)(2,1)S(1)}, bf16[2048]{0:T(1024)(128)(2,1)S(1)}, u32[]{:S(2)}, u32[]{:S(2)}) collective-permute-start(bf16[2048]{0:T(1024)(128)(2,1)S(1)} %convert_element_type.175), channel_id=1, source_target_pairs={{384,0},{385,1},{386,2},{387,3},{388,4},{389,5},{390,6},{391,7},{3... | collective-permute-start | bytes 12296 | tf_op jit(solution)/shard_map/ppermute | solution.py:37
  158.0 4.3 %collective-permute-start.6 = (bf16[2048]{0:T(1024)(128)(2,1)S(1)}, bf16[2048]{0:T(1024)(128)(2,1)S(1)}, u32[]{:S(2)}, u32[]{:S(2)}) collective-permute-start(bf16[2048]{0:T(1024)(128)(2,1)S(1)} %convert_element_type.175), channel_id=1, source_target_pairs={{256,0},{384,128},{257,1},{385,129},{258,2},{386,130},{259,3},{387... | collective-permute-start | bytes 12296 | tf_op jit(solution)/shard_map/ppermute | solution.py:37
  160.4 3.0 %collective-permute-start.5 = (bf16[2048]{0:T(1024)(128)(2,1)S(1)}, bf16[2048]{0:T(1024)(128)(2,1)S(1)}, u32[]{:S(2)}, u32[]{:S(2)}) collective-permute-start(bf16[2048]{0:T(1024)(128)(2,1)S(1)} %convert_element_type.175), channel_id=1, source_target_pairs={{128,0},{256,128},{384,256},{129,1},{257,129},{385,257},{130,2},{2... | collective-permute-start | bytes 12296 | tf_op jit(solution)/shard_map/ppermute | solution.py:37
  163.7 7.2 %copy-start.17 = (bf16[4,128,128]{2,1,0:T(8,128)(2,1)S(1)}, bf16[4,128,128]{2,1,0:T(8,128)(2,1)}, u32[]{:S(2)}) copy-start(bf16[4,128,128]{2,1,0:T(8,128)(2,1)} %copy-done.16) | copy-start | bytes 393220
  165.9 21.0 %all-to-all-start.3 = ((bf16[32,2,1024]{2,1,0:T(2,128)(2,1)}), bf16[32,2,1024]{2,1,0:T(2,128)(2,1)S(1)}, u32[]{:S(2)}, u32[]{:S(2)}) async-start(bf16[32,2,1024]{2,1,0:T(2,128)(2,1)} %reshape.550), calls=%async_computation.3 | async-start | bytes 262144 | tf_op jit(solution)/shard_map/all_to_all | solution.py:53
  170.2 17.9 %copy-start.12 = (bf16[128,512]{1,0:T(8,128)(2,1)S(1)}, bf16[128,512]{1,0:T(8,128)(2,1)}, u32[]{:S(2)}) copy-start(bf16[128,512]{1,0:T(8,128)(2,1)} %param.11) | copy-start | bytes 393220
  171.1 18.0 %copy-start.5 = (bf16[128,512]{1,0:T(8,128)(2,1)S(1)}, bf16[128,512]{1,0:T(8,128)(2,1)}, u32[]{:S(2)}) copy-start(bf16[128,512]{1,0:T(8,128)(2,1)} %param.10) | copy-start | bytes 393220
  (4 other events, 3.5 us)

commit v17 on v13

--- a/solution.py
+++ b/solution.py
@@ -195,11 +195,7 @@
     lin_dv = lin_dv.reshape(token_count, lin_width).astype(jnp.bfloat16)
     width = sm_key.shape[1]
     pair = jnp.concatenate([sm_key, sm_value], axis=1)
-    arrived = []
-    moving = pair
-    for distance in range(1, SPAN + 1):
-        moving = from_behind(moving, CTX, 1)
-        arrived.append(moving)
+    arrived = [from_behind(pair, CTX, distance) for distance in range(1, SPAN + 1)]
     key_window = jnp.concatenate(
         [arrived[SPAN - 1 - place][:, :width] for place in range(SPAN)] + [sm_key], axis=0
     )

time: 181 us -> 202 us (1.12)
  starting transfers between devices: 81 us -> 88.5 us
  other arithmetic: 23.5 us -> 30.7 us
  local copies, waits for them, and re-layouts: 23.6 us -> 30 us
  waiting for transfers between devices: 35.9 us -> 33.2 us
    ppermute x8, starting transfers between devices: 26.8 us -> 34.8 us  [from_behind(): return lax.ppermute(shard, axis, pairs)]
    all_to_all x2, starting transfers between devices: 20.2 us -> 13.8 us  [carried_in(): mine = lax.all_to_all(slices, 'inner', 0, 0, tiled=True).astype(jnp.float32)]
    all_to_all x2, waiting for transfers between devices: 14.8 us -> 19.6 us  [carried_in(): back = lax.all_to_all(states, 'inner', 0, 0, tiled=True)]
    ppermute x6, waiting for transfers between devices: 4.4 us -> 0.02 us  [scan_over(): arrived.append(lax.ppermute(total.astype(jnp.bfloat16), axis, pairs))]
    ppermute x6, starting transfers between devices: 11.4 us -> 14.8 us  [scan_over(): arrived.append(lax.ppermute(total.astype(jnp.bfloat16), axis, pairs))]
    all_to_all x2, starting transfers between devices: 14.2 us -> 17.1 us  [carried_in(): back = lax.all_to_all(states, 'inner', 0, 0, tiled=True)]
    unnamed x70 -> x79, local copies, waits for them, and re-layouts: 12.4 us -> 13.3 us
  transfers between devices with their start and end apart: 20 -> 20, of which waited for: 7 -> 5; matrix products, arithmetic and copies ran while one was open for 30% -> 33% of each run, Pallas kernels for 0% -> 0%
where the time goes in v17:
time: 202 us; the launch traced here: 200 us
  starting transfers between devices  88.5 us (44%)
  waiting for transfers between devices  33.2 us (16%)
  other arithmetic  30.7 us (15%)
  local copies, waits for them, and re-layouts  30 us (15%)
  matrix products  16.3 us (8%)
    ppermute x8, starting transfers between devices, from_behind(): return lax.ppermute(shard, axis, pairs)  34.8 us
    all_to_all x2, waiting for transfers between devices, carried_in(): back = lax.all_to_all(states, 'inner', 0, 0, tiled=True)  19.6 us
    all_to_all x2, starting transfers between devices, carried_in(): back = lax.all_to_all(states, 'inner', 0, 0, tiled=True)  17.1 us
    ppermute x6, starting transfers between devices, scan_over(): arrived.append(lax.ppermute(total.astype(jnp.bfloat16), axis, pairs))  14.8 us
    all_to_all x2, starting transfers between devices, carried_in(): mine = lax.all_to_all(slices, 'inner', 0, 0, tiled=True).astype(jnp.float32)  13.8 us
    unnamed x79, local copies, waits for them, and re-layouts  13.3 us
    all_to_all x2, waiting for transfers between devices, carried_in(): mine = lax.all_to_all(slices, 'inner', 0, 0, tiled=True).astype(jnp.float32)  12.5 us
    ppermute x2, starting transfers between devices, per_device(): lax.ppermute(sums, 'head', [(i, i ^ step) for i in range(heads_dev)])  8.01 us
  transfers between devices with their start and end apart: 20, of which 5 were waited for; matrix products, arithmetic and copies ran while one was open for 33% of the time, Pallas kernels for 0%

profile of v17, /device:TPU:24, one launch (start us, length us, event | category | flops | bytes accessed | tf_op | source)
XLA Modules:
  0.0 200.4 jit_solution(13314922934769595686)
XLA Ops:
  0.7 1.6 constant_dynamic-update-slice_fusion.1
  2.3 1.6 constant_dynamic-update-slice_fusion
  3.9 2.0 %collective-permute-start.11 = (bf16[128,1024]{1,0:T(8,128)(2,1)}, bf16[128,1024]{1,0:T(8,128)(2,1)S(1)}, u32[]{:S(2)}, u32[]{:S(2)}) collective-permute-start(bf16[128,1024]{1,0:T(8,128)(2,1)} %constant_dynamic-update-slice_fusion), channel_id=1, source_target_pairs={{0,4},{4,8},{8,12},{12,16},{16,20},{20,24},{24,28},{28,32},{32,36}... | collective-permute-start | bytes 786440 | tf_op jit(solution)/shard_map/ppermute | solution.py:60
  6.0 3.8 %collective-permute-start.10 = (bf16[128,1024]{1,0:T(8,128)(2,1)}, bf16[128,1024]{1,0:T(8,128)(2,1)S(1)}, u32[]{:S(2)}, u32[]{:S(2)}) collective-permute-start(bf16[128,1024]{1,0:T(8,128)(2,1)} %constant_dynamic-update-slice_fusion), channel_id=1, source_target_pairs={{0,8},{4,12},{8,16},{12,20},{16,24},{20,28},{24,32},{28,36},{32,40... | collective-permute-start | bytes 786440 | tf_op jit(solution)/shard_map/ppermute | solution.py:60
  9.8 5.2 %collective-permute-start.9 = (bf16[128,1024]{1,0:T(8,128)(2,1)}, bf16[128,1024]{1,0:T(8,128)(2,1)S(1)}, u32[]{:S(2)}, u32[]{:S(2)}) collective-permute-start(bf16[128,1024]{1,0:T(8,128)(2,1)} %constant_dynamic-update-slice_fusion), channel_id=1, source_target_pairs={{0,12},{4,16},{8,20},{12,24},{16,28},{20,32},{24,36},{28,40},{32,4... | collective-permute-start | bytes 786440 | tf_op jit(solution)/shard_map/ppermute | solution.py:60
  15.0 6.4 %collective-permute-start.8 = (bf16[128,1024]{1,0:T(8,128)(2,1)}, bf16[128,1024]{1,0:T(8,128)(2,1)}, u32[]{:S(2)}, u32[]{:S(2)}) collective-permute-start(bf16[128,1024]{1,0:T(8,128)(2,1)} %constant_dynamic-update-slice_fusion), channel_id=1, source_target_pairs={{0,16},{4,20},{8,24},{12,28},{16,32},{20,36},{24,40},{28,44},{32,4... | collective-permute-start | bytes 786440 | tf_op jit(solution)/shard_map/ppermute | solution.py:60
  24.1 1.3 reduce.9
  26.2 9.8 %all-to-all-start = ((bf16[32,2,1024]{2,1,0:T(2,128)(2,1)}), bf16[32,2,1024]{2,1,0:T(2,128)(2,1)S(1)}, u32[]{:S(2)}, u32[]{:S(2)}) async-start(bf16[32,2,1024]{2,1,0:T(2,128)(2,1)} %reshape.544), calls=%async_computation | async-start | bytes 262144 | tf_op jit(solution)/shard_map/all_to_all | solution.py:47
  43.9 1.2 gather_fusion.1
  45.5 1.5 fusion.81
  47.0 1.6 fusion.18
  49.3 5.1 %all-to-all-done = bf16[32,2,1024]{2,1,0:T(2,128)(2,1)S(1)} async-done(((bf16[32,2,1024]{2,1,0:T(2,128)(2,1)}), bf16[32,2,1024]{2,1,0:T(2,128)(2,1)S(1)}, u32[]{:S(2)}, u32[]{:S(2)}) %all-to-all-start) | async-done | bytes 131104 | tf_op jit(solution)/shard_map/all_to_all | solution.py:47
  54.7 1.3 collective-permute-start.2
  56.0 1.3 collective-permute-start.1
  57.3 1.3 collective-permute-start
  58.6 1.3 convolution_bitcast_fusion.1
  61.0 1.9 copy.116
  62.9 1.4 reshape.528
  66.8 2.3 %scatter_fusion = f32[5,128,512]{2,1,0:T(8,128)S(1)} fusion(f32[5,128,512]{2,1,0:T(8,128)S(1)} %broadcast.249.clone.1, s32[4]{0:T(128)S(1)} %copy-done.28, f32[4,128,512]{2,1,0:T(8,128)} %reshape.528), kind=kCustom, calls=%fused_computation.2 | custom fusion | flops 262144 | bytes 3145744 | tf_op jit(solution)/shard_map/scatter-add | solution.py:122
  70.5 1.3 reduce.10
  72.5 12.5 %all-to-all-start.1 = ((bf16[32,2,1024]{2,1,0:T(2,128)(2,1)}), bf16[32,2,1024]{2,1,0:T(2,128)(2,1)}, u32[]{:S(2)}, u32[]{:S(2)}) async-start(bf16[32,2,1024]{2,1,0:T(2,128)(2,1)} %reshape.546), calls=%async_computation.1 | async-start | bytes 262144 | tf_op jit(solution)/shard_map/all_to_all | solution.py:53
  85.1 1.9 slice_bitcast_fusion.2
  88.5 6.7 %collective-permute-start.12 = (bf16[128,1024]{1,0:T(8,128)(2,1)}, bf16[128,1024]{1,0:T(8,128)(2,1)}, u32[]{:S(2)}, u32[]{:S(2)}) collective-permute-start(bf16[128,1024]{1,0:T(8,128)(2,1)} %pad_maximum_fusion), channel_id=1, source_target_pairs={{4,0},{8,4},{12,8},{16,12},{20,16},{24,20},{28,24},{32,28},{36,32}... | collective-permute-start | bytes 786440 | tf_op jit(solution)/shard_map/ppermute | solution.py:60
  95.2 7.1 %all-to-all-done.1 = bf16[32,2,1024]{2,1,0:T(2,128)(2,1)} async-done(((bf16[32,2,1024]{2,1,0:T(2,128)(2,1)}), bf16[32,2,1024]{2,1,0:T(2,128)(2,1)}, u32[]{:S(2)}, u32[]{:S(2)}) %all-to-all-start.1) | async-done | bytes 131104 | tf_op jit(solution)/shard_map/all_to_all | solution.py:53
  102.2 2.0 reshape.547
  104.2 2.3 %reduce.7 = bf16[32,2048]{1,0:T(8,128)(2,1)} reduce(bf16[32,1,2048]{2,1,0:T(2,128)(2,1)} %reshape.547, bf16[]{:T(256)} %constant.86), dimensions={1}, to_apply=%all_to_all.22.reduce_sub_computation | reduce | bytes 262146 | tf_op jit(solution)/shard_map/all_to_all | solution.py:53
  106.6 1.6 reshape.495
  108.2 2.1 %multiply_reduce_fusion.1 = (f32[128]{0:T(128)S(1)}, f32[128]{0:T(128)S(1)}, f32[128,4,128]{0,2,1:T(8,128)}) fusion(f32[128,512]{0,1:T(8,128)S(1)} %copy.86, f32[4,128]{1,0:T(4,128)} %bitcast.254, f32[128,4,128]{0,2,1:T(8,128)} %convolution_bitcast_fusion.8, bf16[4,128,128]{2,1,0:T(8,128)(2,1)} %reshape.495, bf16[128,512]{1,0:T(8,128)(2,1)} %param.10), kind=kOutput, calls=%fused_computation.60 | convolution fusion | flops 17170176 | bytes 1051648 | tf_op jit(solution)/shard_map/thi,hij->thj/dot_general | solution.py:156
  110.8 3.4 %collective-permute-start.3 = (f32[2,128]{1,0:T(2,128)}, f32[2,128]{1,0:T(2,128)}, u32[]{:S(2)}, u32[]{:S(2)}) collective-permute-start(f32[2,128]{1,0:T(2,128)} %pad_maximum_fusion.1), channel_id=1, source_target_pairs={{0,1},{1,0},{2,3},{3,2},{4,5},{5,4},{6,7},{7,6},{8,9},{9,8},{10,11... | collective-permute-start | bytes 3080 | tf_op jit(solution)/shard_map/ppermute | solution.py:166
  114.3 2.0 convolution_convert_fusion
  116.2 1.7 copy.122
  118.6 4.6 %collective-permute-start.4 = (f32[2,128]{1,0:T(2,128)S(1)}, f32[2,128]{1,0:T(2,128)S(1)}, u32[]{:S(2)}, u32[]{:S(2)}) collective-permute-start(f32[2,128]{1,0:T(2,128)S(1)} %fusion.78), channel_id=1, source_target_pairs={{0,2},{1,3},{2,0},{3,1},{4,6},{5,7},{6,4},{7,5},{8,10},{9,11},{10,... | collective-permute-start | bytes 3080 | tf_op jit(solution)/shard_map/ppermute | solution.py:166
  123.2 1.8 add_convert_fusion.2
  125.1 1.9 collective-permute-start.13
  130.8 2.2 %reduce.11 = bf16[32,2048]{1,0:T(8,128)(2,1)S(1)} reduce(bf16[32,1,2048]{2,1,0:T(2,128)(2,1)} %all_to_all.27, bf16[]{:T(256)} %broadcast.281), dimensions={1}, to_apply=%all_to_all.27.reduce_sub_computation | reduce | bytes 262146 | tf_op jit(solution)/shard_map/all_to_all | solution.py:47
  133.8 4.0 %all-to-all-start.2 = ((bf16[32,2,1024]{2,1,0:T(2,128)(2,1)}), bf16[32,2,1024]{2,1,0:T(2,128)(2,1)S(1)}, u32[]{:S(2)}, u32[]{:S(2)}) async-start(bf16[32,2,1024]{2,1,0:T(2,128)(2,1)} %reshape.548), calls=%async_computation.2 | async-start | bytes 262144 | tf_op jit(solution)/shard_map/all_to_all | solution.py:47
  137.8 1.8 add_convert_fusion.1
  139.7 6.8 %collective-permute-start.14 = (bf16[128,1024]{1,0:T(8,128)(2,1)}, bf16[128,1024]{1,0:T(8,128)(2,1)}, u32[]{:S(2)}, u32[]{:S(2)}) collective-permute-start(bf16[128,1024]{1,0:T(8,128)(2,1)} %add_convert_fusion.1), channel_id=1, source_target_pairs={{4,0},{8,4},{12,8},{16,12},{20,16},{24,20},{28,24},{32,28},{36,32}... | collective-permute-start | bytes 786440 | tf_op jit(solution)/shard_map/ppermute | solution.py:60
  147.6 7.4 %all-to-all-done.2 = bf16[32,2,1024]{2,1,0:T(2,128)(2,1)S(1)} async-done(((bf16[32,2,1024]{2,1,0:T(2,128)(2,1)}), bf16[32,2,1024]{2,1,0:T(2,128)(2,1)S(1)}, u32[]{:S(2)}, u32[]{:S(2)}) %all-to-all-start.2) | async-done | bytes 131104 | tf_op jit(solution)/shard_map/all_to_all | solution.py:47
  155.4 6.9 %collective-permute-start.7 = (bf16[2048]{0:T(1024)(128)(2,1)S(1)}, bf16[2048]{0:T(1024)(128)(2,1)S(1)}, u32[]{:S(2)}, u32[]{:S(2)}) collective-permute-start(bf16[2048]{0:T(1024)(128)(2,1)S(1)} %convert_element_type.195), channel_id=1, source_target_pairs={{384,0},{385,1},{386,2},{387,3},{388,4},{389,5},{390,6},{391,7},{3... | collective-permute-start | bytes 12296 | tf_op jit(solution)/shard_map/ppermute | solution.py:37
  162.3 1.3 collective-permute-start.6
  163.6 2.8 %collective-permute-start.5 = (bf16[2048]{0:T(1024)(128)(2,1)S(1)}, bf16[2048]{0:T(1024)(128)(2,1)S(1)}, u32[]{:S(2)}, u32[]{:S(2)}) collective-permute-start(bf16[2048]{0:T(1024)(128)(2,1)S(1)} %convert_element_type.195), channel_id=1, source_target_pairs={{128,0},{256,128},{384,256},{129,1},{257,129},{385,257},{130,2},{2... | collective-permute-start | bytes 12296 | tf_op jit(solution)/shard_map/ppermute | solution.py:37
  166.4 1.7 add_convert_fusion
  168.1 2.0 %collective-permute-start.15 = (bf16[128,1024]{1,0:T(8,128)(2,1)}, bf16[128,1024]{1,0:T(8,128)(2,1)}, u32[]{:S(2)}, u32[]{:S(2)}) collective-permute-start(bf16[128,1024]{1,0:T(8,128)(2,1)} %add_convert_fusion), channel_id=1, source_target_pairs={{4,0},{8,4},{12,8},{16,12},{20,16},{24,20},{28,24},{32,28},{36,32}... | collective-permute-start | bytes 786440 | tf_op jit(solution)/shard_map/ppermute | solution.py:60
  171.2 2.2 %reduce.12 = bf16[32,2048]{1,0:T(8,128)(2,1)S(1)} reduce(bf16[32,1,2048]{2,1,0:T(2,128)(2,1)} %add_convert_fusion.3, bf16[]{:T(256)} %broadcast.281), dimensions={1}, to_apply=%add_convert_fusion.3.reduce_sub_computation | reduce | bytes 262146 | tf_op jit(solution)/shard_map/jit(cumsum)/reduce_window_sum | solution.py:48
  174.2 4.6 %all-to-all-start.3 = ((bf16[32,2,1024]{2,1,0:T(2,128)(2,1)}), bf16[32,2,1024]{2,1,0:T(2,128)(2,1)}, u32[]{:S(2)}, u32[]{:S(2)}) async-start(bf16[32,2,1024]{2,1,0:T(2,128)(2,1)} %reshape.550), calls=%async_computation.3 | async-start | bytes 262144 | tf_op jit(solution)/shard_map/all_to_all | solution.py:53
  183.4 12.5 %all-to-all-done.3 = bf16[32,2,1024]{2,1,0:T(2,128)(2,1)} async-done(((bf16[32,2,1024]{2,1,0:T(2,128)(2,1)}), bf16[32,2,1024]{2,1,0:T(2,128)(2,1)}, u32[]{:S(2)}, u32[]{:S(2)}) %all-to-all-start.3) | async-done | bytes 131104 | tf_op jit(solution)/shard_map/all_to_all | solution.py:53
  195.9 1.4 reshape.551
  (156 shorter events, 36.4 us)
Async XLA Ops:
  0.6 44.8 %copy-start = (bf16[128,512]{1,0:T(8,128)(2,1)S(1)}, bf16[128,512]{1,0:T(8,128)(2,1)}, u32[]{:S(2)}) copy-start(bf16[128,512]{1,0:T(8,128)(2,1)} %param.15) | copy-start | bytes 393220
  0.6 35.6 %copy-start.13 = (bf16[128,512]{1,0:T(8,128)(2,1)S(1)}, bf16[128,512]{1,0:T(8,128)(2,1)}, u32[]{:S(2)}) copy-start(bf16[128,512]{1,0:T(8,128)(2,1)} %param.11) | copy-start | bytes 393220
  0.7 35.3 %copy-start.29 = (s32[1,3]{1,0:T(1,128)S(1)}, s32[1,3]{1,0:T(1,128)}, u32[]{:S(2)}) copy-start(s32[1,3]{1,0:T(1,128)} %param.19) | copy-start | bytes 40
  0.7 35.5 %copy-start.5 = (bf16[128,512]{1,0:T(8,128)(2,1)S(1)}, bf16[128,512]{1,0:T(8,128)(2,1)}, u32[]{:S(2)}) copy-start(bf16[128,512]{1,0:T(8,128)(2,1)} %param.10) | copy-start | bytes 393220
  3.9 32.5 %copy-start.10 = (bf16[128,512]{1,0:T(8,128)(2,1)S(1)}, bf16[128,512]{1,0:T(8,128)(2,1)}, u32[]{:S(2)}) copy-start(bf16[128,512]{1,0:T(8,128)(2,1)} %param.12) | copy-start | bytes 393220
  3.9 38.1 %collective-permute-start.11 = (bf16[128,1024]{1,0:T(8,128)(2,1)}, bf16[128,1024]{1,0:T(8,128)(2,1)S(1)}, u32[]{:S(2)}, u32[]{:S(2)}) collective-permute-start(bf16[128,1024]{1,0:T(8,128)(2,1)} %constant_dynamic-update-slice_fusion), channel_id=1, source_target_pairs={{0,4},{4,8},{8,12},{12,16},{16,20},{20,24},{24,28},{28,32},{32,36}... | collective-permute-start | bytes 786440 | tf_op jit(solution)/shard_map/ppermute | solution.py:60
  6.0 36.0 %collective-permute-start.10 = (bf16[128,1024]{1,0:T(8,128)(2,1)}, bf16[128,1024]{1,0:T(8,128)(2,1)S(1)}, u32[]{:S(2)}, u32[]{:S(2)}) collective-permute-start(bf16[128,1024]{1,0:T(8,128)(2,1)} %constant_dynamic-update-slice_fusion), channel_id=1, source_target_pairs={{0,8},{4,12},{8,16},{12,20},{16,24},{20,28},{24,32},{28,36},{32,40... | collective-permute-start | bytes 786440 | tf_op jit(solution)/shard_map/ppermute | solution.py:60
  9.8 32.1 %collective-permute-start.9 = (bf16[128,1024]{1,0:T(8,128)(2,1)}, bf16[128,1024]{1,0:T(8,128)(2,1)S(1)}, u32[]{:S(2)}, u32[]{:S(2)}) collective-permute-start(bf16[128,1024]{1,0:T(8,128)(2,1)} %constant_dynamic-update-slice_fusion), channel_id=1, source_target_pairs={{0,12},{4,16},{8,20},{12,24},{16,28},{20,32},{24,36},{28,40},{32,4... | collective-permute-start | bytes 786440 | tf_op jit(solution)/shard_map/ppermute | solution.py:60
  15.0 26.0 %collective-permute-start.8 = (bf16[128,1024]{1,0:T(8,128)(2,1)}, bf16[128,1024]{1,0:T(8,128)(2,1)}, u32[]{:S(2)}, u32[]{:S(2)}) collective-permute-start(bf16[128,1024]{1,0:T(8,128)(2,1)} %constant_dynamic-update-slice_fusion), channel_id=1, source_target_pairs={{0,16},{4,20},{8,24},{12,28},{16,32},{20,36},{24,40},{28,44},{32,4... | collective-permute-start | bytes 786440 | tf_op jit(solution)/shard_map/ppermute | solution.py:60
  22.4 15.0 %copy-start.8 = (bf16[128,512]{0,1:T(8,128)(2,1)}, bf16[128,512]{0,1:T(8,128)(2,1)S(1)}, u32[]{:S(2)}) copy-start(bf16[128,512]{0,1:T(8,128)(2,1)S(1)} %copy.202) | copy-start | bytes 393220
  23.5 16.0 %copy-start.22 = (bf16[128,512]{1,0:T(8,128)(2,1)S(1)}, bf16[128,512]{1,0:T(8,128)(2,1)}, u32[]{:S(2)}) copy-start(bf16[128,512]{1,0:T(8,128)(2,1)} %param.14) | copy-start | bytes 393220
  23.6 16.1 %copy-start.23 = (bf16[128,512]{1,0:T(8,128)(2,1)S(1)}, bf16[128,512]{1,0:T(8,128)(2,1)}, u32[]{:S(2)}) copy-start(bf16[128,512]{1,0:T(8,128)(2,1)} %param.18) | copy-start | bytes 393220
  26.2 28.2 %all-to-all-start = ((bf16[32,2,1024]{2,1,0:T(2,128)(2,1)}), bf16[32,2,1024]{2,1,0:T(2,128)(2,1)S(1)}, u32[]{:S(2)}, u32[]{:S(2)}) async-start(bf16[32,2,1024]{2,1,0:T(2,128)(2,1)} %reshape.544), calls=%async_computation | async-start | bytes 262144 | tf_op jit(solution)/shard_map/all_to_all | solution.py:47
  36.4 3.1 %copy-start.19 = (bf16[4,128,128]{2,1,0:T(8,128)(2,1)}, bf16[4,128,128]{2,1,0:T(8,128)(2,1)S(1)}, u32[]{:S(2)}) copy-start(bf16[4,128,128]{2,1,0:T(8,128)(2,1)S(1)} %fusion.15) | copy-start | bytes 393220
  39.7 2.3 %copy-start.17 = (bf16[128,512]{1,0:T(8,128)(2,1)S(1)}, bf16[128,512]{1,0:T(8,128)(2,1)}, u32[]{:S(2)}) copy-start(bf16[128,512]{1,0:T(8,128)(2,1)} %param.16) | copy-start | bytes 393220
  39.7 2.3 %copy-start.18 = (bf16[128,512]{1,0:T(8,128)(2,1)S(1)}, bf16[128,512]{1,0:T(8,128)(2,1)}, u32[]{:S(2)}) copy-start(bf16[128,512]{1,0:T(8,128)(2,1)} %param.17) | copy-start | bytes 393220
  43.7 1.8 copy-start.2
  47.0 1.6 copy-start.24
  47.0 1.6 copy-start.30
  49.3 9.3 %copy-start.4 = (bf16[4,128,512]{1,2,0:T(8,128)(2,1)}, bf16[4,128,512]{1,2,0:T(8,128)(2,1)S(1)}, u32[]{:S(2)}) copy-start(bf16[4,128,512]{1,2,0:T(8,128)(2,1)S(1)} %fusion.8) | copy-start | bytes 1572868
  54.7 15.3 %collective-permute-start.2 = (bf16[2048]{0:T(1024)(128)(2,1)S(1)}, bf16[2048]{0:T(1024)(128)(2,1)S(1)}, u32[]{:S(2)}, u32[]{:S(2)}) collective-permute-start(bf16[2048]{0:T(1024)(128)(2,1)S(1)} %convert_element_type.183), channel_id=1, source_target_pairs={{0,384},{1,385},{2,386},{3,387},{4,388},{5,389},{6,390},{7,391},{8... | collective-permute-start | bytes 12296 | tf_op jit(solution)/shard_map/ppermute | solution.py:37
  56.0 14.0 %collective-permute-start.1 = (bf16[2048]{0:T(1024)(128)(2,1)S(1)}, bf16[2048]{0:T(1024)(128)(2,1)S(1)}, u32[]{:S(2)}, u32[]{:S(2)}) collective-permute-start(bf16[2048]{0:T(1024)(128)(2,1)S(1)} %convert_element_type.183), channel_id=1, source_target_pairs={{0,256},{128,384},{1,257},{129,385},{2,258},{130,386},{3,259},{131... | collective-permute-start | bytes 12296 | tf_op jit(solution)/shard_map/ppermute | solution.py:37
  57.3 12.7 %collective-permute-start = (bf16[2048]{0:T(1024)(128)(2,1)S(1)}, bf16[2048]{0:T(1024)(128)(2,1)S(1)}, u32[]{:S(2)}, u32[]{:S(2)}) collective-permute-start(bf16[2048]{0:T(1024)(128)(2,1)S(1)} %convert_element_type.183), channel_id=1, source_target_pairs={{0,128},{128,256},{256,384},{1,129},{129,257},{257,385},{2,130},{1... | collective-permute-start | bytes 12296 | tf_op jit(solution)/shard_map/ppermute | solution.py:37
  72.5 29.7 %all-to-all-start.1 = ((bf16[32,2,1024]{2,1,0:T(2,128)(2,1)}), bf16[32,2,1024]{2,1,0:T(2,128)(2,1)}, u32[]{:S(2)}, u32[]{:S(2)}) async-start(bf16[32,2,1024]{2,1,0:T(2,128)(2,1)} %reshape.546), calls=%async_computation.1 | async-start | bytes 262144 | tf_op jit(solution)/shard_map/all_to_all | solution.py:53
  85.1 1.9 copy-start.1
  87.7 26.5 %copy-start.3 = (bf16[512,4,128]{0,2,1:T(8,128)(2,1)S(1)}, bf16[512,4,128]{0,2,1:T(8,128)(2,1)}, u32[]{:S(2)}) copy-start(bf16[512,4,128]{0,2,1:T(8,128)(2,1)} %copy-done.2) | copy-start | bytes 1572868
  88.5 34.8 %collective-permute-start.12 = (bf16[128,1024]{1,0:T(8,128)(2,1)}, bf16[128,1024]{1,0:T(8,128)(2,1)}, u32[]{:S(2)}, u32[]{:S(2)}) collective-permute-start(bf16[128,1024]{1,0:T(8,128)(2,1)} %pad_maximum_fusion), channel_id=1, source_target_pairs={{4,0},{8,4},{12,8},{16,12},{20,16},{24,20},{28,24},{32,28},{36,32}... | collective-permute-start | bytes 786440 | tf_op jit(solution)/shard_map/ppermute | solution.py:60
  110.3 6.0 %copy-start.26 = (f32[128]{0:T(128)}, f32[128]{0:T(128)S(1)}, u32[]{:S(2)}) copy-start(f32[128]{0:T(128)S(1)} %get-tuple-element.24) | copy-start | bytes 1540
  110.3 6.0 %copy-start.27 = (f32[128]{0:T(128)}, f32[128]{0:T(128)S(1)}, u32[]{:S(2)}) copy-start(f32[128]{0:T(128)S(1)} %get-tuple-element.25) | copy-start | bytes 1540
  110.8 7.1 %collective-permute-start.3 = (f32[2,128]{1,0:T(2,128)}, f32[2,128]{1,0:T(2,128)}, u32[]{:S(2)}, u32[]{:S(2)}) collective-permute-start(f32[2,128]{1,0:T(2,128)} %pad_maximum_fusion.1), channel_id=1, source_target_pairs={{0,1},{1,0},{2,3},{3,2},{4,5},{5,4},{6,7},{7,6},{8,9},{9,8},{10,11... | collective-permute-start | bytes 3080 | tf_op jit(solution)/shard_map/ppermute | solution.py:166
  118.6 8.4 %collective-permute-start.4 = (f32[2,128]{1,0:T(2,128)S(1)}, f32[2,128]{1,0:T(2,128)S(1)}, u32[]{:S(2)}, u32[]{:S(2)}) collective-permute-start(f32[2,128]{1,0:T(2,128)S(1)} %fusion.78), channel_id=1, source_target_pairs={{0,2},{1,3},{2,0},{3,1},{4,6},{5,7},{6,4},{7,5},{8,10},{9,11},{10,... | collective-permute-start | bytes 3080 | tf_op jit(solution)/shard_map/ppermute | solution.py:166
  125.1 12.8 %collective-permute-start.13 = (bf16[128,1024]{1,0:T(8,128)(2,1)}, bf16[128,1024]{1,0:T(8,128)(2,1)}, u32[]{:S(2)}, u32[]{:S(2)}) collective-permute-start(bf16[128,1024]{1,0:T(8,128)(2,1)} %add_convert_fusion.2), channel_id=1, source_target_pairs={{4,0},{8,4},{12,8},{16,12},{20,16},{24,20},{28,24},{32,28},{36,32}... | collective-permute-start | bytes 786440 | tf_op jit(solution)/shard_map/ppermute | solution.py:60
  128.8 17.6 %copy-start.11 = (bf16[128,512]{1,0:T(8,128)(2,1)S(1)}, bf16[128,512]{1,0:T(8,128)(2,1)}, u32[]{:S(2)}) copy-start(bf16[128,512]{1,0:T(8,128)(2,1)} %param.12) | copy-start | bytes 393220
  130.1 16.6 %copy-start.9 = (bf16[128,512]{0,1:T(8,128)(2,1)S(1)}, bf16[128,512]{0,1:T(8,128)(2,1)}, u32[]{:S(2)}) copy-start(bf16[128,512]{0,1:T(8,128)(2,1)} %copy-done.8) | copy-start | bytes 393220
  133.8 32.5 %copy-start.21 = (bf16[128,512]{1,0:T(8,128)(2,1)S(1)}, bf16[128,512]{1,0:T(8,128)(2,1)}, u32[]{:S(2)}) copy-start(bf16[128,512]{1,0:T(8,128)(2,1)} %get-tuple-element.32) | copy-start | bytes 393220
  133.8 21.2 %all-to-all-start.2 = ((bf16[32,2,1024]{2,1,0:T(2,128)(2,1)}), bf16[32,2,1024]{2,1,0:T(2,128)(2,1)S(1)}, u32[]{:S(2)}, u32[]{:S(2)}) async-start(bf16[32,2,1024]{2,1,0:T(2,128)(2,1)} %reshape.548), calls=%async_computation.2 | async-start | bytes 262144 | tf_op jit(solution)/shard_map/all_to_all | solution.py:47
  139.7 26.7 %collective-permute-start.14 = (bf16[128,1024]{1,0:T(8,128)(2,1)}, bf16[128,1024]{1,0:T(8,128)(2,1)}, u32[]{:S(2)}, u32[]{:S(2)}) collective-permute-start(bf16[128,1024]{1,0:T(8,128)(2,1)} %add_convert_fusion.1), channel_id=1, source_target_pairs={{4,0},{8,4},{12,8},{16,12},{20,16},{24,20},{28,24},{32,28},{36,32}... | collective-permute-start | bytes 786440 | tf_op jit(solution)/shard_map/ppermute | solution.py:60
  155.1 23.7 %copy-start.7 = (bf16[4,128,128]{2,1,0:T(8,128)(2,1)S(1)}, bf16[4,128,128]{2,1,0:T(8,128)(2,1)}, u32[]{:S(2)}) copy-start(bf16[4,128,128]{2,1,0:T(8,128)(2,1)} %reshape.495) | copy-start | bytes 393220
  155.4 14.8 %collective-permute-start.7 = (bf16[2048]{0:T(1024)(128)(2,1)S(1)}, bf16[2048]{0:T(1024)(128)(2,1)S(1)}, u32[]{:S(2)}, u32[]{:S(2)}) collective-permute-start(bf16[2048]{0:T(1024)(128)(2,1)S(1)} %convert_element_type.195), channel_id=1, source_target_pairs={{384,0},{385,1},{386,2},{387,3},{388,4},{389,5},{390,6},{391,7},{3... | collective-permute-start | bytes 12296 | tf_op jit(solution)/shard_map/ppermute | solution.py:37
  162.3 7.9 %collective-permute-start.6 = (bf16[2048]{0:T(1024)(128)(2,1)S(1)}, bf16[2048]{0:T(1024)(128)(2,1)S(1)}, u32[]{:S(2)}, u32[]{:S(2)}) collective-permute-start(bf16[2048]{0:T(1024)(128)(2,1)S(1)} %convert_element_type.195), channel_id=1, source_target_pairs={{256,0},{384,128},{257,1},{385,129},{258,2},{386,130},{259,3},{387... | collective-permute-start | bytes 12296 | tf_op jit(solution)/shard_map/ppermute | solution.py:37
  163.6 6.6 %collective-permute-start.5 = (bf16[2048]{0:T(1024)(128)(2,1)S(1)}, bf16[2048]{0:T(1024)(128)(2,1)S(1)}, u32[]{:S(2)}, u32[]{:S(2)}) collective-permute-start(bf16[2048]{0:T(1024)(128)(2,1)S(1)} %convert_element_type.195), channel_id=1, source_target_pairs={{128,0},{256,128},{384,256},{129,1},{257,129},{385,257},{130,2},{2... | collective-permute-start | bytes 12296 | tf_op jit(solution)/shard_map/ppermute | solution.py:37
  168.1 12.6 %copy-start.20 = (bf16[4,128,128]{2,1,0:T(8,128)(2,1)S(1)}, bf16[4,128,128]{2,1,0:T(8,128)(2,1)}, u32[]{:S(2)}) copy-start(bf16[4,128,128]{2,1,0:T(8,128)(2,1)} %copy-done.19) | copy-start | bytes 393220
  168.1 13.5 %collective-permute-start.15 = (bf16[128,1024]{1,0:T(8,128)(2,1)}, bf16[128,1024]{1,0:T(8,128)(2,1)}, u32[]{:S(2)}, u32[]{:S(2)}) collective-permute-start(bf16[128,1024]{1,0:T(8,128)(2,1)} %add_convert_fusion), channel_id=1, source_target_pairs={{4,0},{8,4},{12,8},{16,12},{20,16},{24,20},{28,24},{32,28},{36,32}... | collective-permute-start | bytes 786440 | tf_op jit(solution)/shard_map/ppermute | solution.py:60
  174.2 21.7 %all-to-all-start.3 = ((bf16[32,2,1024]{2,1,0:T(2,128)(2,1)}), bf16[32,2,1024]{2,1,0:T(2,128)(2,1)}, u32[]{:S(2)}, u32[]{:S(2)}) async-start(bf16[32,2,1024]{2,1,0:T(2,128)(2,1)} %reshape.550), calls=%async_computation.3 | async-start | bytes 262144 | tf_op jit(solution)/shard_map/all_to_all | solution.py:53
  182.6 15.8 %copy-start.12 = (f32[4,128,128]{2,1,0:T(8,128)S(1)}, f32[4,128,128]{2,1,0:T(8,128)}, u32[]{:S(2)}) copy-start(f32[4,128,128]{2,1,0:T(8,128)} %fusion.84) | copy-start | bytes 786436
  182.6 15.8 %copy-start.14 = (bf16[128,512]{1,0:T(8,128)(2,1)S(1)}, bf16[128,512]{1,0:T(8,128)(2,1)}, u32[]{:S(2)}) copy-start(bf16[128,512]{1,0:T(8,128)(2,1)} %param.11) | copy-start | bytes 393220
  183.4 16.0 %copy-start.6 = (bf16[128,512]{1,0:T(8,128)(2,1)S(1)}, bf16[128,512]{1,0:T(8,128)(2,1)}, u32[]{:S(2)}) copy-start(bf16[128,512]{1,0:T(8,128)(2,1)} %param.10) | copy-start | bytes 393220
  183.4 16.0 %copy-start.16 = (bf16[4,128,128]{2,1,0:T(8,128)(2,1)S(1)}, bf16[4,128,128]{2,1,0:T(8,128)(2,1)}, u32[]{:S(2)}) copy-start(bf16[4,128,128]{2,1,0:T(8,128)(2,1)} %copy-done.15) | copy-start | bytes 393220
  (3 other events, 4.1 us)

commit v18 on v11

--- a/solution.py
+++ b/solution.py
@@ -13,8 +13,8 @@
 
 
 CTX = ("outer", "inner")
-INNER = 8
-PLAN = (4, 4)
+INNER = 32
+PLAN = (4,)
 
 
 def scan_over(total, axis, backward):

time: 187 us -> 177 us (0.947)
  starting transfers between devices: 93.7 us -> 77.4 us
  waiting for transfers between devices: 25.7 us -> 34.4 us
  other arithmetic: 25.7 us -> 23.4 us
    ppermute x12 -> x6, starting transfers between devices: 46.9 us -> 9.74 us  [scan_over(): arrived.append(lax.ppermute(total.astype(jnp.bfloat16), axis, pairs))]
    all_to_all x2, starting transfers between devices: 10.1 us -> 22.6 us  [carried_in(): mine = lax.all_to_all(slices, 'inner', 0, 0, tiled=True).astype(jnp.float32)]
    all_to_all x2, waiting for transfers between devices: 2.95 us -> 13.8 us  [carried_in(): mine = lax.all_to_all(slices, 'inner', 0, 0, tiled=True).astype(jnp.float32)]
    ppermute x12 -> x6, waiting for transfers between devices: 12.5 us -> 4.4 us  [scan_over(): arrived.append(lax.ppermute(total.astype(jnp.bfloat16), axis, pairs))]
    all_to_all x2, starting transfers between devices: 7.37 us -> 14.2 us  [carried_in(): back = lax.all_to_all(states, 'inner', 0, 0, tiled=True)]
    ppermute x8, waiting for transfers between devices: 8.59 us -> 11.3 us  [from_behind(): return lax.ppermute(shard, axis, pairs)]
    unnamed x78 -> x70, local copies, waits for them, and re-layouts: 13.4 us -> 12.4 us
  transfers between devices with their start and end apart: 25 -> 19, of which waited for: 8 -> 7; matrix products, arithmetic and copies ran while one was open for 30% -> 31% of each run, Pallas kernels for 0% -> 0%
where the time goes in v18:
time: 177 us; the launch traced here: 175 us
  starting transfers between devices  77.4 us (44%)
  waiting for transfers between devices  34.4 us (19%)
  local copies, waits for them, and re-layouts  24.1 us (14%)
  other arithmetic  23.4 us (13%)
  matrix products  14.4 us (8%)
    ppermute x8, starting transfers between devices, from_behind(): return lax.ppermute(shard, axis, pairs)  26.6 us
    all_to_all x2, starting transfers between devices, carried_in(): mine = lax.all_to_all(slices, 'inner', 0, 0, tiled=True).astype(jnp.float32)  22.6 us
    all_to_all x2, starting transfers between devices, carried_in(): back = lax.all_to_all(states, 'inner', 0, 0, tiled=True)  14.2 us
    all_to_all x2, waiting for transfers between devices, carried_in(): mine = lax.all_to_all(slices, 'inner', 0, 0, tiled=True).astype(jnp.float32)  13.8 us
    unnamed x70, local copies, waits for them, and re-layouts  12.4 us
    ppermute x8, waiting for transfers between devices, from_behind(): return lax.ppermute(shard, axis, pairs)  11.3 us
    ppermute x6, starting transfers between devices, scan_over(): arrived.append(lax.ppermute(total.astype(jnp.bfloat16), axis, pairs))  9.74 us
    convert_element_type x4, other arithmetic, per_device(): owed = from_behind(owed.astype(jnp.bfloat16), CTX, -1).astype(jnp.float32)  6.4 us
  transfers between devices with their start and end apart: 19, of which 7 were waited for; matrix products, arithmetic and copies ran while one was open for 31% of the time, Pallas kernels for 0%

profile of v18, /device:TPU:24, one launch (start us, length us, event | category | flops | bytes accessed | tf_op | source)
XLA Modules:
  0.0 175.3 jit_solution(6825852592301979111)
XLA Ops:
  0.7 1.1 copy.280
  1.8 1.1 convolution_convert_fusion.2
  3.5 1.4 reduce.9
  5.6 15.5 %all-to-all-start = ((bf16[32,2,1024]{2,1,0:T(2,128)(2,1)}), bf16[32,2,1024]{2,1,0:T(2,128)(2,1)S(1)}, u32[]{:S(2)}, u32[]{:S(2)}) async-start(bf16[32,2,1024]{2,1,0:T(2,128)(2,1)} %reshape.545), calls=%async_computation | async-start | bytes 262144 | tf_op jit(solution)/shard_map/all_to_all | solution.py:47
  21.1 2.2 %collective-permute-start.6 = (bf16[128,1024]{1,0:T(8,128)(2,1)S(1)}, bf16[128,1024]{1,0:T(8,128)(2,1)S(1)}, u32[]{:S(2)}, u32[]{:S(2)}) collective-permute-start(bf16[128,1024]{1,0:T(8,128)(2,1)S(1)} %pad_maximum_fusion), channel_id=1, source_target_pairs={{0,4},{4,8},{8,12},{12,16},{16,20},{20,24},{24,28},{28,32},{32,36}... | collective-permute-start | bytes 786440 | tf_op jit(solution)/shard_map/ppermute | solution.py:60
  24.7 13.8 %all-to-all-done = bf16[32,2,1024]{2,1,0:T(2,128)(2,1)S(1)} async-done(((bf16[32,2,1024]{2,1,0:T(2,128)(2,1)}), bf16[32,2,1024]{2,1,0:T(2,128)(2,1)S(1)}, u32[]{:S(2)}, u32[]{:S(2)}) %all-to-all-start) | async-done | bytes 131104 | tf_op jit(solution)/shard_map/all_to_all | solution.py:47
  38.8 1.3 collective-permute-start.2
  40.1 1.3 collective-permute-start.1
  41.4 1.3 collective-permute-start
  42.8 2.8 %collective-permute-done.2 = bf16[2048]{0:T(1024)(128)(2,1)S(1)} collective-permute-done((bf16[2048]{0:T(1024)(128)(2,1)S(1)}, bf16[2048]{0:T(1024)(128)(2,1)S(1)}, u32[]{:S(2)}, u32[]{:S(2)}) %collective-permute-start.2) | collective-permute-done | bytes 4128 | tf_op jit(solution)/shard_map/ppermute | solution.py:37
  45.5 1.6 collective-permute-done.1
  47.6 1.4 reduce.10
  49.7 3.9 %all-to-all-start.1 = ((bf16[32,2,1024]{2,1,0:T(2,128)(2,1)}), bf16[32,2,1024]{2,1,0:T(2,128)(2,1)S(1)}, u32[]{:S(2)}, u32[]{:S(2)}) async-start(bf16[32,2,1024]{2,1,0:T(2,128)(2,1)} %reshape.547), calls=%async_computation.1 | async-start | bytes 262144 | tf_op jit(solution)/shard_map/all_to_all | solution.py:53
  53.7 2.1 %collective-permute-start.7 = (bf16[128,1024]{1,0:T(8,128)(2,1)S(1)}, bf16[128,1024]{1,0:T(8,128)(2,1)S(1)}, u32[]{:S(2)}, u32[]{:S(2)}) collective-permute-start(bf16[128,1024]{1,0:T(8,128)(2,1)S(1)} %collective-permute-done.6), channel_id=1, source_target_pairs={{0,4},{4,8},{8,12},{12,16},{16,20},{20,24},{24,28},{28,32},{32,36}... | collective-permute-start | bytes 786440 | tf_op jit(solution)/shard_map/ppermute | solution.py:60
  56.1 11.1 %collective-permute-done.7 = bf16[128,1024]{1,0:T(8,128)(2,1)S(1)} collective-permute-done((bf16[128,1024]{1,0:T(8,128)(2,1)S(1)}, bf16[128,1024]{1,0:T(8,128)(2,1)S(1)}, u32[]{:S(2)}, u32[]{:S(2)}) %collective-permute-start.7) | collective-permute-done | bytes 262176 | tf_op jit(solution)/shard_map/ppermute | solution.py:60
  67.2 1.9 %collective-permute-start.8 = (bf16[128,1024]{1,0:T(8,128)(2,1)S(1)}, bf16[128,1024]{1,0:T(8,128)(2,1)S(1)}, u32[]{:S(2)}, u32[]{:S(2)}) collective-permute-start(bf16[128,1024]{1,0:T(8,128)(2,1)S(1)} %collective-permute-done.7), channel_id=1, source_target_pairs={{0,4},{4,8},{8,12},{12,16},{16,20},{20,24},{24,28},{28,32},{32,36}... | collective-permute-start | bytes 786440 | tf_op jit(solution)/shard_map/ppermute | solution.py:60
  69.1 1.8 %all-to-all-done.1 = bf16[32,2,1024]{2,1,0:T(2,128)(2,1)S(1)} async-done(((bf16[32,2,1024]{2,1,0:T(2,128)(2,1)}), bf16[32,2,1024]{2,1,0:T(2,128)(2,1)S(1)}, u32[]{:S(2)}, u32[]{:S(2)}) %all-to-all-start.1) | async-done | bytes 131104 | tf_op jit(solution)/shard_map/all_to_all | solution.py:53
  72.7 4.3 %all-to-all-start.2 = ((f32[4,2,128]{2,1,0:T(2,128)}), f32[4,2,128]{2,1,0:T(2,128)S(1)}, u32[]{:S(2)}, u32[]{:S(2)}) async-start(f32[4,2,128]{2,1,0:T(2,128)} %broadcast_in_dim.75), calls=%async_computation.2 | async-start | bytes 8192 | tf_op jit(solution)/shard_map/all_to_all | solution.py:165
  77.2 1.9 %collective-permute-start.9 = (bf16[128,1024]{1,0:T(8,128)(2,1)S(1)}, bf16[128,1024]{1,0:T(8,128)(2,1)}, u32[]{:S(2)}, u32[]{:S(2)}) collective-permute-start(bf16[128,1024]{1,0:T(8,128)(2,1)S(1)} %collective-permute-done.8), channel_id=1, source_target_pairs={{0,4},{4,8},{8,12},{12,16},{16,20},{20,24},{24,28},{28,32},{32,36}... | collective-permute-start | bytes 786440 | tf_op jit(solution)/shard_map/ppermute | solution.py:60
  79.1 3.2 %all-to-all-done.2 = f32[4,2,128]{2,1,0:T(2,128)S(1)} async-done(((f32[4,2,128]{2,1,0:T(2,128)}), f32[4,2,128]{2,1,0:T(2,128)S(1)}, u32[]{:S(2)}, u32[]{:S(2)}) %all-to-all-start.2) | async-done | bytes 4128 | tf_op jit(solution)/shard_map/all_to_all | solution.py:165
  83.5 1.4 reduce.11
  85.6 7.1 %all-to-all-start.3 = ((bf16[32,2,1024]{2,1,0:T(2,128)(2,1)}), bf16[32,2,1024]{2,1,0:T(2,128)(2,1)}, u32[]{:S(2)}, u32[]{:S(2)}) async-start(bf16[32,2,1024]{2,1,0:T(2,128)(2,1)} %reshape.549), calls=%async_computation.3 | async-start | bytes 262144 | tf_op jit(solution)/shard_map/all_to_all | solution.py:47
  98.8 1.5 fusion.80
  100.3 1.6 convolution_bitcast_fusion
  104.7 1.4 reshape.529
  106.2 1.2 scatter_fusion.1
  108.4 2.3 %scatter_fusion = f32[5,128,512]{2,1,0:T(8,128)S(1)} fusion(f32[5,128,512]{2,1,0:T(8,128)S(1)} %broadcast.250.clone.1, s32[4]{0:T(128)S(1)} %fusion.68, f32[4,128,512]{2,1,0:T(8,128)} %reshape.529), kind=kCustom, calls=%fused_computation.2 | custom fusion | flops 262144 | bytes 3145744 | tf_op jit(solution)/shard_map/scatter-add | solution.py:122
  112.3 5.8 %collective-permute-start.10 = (bf16[128,1024]{1,0:T(8,128)(2,1)}, bf16[128,1024]{1,0:T(8,128)(2,1)}, u32[]{:S(2)}, u32[]{:S(2)}) collective-permute-start(bf16[128,1024]{1,0:T(8,128)(2,1)} %pad_maximum_fusion.1), channel_id=1, source_target_pairs={{4,0},{8,4},{12,8},{16,12},{20,16},{24,20},{28,24},{32,28},{36,32}... | collective-permute-start | bytes 786440 | tf_op jit(solution)/shard_map/ppermute | solution.py:60
  119.0 1.4 reshape.550
  120.6 1.3 collective-permute-start.5
  121.9 3.1 %collective-permute-start.4 = (bf16[2048]{0:T(1024)(128)(2,1)S(1)}, bf16[2048]{0:T(1024)(128)(2,1)S(1)}, u32[]{:S(2)}, u32[]{:S(2)}) collective-permute-start(bf16[2048]{0:T(1024)(128)(2,1)S(1)} %convert_element_type.195), channel_id=1, source_target_pairs={{256,0},{384,128},{257,1},{385,129},{258,2},{386,130},{259,3},{387... | collective-permute-start | bytes 12296 | tf_op jit(solution)/shard_map/ppermute | solution.py:37
  125.0 1.5 collective-permute-start.3
  126.5 1.8 %add_convert_fusion.2 = bf16[128,1024]{1,0:T(8,128)(2,1)} fusion(bf16[128,1024]{1,0:T(8,128)(2,1)} %collective-permute-done.10, bf16[128,512]{1,0:T(8,128)(2,1)} %get-tuple-element.46, bf16[128,512]{1,0:T(8,128)(2,1)} %get-tuple-element.42), kind=kLoop, calls=%fused_computation.43 | loop fusion | flops 917504 | bytes 786432 | tf_op jit(solution)/shard_map/convert_element_type | solution.py:219
  128.4 2.4 %collective-permute-start.11 = (bf16[128,1024]{1,0:T(8,128)(2,1)}, bf16[128,1024]{1,0:T(8,128)(2,1)}, u32[]{:S(2)}, u32[]{:S(2)}) collective-permute-start(bf16[128,1024]{1,0:T(8,128)(2,1)} %add_convert_fusion.2), channel_id=1, source_target_pairs={{4,0},{8,4},{12,8},{16,12},{20,16},{24,20},{28,24},{32,28},{36,32}... | collective-permute-start | bytes 786440 | tf_op jit(solution)/shard_map/ppermute | solution.py:60
  130.8 1.0 add_convert_fusion.3
  131.9 2.3 %reduce.12 = bf16[32,2048]{1,0:T(8,128)(2,1)S(1)} reduce(bf16[32,1,2048]{2,1,0:T(2,128)(2,1)} %add_convert_fusion.3, bf16[]{:T(256)} %broadcast.282), dimensions={1}, to_apply=%add_convert_fusion.3.reduce_sub_computation | reduce | bytes 262146 | tf_op jit(solution)/shard_map/jit(cumsum)/reduce_window_sum | solution.py:48
  134.9 10.4 %all-to-all-start.4 = ((bf16[32,2,1024]{2,1,0:T(2,128)(2,1)}), bf16[32,2,1024]{2,1,0:T(2,128)(2,1)}, u32[]{:S(2)}, u32[]{:S(2)}) async-start(bf16[32,2,1024]{2,1,0:T(2,128)(2,1)} %reshape.551), calls=%async_computation.4 | async-start | bytes 262144 | tf_op jit(solution)/shard_map/all_to_all | solution.py:53
  145.3 1.8 %add_convert_fusion.1 = bf16[128,1024]{1,0:T(8,128)(2,1)} fusion(bf16[128,1024]{1,0:T(8,128)(2,1)} %collective-permute-done.11, bf16[128,512]{1,0:T(8,128)(2,1)} %get-tuple-element.45, bf16[128,512]{1,0:T(8,128)(2,1)} %get-tuple-element.41), kind=kLoop, calls=%fused_computation.42 | loop fusion | flops 917504 | bytes 786432 | tf_op jit(solution)/shard_map/convert_element_type | solution.py:219
  147.1 4.3 %collective-permute-start.12 = (bf16[128,1024]{1,0:T(8,128)(2,1)}, bf16[128,1024]{1,0:T(8,128)(2,1)}, u32[]{:S(2)}, u32[]{:S(2)}) collective-permute-start(bf16[128,1024]{1,0:T(8,128)(2,1)} %add_convert_fusion.1), channel_id=1, source_target_pairs={{4,0},{8,4},{12,8},{16,12},{20,16},{24,20},{28,24},{32,28},{36,32}... | collective-permute-start | bytes 786440 | tf_op jit(solution)/shard_map/ppermute | solution.py:60
  151.4 1.8 %fusion.83 = f32[4,128,128]{2,1,0:T(8,128)} fusion(bf16[128,4,128]{0,2,1:T(8,128)(2,1)} %copy-done.2, bf16[4,128,128]{2,1,0:T(8,128)(2,1)} %copy-done.17), kind=kOutput, calls=%fused_computation.147 | convolution fusion | flops 16777216 | bytes 524288 | tf_op jit(solution)/shard_map/hts,thd->shd/dot_general | solution.py:188
  154.0 1.3 convolution_convert_fusion
  156.3 1.8 %add_convert_fusion = bf16[128,1024]{1,0:T(8,128)(2,1)} fusion(bf16[128,1024]{1,0:T(8,128)(2,1)} %collective-permute-done.12, bf16[128,512]{1,0:T(8,128)(2,1)S(1)} %copy-done.18, bf16[128,512]{1,0:T(8,128)(2,1)} %get-tuple-element.40), kind=kLoop, calls=%fused_computation.41 | loop fusion | flops 917504 | bytes 786432 | tf_op jit(solution)/shard_map/convert_element_type | solution.py:219
  158.1 6.0 %collective-permute-start.13 = (bf16[128,1024]{1,0:T(8,128)(2,1)}, bf16[128,1024]{1,0:T(8,128)(2,1)}, u32[]{:S(2)}, u32[]{:S(2)}) collective-permute-start(bf16[128,1024]{1,0:T(8,128)(2,1)} %add_convert_fusion), channel_id=1, source_target_pairs={{4,0},{8,4},{12,8},{16,12},{20,16},{24,20},{28,24},{32,28},{36,32}... | collective-permute-start | bytes 786440 | tf_op jit(solution)/shard_map/ppermute | solution.py:60
  164.1 1.4 reshape.552
  165.5 1.4 reduce.8
  167.9 1.8 %fusion.17 = bf16[4,128,128]{2,1,0:T(8,128)(2,1)} fusion(f32[4,128,128]{2,1,0:T(8,128)} %fusion.83, bf16[4,128,128]{2,1,0:T(8,128)(2,1)S(1)} %reshape.497, bf16[128,512]{1,0:T(8,128)(2,1)S(1)} %copy-done.12), kind=kOutput, calls=%fused_computation.35 | convolution fusion | flops 16908288 | bytes 655360 | tf_op jit(solution)/shard_map/shi,hij->shj/dot_general | solution.py:190
  169.9 1.7 copy.196
  171.6 1.1 fusion.14
  (145 shorter events, 27.2 us)
Async XLA Ops:
  0.6 98.1 %copy-start = (bf16[128,512]{1,0:T(8,128)(2,1)S(1)}, bf16[128,512]{1,0:T(8,128)(2,1)}, u32[]{:S(2)}) copy-start(bf16[128,512]{1,0:T(8,128)(2,1)} %param.15) | copy-start | bytes 393220
  0.6 23.8 %copy-start.11 = (bf16[128,512]{1,0:T(8,128)(2,1)S(1)}, bf16[128,512]{1,0:T(8,128)(2,1)}, u32[]{:S(2)}) copy-start(bf16[128,512]{1,0:T(8,128)(2,1)} %param.11) | copy-start | bytes 393220
  0.7 20.4 %copy-start.15 = (bf16[128,512]{1,0:T(8,128)(2,1)S(1)}, bf16[128,512]{1,0:T(8,128)(2,1)}, u32[]{:S(2)}) copy-start(bf16[128,512]{1,0:T(8,128)(2,1)} %param.17) | copy-start | bytes 393220
  0.7 20.4 %copy-start.16 = (bf16[128,512]{1,0:T(8,128)(2,1)S(1)}, bf16[128,512]{1,0:T(8,128)(2,1)}, u32[]{:S(2)}) copy-start(bf16[128,512]{1,0:T(8,128)(2,1)} %param.16) | copy-start | bytes 393220
  0.7 22.7 %copy-start.25 = (s32[1,3]{1,0:T(1,128)S(1)}, s32[1,3]{1,0:T(1,128)}, u32[]{:S(2)}) copy-start(s32[1,3]{1,0:T(1,128)} %param.19) | copy-start | bytes 40
  0.7 23.7 %copy-start.4 = (bf16[128,512]{1,0:T(8,128)(2,1)S(1)}, bf16[128,512]{1,0:T(8,128)(2,1)}, u32[]{:S(2)}) copy-start(bf16[128,512]{1,0:T(8,128)(2,1)} %param.10) | copy-start | bytes 393220
  5.6 32.9 %all-to-all-start = ((bf16[32,2,1024]{2,1,0:T(2,128)(2,1)}), bf16[32,2,1024]{2,1,0:T(2,128)(2,1)S(1)}, u32[]{:S(2)}, u32[]{:S(2)}) async-start(bf16[32,2,1024]{2,1,0:T(2,128)(2,1)} %reshape.545), calls=%async_computation | async-start | bytes 262144 | tf_op jit(solution)/shard_map/all_to_all | solution.py:47
  21.1 32.5 %collective-permute-start.6 = (bf16[128,1024]{1,0:T(8,128)(2,1)S(1)}, bf16[128,1024]{1,0:T(8,128)(2,1)S(1)}, u32[]{:S(2)}, u32[]{:S(2)}) collective-permute-start(bf16[128,1024]{1,0:T(8,128)(2,1)S(1)} %pad_maximum_fusion), channel_id=1, source_target_pairs={{0,4},{4,8},{8,12},{12,16},{16,20},{20,24},{24,28},{28,32},{32,36}... | collective-permute-start | bytes 786440 | tf_op jit(solution)/shard_map/ppermute | solution.py:60
  24.6 31.2 %copy-start.17 = (bf16[4,128,128]{2,1,0:T(8,128)(2,1)}, bf16[4,128,128]{2,1,0:T(8,128)(2,1)S(1)}, u32[]{:S(2)}) copy-start(bf16[4,128,128]{2,1,0:T(8,128)(2,1)S(1)} %fusion.15) | copy-start | bytes 393220
  24.7 31.1 %copy-start.20 = (bf16[128,512]{1,0:T(8,128)(2,1)S(1)}, bf16[128,512]{1,0:T(8,128)(2,1)}, u32[]{:S(2)}) copy-start(bf16[128,512]{1,0:T(8,128)(2,1)} %param.14) | copy-start | bytes 393220
  38.6 17.3 %copy-start.8 = (bf16[128,512]{1,0:T(8,128)(2,1)S(1)}, bf16[128,512]{1,0:T(8,128)(2,1)}, u32[]{:S(2)}) copy-start(bf16[128,512]{1,0:T(8,128)(2,1)} %param.12) | copy-start | bytes 393220
  38.8 6.7 %collective-permute-start.2 = (bf16[2048]{0:T(1024)(128)(2,1)S(1)}, bf16[2048]{0:T(1024)(128)(2,1)S(1)}, u32[]{:S(2)}, u32[]{:S(2)}) collective-permute-start(bf16[2048]{0:T(1024)(128)(2,1)S(1)} %convert_element_type.183), channel_id=1, source_target_pairs={{0,384},{1,385},{2,386},{3,387},{4,388},{5,389},{6,390},{7,391},{8... | collective-permute-start | bytes 12296 | tf_op jit(solution)/shard_map/ppermute | solution.py:37
  40.1 7.0 %collective-permute-start.1 = (bf16[2048]{0:T(1024)(128)(2,1)S(1)}, bf16[2048]{0:T(1024)(128)(2,1)S(1)}, u32[]{:S(2)}, u32[]{:S(2)}) collective-permute-start(bf16[2048]{0:T(1024)(128)(2,1)S(1)} %convert_element_type.183), channel_id=1, source_target_pairs={{0,256},{128,384},{1,257},{129,385},{2,258},{130,386},{3,259},{131... | collective-permute-start | bytes 12296 | tf_op jit(solution)/shard_map/ppermute | solution.py:37
  41.4 5.7 %collective-permute-start = (bf16[2048]{0:T(1024)(128)(2,1)S(1)}, bf16[2048]{0:T(1024)(128)(2,1)S(1)}, u32[]{:S(2)}, u32[]{:S(2)}) collective-permute-start(bf16[2048]{0:T(1024)(128)(2,1)S(1)} %convert_element_type.183), channel_id=1, source_target_pairs={{0,128},{128,256},{256,384},{1,129},{129,257},{257,385},{2,130},{1... | collective-permute-start | bytes 12296 | tf_op jit(solution)/shard_map/ppermute | solution.py:37
  48.9 22.9 %copy-start.24 = (f32[512]{0:T(512)S(1)}, f32[512]{0:T(512)}, u32[]{:S(2)}) copy-start(f32[512]{0:T(512)} %param.13) | copy-start | bytes 6148
  49.7 21.2 %all-to-all-start.1 = ((bf16[32,2,1024]{2,1,0:T(2,128)(2,1)}), bf16[32,2,1024]{2,1,0:T(2,128)(2,1)S(1)}, u32[]{:S(2)}, u32[]{:S(2)}) async-start(bf16[32,2,1024]{2,1,0:T(2,128)(2,1)} %reshape.547), calls=%async_computation.1 | async-start | bytes 262144 | tf_op jit(solution)/shard_map/all_to_all | solution.py:53
  53.7 13.5 %collective-permute-start.7 = (bf16[128,1024]{1,0:T(8,128)(2,1)S(1)}, bf16[128,1024]{1,0:T(8,128)(2,1)S(1)}, u32[]{:S(2)}, u32[]{:S(2)}) collective-permute-start(bf16[128,1024]{1,0:T(8,128)(2,1)S(1)} %collective-permute-done.6), channel_id=1, source_target_pairs={{0,4},{4,8},{8,12},{12,16},{16,20},{20,24},{24,28},{28,32},{32,36}... | collective-permute-start | bytes 786440 | tf_op jit(solution)/shard_map/ppermute | solution.py:60
  55.9 21.2 %copy-start.21 = (bf16[128,512]{1,0:T(8,128)(2,1)S(1)}, bf16[128,512]{1,0:T(8,128)(2,1)}, u32[]{:S(2)}) copy-start(bf16[128,512]{1,0:T(8,128)(2,1)} %param.18) | copy-start | bytes 393220
  67.2 10.0 %collective-permute-start.8 = (bf16[128,1024]{1,0:T(8,128)(2,1)S(1)}, bf16[128,1024]{1,0:T(8,128)(2,1)S(1)}, u32[]{:S(2)}, u32[]{:S(2)}) collective-permute-start(bf16[128,1024]{1,0:T(8,128)(2,1)S(1)} %collective-permute-done.7), channel_id=1, source_target_pairs={{0,4},{4,8},{8,12},{12,16},{16,20},{20,24},{24,28},{28,32},{32,36}... | collective-permute-start | bytes 786440 | tf_op jit(solution)/shard_map/ppermute | solution.py:60
  71.8 11.5 %copy-start.6 = (bf16[4,128,128]{2,1,0:T(8,128)(2,1)}, bf16[4,128,128]{2,1,0:T(8,128)(2,1)S(1)}, u32[]{:S(2)}) copy-start(bf16[4,128,128]{2,1,0:T(8,128)(2,1)S(1)} %reshape.496) | copy-start | bytes 393220
  72.7 9.6 %all-to-all-start.2 = ((f32[4,2,128]{2,1,0:T(2,128)}), f32[4,2,128]{2,1,0:T(2,128)S(1)}, u32[]{:S(2)}, u32[]{:S(2)}) async-start(f32[4,2,128]{2,1,0:T(2,128)} %broadcast_in_dim.75), calls=%async_computation.2 | async-start | bytes 8192 | tf_op jit(solution)/shard_map/all_to_all | solution.py:165
  77.2 8.4 %copy-start.19 = (bf16[128,1024]{1,0:T(8,128)(2,1)}, bf16[128,1024]{1,0:T(8,128)(2,1)S(1)}, u32[]{:S(2)}) copy-start(bf16[128,1024]{1,0:T(8,128)(2,1)S(1)} %collective-permute-done.8) | copy-start | bytes 786436
  77.2 16.5 %collective-permute-start.9 = (bf16[128,1024]{1,0:T(8,128)(2,1)S(1)}, bf16[128,1024]{1,0:T(8,128)(2,1)}, u32[]{:S(2)}, u32[]{:S(2)}) collective-permute-start(bf16[128,1024]{1,0:T(8,128)(2,1)S(1)} %collective-permute-done.8), channel_id=1, source_target_pairs={{0,4},{4,8},{8,12},{12,16},{16,20},{20,24},{24,28},{28,32},{32,36}... | collective-permute-start | bytes 786440 | tf_op jit(solution)/shard_map/ppermute | solution.py:60
  82.5 0.7 copy-start.2
  83.1 10.5 %copy-start.14 = (bf16[4,128,128]{2,1,0:T(8,128)(2,1)}, bf16[4,128,128]{2,1,0:T(8,128)(2,1)S(1)}, u32[]{:S(2)}) copy-start(bf16[4,128,128]{2,1,0:T(8,128)(2,1)S(1)} %fusion.16) | copy-start | bytes 393220
  85.6 33.4 %all-to-all-start.3 = ((bf16[32,2,1024]{2,1,0:T(2,128)(2,1)}), bf16[32,2,1024]{2,1,0:T(2,128)(2,1)}, u32[]{:S(2)}, u32[]{:S(2)}) async-start(bf16[32,2,1024]{2,1,0:T(2,128)(2,1)} %reshape.549), calls=%async_computation.3 | async-start | bytes 262144 | tf_op jit(solution)/shard_map/all_to_all | solution.py:47
  97.4 1.3 copy-start.23
  98.7 1.5 copy-start.22
  100.3 1.6 copy-start.26
  102.6 1.1 copy-start.1
  110.7 7.5 %copy-start.3 = (bf16[128,4,128]{0,2,1:T(8,128)(2,1)S(1)}, bf16[128,4,128]{0,2,1:T(8,128)(2,1)}, u32[]{:S(2)}) copy-start(bf16[128,4,128]{0,2,1:T(8,128)(2,1)} %copy-done.2) | copy-start | bytes 393220
  110.7 7.5 %copy-start.7 = (bf16[4,128,128]{2,1,0:T(8,128)(2,1)S(1)}, bf16[4,128,128]{2,1,0:T(8,128)(2,1)}, u32[]{:S(2)}) copy-start(bf16[4,128,128]{2,1,0:T(8,128)(2,1)} %copy-done.6) | copy-start | bytes 393220
  110.7 7.4 %copy-start.10 = (f32[128,4,128]{0,2,1:T(8,128)S(1)}, f32[128,4,128]{0,2,1:T(8,128)}, u32[]{:S(2)}) copy-start(f32[128,4,128]{0,2,1:T(8,128)} %convolution_bitcast_fusion.6) | copy-start | bytes 786436
  112.3 14.2 %collective-permute-start.10 = (bf16[128,1024]{1,0:T(8,128)(2,1)}, bf16[128,1024]{1,0:T(8,128)(2,1)}, u32[]{:S(2)}, u32[]{:S(2)}) collective-permute-start(bf16[128,1024]{1,0:T(8,128)(2,1)} %pad_maximum_fusion.1), channel_id=1, source_target_pairs={{4,0},{8,4},{12,8},{16,12},{20,16},{24,20},{28,24},{32,28},{36,32}... | collective-permute-start | bytes 786440 | tf_op jit(solution)/shard_map/ppermute | solution.py:60
  120.6 10.2 %collective-permute-start.5 = (bf16[2048]{0:T(1024)(128)(2,1)S(1)}, bf16[2048]{0:T(1024)(128)(2,1)S(1)}, u32[]{:S(2)}, u32[]{:S(2)}) collective-permute-start(bf16[2048]{0:T(1024)(128)(2,1)S(1)} %convert_element_type.195), channel_id=1, source_target_pairs={{384,0},{385,1},{386,2},{387,3},{388,4},{389,5},{390,6},{391,7},{3... | collective-permute-start | bytes 12296 | tf_op jit(solution)/shard_map/ppermute | solution.py:37
  121.9 8.9 %collective-permute-start.4 = (bf16[2048]{0:T(1024)(128)(2,1)S(1)}, bf16[2048]{0:T(1024)(128)(2,1)S(1)}, u32[]{:S(2)}, u32[]{:S(2)}) collective-permute-start(bf16[2048]{0:T(1024)(128)(2,1)S(1)} %convert_element_type.195), channel_id=1, source_target_pairs={{256,0},{384,128},{257,1},{385,129},{258,2},{386,130},{259,3},{387... | collective-permute-start | bytes 12296 | tf_op jit(solution)/shard_map/ppermute | solution.py:37
  125.0 5.8 %collective-permute-start.3 = (bf16[2048]{0:T(1024)(128)(2,1)S(1)}, bf16[2048]{0:T(1024)(128)(2,1)S(1)}, u32[]{:S(2)}, u32[]{:S(2)}) collective-permute-start(bf16[2048]{0:T(1024)(128)(2,1)S(1)} %convert_element_type.195), channel_id=1, source_target_pairs={{128,0},{256,128},{384,256},{129,1},{257,129},{385,257},{130,2},{2... | collective-permute-start | bytes 12296 | tf_op jit(solution)/shard_map/ppermute | solution.py:37
  128.4 16.9 %collective-permute-start.11 = (bf16[128,1024]{1,0:T(8,128)(2,1)}, bf16[128,1024]{1,0:T(8,128)(2,1)}, u32[]{:S(2)}, u32[]{:S(2)}) collective-permute-start(bf16[128,1024]{1,0:T(8,128)(2,1)} %add_convert_fusion.2), channel_id=1, source_target_pairs={{4,0},{8,4},{12,8},{16,12},{20,16},{24,20},{28,24},{32,28},{36,32}... | collective-permute-start | bytes 786440 | tf_op jit(solution)/shard_map/ppermute | solution.py:60
  131.9 21.4 %copy-start.13 = (bf16[128,4,128]{0,2,1:T(8,128)(2,1)S(1)}, bf16[128,4,128]{0,2,1:T(8,128)(2,1)}, u32[]{:S(2)}) copy-start(bf16[128,4,128]{0,2,1:T(8,128)(2,1)} %fusion.13) | copy-start | bytes 393220
  134.9 29.2 %all-to-all-start.4 = ((bf16[32,2,1024]{2,1,0:T(2,128)(2,1)}), bf16[32,2,1024]{2,1,0:T(2,128)(2,1)}, u32[]{:S(2)}, u32[]{:S(2)}) async-start(bf16[32,2,1024]{2,1,0:T(2,128)(2,1)} %reshape.551), calls=%async_computation.4 | async-start | bytes 262144 | tf_op jit(solution)/shard_map/all_to_all | solution.py:53
  147.1 9.2 %copy-start.18 = (bf16[128,512]{1,0:T(8,128)(2,1)S(1)}, bf16[128,512]{1,0:T(8,128)(2,1)}, u32[]{:S(2)}) copy-start(bf16[128,512]{1,0:T(8,128)(2,1)} %get-tuple-element.44) | copy-start | bytes 393220
  147.1 9.2 %collective-permute-start.12 = (bf16[128,1024]{1,0:T(8,128)(2,1)}, bf16[128,1024]{1,0:T(8,128)(2,1)}, u32[]{:S(2)}, u32[]{:S(2)}) collective-permute-start(bf16[128,1024]{1,0:T(8,128)(2,1)} %add_convert_fusion.1), channel_id=1, source_target_pairs={{4,0},{8,4},{12,8},{16,12},{20,16},{24,20},{28,24},{32,28},{36,32}... | collective-permute-start | bytes 786440 | tf_op jit(solution)/shard_map/ppermute | solution.py:60
  155.4 12.5 %copy-start.12 = (bf16[128,512]{1,0:T(8,128)(2,1)S(1)}, bf16[128,512]{1,0:T(8,128)(2,1)}, u32[]{:S(2)}) copy-start(bf16[128,512]{1,0:T(8,128)(2,1)} %param.11) | copy-start | bytes 393220
  156.1 13.6 %copy-start.9 = (bf16[128,512]{1,0:T(8,128)(2,1)S(1)}, bf16[128,512]{1,0:T(8,128)(2,1)}, u32[]{:S(2)}) copy-start(bf16[128,512]{1,0:T(8,128)(2,1)} %param.12) | copy-start | bytes 393220
  158.1 13.5 %copy-start.5 = (bf16[128,512]{1,0:T(8,128)(2,1)S(1)}, bf16[128,512]{1,0:T(8,128)(2,1)}, u32[]{:S(2)}) copy-start(bf16[128,512]{1,0:T(8,128)(2,1)} %param.10) | copy-start | bytes 393220
  158.1 15.4 %collective-permute-start.13 = (bf16[128,1024]{1,0:T(8,128)(2,1)}, bf16[128,1024]{1,0:T(8,128)(2,1)}, u32[]{:S(2)}, u32[]{:S(2)}) collective-permute-start(bf16[128,1024]{1,0:T(8,128)(2,1)} %add_convert_fusion), channel_id=1, source_target_pairs={{4,0},{8,4},{12,8},{16,12},{20,16},{24,20},{28,24},{32,28},{36,32}... | collective-permute-start | bytes 786440 | tf_op jit(solution)/shard_map/ppermute | solution.py:60

commit v19 on v16

--- a/solution.py
+++ b/solution.py
@@ -161,10 +161,8 @@
     cross_sum = jnp.sum(gain_grad * output_lin, axis=(1, 2))
     sums = jnp.stack([square_sum, cross_sum])
     heads_dev = lax.axis_size("head")
-    step = 1
-    while step < heads_dev:
-        sums = sums + lax.ppermute(sums, "head", [(i, i ^ step) for i in range(heads_dev)])
-        step *= 2
+    spread = jnp.broadcast_to(sums[None], (heads_dev,) + sums.shape)
+    sums = jnp.sum(lax.all_to_all(spread, "head", 0, 0, tiled=True), axis=0)
     square_sum, cross_sum = sums[0], sums[1]
     full_width = LIN_HEADS * HEAD
     inv_rms = lax.rsqrt(square_sum / full_width + 1e-06)[:, None, None]
@@ -195,7 +193,11 @@
     lin_dv = lin_dv.reshape(token_count, lin_width).astype(jnp.bfloat16)
     width = sm_key.shape[1]
     pair = jnp.concatenate([sm_key, sm_value], axis=1)
-    arrived = [from_behind(pair, CTX, distance) for distance in range(1, SPAN + 1)]
+    arrived = []
+    moving = pair
+    for distance in range(1, SPAN + 1):
+        moving = from_behind(moving, CTX, 1)
+        arrived.append(moving)
     key_window = jnp.concatenate(
         [arrived[SPAN - 1 - place][:, :width] for place in range(SPAN)] + [sm_key], axis=0
     )

time: 193 us -> 172 us (0.89)
  starting transfers between devices: 87.6 us -> 71.7 us
  local copies, waits for them, and re-layouts: 32.2 us -> 20.3 us
  waiting for transfers between devices: 32.8 us -> 44.4 us
  other arithmetic: 25.6 us -> 23.4 us
    ppermute x8, waiting for transfers between devices: 0.18 us -> 11.1 us  [from_behind(): return lax.ppermute(shard, axis, pairs)]
    all_to_all x2, starting transfers between devices: 19.3 us -> 9.19 us  [carried_in(): back = lax.all_to_all(states, 'inner', 0, 0, tiled=True)]
    ppermute x8, starting transfers between devices: 34.5 us -> 25.9 us  [from_behind(): return lax.ppermute(shard, axis, pairs)]
    all_to_all x2, starting transfers between devices: 14.3 us -> 22.6 us  [carried_in(): mine = lax.all_to_all(slices, 'inner', 0, 0, tiled=True).astype(jnp.float32)]
    ppermute x2 -> x0, starting transfers between devices: 8.04 us -> none  [per_device(): lax.ppermute(sums, 'head', [(i, i ^ step) for i in range(heads_dev)])]
    unnamed x81 -> x66, local copies, waits for them, and re-layouts: 15.1 us -> 9.61 us
    all_to_all x0 -> x1, starting transfers between devices: none -> 4.29 us  [per_device(): sums = jnp.sum(lax.all_to_all(spread, 'head', 0, 0, tiled=True), axis=0)]
    all_to_all x2, waiting for transfers between devices: 15.8 us -> 11.9 us  [carried_in(): back = lax.all_to_all(states, 'inner', 0, 0, tiled=True)]
  transfers between devices with their start and end apart: 20 -> 19, of which waited for: 7 -> 7; matrix products, arithmetic and copies ran while one was open for 27% -> 26% of each run, Pallas kernels for 0% -> 0%
where the time goes in v19:
time: 172 us; the launch traced here: 171 us
  starting transfers between devices  71.7 us (42%)
  waiting for transfers between devices  44.4 us (26%)
  other arithmetic  23.4 us (14%)
  local copies, waits for them, and re-layouts  20.3 us (12%)
  matrix products  9.52 us (6%)
    ppermute x8, starting transfers between devices, from_behind(): return lax.ppermute(shard, axis, pairs)  25.9 us
    all_to_all x2, starting transfers between devices, carried_in(): mine = lax.all_to_all(slices, 'inner', 0, 0, tiled=True).astype(jnp.float32)  22.6 us
    all_to_all x2, waiting for transfers between devices, carried_in(): mine = lax.all_to_all(slices, 'inner', 0, 0, tiled=True).astype(jnp.float32)  13.8 us
    all_to_all x2, waiting for transfers between devices, carried_in(): back = lax.all_to_all(states, 'inner', 0, 0, tiled=True)  11.9 us
    ppermute x8, waiting for transfers between devices, from_behind(): return lax.ppermute(shard, axis, pairs)  11.1 us
    ppermute x6, starting transfers between devices, scan_over(): arrived.append(lax.ppermute(total.astype(jnp.bfloat16), axis, pairs))  9.75 us
    unnamed x66, local copies, waits for them, and re-layouts  9.61 us
    all_to_all x2, starting transfers between devices, carried_in(): back = lax.all_to_all(states, 'inner', 0, 0, tiled=True)  9.19 us
  transfers between devices with their start and end apart: 19, of which 7 were waited for; matrix products, arithmetic and copies ran while one was open for 26% of the time, Pallas kernels for 0%

profile of v19, /device:TPU:24, one launch (start us, length us, event | category | flops | bytes accessed | tf_op | source)
XLA Modules:
  0.0 170.9 jit_solution(8622214713552927654)
XLA Ops:
  0.7 1.1 copy.280
  1.8 1.1 convolution_convert_fusion.2
  3.5 1.3 reduce.9
  5.5 15.5 %all-to-all-start = ((bf16[32,2,1024]{2,1,0:T(2,128)(2,1)}), bf16[32,2,1024]{2,1,0:T(2,128)(2,1)S(1)}, u32[]{:S(2)}, u32[]{:S(2)}) async-start(bf16[32,2,1024]{2,1,0:T(2,128)(2,1)} %reshape.545), calls=%async_computation | async-start | bytes 262144 | tf_op jit(solution)/shard_map/all_to_all | solution.py:47
  21.0 2.2 %collective-permute-start.6 = (bf16[128,1024]{1,0:T(8,128)(2,1)S(1)}, bf16[128,1024]{1,0:T(8,128)(2,1)S(1)}, u32[]{:S(2)}, u32[]{:S(2)}) collective-permute-start(bf16[128,1024]{1,0:T(8,128)(2,1)S(1)} %pad_maximum_fusion), channel_id=1, source_target_pairs={{0,4},{4,8},{8,12},{12,16},{16,20},{20,24},{24,28},{28,32},{32,36}... | collective-permute-start | bytes 786440 | tf_op jit(solution)/shard_map/ppermute | solution.py:60
  24.6 13.8 %all-to-all-done = bf16[32,2,1024]{2,1,0:T(2,128)(2,1)S(1)} async-done(((bf16[32,2,1024]{2,1,0:T(2,128)(2,1)}), bf16[32,2,1024]{2,1,0:T(2,128)(2,1)S(1)}, u32[]{:S(2)}, u32[]{:S(2)}) %all-to-all-start) | async-done | bytes 131104 | tf_op jit(solution)/shard_map/all_to_all | solution.py:47
  38.8 1.3 collective-permute-start.2
  40.1 1.3 collective-permute-start.1
  41.4 1.3 collective-permute-start
  42.7 2.8 %collective-permute-done.2 = bf16[2048]{0:T(1024)(128)(2,1)S(1)} collective-permute-done((bf16[2048]{0:T(1024)(128)(2,1)S(1)}, bf16[2048]{0:T(1024)(128)(2,1)S(1)}, u32[]{:S(2)}, u32[]{:S(2)}) %collective-permute-start.2) | collective-permute-done | bytes 4128 | tf_op jit(solution)/shard_map/ppermute | solution.py:37
  45.5 1.6 collective-permute-done.1
  47.5 1.3 reduce.10
  49.5 3.9 %all-to-all-start.1 = ((bf16[32,2,1024]{2,1,0:T(2,128)(2,1)}), bf16[32,2,1024]{2,1,0:T(2,128)(2,1)S(1)}, u32[]{:S(2)}, u32[]{:S(2)}) async-start(bf16[32,2,1024]{2,1,0:T(2,128)(2,1)} %reshape.547), calls=%async_computation.1 | async-start | bytes 262144 | tf_op jit(solution)/shard_map/all_to_all | solution.py:53
  53.5 2.1 %collective-permute-start.7 = (bf16[128,1024]{1,0:T(8,128)(2,1)S(1)}, bf16[128,1024]{1,0:T(8,128)(2,1)S(1)}, u32[]{:S(2)}, u32[]{:S(2)}) collective-permute-start(bf16[128,1024]{1,0:T(8,128)(2,1)S(1)} %collective-permute-done.6), channel_id=1, source_target_pairs={{0,4},{4,8},{8,12},{12,16},{16,20},{20,24},{24,28},{28,32},{32,36}... | collective-permute-start | bytes 786440 | tf_op jit(solution)/shard_map/ppermute | solution.py:60
  56.0 11.1 %collective-permute-done.7 = bf16[128,1024]{1,0:T(8,128)(2,1)S(1)} collective-permute-done((bf16[128,1024]{1,0:T(8,128)(2,1)S(1)}, bf16[128,1024]{1,0:T(8,128)(2,1)S(1)}, u32[]{:S(2)}, u32[]{:S(2)}) %collective-permute-start.7) | collective-permute-done | bytes 262176 | tf_op jit(solution)/shard_map/ppermute | solution.py:60
  67.0 1.9 %collective-permute-start.8 = (bf16[128,1024]{1,0:T(8,128)(2,1)S(1)}, bf16[128,1024]{1,0:T(8,128)(2,1)S(1)}, u32[]{:S(2)}, u32[]{:S(2)}) collective-permute-start(bf16[128,1024]{1,0:T(8,128)(2,1)S(1)} %collective-permute-done.7), channel_id=1, source_target_pairs={{0,4},{4,8},{8,12},{12,16},{16,20},{20,24},{24,28},{28,32},{32,36}... | collective-permute-start | bytes 786440 | tf_op jit(solution)/shard_map/ppermute | solution.py:60
  69.0 1.8 %all-to-all-done.1 = bf16[32,2,1024]{2,1,0:T(2,128)(2,1)S(1)} async-done(((bf16[32,2,1024]{2,1,0:T(2,128)(2,1)}), bf16[32,2,1024]{2,1,0:T(2,128)(2,1)S(1)}, u32[]{:S(2)}, u32[]{:S(2)}) %all-to-all-start.1) | async-done | bytes 131104 | tf_op jit(solution)/shard_map/all_to_all | solution.py:53
  72.6 4.3 %all-to-all-start.2 = ((f32[4,2,128]{2,1,0:T(2,128)}), f32[4,2,128]{2,1,0:T(2,128)S(1)}, u32[]{:S(2)}, u32[]{:S(2)}) async-start(f32[4,2,128]{2,1,0:T(2,128)} %broadcast_in_dim.75), calls=%async_computation.2 | async-start | bytes 8192 | tf_op jit(solution)/shard_map/all_to_all | solution.py:165
  77.1 1.9 %collective-permute-start.9 = (bf16[128,1024]{1,0:T(8,128)(2,1)S(1)}, bf16[128,1024]{1,0:T(8,128)(2,1)}, u32[]{:S(2)}, u32[]{:S(2)}) collective-permute-start(bf16[128,1024]{1,0:T(8,128)(2,1)S(1)} %collective-permute-done.8), channel_id=1, source_target_pairs={{0,4},{4,8},{8,12},{12,16},{16,20},{20,24},{24,28},{28,32},{32,36}... | collective-permute-start | bytes 786440 | tf_op jit(solution)/shard_map/ppermute | solution.py:60
  79.0 3.2 %all-to-all-done.2 = f32[4,2,128]{2,1,0:T(2,128)S(1)} async-done(((f32[4,2,128]{2,1,0:T(2,128)}), f32[4,2,128]{2,1,0:T(2,128)S(1)}, u32[]{:S(2)}, u32[]{:S(2)}) %all-to-all-start.2) | async-done | bytes 4128 | tf_op jit(solution)/shard_map/all_to_all | solution.py:165
  84.2 1.3 reduce.11
  86.3 7.1 %all-to-all-start.3 = ((bf16[32,2,1024]{2,1,0:T(2,128)(2,1)}), bf16[32,2,1024]{2,1,0:T(2,128)(2,1)}, u32[]{:S(2)}, u32[]{:S(2)}) async-start(bf16[32,2,1024]{2,1,0:T(2,128)(2,1)} %reshape.549), calls=%async_computation.3 | async-start | bytes 262144 | tf_op jit(solution)/shard_map/all_to_all | solution.py:47
  94.3 1.0 slice_dynamic-update-slice_fusion.3
  95.6 1.0 gather_fusion
  97.1 1.0 gather_fusion.1
  98.4 1.5 fusion.80
  99.9 1.6 convolution_bitcast_fusion
  104.9 1.4 reshape.529
  106.5 1.2 scatter_fusion.1
  108.6 2.3 %scatter_fusion = f32[5,128,512]{2,1,0:T(8,128)S(1)} fusion(f32[5,128,512]{2,1,0:T(8,128)S(1)} %broadcast.250.clone.1, s32[4]{0:T(128)S(1)} %fusion.68, f32[4,128,512]{2,1,0:T(8,128)} %reshape.529), kind=kCustom, calls=%fused_computation.2 | custom fusion | flops 262144 | bytes 3145744 | tf_op jit(solution)/shard_map/scatter-add | solution.py:122
  112.6 6.1 %collective-permute-start.11 = (bf16[128,1024]{1,0:T(8,128)(2,1)}, bf16[128,1024]{1,0:T(8,128)(2,1)}, u32[]{:S(2)}, u32[]{:S(2)}) collective-permute-start(bf16[128,1024]{1,0:T(8,128)(2,1)} %pad_maximum_fusion.2), channel_id=1, source_target_pairs={{8,0},{12,4},{16,8},{20,12},{24,16},{28,20},{32,24},{36,28},{40,32... | collective-permute-start | bytes 786440 | tf_op jit(solution)/shard_map/ppermute | solution.py:60
  119.4 3.7 %collective-permute-start.12 = (bf16[128,1024]{1,0:T(8,128)(2,1)}, bf16[128,1024]{1,0:T(8,128)(2,1)}, u32[]{:S(2)}, u32[]{:S(2)}) collective-permute-start(bf16[128,1024]{1,0:T(8,128)(2,1)} %pad_maximum_fusion.3), channel_id=1, source_target_pairs={{12,0},{16,4},{20,8},{24,12},{28,16},{32,20},{36,24},{40,28},{44,3... | collective-permute-start | bytes 786440 | tf_op jit(solution)/shard_map/ppermute | solution.py:60
  123.8 1.4 reshape.550
  125.4 1.3 collective-permute-start.5
  126.7 3.1 %collective-permute-start.4 = (bf16[2048]{0:T(1024)(128)(2,1)S(1)}, bf16[2048]{0:T(1024)(128)(2,1)S(1)}, u32[]{:S(2)}, u32[]{:S(2)}) collective-permute-start(bf16[2048]{0:T(1024)(128)(2,1)S(1)} %convert_element_type.175), channel_id=1, source_target_pairs={{256,0},{384,128},{257,1},{385,129},{258,2},{386,130},{259,3},{387... | collective-permute-start | bytes 12296 | tf_op jit(solution)/shard_map/ppermute | solution.py:37
  129.8 1.5 collective-permute-start.3
  131.3 1.7 pad_maximum_fusion.4
  133.0 5.9 %collective-permute-start.13 = (bf16[128,1024]{1,0:T(8,128)(2,1)}, bf16[128,1024]{1,0:T(8,128)(2,1)}, u32[]{:S(2)}, u32[]{:S(2)}) collective-permute-start(bf16[128,1024]{1,0:T(8,128)(2,1)} %pad_maximum_fusion.4), channel_id=1, source_target_pairs={{16,0},{20,4},{24,8},{28,12},{32,16},{36,20},{40,24},{44,28},{48,3... | collective-permute-start | bytes 786440 | tf_op jit(solution)/shard_map/ppermute | solution.py:60
  139.0 2.2 %collective-permute-start.10 = (bf16[128,1024]{1,0:T(8,128)(2,1)}, bf16[128,1024]{1,0:T(8,128)(2,1)}, u32[]{:S(2)}, u32[]{:S(2)}) collective-permute-start(bf16[128,1024]{1,0:T(8,128)(2,1)} %pad_maximum_fusion.1), channel_id=1, source_target_pairs={{4,0},{8,4},{12,8},{16,12},{20,16},{24,20},{28,24},{32,28},{36,32}... | collective-permute-start | bytes 786440 | tf_op jit(solution)/shard_map/ppermute | solution.py:60
  141.1 1.0 add_convert_fusion
  142.2 2.2 %reduce.12 = bf16[32,2048]{1,0:T(8,128)(2,1)S(1)} reduce(bf16[32,1,2048]{2,1,0:T(2,128)(2,1)} %add_convert_fusion, bf16[]{:T(256)} %broadcast.282), dimensions={1}, to_apply=%add_convert_fusion.reduce_sub_computation | reduce | bytes 262146 | tf_op jit(solution)/shard_map/jit(cumsum)/reduce_window_sum | solution.py:48
  145.1 5.3 %all-to-all-start.4 = ((bf16[32,2,1024]{2,1,0:T(2,128)(2,1)}), bf16[32,2,1024]{2,1,0:T(2,128)(2,1)S(1)}, u32[]{:S(2)}, u32[]{:S(2)}) async-start(bf16[32,2,1024]{2,1,0:T(2,128)(2,1)} %reshape.551), calls=%async_computation.4 | async-start | bytes 262144 | tf_op jit(solution)/shard_map/all_to_all | solution.py:53
  150.5 1.3 convolution_convert_fusion
  152.6 1.0 convert_element_type.194
  153.6 1.0 convert_element_type.195
  154.6 1.0 convert_element_type.196
  155.6 1.0 convert_element_type.193
  157.6 10.1 %all-to-all-done.4 = bf16[32,2,1024]{2,1,0:T(2,128)(2,1)S(1)} async-done(((bf16[32,2,1024]{2,1,0:T(2,128)(2,1)}), bf16[32,2,1024]{2,1,0:T(2,128)(2,1)S(1)}, u32[]{:S(2)}, u32[]{:S(2)}) %all-to-all-start.4) | async-done | bytes 131104 | tf_op jit(solution)/shard_map/all_to_all | solution.py:53
  (144 shorter events, 24.6 us)
Async XLA Ops:
  0.6 97.8 %copy-start = (bf16[128,512]{1,0:T(8,128)(2,1)S(1)}, bf16[128,512]{1,0:T(8,128)(2,1)}, u32[]{:S(2)}) copy-start(bf16[128,512]{1,0:T(8,128)(2,1)} %param.15) | copy-start | bytes 393220
  0.6 23.7 %copy-start.7 = (bf16[128,512]{1,0:T(8,128)(2,1)S(1)}, bf16[128,512]{1,0:T(8,128)(2,1)}, u32[]{:S(2)}) copy-start(bf16[128,512]{1,0:T(8,128)(2,1)} %param.11) | copy-start | bytes 393220
  0.7 20.3 %copy-start.11 = (bf16[128,512]{1,0:T(8,128)(2,1)S(1)}, bf16[128,512]{1,0:T(8,128)(2,1)}, u32[]{:S(2)}) copy-start(bf16[128,512]{1,0:T(8,128)(2,1)} %param.17) | copy-start | bytes 393220
  0.7 20.3 %copy-start.12 = (bf16[128,512]{1,0:T(8,128)(2,1)S(1)}, bf16[128,512]{1,0:T(8,128)(2,1)}, u32[]{:S(2)}) copy-start(bf16[128,512]{1,0:T(8,128)(2,1)} %param.16) | copy-start | bytes 393220
  0.7 22.6 %copy-start.23 = (s32[1,3]{1,0:T(1,128)S(1)}, s32[1,3]{1,0:T(1,128)}, u32[]{:S(2)}) copy-start(s32[1,3]{1,0:T(1,128)} %param.19) | copy-start | bytes 40
  0.7 23.7 %copy-start.2 = (bf16[128,512]{1,0:T(8,128)(2,1)S(1)}, bf16[128,512]{1,0:T(8,128)(2,1)}, u32[]{:S(2)}) copy-start(bf16[128,512]{1,0:T(8,128)(2,1)} %param.10) | copy-start | bytes 393220
  5.5 32.9 %all-to-all-start = ((bf16[32,2,1024]{2,1,0:T(2,128)(2,1)}), bf16[32,2,1024]{2,1,0:T(2,128)(2,1)S(1)}, u32[]{:S(2)}, u32[]{:S(2)}) async-start(bf16[32,2,1024]{2,1,0:T(2,128)(2,1)} %reshape.545), calls=%async_computation | async-start | bytes 262144 | tf_op jit(solution)/shard_map/all_to_all | solution.py:47
  21.0 32.5 %collective-permute-start.6 = (bf16[128,1024]{1,0:T(8,128)(2,1)S(1)}, bf16[128,1024]{1,0:T(8,128)(2,1)S(1)}, u32[]{:S(2)}, u32[]{:S(2)}) collective-permute-start(bf16[128,1024]{1,0:T(8,128)(2,1)S(1)} %pad_maximum_fusion), channel_id=1, source_target_pairs={{0,4},{4,8},{8,12},{12,16},{16,20},{20,24},{24,28},{28,32},{32,36}... | collective-permute-start | bytes 786440 | tf_op jit(solution)/shard_map/ppermute | solution.py:60
  24.6 31.0 %copy-start.18 = (bf16[128,512]{1,0:T(8,128)(2,1)S(1)}, bf16[128,512]{1,0:T(8,128)(2,1)}, u32[]{:S(2)}) copy-start(bf16[128,512]{1,0:T(8,128)(2,1)} %param.14) | copy-start | bytes 393220
  38.5 17.2 %copy-start.4 = (bf16[128,512]{1,0:T(8,128)(2,1)S(1)}, bf16[128,512]{1,0:T(8,128)(2,1)}, u32[]{:S(2)}) copy-start(bf16[128,512]{1,0:T(8,128)(2,1)} %param.12) | copy-start | bytes 393220
  38.8 6.7 %collective-permute-start.2 = (bf16[2048]{0:T(1024)(128)(2,1)S(1)}, bf16[2048]{0:T(1024)(128)(2,1)S(1)}, u32[]{:S(2)}, u32[]{:S(2)}) collective-permute-start(bf16[2048]{0:T(1024)(128)(2,1)S(1)} %convert_element_type.163), channel_id=1, source_target_pairs={{0,384},{1,385},{2,386},{3,387},{4,388},{5,389},{6,390},{7,391},{8... | collective-permute-start | bytes 12296 | tf_op jit(solution)/shard_map/ppermute | solution.py:37
  40.1 7.0 %collective-permute-start.1 = (bf16[2048]{0:T(1024)(128)(2,1)S(1)}, bf16[2048]{0:T(1024)(128)(2,1)S(1)}, u32[]{:S(2)}, u32[]{:S(2)}) collective-permute-start(bf16[2048]{0:T(1024)(128)(2,1)S(1)} %convert_element_type.163), channel_id=1, source_target_pairs={{0,256},{128,384},{1,257},{129,385},{2,258},{130,386},{3,259},{131... | collective-permute-start | bytes 12296 | tf_op jit(solution)/shard_map/ppermute | solution.py:37
  41.4 5.7 %collective-permute-start = (bf16[2048]{0:T(1024)(128)(2,1)S(1)}, bf16[2048]{0:T(1024)(128)(2,1)S(1)}, u32[]{:S(2)}, u32[]{:S(2)}) collective-permute-start(bf16[2048]{0:T(1024)(128)(2,1)S(1)} %convert_element_type.163), channel_id=1, source_target_pairs={{0,128},{128,256},{256,384},{1,129},{129,257},{257,385},{2,130},{1... | collective-permute-start | bytes 12296 | tf_op jit(solution)/shard_map/ppermute | solution.py:37
  48.8 22.9 %copy-start.22 = (f32[512]{0:T(512)S(1)}, f32[512]{0:T(512)}, u32[]{:S(2)}) copy-start(f32[512]{0:T(512)} %param.13) | copy-start | bytes 6148
  49.5 21.2 %all-to-all-start.1 = ((bf16[32,2,1024]{2,1,0:T(2,128)(2,1)}), bf16[32,2,1024]{2,1,0:T(2,128)(2,1)S(1)}, u32[]{:S(2)}, u32[]{:S(2)}) async-start(bf16[32,2,1024]{2,1,0:T(2,128)(2,1)} %reshape.547), calls=%async_computation.1 | async-start | bytes 262144 | tf_op jit(solution)/shard_map/all_to_all | solution.py:53
  53.5 13.5 %collective-permute-start.7 = (bf16[128,1024]{1,0:T(8,128)(2,1)S(1)}, bf16[128,1024]{1,0:T(8,128)(2,1)S(1)}, u32[]{:S(2)}, u32[]{:S(2)}) collective-permute-start(bf16[128,1024]{1,0:T(8,128)(2,1)S(1)} %collective-permute-done.6), channel_id=1, source_target_pairs={{0,4},{4,8},{8,12},{12,16},{16,20},{20,24},{24,28},{28,32},{32,36}... | collective-permute-start | bytes 786440 | tf_op jit(solution)/shard_map/ppermute | solution.py:60
  55.7 21.2 %copy-start.19 = (bf16[128,512]{1,0:T(8,128)(2,1)S(1)}, bf16[128,512]{1,0:T(8,128)(2,1)}, u32[]{:S(2)}) copy-start(bf16[128,512]{1,0:T(8,128)(2,1)} %param.18) | copy-start | bytes 393220
  67.0 15.3 %copy-start.14 = (bf16[128,1024]{1,0:T(8,128)(2,1)}, bf16[128,1024]{1,0:T(8,128)(2,1)S(1)}, u32[]{:S(2)}) copy-start(bf16[128,1024]{1,0:T(8,128)(2,1)S(1)} %collective-permute-done.7) | copy-start | bytes 786436
  67.0 10.0 %collective-permute-start.8 = (bf16[128,1024]{1,0:T(8,128)(2,1)S(1)}, bf16[128,1024]{1,0:T(8,128)(2,1)S(1)}, u32[]{:S(2)}, u32[]{:S(2)}) collective-permute-start(bf16[128,1024]{1,0:T(8,128)(2,1)S(1)} %collective-permute-done.7), channel_id=1, source_target_pairs={{0,4},{4,8},{8,12},{12,16},{16,20},{20,24},{24,28},{28,32},{32,36}... | collective-permute-start | bytes 786440 | tf_op jit(solution)/shard_map/ppermute | solution.py:60
  72.6 9.6 %all-to-all-start.2 = ((f32[4,2,128]{2,1,0:T(2,128)}), f32[4,2,128]{2,1,0:T(2,128)S(1)}, u32[]{:S(2)}, u32[]{:S(2)}) async-start(f32[4,2,128]{2,1,0:T(2,128)} %broadcast_in_dim.75), calls=%async_computation.2 | async-start | bytes 8192 | tf_op jit(solution)/shard_map/all_to_all | solution.py:165
  77.1 6.1 %copy-start.16 = (bf16[128,1024]{1,0:T(8,128)(2,1)}, bf16[128,1024]{1,0:T(8,128)(2,1)S(1)}, u32[]{:S(2)}) copy-start(bf16[128,1024]{1,0:T(8,128)(2,1)S(1)} %collective-permute-done.8) | copy-start | bytes 786436
  77.1 17.2 %collective-permute-start.9 = (bf16[128,1024]{1,0:T(8,128)(2,1)S(1)}, bf16[128,1024]{1,0:T(8,128)(2,1)}, u32[]{:S(2)}, u32[]{:S(2)}) collective-permute-start(bf16[128,1024]{1,0:T(8,128)(2,1)S(1)} %collective-permute-done.8), channel_id=1, source_target_pairs={{0,4},{4,8},{8,12},{12,16},{16,20},{20,24},{24,28},{28,32},{32,36}... | collective-permute-start | bytes 786440 | tf_op jit(solution)/shard_map/ppermute | solution.py:60
  82.6 0.7 copy-start.9
  84.0 11.3 %copy-start.17 = (bf16[128,1024]{1,0:T(8,128)(2,1)S(1)}, bf16[128,1024]{1,0:T(8,128)(2,1)}, u32[]{:S(2)}) copy-start(bf16[128,1024]{1,0:T(8,128)(2,1)} %copy-done.16) | copy-start | bytes 786436
  84.2 11.1 %copy-start.15 = (bf16[128,1024]{1,0:T(8,128)(2,1)S(1)}, bf16[128,1024]{1,0:T(8,128)(2,1)}, u32[]{:S(2)}) copy-start(bf16[128,1024]{1,0:T(8,128)(2,1)} %copy-done.14) | copy-start | bytes 786436
  86.3 37.5 %all-to-all-start.3 = ((bf16[32,2,1024]{2,1,0:T(2,128)(2,1)}), bf16[32,2,1024]{2,1,0:T(2,128)(2,1)}, u32[]{:S(2)}, u32[]{:S(2)}) async-start(bf16[32,2,1024]{2,1,0:T(2,128)(2,1)} %reshape.549), calls=%async_computation.3 | async-start | bytes 262144 | tf_op jit(solution)/shard_map/all_to_all | solution.py:47
  97.1 1.3 copy-start.21
  99.9 1.6 copy-start.24
  101.5 0.9 copy-start.20
  102.8 1.1 copy-start.1
  111.0 0.9 copy-start.13
  112.6 40.0 %collective-permute-start.11 = (bf16[128,1024]{1,0:T(8,128)(2,1)}, bf16[128,1024]{1,0:T(8,128)(2,1)}, u32[]{:S(2)}, u32[]{:S(2)}) collective-permute-start(bf16[128,1024]{1,0:T(8,128)(2,1)} %pad_maximum_fusion.2), channel_id=1, source_target_pairs={{8,0},{12,4},{16,8},{20,12},{24,16},{28,20},{32,24},{36,28},{40,32... | collective-permute-start | bytes 786440 | tf_op jit(solution)/shard_map/ppermute | solution.py:60
  119.4 34.2 %collective-permute-start.12 = (bf16[128,1024]{1,0:T(8,128)(2,1)}, bf16[128,1024]{1,0:T(8,128)(2,1)}, u32[]{:S(2)}, u32[]{:S(2)}) collective-permute-start(bf16[128,1024]{1,0:T(8,128)(2,1)} %pad_maximum_fusion.3), channel_id=1, source_target_pairs={{12,0},{16,4},{20,8},{24,12},{28,16},{32,20},{36,24},{40,28},{44,3... | collective-permute-start | bytes 786440 | tf_op jit(solution)/shard_map/ppermute | solution.py:60
  125.4 7.6 %collective-permute-start.5 = (bf16[2048]{0:T(1024)(128)(2,1)S(1)}, bf16[2048]{0:T(1024)(128)(2,1)S(1)}, u32[]{:S(2)}, u32[]{:S(2)}) collective-permute-start(bf16[2048]{0:T(1024)(128)(2,1)S(1)} %convert_element_type.175), channel_id=1, source_target_pairs={{384,0},{385,1},{386,2},{387,3},{388,4},{389,5},{390,6},{391,7},{3... | collective-permute-start | bytes 12296 | tf_op jit(solution)/shard_map/ppermute | solution.py:37
  126.7 12.2 %collective-permute-start.4 = (bf16[2048]{0:T(1024)(128)(2,1)S(1)}, bf16[2048]{0:T(1024)(128)(2,1)S(1)}, u32[]{:S(2)}, u32[]{:S(2)}) collective-permute-start(bf16[2048]{0:T(1024)(128)(2,1)S(1)} %convert_element_type.175), channel_id=1, source_target_pairs={{256,0},{384,128},{257,1},{385,129},{258,2},{386,130},{259,3},{387... | collective-permute-start | bytes 12296 | tf_op jit(solution)/shard_map/ppermute | solution.py:37
  129.8 11.3 %collective-permute-start.3 = (bf16[2048]{0:T(1024)(128)(2,1)S(1)}, bf16[2048]{0:T(1024)(128)(2,1)S(1)}, u32[]{:S(2)}, u32[]{:S(2)}) collective-permute-start(bf16[2048]{0:T(1024)(128)(2,1)S(1)} %convert_element_type.175), channel_id=1, source_target_pairs={{128,0},{256,128},{384,256},{129,1},{257,129},{385,257},{130,2},{2... | collective-permute-start | bytes 12296 | tf_op jit(solution)/shard_map/ppermute | solution.py:37
  133.0 21.6 %collective-permute-start.13 = (bf16[128,1024]{1,0:T(8,128)(2,1)}, bf16[128,1024]{1,0:T(8,128)(2,1)}, u32[]{:S(2)}, u32[]{:S(2)}) collective-permute-start(bf16[128,1024]{1,0:T(8,128)(2,1)} %pad_maximum_fusion.4), channel_id=1, source_target_pairs={{16,0},{20,4},{24,8},{28,12},{32,16},{36,20},{40,24},{44,28},{48,3... | collective-permute-start | bytes 786440 | tf_op jit(solution)/shard_map/ppermute | solution.py:60
  139.0 16.7 %collective-permute-start.10 = (bf16[128,1024]{1,0:T(8,128)(2,1)}, bf16[128,1024]{1,0:T(8,128)(2,1)}, u32[]{:S(2)}, u32[]{:S(2)}) collective-permute-start(bf16[128,1024]{1,0:T(8,128)(2,1)} %pad_maximum_fusion.1), channel_id=1, source_target_pairs={{4,0},{8,4},{12,8},{16,12},{20,16},{24,20},{28,24},{32,28},{36,32}... | collective-permute-start | bytes 786440 | tf_op jit(solution)/shard_map/ppermute | solution.py:60
  145.1 22.6 %all-to-all-start.4 = ((bf16[32,2,1024]{2,1,0:T(2,128)(2,1)}), bf16[32,2,1024]{2,1,0:T(2,128)(2,1)S(1)}, u32[]{:S(2)}, u32[]{:S(2)}) async-start(bf16[32,2,1024]{2,1,0:T(2,128)(2,1)} %reshape.551), calls=%async_computation.4 | async-start | bytes 262144 | tf_op jit(solution)/shard_map/all_to_all | solution.py:53
  156.6 12.0 %copy-start.5 = (bf16[128,512]{1,0:T(8,128)(2,1)S(1)}, bf16[128,512]{1,0:T(8,128)(2,1)}, u32[]{:S(2)}) copy-start(bf16[128,512]{1,0:T(8,128)(2,1)} %param.12) | copy-start | bytes 393220
  157.6 11.3 %copy-start.6 = (f32[4,128,128]{2,1,0:T(8,128)S(1)}, f32[4,128,128]{2,1,0:T(8,128)}, u32[]{:S(2)}) copy-start(f32[4,128,128]{2,1,0:T(8,128)} %fusion.83) | copy-start | bytes 786436
  157.6 11.3 %copy-start.8 = (bf16[128,512]{1,0:T(8,128)(2,1)S(1)}, bf16[128,512]{1,0:T(8,128)(2,1)}, u32[]{:S(2)}) copy-start(bf16[128,512]{1,0:T(8,128)(2,1)} %param.11) | copy-start | bytes 393220
  157.6 12.3 %copy-start.3 = (bf16[128,512]{1,0:T(8,128)(2,1)S(1)}, bf16[128,512]{1,0:T(8,128)(2,1)}, u32[]{:S(2)}) copy-start(bf16[128,512]{1,0:T(8,128)(2,1)} %param.10) | copy-start | bytes 393220
  157.6 12.3 %copy-start.10 = (bf16[4,128,128]{2,1,0:T(8,128)(2,1)S(1)}, bf16[4,128,128]{2,1,0:T(8,128)(2,1)}, u32[]{:S(2)}) copy-start(bf16[4,128,128]{2,1,0:T(8,128)(2,1)} %copy-done.9) | copy-start | bytes 393220

commit v20 on v19

--- a/solution.py
+++ b/solution.py
@@ -41,6 +41,17 @@
     return total - own
 
 
+def gathered_before(total, axis, backward):
+    count = lax.axis_size(axis)
+    sent = jnp.broadcast_to(total.astype(jnp.bfloat16)[None], (count,) + total.shape)
+    got = lax.all_to_all(sent, axis, 0, 0, tiled=True).astype(jnp.float32)
+    index = jnp.arange(count)
+    place = lax.axis_index(axis)
+    mask = index > place if backward else index < place
+    picked = jnp.where(mask.reshape((-1,) + (1,) * total.ndim), got, 0.0)
+    return jnp.sum(picked, axis=0)
+
+
 def carried_in(shard, backward):
     members = lax.axis_size("inner")
     slices = shard.astype(jnp.bfloat16).reshape(members, -1)
@@ -48,7 +59,7 @@
     running = jnp.cumsum(mine, axis=0)
     group = jnp.sum(mine, axis=0)
     within = group[None] - running if backward else running - mine
-    earlier = scan_over(group, "outer", backward)
+    earlier = gathered_before(group, "outer", backward)
     states = (within + earlier[None]).astype(jnp.bfloat16)
     back = lax.all_to_all(states, "inner", 0, 0, tiled=True)
     return back.reshape(shard.shape).astype(shard.dtype)

time: 172 us -> 180 us (1.047)
  the two profiles are of different devices: /device:TPU:24 before, /device:TPU:8 now
where the time goes in v20:
time: 180 us; the launch traced here: 179 us
  starting transfers between devices  72.8 us (40%)
  waiting for transfers between devices  43.8 us (24%)
  other arithmetic  26.9 us (15%)
  local copies, waits for them, and re-layouts  24.3 us (14%)
  matrix products  9.54 us (5%)
    ppermute x8, starting transfers between devices, from_behind(): return lax.ppermute(shard, axis, pairs)  25.3 us
    all_to_all x2, starting transfers between devices, carried_in(): mine = lax.all_to_all(slices, 'inner', 0, 0, tiled=True).astype(jnp.float32)  22.6 us
    all_to_all x2, waiting for transfers between devices, carried_in(): mine = lax.all_to_all(slices, 'inner', 0, 0, tiled=True).astype(jnp.float32)  13.8 us
    unnamed x70, local copies, waits for them, and re-layouts  12.9 us
    all_to_all x2, waiting for transfers between devices, carried_in(): back = lax.all_to_all(states, 'inner', 0, 0, tiled=True)  12.3 us
    all_to_all x2, starting transfers between devices, carried_in(): back = lax.all_to_all(states, 'inner', 0, 0, tiled=True)  11.8 us
    ppermute x8, waiting for transfers between devices, from_behind(): return lax.ppermute(shard, axis, pairs)  10.7 us
    all_to_all x2, starting transfers between devices, gathered_before(): got = lax.all_to_all(sent, axis, 0, 0, tiled=True).astype(jnp.float32)  8.81 us
  transfers between devices with their start and end apart: 15, of which 6 were waited for; matrix products, arithmetic and copies ran while one was open for 29% of the time, Pallas kernels for 0%

profile of v20, /device:TPU:8, one launch (start us, length us, event | category | flops | bytes accessed | tf_op | source)
XLA Modules:
  0.0 178.9 jit_solution(2178237670416054396)
XLA Ops:
  0.7 1.1 copy.286
  1.8 1.1 convolution_convert_fusion.2
  3.4 1.3 reduce.10
  5.5 15.5 %all-to-all-start = ((bf16[32,2,1024]{2,1,0:T(2,128)(2,1)}), bf16[32,2,1024]{2,1,0:T(2,128)(2,1)S(1)}, u32[]{:S(2)}, u32[]{:S(2)}) async-start(bf16[32,2,1024]{2,1,0:T(2,128)(2,1)} %reshape.575), calls=%async_computation | async-start | bytes 262144 | tf_op jit(solution)/shard_map/all_to_all | solution.py:58
  21.0 2.2 %collective-permute-start = (bf16[128,1024]{1,0:T(8,128)(2,1)S(1)}, bf16[128,1024]{1,0:T(8,128)(2,1)S(1)}, u32[]{:S(2)}, u32[]{:S(2)}) collective-permute-start(bf16[128,1024]{1,0:T(8,128)(2,1)S(1)} %pad_maximum_fusion), channel_id=1, source_target_pairs={{0,4},{4,8},{8,12},{12,16},{16,20},{20,24},{24,28},{28,32},{32,36}... | collective-permute-start | bytes 786440 | tf_op jit(solution)/shard_map/ppermute | solution.py:71
  23.4 0.9 fusion.32
  24.6 13.8 %all-to-all-done = bf16[32,2,1024]{2,1,0:T(2,128)(2,1)S(1)} async-done(((bf16[32,2,1024]{2,1,0:T(2,128)(2,1)}), bf16[32,2,1024]{2,1,0:T(2,128)(2,1)S(1)}, u32[]{:S(2)}, u32[]{:S(2)}) %all-to-all-start) | async-done | bytes 131104 | tf_op jit(solution)/shard_map/all_to_all | solution.py:58
  40.0 4.9 %all-to-all-start.1 = ((bf16[4,2,1024]{2,1,0:T(2,128)(2,1)}), bf16[4,2,1024]{2,1,0:T(2,128)(2,1)S(1)}, u32[]{:S(2)}, u32[]{:S(2)}) async-start(bf16[4,2,1024]{2,1,0:T(2,128)(2,1)} %reshape.577), calls=%async_computation.1 | async-start | bytes 32768 | tf_op jit(solution)/shard_map/all_to_all | solution.py:47
  44.9 3.9 %all-to-all-done.1 = bf16[4,2,1024]{2,1,0:T(2,128)(2,1)S(1)} async-done(((bf16[4,2,1024]{2,1,0:T(2,128)(2,1)}), bf16[4,2,1024]{2,1,0:T(2,128)(2,1)S(1)}, u32[]{:S(2)}, u32[]{:S(2)}) %all-to-all-start.1) | async-done | bytes 16416 | tf_op jit(solution)/shard_map/all_to_all | solution.py:47
  49.4 1.3 reduce.12
  51.4 3.9 %all-to-all-start.2 = ((bf16[32,2,1024]{2,1,0:T(2,128)(2,1)}), bf16[32,2,1024]{2,1,0:T(2,128)(2,1)S(1)}, u32[]{:S(2)}, u32[]{:S(2)}) async-start(bf16[32,2,1024]{2,1,0:T(2,128)(2,1)} %reshape.579), calls=%async_computation.2 | async-start | bytes 262144 | tf_op jit(solution)/shard_map/all_to_all | solution.py:64
  55.4 2.1 %collective-permute-start.1 = (bf16[128,1024]{1,0:T(8,128)(2,1)S(1)}, bf16[128,1024]{1,0:T(8,128)(2,1)S(1)}, u32[]{:S(2)}, u32[]{:S(2)}) collective-permute-start(bf16[128,1024]{1,0:T(8,128)(2,1)S(1)} %collective-permute-done), channel_id=1, source_target_pairs={{0,4},{4,8},{8,12},{12,16},{16,20},{20,24},{24,28},{28,32},{32,36}... | collective-permute-start | bytes 786440 | tf_op jit(solution)/shard_map/ppermute | solution.py:71
  57.8 10.7 %collective-permute-done.1 = bf16[128,1024]{1,0:T(8,128)(2,1)S(1)} collective-permute-done((bf16[128,1024]{1,0:T(8,128)(2,1)S(1)}, bf16[128,1024]{1,0:T(8,128)(2,1)S(1)}, u32[]{:S(2)}, u32[]{:S(2)}) %collective-permute-start.1) | collective-permute-done | bytes 262176 | tf_op jit(solution)/shard_map/ppermute | solution.py:71
  68.5 1.9 %collective-permute-start.2 = (bf16[128,1024]{1,0:T(8,128)(2,1)S(1)}, bf16[128,1024]{1,0:T(8,128)(2,1)S(1)}, u32[]{:S(2)}, u32[]{:S(2)}) collective-permute-start(bf16[128,1024]{1,0:T(8,128)(2,1)S(1)} %collective-permute-done.1), channel_id=1, source_target_pairs={{0,4},{4,8},{8,12},{12,16},{16,20},{20,24},{24,28},{28,32},{32,36}... | collective-permute-start | bytes 786440 | tf_op jit(solution)/shard_map/ppermute | solution.py:71
  70.4 2.2 %all-to-all-done.2 = bf16[32,2,1024]{2,1,0:T(2,128)(2,1)S(1)} async-done(((bf16[32,2,1024]{2,1,0:T(2,128)(2,1)}), bf16[32,2,1024]{2,1,0:T(2,128)(2,1)S(1)}, u32[]{:S(2)}, u32[]{:S(2)}) %all-to-all-start.2) | async-done | bytes 131104 | tf_op jit(solution)/shard_map/all_to_all | solution.py:64
  74.4 4.3 %all-to-all-start.3 = ((f32[4,2,128]{2,1,0:T(2,128)}), f32[4,2,128]{2,1,0:T(2,128)S(1)}, u32[]{:S(2)}, u32[]{:S(2)}) async-start(f32[4,2,128]{2,1,0:T(2,128)} %broadcast_in_dim.108), calls=%async_computation.3 | async-start | bytes 8192 | tf_op jit(solution)/shard_map/all_to_all | solution.py:176
  78.9 1.9 %collective-permute-start.3 = (bf16[128,1024]{1,0:T(8,128)(2,1)S(1)}, bf16[128,1024]{1,0:T(8,128)(2,1)}, u32[]{:S(2)}, u32[]{:S(2)}) collective-permute-start(bf16[128,1024]{1,0:T(8,128)(2,1)S(1)} %collective-permute-done.2), channel_id=1, source_target_pairs={{0,4},{4,8},{8,12},{12,16},{16,20},{20,24},{24,28},{28,32},{32,36}... | collective-permute-start | bytes 786440 | tf_op jit(solution)/shard_map/ppermute | solution.py:71
  80.9 3.2 %all-to-all-done.3 = f32[4,2,128]{2,1,0:T(2,128)S(1)} async-done(((f32[4,2,128]{2,1,0:T(2,128)}), f32[4,2,128]{2,1,0:T(2,128)S(1)}, u32[]{:S(2)}, u32[]{:S(2)}) %all-to-all-start.3) | async-done | bytes 4128 | tf_op jit(solution)/shard_map/all_to_all | solution.py:176
  86.1 1.3 reduce.13
  88.2 7.1 %all-to-all-start.4 = ((bf16[32,2,1024]{2,1,0:T(2,128)(2,1)}), bf16[32,2,1024]{2,1,0:T(2,128)(2,1)}, u32[]{:S(2)}, u32[]{:S(2)}) async-start(bf16[32,2,1024]{2,1,0:T(2,128)(2,1)} %reshape.581), calls=%async_computation.4 | async-start | bytes 262144 | tf_op jit(solution)/shard_map/all_to_all | solution.py:58
  96.2 1.0 slice_dynamic-update-slice_fusion.3
  97.5 1.0 gather_fusion
  98.9 1.0 gather_fusion.1
  100.3 1.5 fusion.82
  101.8 1.6 convolution_bitcast_fusion
  106.8 1.4 reshape.559
  108.4 1.2 scatter_fusion.1
  110.5 2.3 %scatter_fusion = f32[5,128,512]{2,1,0:T(8,128)S(1)} fusion(f32[5,128,512]{2,1,0:T(8,128)S(1)} %broadcast.265.clone.1, s32[4]{0:T(128)S(1)} %fusion.74, f32[4,128,512]{2,1,0:T(8,128)} %reshape.559), kind=kCustom, calls=%fused_computation.2 | custom fusion | flops 262144 | bytes 3145744 | tf_op jit(solution)/shard_map/scatter-add | solution.py:133
  114.5 5.6 %collective-permute-start.5 = (bf16[128,1024]{1,0:T(8,128)(2,1)}, bf16[128,1024]{1,0:T(8,128)(2,1)}, u32[]{:S(2)}, u32[]{:S(2)}) collective-permute-start(bf16[128,1024]{1,0:T(8,128)(2,1)} %pad_maximum_fusion.2), channel_id=1, source_target_pairs={{8,0},{12,4},{16,8},{20,12},{24,16},{28,20},{32,24},{36,28},{40,32... | collective-permute-start | bytes 786440 | tf_op jit(solution)/shard_map/ppermute | solution.py:71
  120.9 3.7 %collective-permute-start.6 = (bf16[128,1024]{1,0:T(8,128)(2,1)}, bf16[128,1024]{1,0:T(8,128)(2,1)}, u32[]{:S(2)}, u32[]{:S(2)}) collective-permute-start(bf16[128,1024]{1,0:T(8,128)(2,1)} %pad_maximum_fusion.3), channel_id=1, source_target_pairs={{12,0},{16,4},{20,8},{24,12},{28,16},{32,20},{36,24},{40,28},{44,3... | collective-permute-start | bytes 786440 | tf_op jit(solution)/shard_map/ppermute | solution.py:71
  125.3 5.4 %collective-permute-start.7 = (bf16[128,1024]{1,0:T(8,128)(2,1)}, bf16[128,1024]{1,0:T(8,128)(2,1)}, u32[]{:S(2)}, u32[]{:S(2)}) collective-permute-start(bf16[128,1024]{1,0:T(8,128)(2,1)} %pad_maximum_fusion.4), channel_id=1, source_target_pairs={{16,0},{20,4},{24,8},{28,12},{32,16},{36,20},{40,24},{44,28},{48,3... | collective-permute-start | bytes 786440 | tf_op jit(solution)/shard_map/ppermute | solution.py:71
  130.8 1.4 reshape.582
  133.0 2.0 %reduce.14 = bf16[4,2048]{1,0:T(4,128)(2,1)} reduce(bf16[4,1,2048]{2,1,0:T(2,128)(2,1)} %broadcast_in_dim.110, bf16[]{:T(256)} %broadcast.298), dimensions={1}, to_apply=%broadcast_in_dim.110.reduce_sub_computation | reduce | bytes 32770 | tf_op jit(solution)/shard_map/broadcast_in_dim | solution.py:46
  135.0 1.3 reshape.583
  136.4 3.9 %all-to-all-start.5 = ((bf16[4,2,1024]{2,1,0:T(2,128)(2,1)}), bf16[4,2,1024]{2,1,0:T(2,128)(2,1)}, u32[]{:S(2)}, u32[]{:S(2)}) async-start(bf16[4,2,1024]{2,1,0:T(2,128)(2,1)} %reshape.583), calls=%async_computation.5 | async-start | bytes 32768 | tf_op jit(solution)/shard_map/all_to_all | solution.py:47
  140.3 1.7 pad_maximum_fusion.1
  142.0 2.4 %collective-permute-start.4 = (bf16[128,1024]{1,0:T(8,128)(2,1)}, bf16[128,1024]{1,0:T(8,128)(2,1)}, u32[]{:S(2)}, u32[]{:S(2)}) collective-permute-start(bf16[128,1024]{1,0:T(8,128)(2,1)} %pad_maximum_fusion.1), channel_id=1, source_target_pairs={{4,0},{8,4},{12,8},{16,12},{20,16},{24,20},{28,24},{32,28},{36,32}... | collective-permute-start | bytes 786440 | tf_op jit(solution)/shard_map/ppermute | solution.py:71
  144.4 1.3 reshape.584
  146.6 1.0 add_convert_fusion
  147.6 2.2 %reduce.15 = bf16[32,2048]{1,0:T(8,128)(2,1)S(1)} reduce(bf16[32,1,2048]{2,1,0:T(2,128)(2,1)} %add_convert_fusion, bf16[]{:T(256)} %broadcast.298), dimensions={1}, to_apply=%add_convert_fusion.reduce_sub_computation | reduce | bytes 262146 | tf_op jit(solution)/shard_map/jit(cumsum)/reduce_window_sum | solution.py:59
  150.6 7.9 %all-to-all-start.6 = ((bf16[32,2,1024]{2,1,0:T(2,128)(2,1)}), bf16[32,2,1024]{2,1,0:T(2,128)(2,1)S(1)}, u32[]{:S(2)}, u32[]{:S(2)}) async-start(bf16[32,2,1024]{2,1,0:T(2,128)(2,1)} %reshape.585), calls=%async_computation.6 | async-start | bytes 262144 | tf_op jit(solution)/shard_map/all_to_all | solution.py:64
  158.5 1.3 convolution_convert_fusion
  160.6 1.0 convert_element_type.182
  161.6 1.0 convert_element_type.183
  162.6 1.0 convert_element_type.184
  163.6 1.0 convert_element_type.181
  164.7 0.9 fusion.21
  165.6 10.1 %all-to-all-done.6 = bf16[32,2,1024]{2,1,0:T(2,128)(2,1)S(1)} async-done(((bf16[32,2,1024]{2,1,0:T(2,128)(2,1)}), bf16[32,2,1024]{2,1,0:T(2,128)(2,1)S(1)}, u32[]{:S(2)}, u32[]{:S(2)}) %all-to-all-start.6) | async-done | bytes 131104 | tf_op jit(solution)/shard_map/all_to_all | solution.py:64
  (146 shorter events, 25.6 us)
Async XLA Ops:
  0.6 99.6 %copy-start = (bf16[128,512]{1,0:T(8,128)(2,1)S(1)}, bf16[128,512]{1,0:T(8,128)(2,1)}, u32[]{:S(2)}) copy-start(bf16[128,512]{1,0:T(8,128)(2,1)} %param.15) | copy-start | bytes 393220
  0.6 23.7 %copy-start.7 = (bf16[128,512]{1,0:T(8,128)(2,1)S(1)}, bf16[128,512]{1,0:T(8,128)(2,1)}, u32[]{:S(2)}) copy-start(bf16[128,512]{1,0:T(8,128)(2,1)} %param.11) | copy-start | bytes 393220
  0.7 20.3 %copy-start.11 = (bf16[128,512]{1,0:T(8,128)(2,1)S(1)}, bf16[128,512]{1,0:T(8,128)(2,1)}, u32[]{:S(2)}) copy-start(bf16[128,512]{1,0:T(8,128)(2,1)} %param.17) | copy-start | bytes 393220
  0.7 20.3 %copy-start.12 = (bf16[128,512]{1,0:T(8,128)(2,1)S(1)}, bf16[128,512]{1,0:T(8,128)(2,1)}, u32[]{:S(2)}) copy-start(bf16[128,512]{1,0:T(8,128)(2,1)} %param.16) | copy-start | bytes 393220
  0.7 22.5 %copy-start.23 = (s32[1,3]{1,0:T(1,128)S(1)}, s32[1,3]{1,0:T(1,128)}, u32[]{:S(2)}) copy-start(s32[1,3]{1,0:T(1,128)} %param.19) | copy-start | bytes 40
  0.7 23.7 %copy-start.2 = (bf16[128,512]{1,0:T(8,128)(2,1)S(1)}, bf16[128,512]{1,0:T(8,128)(2,1)}, u32[]{:S(2)}) copy-start(bf16[128,512]{1,0:T(8,128)(2,1)} %param.10) | copy-start | bytes 393220
  5.5 32.9 %all-to-all-start = ((bf16[32,2,1024]{2,1,0:T(2,128)(2,1)}), bf16[32,2,1024]{2,1,0:T(2,128)(2,1)S(1)}, u32[]{:S(2)}, u32[]{:S(2)}) async-start(bf16[32,2,1024]{2,1,0:T(2,128)(2,1)} %reshape.575), calls=%async_computation | async-start | bytes 262144 | tf_op jit(solution)/shard_map/all_to_all | solution.py:58
  21.0 34.4 %collective-permute-start = (bf16[128,1024]{1,0:T(8,128)(2,1)S(1)}, bf16[128,1024]{1,0:T(8,128)(2,1)S(1)}, u32[]{:S(2)}, u32[]{:S(2)}) collective-permute-start(bf16[128,1024]{1,0:T(8,128)(2,1)S(1)} %pad_maximum_fusion), channel_id=1, source_target_pairs={{0,4},{4,8},{8,12},{12,16},{16,20},{20,24},{24,28},{28,32},{32,36}... | collective-permute-start | bytes 786440 | tf_op jit(solution)/shard_map/ppermute | solution.py:71
  24.6 32.9 %copy-start.18 = (bf16[128,512]{1,0:T(8,128)(2,1)S(1)}, bf16[128,512]{1,0:T(8,128)(2,1)}, u32[]{:S(2)}) copy-start(bf16[128,512]{1,0:T(8,128)(2,1)} %param.14) | copy-start | bytes 393220
  38.5 19.1 %copy-start.4 = (bf16[128,512]{1,0:T(8,128)(2,1)S(1)}, bf16[128,512]{1,0:T(8,128)(2,1)}, u32[]{:S(2)}) copy-start(bf16[128,512]{1,0:T(8,128)(2,1)} %param.12) | copy-start | bytes 393220
  40.0 8.8 %all-to-all-start.1 = ((bf16[4,2,1024]{2,1,0:T(2,128)(2,1)}), bf16[4,2,1024]{2,1,0:T(2,128)(2,1)S(1)}, u32[]{:S(2)}, u32[]{:S(2)}) async-start(bf16[4,2,1024]{2,1,0:T(2,128)(2,1)} %reshape.577), calls=%async_computation.1 | async-start | bytes 32768 | tf_op jit(solution)/shard_map/all_to_all | solution.py:47
  50.7 22.9 %copy-start.22 = (f32[512]{0:T(512)S(1)}, f32[512]{0:T(512)}, u32[]{:S(2)}) copy-start(f32[512]{0:T(512)} %param.13) | copy-start | bytes 6148
  51.4 21.2 %all-to-all-start.2 = ((bf16[32,2,1024]{2,1,0:T(2,128)(2,1)}), bf16[32,2,1024]{2,1,0:T(2,128)(2,1)S(1)}, u32[]{:S(2)}, u32[]{:S(2)}) async-start(bf16[32,2,1024]{2,1,0:T(2,128)(2,1)} %reshape.579), calls=%async_computation.2 | async-start | bytes 262144 | tf_op jit(solution)/shard_map/all_to_all | solution.py:64
  55.4 13.1 %collective-permute-start.1 = (bf16[128,1024]{1,0:T(8,128)(2,1)S(1)}, bf16[128,1024]{1,0:T(8,128)(2,1)S(1)}, u32[]{:S(2)}, u32[]{:S(2)}) collective-permute-start(bf16[128,1024]{1,0:T(8,128)(2,1)S(1)} %collective-permute-done), channel_id=1, source_target_pairs={{0,4},{4,8},{8,12},{12,16},{16,20},{20,24},{24,28},{28,32},{32,36}... | collective-permute-start | bytes 786440 | tf_op jit(solution)/shard_map/ppermute | solution.py:71
  57.6 21.2 %copy-start.19 = (bf16[128,512]{1,0:T(8,128)(2,1)S(1)}, bf16[128,512]{1,0:T(8,128)(2,1)}, u32[]{:S(2)}) copy-start(bf16[128,512]{1,0:T(8,128)(2,1)} %param.18) | copy-start | bytes 393220
  68.5 15.7 %copy-start.14 = (bf16[128,1024]{1,0:T(8,128)(2,1)}, bf16[128,1024]{1,0:T(8,128)(2,1)S(1)}, u32[]{:S(2)}) copy-start(bf16[128,1024]{1,0:T(8,128)(2,1)S(1)} %collective-permute-done.1) | copy-start | bytes 786436
  68.5 10.4 %collective-permute-start.2 = (bf16[128,1024]{1,0:T(8,128)(2,1)S(1)}, bf16[128,1024]{1,0:T(8,128)(2,1)S(1)}, u32[]{:S(2)}, u32[]{:S(2)}) collective-permute-start(bf16[128,1024]{1,0:T(8,128)(2,1)S(1)} %collective-permute-done.1), channel_id=1, source_target_pairs={{0,4},{4,8},{8,12},{12,16},{16,20},{20,24},{24,28},{28,32},{32,36}... | collective-permute-start | bytes 786440 | tf_op jit(solution)/shard_map/ppermute | solution.py:71
  74.4 9.6 %all-to-all-start.3 = ((f32[4,2,128]{2,1,0:T(2,128)}), f32[4,2,128]{2,1,0:T(2,128)S(1)}, u32[]{:S(2)}, u32[]{:S(2)}) async-start(f32[4,2,128]{2,1,0:T(2,128)} %broadcast_in_dim.108), calls=%async_computation.3 | async-start | bytes 8192 | tf_op jit(solution)/shard_map/all_to_all | solution.py:176
  78.9 6.1 %copy-start.16 = (bf16[128,1024]{1,0:T(8,128)(2,1)}, bf16[128,1024]{1,0:T(8,128)(2,1)S(1)}, u32[]{:S(2)}) copy-start(bf16[128,1024]{1,0:T(8,128)(2,1)S(1)} %collective-permute-done.2) | copy-start | bytes 786436
  78.9 17.2 %collective-permute-start.3 = (bf16[128,1024]{1,0:T(8,128)(2,1)S(1)}, bf16[128,1024]{1,0:T(8,128)(2,1)}, u32[]{:S(2)}, u32[]{:S(2)}) collective-permute-start(bf16[128,1024]{1,0:T(8,128)(2,1)S(1)} %collective-permute-done.2), channel_id=1, source_target_pairs={{0,4},{4,8},{8,12},{12,16},{16,20},{20,24},{24,28},{28,32},{32,36}... | collective-permute-start | bytes 786440 | tf_op jit(solution)/shard_map/ppermute | solution.py:71
  84.5 0.7 copy-start.9
  85.9 11.3 %copy-start.17 = (bf16[128,1024]{1,0:T(8,128)(2,1)S(1)}, bf16[128,1024]{1,0:T(8,128)(2,1)}, u32[]{:S(2)}) copy-start(bf16[128,1024]{1,0:T(8,128)(2,1)} %copy-done.16) | copy-start | bytes 786436
  86.1 11.1 %copy-start.15 = (bf16[128,1024]{1,0:T(8,128)(2,1)S(1)}, bf16[128,1024]{1,0:T(8,128)(2,1)}, u32[]{:S(2)}) copy-start(bf16[128,1024]{1,0:T(8,128)(2,1)} %copy-done.14) | copy-start | bytes 786436
  88.2 42.6 %all-to-all-start.4 = ((bf16[32,2,1024]{2,1,0:T(2,128)(2,1)}), bf16[32,2,1024]{2,1,0:T(2,128)(2,1)}, u32[]{:S(2)}, u32[]{:S(2)}) async-start(bf16[32,2,1024]{2,1,0:T(2,128)(2,1)} %reshape.581), calls=%async_computation.4 | async-start | bytes 262144 | tf_op jit(solution)/shard_map/all_to_all | solution.py:58
  98.9 1.3 copy-start.21
  101.8 1.6 copy-start.24
  103.4 0.9 copy-start.20
  104.7 1.1 copy-start.1
  112.9 0.9 copy-start.13
  114.5 46.1 %collective-permute-start.5 = (bf16[128,1024]{1,0:T(8,128)(2,1)}, bf16[128,1024]{1,0:T(8,128)(2,1)}, u32[]{:S(2)}, u32[]{:S(2)}) collective-permute-start(bf16[128,1024]{1,0:T(8,128)(2,1)} %pad_maximum_fusion.2), channel_id=1, source_target_pairs={{8,0},{12,4},{16,8},{20,12},{24,16},{28,20},{32,24},{36,28},{40,32... | collective-permute-start | bytes 786440 | tf_op jit(solution)/shard_map/ppermute | solution.py:71
  120.9 40.7 %collective-permute-start.6 = (bf16[128,1024]{1,0:T(8,128)(2,1)}, bf16[128,1024]{1,0:T(8,128)(2,1)}, u32[]{:S(2)}, u32[]{:S(2)}) collective-permute-start(bf16[128,1024]{1,0:T(8,128)(2,1)} %pad_maximum_fusion.3), channel_id=1, source_target_pairs={{12,0},{16,4},{20,8},{24,12},{28,16},{32,20},{36,24},{40,28},{44,3... | collective-permute-start | bytes 786440 | tf_op jit(solution)/shard_map/ppermute | solution.py:71
  125.3 37.3 %collective-permute-start.7 = (bf16[128,1024]{1,0:T(8,128)(2,1)}, bf16[128,1024]{1,0:T(8,128)(2,1)}, u32[]{:S(2)}, u32[]{:S(2)}) collective-permute-start(bf16[128,1024]{1,0:T(8,128)(2,1)} %pad_maximum_fusion.4), channel_id=1, source_target_pairs={{16,0},{20,4},{24,8},{28,12},{32,16},{36,20},{40,24},{44,28},{48,3... | collective-permute-start | bytes 786440 | tf_op jit(solution)/shard_map/ppermute | solution.py:71
  136.4 8.0 %all-to-all-start.5 = ((bf16[4,2,1024]{2,1,0:T(2,128)(2,1)}), bf16[4,2,1024]{2,1,0:T(2,128)(2,1)}, u32[]{:S(2)}, u32[]{:S(2)}) async-start(bf16[4,2,1024]{2,1,0:T(2,128)(2,1)} %reshape.583), calls=%async_computation.5 | async-start | bytes 32768 | tf_op jit(solution)/shard_map/all_to_all | solution.py:47
  142.0 21.7 %collective-permute-start.4 = (bf16[128,1024]{1,0:T(8,128)(2,1)}, bf16[128,1024]{1,0:T(8,128)(2,1)}, u32[]{:S(2)}, u32[]{:S(2)}) collective-permute-start(bf16[128,1024]{1,0:T(8,128)(2,1)} %pad_maximum_fusion.1), channel_id=1, source_target_pairs={{4,0},{8,4},{12,8},{16,12},{20,16},{24,20},{28,24},{32,28},{36,32}... | collective-permute-start | bytes 786440 | tf_op jit(solution)/shard_map/ppermute | solution.py:71
  150.6 25.2 %all-to-all-start.6 = ((bf16[32,2,1024]{2,1,0:T(2,128)(2,1)}), bf16[32,2,1024]{2,1,0:T(2,128)(2,1)S(1)}, u32[]{:S(2)}, u32[]{:S(2)}) async-start(bf16[32,2,1024]{2,1,0:T(2,128)(2,1)} %reshape.585), calls=%async_computation.6 | async-start | bytes 262144 | tf_op jit(solution)/shard_map/all_to_all | solution.py:64
  164.6 12.0 %copy-start.5 = (bf16[128,512]{1,0:T(8,128)(2,1)S(1)}, bf16[128,512]{1,0:T(8,128)(2,1)}, u32[]{:S(2)}) copy-start(bf16[128,512]{1,0:T(8,128)(2,1)} %param.12) | copy-start | bytes 393220
  165.6 11.3 %copy-start.6 = (f32[4,128,128]{2,1,0:T(8,128)S(1)}, f32[4,128,128]{2,1,0:T(8,128)}, u32[]{:S(2)}) copy-start(f32[4,128,128]{2,1,0:T(8,128)} %fusion.85) | copy-start | bytes 786436
  165.6 11.3 %copy-start.8 = (bf16[128,512]{1,0:T(8,128)(2,1)S(1)}, bf16[128,512]{1,0:T(8,128)(2,1)}, u32[]{:S(2)}) copy-start(bf16[128,512]{1,0:T(8,128)(2,1)} %param.11) | copy-start | bytes 393220
  165.6 12.3 %copy-start.3 = (bf16[128,512]{1,0:T(8,128)(2,1)S(1)}, bf16[128,512]{1,0:T(8,128)(2,1)}, u32[]{:S(2)}) copy-start(bf16[128,512]{1,0:T(8,128)(2,1)} %param.10) | copy-start | bytes 393220
  165.6 12.3 %copy-start.10 = (bf16[4,128,128]{2,1,0:T(8,128)(2,1)S(1)}, bf16[4,128,128]{2,1,0:T(8,128)(2,1)}, u32[]{:S(2)}) copy-start(bf16[4,128,128]{2,1,0:T(8,128)(2,1)} %copy-done.9) | copy-start | bytes 393220
